TPU v7x, 128 devices: a whole 4x4x4 slice. The times are simulated.
128 devices in a mesh: gx: 8 (over y, core), gy: 16 (over x, z).
Axes of the slice: x: 4, y: 4, z: 4, core: 2. Of those that a mesh axis runs over, the one named last changes fastest.
Arguments:
- scalars: float32 [4, 512, 512, 128], P(None, 'gx', 'gy'), may hold values from -6 to 6
- velocity: float32 [3, 512, 512, 128], P(None, 'gx', 'gy'), may hold values from -12 to 12
- diffusivity: float32 [512, 512, 128], P('gx', 'gy'), may hold values from 0.05 to 0.6
- diff_scale: float32 [4], replicated, may hold values from 0.3 to 1
- basis_old: bfloat16 [48, 256, 16384], P(None, 'gx', 'gy'), may hold values from -5 to 5
- sing_values: float32 [48], replicated, may hold values from 0.5 to 2
- stored: bfloat16 [16, 256, 16384], P(None, 'gx', 'gy'), may hold values from -9 to 9
Outputs:
- scalars_out: float32 [4, 512, 512, 128], P(None, 'gx', 'gy')
- basis_new: float32 [65, 256, 16384], P(None, 'gx', 'gy')
- factor: float32 [65, 65], replicated
All inputs are finite; a program needn't handle non-finite values.
Results may differ from a plain program's by a relative error of at most 0.0003.
Values sent between devices are 32-bit elements; how exact they have to be, the bound alone decides.
No kernel may reach another device: no remote copies, remote signals or barrier semaphores. Data moves between devices by JAX's collectives and lax.ppermute only.
A program may use at most 192 MiB of HBM per device.

v0:
```python
import jax
import jax.numpy as jnp
from jax import lax
from jax.sharding import PartitionSpec as P
from jax.experimental import pallas as pl
from jax.experimental.pallas import tpu as pltpu

time_step = 0.25


def ring(axis):
    count = lax.axis_size(axis)
    forward = [(i, (i + 1) % count) for i in range(count)]
    backward = [(target, source) for source, target in forward]
    return forward, backward


def halo(block, width=2):
    fx, bx = ring("gx")
    fy, by = ring("gy")
    nx, ny = block.shape[1], block.shape[2]
    low_x = lax.ppermute(block[:, nx - width :], "gx", fx)
    high_x = lax.ppermute(block[:, :width], "gx", bx)
    low_y = lax.ppermute(block[:, :, ny - width :], "gy", fy)
    high_y = lax.ppermute(block[:, :, :width], "gy", by)
    rows = jnp.concatenate([low_x, block, high_x], axis=1)
    edge = ((0, 0), (width, width), (0, 0), (0, 0))
    return jnp.concatenate([jnp.pad(low_y, edge), rows, jnp.pad(high_y, edge)], axis=2)


def butterfly_sum(value):
    for axis in ("gx", "gy"):
        count = lax.axis_size(axis)
        bit = 1
        while bit < count:
            pairs = [(i, i ^ bit) for i in range(count)]
            value = value + lax.ppermute(value, axis, pairs)
            bit *= 2
    return value


def put_last_row(basis_ext, last):
    def body(_, last_ref, out_ref):
        out_ref[...] = last_ref[...]

    row = basis_ext.shape[0] - 1
    return pl.pallas_call(
        body,
        out_shape=jax.ShapeDtypeStruct(basis_ext.shape, basis_ext.dtype),
        grid=(1,),
        in_specs=[pl.BlockSpec(memory_space=pl.ANY), pl.BlockSpec(last.shape, lambda i: (0, 0, 0))],
        out_specs=pl.BlockSpec(last.shape, lambda i: (row, 0, 0)),
        input_output_aliases={0: 0},
    )(basis_ext, last)


def tendency(concen, coeffs, diff_scale):
    velocity = coeffs[:3]
    kappa = coeffs[3]
    center = concen[:, 2:-2, 2:-2, :]
    flux_first = velocity[0][None] * concen
    slope = (
        8.0 * (flux_first[:, 3:-1, 2:-2] - flux_first[:, 1:-3, 2:-2])
        - (flux_first[:, 4:, 2:-2] - flux_first[:, :-4, 2:-2])
    ) / 12.0
    flux_second = velocity[1][None] * concen
    slope = (
        slope
        + (
            8.0 * (flux_second[:, 2:-2, 3:-1] - flux_second[:, 2:-2, 1:-3])
            - (flux_second[:, 2:-2, 4:] - flux_second[:, 2:-2, :-4])
        )
        / 12.0
    )
    flux_third = jnp.pad(velocity[2][2:-2, 2:-2][None] * center, ((0, 0), (0, 0), (0, 0), (2, 2)))
    slope = (
        slope
        + (
            8.0 * (flux_third[..., 3:-1] - flux_third[..., 1:-3])
            - (flux_third[..., 4:] - flux_third[..., :-4])
        )
        / 12.0
    )
    kappa_mid = kappa[2:-2, 2:-2][None]
    spread = (kappa_mid + kappa[3:-1, 2:-2][None]) * 0.5 * (concen[:, 3:-1, 2:-2] - center) - (
        kappa_mid + kappa[1:-3, 2:-2][None]
    ) * 0.5 * (center - concen[:, 1:-3, 2:-2])
    spread = (
        spread
        + (kappa_mid + kappa[2:-2, 3:-1][None]) * 0.5 * (concen[:, 2:-2, 3:-1] - center)
        - (kappa_mid + kappa[2:-2, 1:-3][None]) * 0.5 * (center - concen[:, 2:-2, 1:-3])
    )
    kappa_pad = jnp.pad(kappa_mid, ((0, 0), (0, 0), (0, 0), (1, 1)))
    center_pad = jnp.pad(center, ((0, 0), (0, 0), (0, 0), (1, 1)))
    spread = (
        spread
        + (kappa_mid + kappa_pad[..., 2:]) * 0.5 * (center_pad[..., 2:] - center)
        - (kappa_mid + kappa_pad[..., :-2]) * 0.5 * (center - center_pad[..., :-2])
    )
    return center + time_step * (diff_scale[:, None, None, None] * spread - slope)


def stencil_body(scale_ref, conc_ref, coeff_ref, out_ref):
    s = pl.program_id(0)
    scale = scale_ref[s]
    rows = out_ref.shape[2]
    depth = out_ref.shape[3]
    lane = lax.broadcasted_iota(jnp.int32, (rows, depth), 1)

    def shifted(value, d):
        rolled = pltpu.roll(value, (-d) % depth, 1)
        keep = (lane + d >= 0) & (lane + d < depth)
        return jnp.where(keep, rolled, 0.0)

    def row(i, carry):
        def c(dx, dy):
            return conc_ref[0, i + 2 + dx, pl.ds(2 + dy, rows), :]

        def k(field, dx, dy):
            return coeff_ref[field, i + 2 + dx, pl.ds(2 + dy, rows), :]

        center = c(0, 0)

        def f1(d):
            return k(0, d, 0) * c(d, 0)

        slope = (8.0 * (f1(1) - f1(-1)) - (f1(2) - f1(-2))) / 12.0

        def f2(d):
            return k(1, 0, d) * c(0, d)

        slope = slope + (8.0 * (f2(1) - f2(-1)) - (f2(2) - f2(-2))) / 12.0
        f3 = k(2, 0, 0) * center
        slope = slope + (
            8.0 * (shifted(f3, 1) - shifted(f3, -1)) - (shifted(f3, 2) - shifted(f3, -2))
        ) / 12.0
        kmid = k(3, 0, 0)
        spread = (kmid + k(3, 1, 0)) * 0.5 * (c(1, 0) - center) - (kmid + k(3, -1, 0)) * 0.5 * (
            center - c(-1, 0)
        )
        spread = (
            spread
            + (kmid + k(3, 0, 1)) * 0.5 * (c(0, 1) - center)
            - (kmid + k(3, 0, -1)) * 0.5 * (center - c(0, -1))
        )
        spread = (
            spread
            + (kmid + shifted(kmid, 1)) * 0.5 * (shifted(center, 1) - center)
            - (kmid + shifted(kmid, -1)) * 0.5 * (center - shifted(center, -1))
        )
        out_ref[0, i] = center + time_step * (scale * spread - slope)
        return carry

    lax.fori_loop(0, out_ref.shape[1], row, 0)


def stencil_step(conc_pad, coeff_pad, scale):
    count, px, py, depth = conc_pad.shape
    nx, ny = px - 4, py - 4
    return pl.pallas_call(
        stencil_body,
        out_shape=jax.ShapeDtypeStruct((count, nx, ny, depth), jnp.float32),
        grid=(count,),
        in_specs=[
            pl.BlockSpec(memory_space=pltpu.SMEM),
            pl.BlockSpec((1, px, py, depth), lambda s: (s, 0, 0, 0)),
            pl.BlockSpec(coeff_pad.shape, lambda s: (0, 0, 0, 0)),
        ],
        out_specs=pl.BlockSpec((1, nx, ny, depth), lambda s: (s, 0, 0, 0)),
        compiler_params=pltpu.CompilerParams(vmem_limit_bytes=48 * 1024 * 1024),
        cost_estimate=pl.CostEstimate(
            flops=80 * count * nx * ny * depth,
            transcendentals=0,
            bytes_accessed=4 * (conc_pad.size + coeff_pad.size + count * nx * ny * depth),
        ),
    )(scale, conc_pad, coeff_pad)


def per_device(scalars, velocity, diffusivity, diff_scale, basis_old, sing_values, stored):
    rank = basis_old.shape[0]
    snaps = stored.shape[0]
    static = jnp.concatenate([basis_old, stored], 0)
    weight = jnp.concatenate([sing_values, jnp.ones((snaps,), jnp.float32)], 0)
    total_rows = static.shape[1] * static.shape[2] * lax.axis_size("gx") * lax.axis_size("gy")

    local_gram = lax.dot_general(
        static, static, (((1, 2), (1, 2)), ((), ())), preferred_element_type=jnp.float32
    )
    gram_static = butterfly_sum(local_gram) * (weight[:, None] * weight[None, :]) / total_rows
    lower_static = jnp.linalg.cholesky(gram_static)
    width = rank + snaps
    inv_static = lax.linalg.triangular_solve(
        lower_static, jnp.eye(width, dtype=jnp.float32), left_side=True, lower=True
    )
    mix = inv_static * weight[None, :]
    mix_ext = jnp.concatenate([mix, jnp.zeros((1, width), jnp.float32)], 0)
    basis_ext = lax.dot_general(
        mix_ext,
        static.astype(jnp.float32),
        (((1,), (0,)), ((), ())),
        precision=lax.Precision.HIGHEST,
    )

    coeffs = jnp.concatenate([velocity, diffusivity[None]], 0)
    first = halo(jnp.concatenate([scalars[:1], coeffs], 0))
    coeff_pad = first[1:]
    middle0 = stencil_step(first[:1], coeff_pad, diff_scale[:1])
    result0 = stencil_step(halo(middle0), coeff_pad, diff_scale[:1])

    coarse = result0[0, ::2]
    span, depth = coarse.shape[1], coarse.shape[2]
    pick_z = (jnp.arange(depth)[:, None] == 2 * jnp.arange(depth // 2)[None, :]).astype(jnp.float32)
    pick_y = (2 * jnp.arange(span // 2)[:, None] == jnp.arange(span)[None, :]).astype(jnp.float32)
    thin = jnp.einsum("ayz,zk->ayk", coarse, pick_z, precision=lax.Precision.HIGHEST)
    fresh = jnp.einsum("jy,ayk->ajk", pick_y, thin, precision=lax.Precision.HIGHEST).reshape(
        coarse.shape[0], -1
    )
    static_f32 = static.astype(jnp.float32)
    cross = jnp.sum(static_f32 * fresh[None], axis=(1, 2))
    self_dot = jnp.sum(fresh * fresh)
    moments = butterfly_sum(jnp.concatenate([cross, self_dot[None]], 0)) / total_rows
    cross_g = moments[:width] * weight
    self_g = moments[width]

    rest = halo(scalars[1:])
    middle_r = stencil_step(rest, coeff_pad, diff_scale[1:])
    result_r = stencil_step(halo(middle_r), coeff_pad, diff_scale[1:])
    result = jnp.concatenate([result0, result_r], 0)

    link = lax.linalg.triangular_solve(
        lower_static, cross_g[:, None], left_side=True, lower=True
    )[:, 0]
    corner = jnp.sqrt(self_g - jnp.sum(link * link))
    lower = jnp.zeros((width + 1, width + 1), jnp.float32)
    lower = lower.at[:width, :width].set(lower_static)
    lower = lower.at[width, :width].set(link)
    lower = lower.at[width, width].set(corner)

    along = jnp.sum(mix * link[:, None], axis=0)
    last = (fresh - jnp.sum(static_f32 * along[:, None, None], axis=0)) / corner
    basis_new = put_last_row(basis_ext, last.reshape((1,) + basis_ext.shape[1:]))
    return (result, basis_new, lower.T)


def solution(mesh):
    return jax.shard_map(
        per_device,
        mesh=mesh,
        in_specs=(
            P(None, "gx", "gy", None),
            P(None, "gx", "gy", None),
            P("gx", "gy", None),
            P(),
            P(None, "gx", "gy"),
            P(),
            P(None, "gx", "gy"),
        ),
        out_specs=(P(None, "gx", "gy", None), P(None, "gx", "gy"), P()),
        check_vma=False,
    )
```

profile of v0, /device:TPU:0, one launch (start us, length us, event | category | flops | bytes accessed | tf_op | source)
XLA Modules:
  0.0 213.9 jit_solution(10494357988155808969)
XLA Ops:
  0.6 3.7 %copy_dynamic-update-slice_fusion = bf16[64,32,1024]{2,0,1:T(8,128)(2,1)S(1)} fusion(bf16[48,32,1024]{2,1,0:T(8,128)(2,1)} %param.17), kind=kLoop, calls=%fused_computation.15 | loop fusion | bytes 6291456
  4.4 0.6 copy_dynamic-update-slice_fusion.1
  5.0 1.2 convolution_bitcast_fusion.1
  6.2 0.9 copy-done.3
  7.1 1.2 collective-permute-done.16
  8.3 1.7 collective-permute-start.17
  10.0 0.7 fusion.24
  10.8 1.4 collective-permute-done.17
  12.2 3.3 %collective-permute-start.18 = (f32[64,64]{0,1:T(8,128)S(1)}, f32[64,64]{0,1:T(8,128)S(1)}, u32[]{:S(2)}, u32[]{:S(2)}) collective-permute-start(f32[64,64]{0,1:T(8,128)S(1)} %add.84), channel_id=1, source_target_pairs={{0,64},{16,80},{32,96},{48,112},{64,0},{80,16},{96,32},{112,48},{1... | collective-permute-start | bytes 49160 | tf_op jit(solution)/shard_map/ppermute | solution.py:37
  15.5 0.7 pad_maximum_fusion.5
  16.3 3.0 %collective-permute-start.2 = (f32[5,2,32,128]{3,2,1,0:T(8,128)}, f32[5,2,32,128]{3,2,1,0:T(8,128)}, u32[]{:S(2)}, u32[]{:S(2)}) collective-permute-start(f32[5,2,32,128]{3,2,1,0:T(8,128)} %get-tuple-element.45), channel_id=1, source_target_pairs={{16,0},{32,16},{48,32},{64,48},{80,64},{96,80},{112,96},{0,112},{1... | collective-permute-start | bytes 491528 | tf_op jit(solution)/shard_map/ppermute | solution.py:23
  19.3 2.0 collective-permute-start.19
  21.3 1.1 pad_maximum_fusion.3
  22.5 0.8 collective-permute-done.19
  23.3 3.9 %collective-permute-start.20 = (f32[64,64]{0,1:T(8,128)S(1)}, f32[64,64]{0,1:T(8,128)S(1)}, u32[]{:S(2)}, u32[]{:S(2)}) collective-permute-start(f32[64,64]{0,1:T(8,128)S(1)} %add.86), channel_id=1, source_target_pairs={{0,2},{1,3},{2,0},{3,1},{4,6},{5,7},{6,4},{7,5},{8,10},{9,11},{10,... | collective-permute-start | bytes 49160 | tf_op jit(solution)/shard_map/ppermute | solution.py:37
  27.1 0.9 fusion.25
  28.0 5.1 %collective-permute-done.20 = f32[64,64]{0,1:T(8,128)S(1)} collective-permute-done((f32[64,64]{0,1:T(8,128)S(1)}, f32[64,64]{0,1:T(8,128)S(1)}, u32[]{:S(2)}, u32[]{:S(2)}) %collective-permute-start.20) | collective-permute-done | bytes 16416 | tf_op jit(solution)/shard_map/ppermute | solution.py:37
  33.2 1.1 collective-permute-start.21
  34.8 2.4 %collective-permute-done.21 = f32[64,64]{0,1:T(8,128)S(1)} collective-permute-done((f32[64,64]{0,1:T(8,128)S(1)}, f32[64,64]{0,1:T(8,128)S(1)}, u32[]{:S(2)}, u32[]{:S(2)}) %collective-permute-start.21) | collective-permute-done | bytes 16416 | tf_op jit(solution)/shard_map/ppermute | solution.py:37
  37.1 2.7 %collective-permute-start.22 = (f32[64,64]{0,1:T(8,128)S(1)}, f32[64,64]{0,1:T(8,128)S(1)}, u32[]{:S(2)}, u32[]{:S(2)}) collective-permute-start(f32[64,64]{0,1:T(8,128)S(1)} %add.88), channel_id=1, source_target_pairs={{0,8},{1,9},{2,10},{3,11},{4,12},{5,13},{6,14},{7,15},{8,0},{9,1},... | collective-permute-start | bytes 49160 | tf_op jit(solution)/shard_map/ppermute | solution.py:37
  40.4 2.1 %collective-permute-done.22 = f32[64,64]{0,1:T(8,128)S(1)} collective-permute-done((f32[64,64]{0,1:T(8,128)S(1)}, f32[64,64]{0,1:T(8,128)S(1)}, u32[]{:S(2)}, u32[]{:S(2)}) %collective-permute-start.22) | collective-permute-done | bytes 16416 | tf_op jit(solution)/shard_map/ppermute | solution.py:37
  42.6 2.1 collective-permute-start.3
  44.8 0.6 fusion.13
  45.4 6.6 %cholesky.17 = f32[64,64]{1,0:T(8,128)S(1)} custom-call(f32[64,64]{1,0:T(8,128)} %fusion.13), custom_call_target="Cholesky" | custom-call | tf_op jit(solution)/shard_map/jit(cholesky)/cholesky | solution.py:190
  52.1 4.4 %select_maximum_fusion = f32[5,68,36,128]{3,2,1,0:T(8,128)S(1)} fusion(f32[5,64,2,128]{3,2,1,0:T(2,128)} %collective-permute-done.3, f32[5,64,2,128]{3,2,1,0:T(2,128)S(1)} %collective-permute-done, f32[5,2,32,128]{3,2,1,0:T(8,128)} %collective-permute-done.2, f32[1,64,32,128]{3,2,1,0:T(8,128)} %bitcast.58, f32[3,64,32,128]{3,2,1,0:T(8,128)S(1)} %copy-done.5, ...), kind=kLoop, calls=%fused_computation.4 | loop fusion | flops 15667200 | bytes 12492800 | tf_op jit(solution)/shard_map/concatenate | solution.py:28
  56.6 2.8 %slice.177.coeff_ref = f32[4,68,36,128]{3,2,1,0:T(8,128)} slice(f32[5,68,36,128]{3,2,1,0:T(8,128)S(1)} %select_maximum_fusion), slice={[1:5], [0:68], [0:36], [0:128]} | slice | bytes 10027008 | tf_op jit(solution)/shard_map/slice | solution.py:206
  59.4 9.5 %shard_map.94 = f32[1,64,32,128]{3,2,1,0:T(8,128)S(1)} custom-call(f32[1]{0:T(128)S(1)} %bitcast.56, f32[1,68,36,128]{3,2,1,0:T(8,128)S(1)} %slice.176.conc_ref, f32[4,68,36,128]{3,2,1,0:T(8,128)} %slice.177.coeff_ref), custom_call_target="tpu_custom_call" | custom-call | flops 20971520 | bytes 7315456 | tf_op jit(solution)/shard_map/pallas_call | solution.py:160
  69.0 2.9 %collective-permute-start.6 = (f32[1,2,32,128]{3,2,1,0:T(8,128)S(1)}, f32[1,2,32,128]{3,2,1,0:T(8,128)S(1)}, u32[]{:S(2)}, u32[]{:S(2)}) collective-permute-start(f32[1,2,32,128]{3,2,1,0:T(8,128)S(1)} %get-tuple-element.57), channel_id=1, source_target_pairs={{16,0},{32,16},{48,32},{64,48},{80,64},{96,80},{112,96},{0,112},{1... | collective-permute-start | bytes 98312 | tf_op jit(solution)/shard_map/ppermute | solution.py:23
  72.0 5.3 %collective-permute-start.7 = (f32[1,64,2,128]{3,2,1,0:T(2,128)S(1)}, f32[1,64,2,128]{3,2,1,0:T(2,128)S(1)}, u32[]{:S(2)}, u32[]{:S(2)}) collective-permute-start(f32[1,64,2,128]{3,2,1,0:T(2,128)S(1)} %get-tuple-element.59), channel_id=1, source_target_pairs={{1,0},{2,1},{3,2},{4,3},{5,4},{6,5},{7,6},{8,7},{9,8},{10,9},{11,1... | collective-permute-start | bytes 196616 | tf_op jit(solution)/shard_map/ppermute | solution.py:25
  77.3 0.7 compare_reduce_fusion
  78.1 1.4 collective-permute-done.4
  79.5 3.9 %collective-permute-start.11 = (f32[3,64,2,128]{3,2,1,0:T(2,128)}, f32[3,64,2,128]{3,2,1,0:T(2,128)}, u32[]{:S(2)}, u32[]{:S(2)}) collective-permute-start(f32[3,64,2,128]{3,2,1,0:T(2,128)} %get-tuple-element.51), channel_id=1, source_target_pairs={{1,0},{2,1},{3,2},{4,3},{5,4},{6,5},{7,6},{8,7},{9,8},{10,9},{11,1... | collective-permute-start | bytes 589832 | tf_op jit(solution)/shard_map/ppermute | solution.py:25
  83.7 9.5 %shard_map.95 = f32[1,64,32,128]{3,2,1,0:T(8,128)S(1)} custom-call(f32[1]{0:T(128)S(1)} %bitcast.57, f32[1,68,36,128]{3,2,1,0:T(8,128)S(1)} %select_maximum_fusion.6.conc_ref, f32[4,68,36,128]{3,2,1,0:T(8,128)} %slice.177.coeff_ref), custom_call_target="tpu_custom_call" | custom-call | flops 20971520 | bytes 7315456 | tf_op jit(solution)/shard_map/pallas_call | solution.py:160
  93.2 1.0 copy-done
  94.6 0.9 multiply_reduce_fusion
  95.7 3.3 %fusion = f32[64]{0:T(128)S(1)} fusion(bf16[64,32,1024]{2,0,1:T(8,128)(2,1)} %copy-done.3, f32[32,1024]{1,0:T(8,128)S(1)} %mul.85), kind=kLoop, calls=%fused_computation.2 | loop fusion | flops 6291392 | bytes 4325632 | tf_op jit(solution)/shard_map/reduce_sum | solution.py:219
  99.0 0.7 pad_maximum_fusion.6
  99.8 0.6 select_bitcast_fusion
  100.9 0.7 fusion.35
  101.7 5.5 %custom-call.8 = f32[1,64,64]{1,2,0:T(8,128)} custom-call(f32[1,64,64]{2,1,0:T(8,128)S(1)} %get-tuple-element.42), custom_call_target="InvertDiagBlocksLowerTriangular" | custom-call | tf_op jit(solution)/shard_map/triangular_solve | solution.py:192
  107.2 0.6 scatter.10
  107.8 1.7 collective-permute-start.25
  109.5 3.8 %select_maximum_fusion.4.conc_ref = f32[3,68,36,128]{3,2,1,0:T(8,128)} fusion(f32[3,64,2,128]{3,2,1,0:T(2,128)} %collective-permute-done.11, f32[3,64,2,128]{3,2,1,0:T(2,128)} %collective-permute-done.8, f32[3,2,32,128]{3,2,1,0:T(8,128)} %collective-permute-done.10, f32[3,64,32,128]{3,2,1,0:T(8,128)S(1)} %slice-done, f32[3,2,32,128]{3,2,1,0:T(8,128)} %collective-permute-done.9), kind=kLoop, calls=%fused_computation.11 | loop fusion | flops 7520256 | bytes 7495680 | tf_op jit(solution)/shard_map/concatenate | solution.py:28
  113.4 23.8 %shard_map.96 = f32[3,64,32,128]{3,2,1,0:T(8,128)S(1)} custom-call(f32[3]{0:T(128)S(1)} %slice.163.scale_ref, f32[3,68,36,128]{3,2,1,0:T(8,128)} %select_maximum_fusion.4.conc_ref, f32[4,68,36,128]{3,2,1,0:T(8,128)} %slice.177.coeff_ref), custom_call_target="tpu_custom_call" | custom-call | flops 62914560 | bytes 11919360 | tf_op jit(solution)/shard_map/pallas_call | solution.py:160
  137.4 0.9 fusion.27
  138.3 4.2 %collective-permute-done.27 = f32[65]{0:T(128)S(1)} collective-permute-done((f32[65]{0:T(128)S(1)}, f32[65]{0:T(128)S(1)}, u32[]{:S(2)}, u32[]{:S(2)}) %collective-permute-start.27) | collective-permute-done | bytes 292 | tf_op jit(solution)/shard_map/ppermute | solution.py:37
  142.5 0.7 fusion.26
  143.1 3.0 %collective-permute-start.14 = (f32[3,2,32,128]{3,2,1,0:T(8,128)}, f32[3,2,32,128]{3,2,1,0:T(8,128)}, u32[]{:S(2)}, u32[]{:S(2)}) collective-permute-start(f32[3,2,32,128]{3,2,1,0:T(8,128)} %get-tuple-element.53), channel_id=1, source_target_pairs={{16,0},{32,16},{48,32},{64,48},{80,64},{96,80},{112,96},{0,112},{1... | collective-permute-start | bytes 294920 | tf_op jit(solution)/shard_map/ppermute | solution.py:23
  146.1 1.4 collective-permute-start.29
  147.5 1.4 collective-permute-start.12
  148.9 4.0 %collective-permute-start.15 = (f32[3,64,2,128]{3,2,1,0:T(2,128)}, f32[3,64,2,128]{3,2,1,0:T(2,128)}, u32[]{:S(2)}, u32[]{:S(2)}) collective-permute-start(f32[3,64,2,128]{3,2,1,0:T(2,128)} %get-tuple-element.55), channel_id=1, source_target_pairs={{1,0},{2,1},{3,2},{4,3},{5,4},{6,5},{7,6},{8,7},{9,8},{10,9},{11,1... | collective-permute-start | bytes 589832 | tf_op jit(solution)/shard_map/ppermute | solution.py:25
  153.0 0.6 add_multiply_fusion
  153.6 0.6 slice.175
  154.2 1.5 multiply_reduce_fusion.2
  157.0 1.2 multiply_reduce_fusion.1
  158.3 3.6 %fusion.1 = f32[32,1024]{1,0:T(8,128)S(1)} fusion(bf16[64,32,1024]{2,0,1:T(8,128)(2,1)} %copy-done.3, f32[64]{0:T(128)S(1)} %get-tuple-element.62), kind=kLoop, calls=%fused_computation.3 | loop fusion | flops 6258688 | bytes 4325632 | tf_op jit(solution)/shard_map/reduce_sum | solution.py:240
  161.8 6.4 %fusion.8 = f32[65,32,1024]{2,0,1:T(8,128)} fusion(bf16[64,32,1024]{2,0,1:T(8,128)(2,1)S(1)} %copy-done.4, f32[64,64]{0,1:T(8,128)S(1)} %get-tuple-element.63), kind=kOutput, calls=%fused_computation.37 | convolution fusion | flops 1635778560 | bytes 12730368 | tf_op jit(solution)/shard_map/dot_general | solution.py:197
  168.2 0.7 fusion.5.last_ref
  169.4 0.7 copy.17
  170.1 12.0 %copy.16._ = f32[65,32,1024]{2,1,0:T(8,128)} copy(f32[65,32,1024]{2,0,1:T(8,128)} %fusion.8) | data formatting | bytes 17039360 | tf_op jit(solution)/shard_map/dot_general | solution.py:197
  182.1 1.6 shard_map.98
  183.7 3.8 %select_maximum_fusion.2.conc_ref = f32[3,68,36,128]{3,2,1,0:T(8,128)} fusion(f32[3,64,2,128]{3,2,1,0:T(2,128)} %collective-permute-done.15, f32[3,64,2,128]{3,2,1,0:T(2,128)} %collective-permute-done.12, f32[3,2,32,128]{3,2,1,0:T(8,128)} %collective-permute-done.14, f32[3,64,32,128]{3,2,1,0:T(8,128)S(1)} %shard_map.96, ...), kind=kLoop, calls=%fused_computation.9 | loop fusion | flops 7520256 | bytes 7495680 | tf_op jit(solution)/shard_map/concatenate | solution.py:28
  187.5 23.9 %shard_map.97 = f32[3,64,32,128]{3,2,1,0:T(8,128)S(1)} custom-call(f32[3]{0:T(128)S(1)} %slice.163.scale_ref, f32[3,68,36,128]{3,2,1,0:T(8,128)} %select_maximum_fusion.2.conc_ref, f32[4,68,36,128]{3,2,1,0:T(8,128)} %slice.177.coeff_ref), custom_call_target="tpu_custom_call" | custom-call | flops 62914560 | bytes 11919360 | tf_op jit(solution)/shard_map/pallas_call | solution.py:160
  211.4 2.5 %pad_maximum_fusion = f32[4,64,32,128]{3,2,1,0:T(8,128)} fusion(f32[3,64,32,128]{3,2,1,0:T(8,128)S(1)} %shard_map.97, f32[1,64,32,128]{3,2,1,0:T(8,128)S(1)} %copy-done.1), kind=kLoop, calls=%fused_computation.8 | loop fusion | flops 1048576 | bytes 8388608 | tf_op jit(solution)/shard_map/concatenate | solution.py:228
  (96 shorter events, 3.9 us)
Async XLA Ops:
  0.6 3.7 %copy-start.9 = (bf16[16,32,1024]{2,1,0:T(8,128)(2,1)S(1)}, bf16[16,32,1024]{2,1,0:T(8,128)(2,1)}, u32[]{:S(2)}) copy-start(bf16[16,32,1024]{2,1,0:T(8,128)(2,1)} %param.19) | copy-start | bytes 3145732
  5.0 2.1 copy-start.3
  5.0 5.0 %copy-start.7 = (f32[4,64,32,128]{3,2,1,0:T(8,128)S(1)}, f32[4,64,32,128]{3,2,1,0:T(8,128)}, u32[]{:S(2)}) copy-start(f32[4,64,32,128]{3,2,1,0:T(8,128)} %param.13) | copy-start | bytes 12582916
  5.0 10.6 %copy-start.5 = (f32[3,64,32,128]{3,2,1,0:T(8,128)S(1)}, f32[3,64,32,128]{3,2,1,0:T(8,128)}, u32[]{:S(2)}) copy-start(f32[3,64,32,128]{3,2,1,0:T(8,128)} %param.14) | copy-start | bytes 9437188
  5.0 10.5 %copy-start.8 = (f32[64,32,128]{2,1,0:T(8,128)S(1)}, f32[64,32,128]{2,1,0:T(8,128)}, u32[]{:S(2)}) copy-start(f32[64,32,128]{2,1,0:T(8,128)} %param.15) | copy-start | bytes 3145732
  7.1 1.2 collective-permute-start.16
  8.3 3.9 %collective-permute-start.17 = (f32[64,64]{0,1:T(8,128)S(1)}, f32[64,64]{0,1:T(8,128)S(1)}, u32[]{:S(2)}, u32[]{:S(2)}) collective-permute-start(f32[64,64]{0,1:T(8,128)S(1)} %add.83), channel_id=1, source_target_pairs={{0,32},{16,48},{32,0},{48,16},{64,96},{80,112},{96,64},{112,80},{1... | collective-permute-start | bytes 49160 | tf_op jit(solution)/shard_map/ppermute | solution.py:37
  10.7 98.8 %collective-permute-start.9 = (f32[3,2,32,128]{3,2,1,0:T(8,128)}, f32[3,2,32,128]{3,2,1,0:T(8,128)}, u32[]{:S(2)}, u32[]{:S(2)}) collective-permute-start(f32[3,2,32,128]{3,2,1,0:T(8,128)} %get-tuple-element.48), channel_id=1, source_target_pairs={{0,16},{16,32},{32,48},{48,64},{64,80},{80,96},{96,112},{112,0},{1... | collective-permute-start | bytes 294920 | tf_op jit(solution)/shard_map/ppermute | solution.py:22
  10.8 11.6 %copy-start.6 = (f32[1,64,32,128]{3,2,1,0:T(8,128)}, f32[1,64,32,128]{3,2,1,0:T(8,128)S(1)}, u32[]{:S(2)}) copy-start(f32[1,64,32,128]{3,2,1,0:T(8,128)S(1)} %slice.152) | copy-start | bytes 3145732
  12.2 7.0 %collective-permute-start.18 = (f32[64,64]{0,1:T(8,128)S(1)}, f32[64,64]{0,1:T(8,128)S(1)}, u32[]{:S(2)}, u32[]{:S(2)}) collective-permute-start(f32[64,64]{0,1:T(8,128)S(1)} %add.84), channel_id=1, source_target_pairs={{0,64},{16,80},{32,96},{48,112},{64,0},{80,16},{96,32},{112,48},{1... | collective-permute-start | bytes 49160 | tf_op jit(solution)/shard_map/ppermute | solution.py:37
  16.3 35.8 %collective-permute-start.1 = (f32[5,2,32,128]{3,2,1,0:T(8,128)}, f32[5,2,32,128]{3,2,1,0:T(8,128)}, u32[]{:S(2)}, u32[]{:S(2)}) collective-permute-start(f32[5,2,32,128]{3,2,1,0:T(8,128)} %get-tuple-element.44), channel_id=1, source_target_pairs={{0,16},{16,32},{32,48},{48,64},{64,80},{80,96},{96,112},{112,0},{1... | collective-permute-start | bytes 491528 | tf_op jit(solution)/shard_map/ppermute | solution.py:22
  16.3 35.8 %collective-permute-start.2 = (f32[5,2,32,128]{3,2,1,0:T(8,128)}, f32[5,2,32,128]{3,2,1,0:T(8,128)}, u32[]{:S(2)}, u32[]{:S(2)}) collective-permute-start(f32[5,2,32,128]{3,2,1,0:T(8,128)} %get-tuple-element.45), channel_id=1, source_target_pairs={{16,0},{32,16},{48,32},{64,48},{80,64},{96,80},{112,96},{0,112},{1... | collective-permute-start | bytes 491528 | tf_op jit(solution)/shard_map/ppermute | solution.py:23
  19.3 4.0 %collective-permute-start.19 = (f32[64,64]{0,1:T(8,128)S(1)}, f32[64,64]{0,1:T(8,128)S(1)}, u32[]{:S(2)}, u32[]{:S(2)}) collective-permute-start(f32[64,64]{0,1:T(8,128)S(1)} %add.85), channel_id=1, source_target_pairs={{0,1},{1,0},{2,3},{3,2},{4,5},{5,4},{6,7},{7,6},{8,9},{9,8},{10,11... | collective-permute-start | bytes 49160 | tf_op jit(solution)/shard_map/ppermute | solution.py:37
  22.3 18.0 %copy-start.2 = (f32[4]{0:T(128)S(1)}, f32[4]{0:T(128)}, u32[]{:S(2)}) copy-start(f32[4]{0:T(128)} %param.16) | copy-start | bytes 52
  22.3 18.1 %copy-start.13 = (f32[48]{0:T(128)S(1)}, f32[48]{0:T(128)}, u32[]{:S(2)}) copy-start(f32[48]{0:T(128)} %param.18) | copy-start | bytes 580
  22.3 29.7 %collective-permute-start = (f32[5,64,2,128]{3,2,1,0:T(2,128)}, f32[5,64,2,128]{3,2,1,0:T(2,128)S(1)}, u32[]{:S(2)}, u32[]{:S(2)}) collective-permute-start(f32[5,64,2,128]{3,2,1,0:T(2,128)} %get-tuple-element.46), channel_id=1, source_target_pairs={{0,1},{1,2},{2,3},{3,4},{4,5},{5,6},{6,7},{7,8},{8,9},{9,10},{10,1... | collective-permute-start | bytes 983048 | tf_op jit(solution)/shard_map/ppermute | solution.py:24
  23.3 9.9 %collective-permute-start.20 = (f32[64,64]{0,1:T(8,128)S(1)}, f32[64,64]{0,1:T(8,128)S(1)}, u32[]{:S(2)}, u32[]{:S(2)}) collective-permute-start(f32[64,64]{0,1:T(8,128)S(1)} %add.86), channel_id=1, source_target_pairs={{0,2},{1,3},{2,0},{3,1},{4,6},{5,7},{6,4},{7,5},{8,10},{9,11},{10,... | collective-permute-start | bytes 49160 | tf_op jit(solution)/shard_map/ppermute | solution.py:37
  33.2 3.9 %collective-permute-start.21 = (f32[64,64]{0,1:T(8,128)S(1)}, f32[64,64]{0,1:T(8,128)S(1)}, u32[]{:S(2)}, u32[]{:S(2)}) collective-permute-start(f32[64,64]{0,1:T(8,128)S(1)} %add.87), channel_id=1, source_target_pairs={{0,4},{1,5},{2,6},{3,7},{4,0},{5,1},{6,2},{7,3},{8,12},{9,13},{10,... | collective-permute-start | bytes 49160 | tf_op jit(solution)/shard_map/ppermute | solution.py:37
  37.1 5.4 %collective-permute-start.22 = (f32[64,64]{0,1:T(8,128)S(1)}, f32[64,64]{0,1:T(8,128)S(1)}, u32[]{:S(2)}, u32[]{:S(2)}) collective-permute-start(f32[64,64]{0,1:T(8,128)S(1)} %add.88), channel_id=1, source_target_pairs={{0,8},{1,9},{2,10},{3,11},{4,12},{5,13},{6,14},{7,15},{8,0},{9,1},... | collective-permute-start | bytes 49160 | tf_op jit(solution)/shard_map/ppermute | solution.py:37
  42.6 9.5 %collective-permute-start.3 = (f32[5,64,2,128]{3,2,1,0:T(2,128)}, f32[5,64,2,128]{3,2,1,0:T(2,128)}, u32[]{:S(2)}, u32[]{:S(2)}) collective-permute-start(f32[5,64,2,128]{3,2,1,0:T(2,128)} %get-tuple-element.47), channel_id=1, source_target_pairs={{1,0},{2,1},{3,2},{4,3},{5,4},{6,5},{7,6},{8,7},{9,8},{10,9},{11,1... | collective-permute-start | bytes 983048 | tf_op jit(solution)/shard_map/ppermute | solution.py:25
  52.0 4.5 %copy-start.11 = (f32[64,64]{1,0:T(8,128)}, f32[64,64]{1,0:T(8,128)S(1)}, u32[]{:S(2)}) copy-start(f32[64,64]{1,0:T(8,128)S(1)} %cholesky.17) | copy-start | bytes 49156
  69.0 9.0 %collective-permute-start.5 = (f32[1,2,32,128]{3,2,1,0:T(8,128)S(1)}, f32[1,2,32,128]{3,2,1,0:T(8,128)S(1)}, u32[]{:S(2)}, u32[]{:S(2)}) collective-permute-start(f32[1,2,32,128]{3,2,1,0:T(8,128)S(1)} %get-tuple-element.56), channel_id=1, source_target_pairs={{0,16},{16,32},{32,48},{48,64},{64,80},{80,96},{96,112},{112,0},{1... | collective-permute-start | bytes 98312 | tf_op jit(solution)/shard_map/ppermute | solution.py:22
  69.0 9.0 %collective-permute-start.6 = (f32[1,2,32,128]{3,2,1,0:T(8,128)S(1)}, f32[1,2,32,128]{3,2,1,0:T(8,128)S(1)}, u32[]{:S(2)}, u32[]{:S(2)}) collective-permute-start(f32[1,2,32,128]{3,2,1,0:T(8,128)S(1)} %get-tuple-element.57), channel_id=1, source_target_pairs={{16,0},{32,16},{48,32},{64,48},{80,64},{96,80},{112,96},{0,112},{1... | collective-permute-start | bytes 98312 | tf_op jit(solution)/shard_map/ppermute | solution.py:23
  72.0 7.6 %collective-permute-start.4 = (f32[1,64,2,128]{3,2,1,0:T(2,128)S(1)}, f32[1,64,2,128]{3,2,1,0:T(2,128)S(1)}, u32[]{:S(2)}, u32[]{:S(2)}) collective-permute-start(f32[1,64,2,128]{3,2,1,0:T(2,128)S(1)} %get-tuple-element.58), channel_id=1, source_target_pairs={{0,1},{1,2},{2,3},{3,4},{4,5},{5,6},{6,7},{7,8},{8,9},{9,10},{10,1... | collective-permute-start | bytes 196616 | tf_op jit(solution)/shard_map/ppermute | solution.py:24
  72.0 11.5 %collective-permute-start.7 = (f32[1,64,2,128]{3,2,1,0:T(2,128)S(1)}, f32[1,64,2,128]{3,2,1,0:T(2,128)S(1)}, u32[]{:S(2)}, u32[]{:S(2)}) collective-permute-start(f32[1,64,2,128]{3,2,1,0:T(2,128)S(1)} %get-tuple-element.59), channel_id=1, source_target_pairs={{1,0},{2,1},{3,2},{4,3},{5,4},{6,5},{7,6},{8,7},{9,8},{10,9},{11,1... | collective-permute-start | bytes 196616 | tf_op jit(solution)/shard_map/ppermute | solution.py:25
  78.0 31.5 %collective-permute-start.10 = (f32[3,2,32,128]{3,2,1,0:T(8,128)}, f32[3,2,32,128]{3,2,1,0:T(8,128)}, u32[]{:S(2)}, u32[]{:S(2)}) collective-permute-start(f32[3,2,32,128]{3,2,1,0:T(8,128)} %get-tuple-element.49), channel_id=1, source_target_pairs={{16,0},{32,16},{48,32},{64,48},{80,64},{96,80},{112,96},{0,112},{1... | collective-permute-start | bytes 294920 | tf_op jit(solution)/shard_map/ppermute | solution.py:23
  78.0 31.5 %collective-permute-start.8 = (f32[3,64,2,128]{3,2,1,0:T(2,128)}, f32[3,64,2,128]{3,2,1,0:T(2,128)}, u32[]{:S(2)}, u32[]{:S(2)}) collective-permute-start(f32[3,64,2,128]{3,2,1,0:T(2,128)} %get-tuple-element.50), channel_id=1, source_target_pairs={{0,1},{1,2},{2,3},{3,4},{4,5},{5,6},{6,7},{7,8},{8,9},{9,10},{10,1... | collective-permute-start | bytes 589832 | tf_op jit(solution)/shard_map/ppermute | solution.py:24
  79.5 30.0 %collective-permute-start.11 = (f32[3,64,2,128]{3,2,1,0:T(2,128)}, f32[3,64,2,128]{3,2,1,0:T(2,128)}, u32[]{:S(2)}, u32[]{:S(2)}) collective-permute-start(f32[3,64,2,128]{3,2,1,0:T(2,128)} %get-tuple-element.51), channel_id=1, source_target_pairs={{1,0},{2,1},{3,2},{4,3},{5,4},{6,5},{7,6},{8,7},{9,8},{10,9},{11,1... | collective-permute-start | bytes 589832 | tf_op jit(solution)/shard_map/ppermute | solution.py:25
  83.7 10.5 %copy-start.14 = (s32[64]{0:T(128)S(1)}, s32[64]{0:T(128)}, u32[]{:S(2)}) copy-start(s32[64]{0:T(128)} %iota_multiply_fusion.1) | copy-start | bytes 772
  83.7 10.9 %copy-start.15 = (s32[16]{0:T(128)S(1)}, s32[16]{0:T(128)}, u32[]{:S(2)}) copy-start(s32[16]{0:T(128)} %iota_multiply_fusion) | copy-start | bytes 196
  93.2 1.0 copy-start
  94.2 15.3 %slice-start = ((f32[4,64,32,128]{3,2,1,0:T(8,128)}), f32[3,64,32,128]{3,2,1,0:T(8,128)S(1)}, s32[]{:S(2)}) async-start(f32[4,64,32,128]{3,2,1,0:T(8,128)} %param.13), calls=%async_computation | async-start | bytes 6291456 | tf_op jit(solution)/shard_map/slice | solution.py:225
  95.7 4.1 %copy-start.12 = (f32[64,64]{1,0:T(8,128)S(1)}, f32[64,64]{1,0:T(8,128)}, u32[]{:S(2)}) copy-start(f32[64,64]{1,0:T(8,128)} %copy-done.11) | copy-start | bytes 49156
  99.8 1.2 collective-permute-start.23
  101.7 6.2 %collective-permute-start.24 = (f32[65]{0:T(128)S(1)}, f32[65]{0:T(128)S(1)}, u32[]{:S(2)}, u32[]{:S(2)}) collective-permute-start(f32[65]{0:T(128)S(1)} %fusion.35), channel_id=1, source_target_pairs={{0,32},{16,48},{32,0},{48,16},{64,96},{80,112},{96,64},{112,80},{1... | collective-permute-start | bytes 788 | tf_op jit(solution)/shard_map/ppermute | solution.py:37
  107.8 5.5 %collective-permute-start.25 = (f32[65]{0:T(128)S(1)}, f32[65]{0:T(128)S(1)}, u32[]{:S(2)}, u32[]{:S(2)}) collective-permute-start(f32[65]{0:T(128)S(1)} %add.92), channel_id=1, source_target_pairs={{0,64},{16,80},{32,96},{48,112},{64,0},{80,16},{96,32},{112,48},{1... | collective-permute-start | bytes 788 | tf_op jit(solution)/shard_map/ppermute | solution.py:37
  113.3 23.9 %collective-permute-start.26 = (f32[65]{0:T(128)S(1)}, f32[65]{0:T(128)S(1)}, u32[]{:S(2)}, u32[]{:S(2)}) collective-permute-start(f32[65]{0:T(128)S(1)} %add.93), channel_id=1, source_target_pairs={{0,1},{1,0},{2,3},{3,2},{4,5},{5,4},{6,7},{7,6},{8,9},{9,8},{10,11... | collective-permute-start | bytes 788 | tf_op jit(solution)/shard_map/ppermute | solution.py:37
  137.3 5.2 %collective-permute-start.27 = (f32[65]{0:T(128)S(1)}, f32[65]{0:T(128)S(1)}, u32[]{:S(2)}, u32[]{:S(2)}) collective-permute-start(f32[65]{0:T(128)S(1)} %add.94), channel_id=1, source_target_pairs={{0,2},{1,3},{2,0},{3,1},{4,6},{5,7},{6,4},{7,5},{8,10},{9,11},{10,... | collective-permute-start | bytes 788 | tf_op jit(solution)/shard_map/ppermute | solution.py:37
  142.5 3.6 %collective-permute-start.28 = (f32[65]{0:T(128)S(1)}, f32[65]{0:T(128)S(1)}, u32[]{:S(2)}, u32[]{:S(2)}) collective-permute-start(f32[65]{0:T(128)S(1)} %add.95), channel_id=1, source_target_pairs={{0,4},{1,5},{2,6},{3,7},{4,0},{5,1},{6,2},{7,3},{8,12},{9,13},{10,... | collective-permute-start | bytes 788 | tf_op jit(solution)/shard_map/ppermute | solution.py:37
  143.1 40.6 %collective-permute-start.13 = (f32[3,2,32,128]{3,2,1,0:T(8,128)}, f32[3,2,32,128]{3,2,1,0:T(8,128)}, u32[]{:S(2)}, u32[]{:S(2)}) collective-permute-start(f32[3,2,32,128]{3,2,1,0:T(8,128)} %get-tuple-element.52), channel_id=1, source_target_pairs={{0,16},{16,32},{32,48},{48,64},{64,80},{80,96},{96,112},{112,0},{1... | collective-permute-start | bytes 294920 | tf_op jit(solution)/shard_map/ppermute | solution.py:22
  143.1 40.6 %collective-permute-start.14 = (f32[3,2,32,128]{3,2,1,0:T(8,128)}, f32[3,2,32,128]{3,2,1,0:T(8,128)}, u32[]{:S(2)}, u32[]{:S(2)}) collective-permute-start(f32[3,2,32,128]{3,2,1,0:T(8,128)} %get-tuple-element.53), channel_id=1, source_target_pairs={{16,0},{32,16},{48,32},{64,48},{80,64},{96,80},{112,96},{0,112},{1... | collective-permute-start | bytes 294920 | tf_op jit(solution)/shard_map/ppermute | solution.py:23
  146.1 6.9 %collective-permute-start.29 = (f32[65]{0:T(128)S(1)}, f32[65]{0:T(128)}, u32[]{:S(2)}, u32[]{:S(2)}) collective-permute-start(f32[65]{0:T(128)S(1)} %add.96), channel_id=1, source_target_pairs={{0,8},{1,9},{2,10},{3,11},{4,12},{5,13},{6,14},{7,15},{8,0},{9,1},... | collective-permute-start | bytes 788 | tf_op jit(solution)/shard_map/ppermute | solution.py:37
  147.5 36.2 %collective-permute-start.12 = (f32[3,64,2,128]{3,2,1,0:T(2,128)}, f32[3,64,2,128]{3,2,1,0:T(2,128)}, u32[]{:S(2)}, u32[]{:S(2)}) collective-permute-start(f32[3,64,2,128]{3,2,1,0:T(2,128)} %get-tuple-element.54), channel_id=1, source_target_pairs={{0,1},{1,2},{2,3},{3,4},{4,5},{5,6},{6,7},{7,8},{8,9},{9,10},{10,1... | collective-permute-start | bytes 589832 | tf_op jit(solution)/shard_map/ppermute | solution.py:24
  148.9 34.8 %collective-permute-start.15 = (f32[3,64,2,128]{3,2,1,0:T(2,128)}, f32[3,64,2,128]{3,2,1,0:T(2,128)}, u32[]{:S(2)}, u32[]{:S(2)}) collective-permute-start(f32[3,64,2,128]{3,2,1,0:T(2,128)} %get-tuple-element.55), channel_id=1, source_target_pairs={{1,0},{2,1},{3,2},{4,3},{5,4},{6,5},{7,6},{8,7},{9,8},{10,9},{11,1... | collective-permute-start | bytes 589832 | tf_op jit(solution)/shard_map/ppermute | solution.py:25
  157.0 4.8 %copy-start.4 = (bf16[64,32,1024]{2,0,1:T(8,128)(2,1)S(1)}, bf16[64,32,1024]{2,0,1:T(8,128)(2,1)}, u32[]{:S(2)}) copy-start(bf16[64,32,1024]{2,0,1:T(8,128)(2,1)} %copy-done.3) | copy-start | bytes 12582916
  161.8 7.1 %copy-start.10 = (f32[65,65]{1,0:T(8,128)S(1)}, f32[65,65]{1,0:T(8,128)}, u32[]{:S(2)}) copy-start(f32[65,65]{1,0:T(8,128)} %scatter.10) | copy-start | bytes 50704
  187.5 23.9 %copy-start.1 = (f32[1,64,32,128]{3,2,1,0:T(8,128)S(1)}, f32[1,64,32,128]{3,2,1,0:T(8,128)}, u32[]{:S(2)}) copy-start(f32[1,64,32,128]{3,2,1,0:T(8,128)} %copy-done) | copy-start | bytes 3145732
where the time goes:
time: 214 us
  Pallas kernels  68.3 us (32%)
  starting transfers between devices  43.6 us (20%)
  other arithmetic  41.3 us (19%)
  local copies, waits for them, and re-layouts  27.3 us (13%)
  waiting for transfers between devices  19.3 us (9%)
  matrix products  11.7 us (5%)
  between operations  2.42 us (1%)
    pallas_call x4, Pallas kernels, stencil_step(): pl.pallas_call(stencil_body, out_shape=jax.ShapeDtypeStruct((count, nx, n...  66.7 us
    ppermute x14, starting transfers between devices, butterfly_sum(): value = value + lax.ppermute(value, axis, pairs)  17.9 us
    ppermute x14, waiting for transfers between devices, butterfly_sum(): value = value + lax.ppermute(value, axis, pairs)  17.8 us
    ppermute x4, starting transfers between devices, halo(): high_y = lax.ppermute(block[:, :, :width], 'gy', by)  15.2 us
    concatenate x4, other arithmetic, halo(): jnp.concatenate([jnp.pad(low_y, edge), rows, jnp.pad(high_y, edge)], axis=2)  12.2 us
    dot_general x1, local copies, waits for them, and re-layouts, per_device(): lax.dot_general(mix_ext, static.astype(jnp.float32), (((1,), (0,)), ((),...  12 us
    ppermute x4, starting transfers between devices, halo(): high_x = lax.ppermute(block[:, :width], 'gx', bx)  8.85 us
    another operation x3, other arithmetic, per_device(): lower_static = jnp.linalg.cholesky(gram_static)  7.33 us
  transfers between devices with their start and end apart: 30, of which 9 were waited for; matrix products, arithmetic and copies ran while one was open for 31% of the time, Pallas kernels for 21%

commit v1 on v0

--- a/solution.py
+++ b/solution.py
@@ -176,6 +176,43 @@
     )(scale, conc_pad, coeff_pad)
 
 
+def basis_body(mix_ref, xt_ref, out_ref):
+    for a in range(xt_ref.shape[0]):
+        xa = xt_ref[a]
+        res = jnp.dot(mix_ref[0], xa, preferred_element_type=jnp.float32)
+        res = res + jnp.dot(mix_ref[1], xa, preferred_element_type=jnp.float32)
+        res = res + jnp.dot(mix_ref[2], xa, preferred_element_type=jnp.float32)
+        out_ref[:, a, :] = res
+
+
+def basis_rows(mix_ext, static):
+    hi = lax.reduce_precision(mix_ext, exponent_bits=8, mantissa_bits=7)
+    rem = mix_ext - hi
+    mid = lax.reduce_precision(rem, exponent_bits=8, mantissa_bits=7)
+    lo = rem - mid
+    parts = jnp.stack([hi, mid, lo], 0).astype(jnp.bfloat16)
+    xt = jnp.transpose(static, (1, 0, 2))
+    span, width, cols = xt.shape
+    rows = mix_ext.shape[0]
+    block = 8
+    return pl.pallas_call(
+        basis_body,
+        out_shape=jax.ShapeDtypeStruct((rows, span, cols), jnp.float32),
+        grid=(span // block,),
+        in_specs=[
+            pl.BlockSpec(parts.shape, lambda i: (0, 0, 0)),
+            pl.BlockSpec((block, width, cols), lambda i: (i, 0, 0)),
+        ],
+        out_specs=pl.BlockSpec((rows, block, cols), lambda i: (0, i, 0)),
+        compiler_params=pltpu.CompilerParams(vmem_limit_bytes=48 * 1024 * 1024),
+        cost_estimate=pl.CostEstimate(
+            flops=6 * rows * width * span * cols,
+            transcendentals=0,
+            bytes_accessed=2 * xt.size + 4 * rows * span * cols,
+        ),
+    )(parts, xt)
+
+
 def per_device(scalars, velocity, diffusivity, diff_scale, basis_old, sing_values, stored):
     rank = basis_old.shape[0]
     snaps = stored.shape[0]
@@ -194,12 +231,7 @@
     )
     mix = inv_static * weight[None, :]
     mix_ext = jnp.concatenate([mix, jnp.zeros((1, width), jnp.float32)], 0)
-    basis_ext = lax.dot_general(
-        mix_ext,
-        static.astype(jnp.float32),
-        (((1,), (0,)), ((), ())),
-        precision=lax.Precision.HIGHEST,
-    )
+    basis_ext = basis_rows(mix_ext, static)
 
     coeffs = jnp.concatenate([velocity, diffusivity[None]], 0)
     first = halo(jnp.concatenate([scalars[:1], coeffs], 0))

time: 214 us -> 207 us (0.967)
  local copies, waits for them, and re-layouts: 27.3 us -> 17.4 us
  Pallas kernels: 68.3 us -> 75.8 us
  waiting for transfers between devices: 19.3 us -> 26.4 us
  starting transfers between devices: 43.6 us -> 36.6 us
  matrix products: 11.7 us -> 5.04 us
    dot_general x1 -> x0, local copies, waits for them, and re-layouts: 12 us -> none  [per_device(): lax.dot_general(mix_ext, static.astype(jnp.float32), (((1,), (0,)), ((),...]
    pallas_call x0 -> x1, Pallas kernels: none -> 7.5 us  [basis_rows(): pl.pallas_call(basis_body, out_shape=jax.ShapeDtypeStruct((rows, span, co...]
    dot_general x1 -> x0, matrix products: 6.4 us -> none  [per_device(): lax.dot_general(mix_ext, static.astype(jnp.float32), (((1,), (0,)), ((),...]
    ppermute x14, waiting for transfers between devices: 17.8 us -> 24.1 us  [butterfly_sum(): value = value + lax.ppermute(value, axis, pairs)]
    ppermute x4, starting transfers between devices: 8.85 us -> 4.07 us  [halo(): high_x = lax.ppermute(block[:, :width], 'gx', bx)]
    unnamed x34, local copies, waits for them, and re-layouts: 6.36 us -> 8.54 us
    ppermute x14, starting transfers between devices: 17.9 us -> 15.7 us  [butterfly_sum(): value = value + lax.ppermute(value, axis, pairs)]
    ppermute x4, starting transfers between devices: 15.2 us -> 13.1 us  [halo(): high_y = lax.ppermute(block[:, :, :width], 'gy', by)]
  transfers between devices with their start and end apart: 30 -> 30, of which waited for: 9 -> 10; matrix products, arithmetic and copies ran while one was open for 31% -> 23% of each run, Pallas kernels for 21% -> 25%
where the time goes in v1:
time: 207 us; the launch traced here: 205 us
  Pallas kernels  75.8 us (37%)
  other arithmetic  41.5 us (20%)
  starting transfers between devices  36.6 us (18%)
  waiting for transfers between devices  26.4 us (13%)
  local copies, waits for them, and re-layouts  17.4 us (8%)
  matrix products  5.04 us (2%)
  between operations  2.49 us (1%)
    pallas_call x4, Pallas kernels, stencil_step(): pl.pallas_call(stencil_body, out_shape=jax.ShapeDtypeStruct((count, nx, n...  66.7 us
    ppermute x14, waiting for transfers between devices, butterfly_sum(): value = value + lax.ppermute(value, axis, pairs)  24.1 us
    ppermute x14, starting transfers between devices, butterfly_sum(): value = value + lax.ppermute(value, axis, pairs)  15.7 us
    ppermute x4, starting transfers between devices, halo(): high_y = lax.ppermute(block[:, :, :width], 'gy', by)  13.1 us
    concatenate x4, other arithmetic, halo(): jnp.concatenate([jnp.pad(low_y, edge), rows, jnp.pad(high_y, edge)], axis=2)  12.2 us
    unnamed x34, local copies, waits for them, and re-layouts  8.54 us
    pallas_call x1, Pallas kernels, basis_rows(): pl.pallas_call(basis_body, out_shape=jax.ShapeDtypeStruct((rows, span, co...  7.5 us
    another operation x3, other arithmetic, per_device(): lower_static = jnp.linalg.cholesky(gram_static)  7.29 us
  transfers between devices with their start and end apart: 30, of which 10 were waited for; matrix products, arithmetic and copies ran while one was open for 23% of the time, Pallas kernels for 25%

profile of v1, /device:TPU:0, one launch (start us, length us, event | category | flops | bytes accessed | tf_op | source)
XLA Modules:
  0.0 205.2 jit_solution(18427414558790753646)
XLA Ops:
  0.6 3.7 %copy_dynamic-update-slice_fusion = bf16[64,32,1024]{2,0,1:T(8,128)(2,1)S(1)} fusion(bf16[48,32,1024]{2,1,0:T(8,128)(2,1)} %param.17), kind=kLoop, calls=%fused_computation.15 | loop fusion | bytes 6291456
  4.4 0.6 copy_dynamic-update-slice_fusion.1
  5.0 1.2 convolution_bitcast_fusion.1
  6.2 0.9 copy-done
  7.1 1.2 collective-permute-done.16
  8.3 1.7 collective-permute-start.17
  10.0 0.9 fusion.25
  10.9 6.2 %collective-permute-start.11 = (f32[3,64,2,128]{3,2,1,0:T(2,128)}, f32[3,64,2,128]{3,2,1,0:T(2,128)}, u32[]{:S(2)}, u32[]{:S(2)}) collective-permute-start(f32[3,64,2,128]{3,2,1,0:T(2,128)} %get-tuple-element.51), channel_id=1, source_target_pairs={{1,0},{2,1},{3,2},{4,3},{5,4},{6,5},{7,6},{8,7},{9,8},{10,9},{11,1... | collective-permute-start | bytes 589832 | tf_op jit(solution)/shard_map/ppermute | solution.py:25
  17.3 3.0 %collective-permute-start.18 = (f32[64,64]{1,0:T(8,128)S(1)}, f32[64,64]{1,0:T(8,128)S(1)}, u32[]{:S(2)}, u32[]{:S(2)}) collective-permute-start(f32[64,64]{1,0:T(8,128)S(1)} %add.84), channel_id=1, source_target_pairs={{0,64},{16,80},{32,96},{48,112},{64,0},{80,16},{96,32},{112,48},{1... | collective-permute-start | bytes 49160 | tf_op jit(solution)/shard_map/ppermute | solution.py:37
  20.2 1.1 pad_maximum_fusion.3
  21.3 1.5 collective-permute-start.3
  23.5 0.7 pad_maximum_fusion.5
  24.2 7.0 %collective-permute-done.19 = f32[64,64]{1,0:T(8,128)S(1)} collective-permute-done((f32[64,64]{1,0:T(8,128)S(1)}, f32[64,64]{1,0:T(8,128)S(1)}, u32[]{:S(2)}, u32[]{:S(2)}) %collective-permute-start.19) | collective-permute-done | bytes 16416 | tf_op jit(solution)/shard_map/ppermute | solution.py:37
  31.2 0.7 fusion.24
  31.9 4.7 %collective-permute-done.20 = f32[64,64]{1,0:T(8,128)S(1)} collective-permute-done((f32[64,64]{1,0:T(8,128)S(1)}, f32[64,64]{1,0:T(8,128)S(1)}, u32[]{:S(2)}, u32[]{:S(2)}) %collective-permute-start.20) | collective-permute-done | bytes 16416 | tf_op jit(solution)/shard_map/ppermute | solution.py:37
  36.6 0.6 iota_multiply_fusion.1
  37.2 3.3 %collective-permute-done.21 = f32[64,64]{1,0:T(8,128)S(1)} collective-permute-done((f32[64,64]{1,0:T(8,128)S(1)}, f32[64,64]{1,0:T(8,128)S(1)}, u32[]{:S(2)}, u32[]{:S(2)}) %collective-permute-start.21) | collective-permute-done | bytes 16416 | tf_op jit(solution)/shard_map/ppermute | solution.py:37
  40.5 0.8 collective-permute-start.22
  42.0 4.0 %collective-permute-done.22 = f32[64,64]{1,0:T(8,128)S(1)} collective-permute-done((f32[64,64]{1,0:T(8,128)S(1)}, f32[64,64]{1,0:T(8,128)S(1)}, u32[]{:S(2)}, u32[]{:S(2)}) %collective-permute-start.22) | collective-permute-done | bytes 16416 | tf_op jit(solution)/shard_map/ppermute | solution.py:37
  46.1 0.6 fusion.12
  46.7 6.6 %cholesky.17 = f32[64,64]{1,0:T(8,128)S(1)} custom-call(f32[64,64]{1,0:T(8,128)} %fusion.12), custom_call_target="Cholesky" | custom-call | tf_op jit(solution)/shard_map/jit(cholesky)/cholesky | solution.py:227
  53.4 4.4 %select_maximum_fusion = f32[5,68,36,128]{3,2,1,0:T(8,128)S(1)} fusion(f32[5,64,2,128]{3,2,1,0:T(2,128)S(1)} %collective-permute-done.3, f32[5,64,2,128]{3,2,1,0:T(2,128)} %collective-permute-done, f32[5,2,32,128]{3,2,1,0:T(8,128)} %collective-permute-done.2, f32[1,64,32,128]{3,2,1,0:T(8,128)} %bitcast.60, f32[3,64,32,128]{3,2,1,0:T(8,128)S(1)} %copy-done.5, ...), kind=kLoop, calls=%fused_computation.4 | loop fusion | flops 15667200 | bytes 12492800 | tf_op jit(solution)/shard_map/concatenate | solution.py:28
  57.8 2.8 %slice.177.coeff_ref = f32[4,68,36,128]{3,2,1,0:T(8,128)} slice(f32[5,68,36,128]{3,2,1,0:T(8,128)S(1)} %select_maximum_fusion), slice={[1:5], [0:68], [0:36], [0:128]} | slice | bytes 10027008 | tf_op jit(solution)/shard_map/slice | solution.py:238
  60.7 9.5 %shard_map.94 = f32[1,64,32,128]{3,2,1,0:T(8,128)S(1)} custom-call(f32[1]{0:T(128)S(1)} %bitcast.58, f32[1,68,36,128]{3,2,1,0:T(8,128)S(1)} %slice.176.conc_ref, f32[4,68,36,128]{3,2,1,0:T(8,128)} %slice.177.coeff_ref), custom_call_target="tpu_custom_call" | custom-call | flops 20971520 | bytes 7315456 | tf_op jit(solution)/shard_map/pallas_call | solution.py:160
  70.3 1.2 collective-permute-start.7
  71.5 1.0 collective-permute-start.4
  72.6 2.7 %collective-permute-start.6 = (f32[1,2,32,128]{3,2,1,0:T(8,128)S(1)}, f32[1,2,32,128]{3,2,1,0:T(8,128)S(1)}, u32[]{:S(2)}, u32[]{:S(2)}) collective-permute-start(f32[1,2,32,128]{3,2,1,0:T(8,128)S(1)} %get-tuple-element.57), channel_id=1, source_target_pairs={{16,0},{32,16},{48,32},{64,48},{80,64},{96,80},{112,96},{0,112},{1... | collective-permute-start | bytes 98312 | tf_op jit(solution)/shard_map/ppermute | solution.py:23
  75.2 0.7 compare_reduce_fusion
  75.9 0.9 collective-permute-done.6
  76.8 1.7 collective-permute-start.8
  78.5 1.3 collective-permute-done.5
  79.8 1.4 collective-permute-start.10
  81.4 9.5 %shard_map.95 = f32[1,64,32,128]{3,2,1,0:T(8,128)S(1)} custom-call(f32[1]{0:T(128)S(1)} %bitcast.59, f32[1,68,36,128]{3,2,1,0:T(8,128)S(1)} %select_maximum_fusion.6.conc_ref, f32[4,68,36,128]{3,2,1,0:T(8,128)} %slice.177.coeff_ref), custom_call_target="tpu_custom_call" | custom-call | flops 20971520 | bytes 7315456 | tf_op jit(solution)/shard_map/pallas_call | solution.py:160
  91.0 1.0 copy-done.2
  92.4 0.9 multiply_reduce_fusion
  93.4 3.3 %fusion = f32[64]{0:T(128)S(1)} fusion(bf16[64,32,1024]{2,0,1:T(8,128)(2,1)} %copy-done, f32[32,1024]{1,0:T(8,128)S(1)} %mul.85), kind=kLoop, calls=%fused_computation.2 | loop fusion | flops 6291392 | bytes 4325632 | tf_op jit(solution)/shard_map/reduce_sum | solution.py:251
  96.8 0.7 pad_maximum_fusion.7
  97.5 0.6 select_bitcast_fusion
  98.7 0.7 fusion.34
  99.4 5.5 %custom-call.8 = f32[1,64,64]{1,2,0:T(8,128)} custom-call(f32[1,64,64]{2,1,0:T(8,128)S(1)} %get-tuple-element.42), custom_call_target="InvertDiagBlocksLowerTriangular" | custom-call | tf_op jit(solution)/shard_map/triangular_solve | solution.py:229
  105.0 0.6 scatter.10
  105.6 4.5 %collective-permute-start.25 = (f32[65]{0:T(128)S(1)}, f32[65]{0:T(128)S(1)}, u32[]{:S(2)}, u32[]{:S(2)}) collective-permute-start(f32[65]{0:T(128)S(1)} %add.92), channel_id=1, source_target_pairs={{0,64},{16,80},{32,96},{48,112},{64,0},{80,16},{96,32},{112,48},{1... | collective-permute-start | bytes 788 | tf_op jit(solution)/shard_map/ppermute | solution.py:37
  110.1 3.8 %select_maximum_fusion.4.conc_ref = f32[3,68,36,128]{3,2,1,0:T(8,128)} fusion(f32[3,64,2,128]{3,2,1,0:T(2,128)} %collective-permute-done.11, f32[3,64,2,128]{3,2,1,0:T(2,128)} %collective-permute-done.8, f32[3,2,32,128]{3,2,1,0:T(8,128)} %collective-permute-done.10, f32[3,64,32,128]{3,2,1,0:T(8,128)S(1)} %slice-done, f32[3,2,32,128]{3,2,1,0:T(8,128)} %collective-permute-done.9), kind=kLoop, calls=%fused_computation.11 | loop fusion | flops 7520256 | bytes 7495680 | tf_op jit(solution)/shard_map/concatenate | solution.py:28
  114.2 23.8 %shard_map.96 = f32[3,64,32,128]{3,2,1,0:T(8,128)S(1)} custom-call(f32[3]{0:T(128)S(1)} %slice.163.scale_ref, f32[3,68,36,128]{3,2,1,0:T(8,128)} %select_maximum_fusion.4.conc_ref, f32[4,68,36,128]{3,2,1,0:T(8,128)} %slice.177.coeff_ref), custom_call_target="tpu_custom_call" | custom-call | flops 62914560 | bytes 11919360 | tf_op jit(solution)/shard_map/pallas_call | solution.py:160
  138.1 2.8 %collective-permute-start.27 = (f32[65]{0:T(128)S(1)}, f32[65]{0:T(128)S(1)}, u32[]{:S(2)}, u32[]{:S(2)}) collective-permute-start(f32[65]{0:T(128)S(1)} %add.94), channel_id=1, source_target_pairs={{0,2},{1,3},{2,0},{3,1},{4,6},{5,7},{6,4},{7,5},{8,10},{9,11},{10,... | collective-permute-start | bytes 788 | tf_op jit(solution)/shard_map/ppermute | solution.py:37
  140.9 0.9 fusion.27
  141.8 1.4 collective-permute-done.27
  143.3 0.7 fusion.26
  144.0 4.1 %collective-permute-start.15 = (f32[3,64,2,128]{3,2,1,0:T(2,128)}, f32[3,64,2,128]{3,2,1,0:T(2,128)}, u32[]{:S(2)}, u32[]{:S(2)}) collective-permute-start(f32[3,64,2,128]{3,2,1,0:T(2,128)} %get-tuple-element.55), channel_id=1, source_target_pairs={{1,0},{2,1},{3,2},{4,3},{5,4},{6,5},{7,6},{8,7},{9,8},{10,9},{11,1... | collective-permute-start | bytes 589832 | tf_op jit(solution)/shard_map/ppermute | solution.py:25
  148.1 2.5 %collective-permute-start.29 = (f32[65]{0:T(128)S(1)}, f32[65]{0:T(128)}, u32[]{:S(2)}, u32[]{:S(2)}) collective-permute-start(f32[65]{0:T(128)S(1)} %add.96), channel_id=1, source_target_pairs={{0,8},{1,9},{2,10},{3,11},{4,12},{5,13},{6,14},{7,15},{8,0},{9,1},... | collective-permute-start | bytes 788 | tf_op jit(solution)/shard_map/ppermute | solution.py:37
  151.2 2.0 collective-permute-done.29
  153.2 0.7 add_multiply_fusion
  153.9 0.7 slice.175
  154.5 1.5 multiply_reduce_fusion.2
  156.0 1.0 multiply_reduce_fusion.1
  157.0 3.5 %fusion.1 = f32[32,1024]{1,0:T(8,128)S(1)} fusion(bf16[64,32,1024]{2,0,1:T(8,128)(2,1)} %copy-done, f32[64]{0:T(128)S(1)} %get-tuple-element.65), kind=kLoop, calls=%fused_computation.3 | loop fusion | flops 6258688 | bytes 4325632 | tf_op jit(solution)/shard_map/reduce_sum | solution.py:272
  162.0 0.7 fusion.5.last_ref
  163.0 0.7 copy.15
  163.7 2.2 %copy-done.1 = bf16[64,32,1024]{2,0,1:T(8,128)(2,1)S(1)} copy-done((bf16[64,32,1024]{2,0,1:T(8,128)(2,1)S(1)}, bf16[64,32,1024]{2,0,1:T(8,128)(2,1)}, u32[]{:S(2)}) %copy-start.1) | copy-done | bytes 4194328
  165.9 7.5 %shard_map.98._ = f32[65,32,1024]{2,1,0:T(8,128)} custom-call(bf16[3,65,64]{2,1,0:T(8,128)(2,1)S(1)} %pad_maximum_fusion.6.mix_ref, bf16[32,64,1024]{2,1,0:T(8,128)(2,1)S(1)} %bitcast.57), custom_call_target="tpu_custom_call" | custom-call | flops 817889280 | bytes 12713984 | tf_op jit(solution)/shard_map/pallas_call | solution.py:198
  173.4 1.6 shard_map.99
  175.0 3.8 %select_maximum_fusion.2.conc_ref = f32[3,68,36,128]{3,2,1,0:T(8,128)} fusion(f32[3,64,2,128]{3,2,1,0:T(2,128)} %collective-permute-done.15, f32[3,64,2,128]{3,2,1,0:T(2,128)} %collective-permute-done.12, f32[3,2,32,128]{3,2,1,0:T(8,128)} %collective-permute-done.14, f32[3,64,32,128]{3,2,1,0:T(8,128)S(1)} %shard_map.96, ...), kind=kLoop, calls=%fused_computation.9 | loop fusion | flops 7520256 | bytes 7495680 | tf_op jit(solution)/shard_map/concatenate | solution.py:28
  178.8 23.9 %shard_map.97 = f32[3,64,32,128]{3,2,1,0:T(8,128)S(1)} custom-call(f32[3]{0:T(128)S(1)} %slice.163.scale_ref, f32[3,68,36,128]{3,2,1,0:T(8,128)} %select_maximum_fusion.2.conc_ref, f32[4,68,36,128]{3,2,1,0:T(8,128)} %slice.177.coeff_ref), custom_call_target="tpu_custom_call" | custom-call | flops 62914560 | bytes 11919360 | tf_op jit(solution)/shard_map/pallas_call | solution.py:160
  202.7 2.5 %pad_maximum_fusion = f32[4,64,32,128]{3,2,1,0:T(8,128)} fusion(f32[3,64,32,128]{3,2,1,0:T(8,128)S(1)} %shard_map.97, f32[1,64,32,128]{3,2,1,0:T(8,128)S(1)} %copy-done.3), kind=kLoop, calls=%fused_computation.8 | loop fusion | flops 1048576 | bytes 8388608 | tf_op jit(solution)/shard_map/concatenate | solution.py:260
  (97 shorter events, 4.5 us)
Async XLA Ops:
  0.6 3.7 %copy-start.9 = (bf16[16,32,1024]{2,1,0:T(8,128)(2,1)S(1)}, bf16[16,32,1024]{2,1,0:T(8,128)(2,1)}, u32[]{:S(2)}) copy-start(bf16[16,32,1024]{2,1,0:T(8,128)(2,1)} %param.19) | copy-start | bytes 3145732
  5.0 2.1 %copy-start = (bf16[64,32,1024]{2,0,1:T(8,128)(2,1)}, bf16[64,32,1024]{2,0,1:T(8,128)(2,1)S(1)}, u32[]{:S(2)}) copy-start(bf16[64,32,1024]{2,0,1:T(8,128)(2,1)S(1)} %copy_dynamic-update-slice_fusion.1) | copy-start | bytes 12582916
  5.0 5.0 %copy-start.7 = (f32[4,64,32,128]{3,2,1,0:T(8,128)S(1)}, f32[4,64,32,128]{3,2,1,0:T(8,128)}, u32[]{:S(2)}) copy-start(f32[4,64,32,128]{3,2,1,0:T(8,128)} %param.13) | copy-start | bytes 12582916
  5.0 15.3 %copy-start.5 = (f32[3,64,32,128]{3,2,1,0:T(8,128)S(1)}, f32[3,64,32,128]{3,2,1,0:T(8,128)}, u32[]{:S(2)}) copy-start(f32[3,64,32,128]{3,2,1,0:T(8,128)} %param.14) | copy-start | bytes 9437188
  5.0 15.2 %copy-start.8 = (f32[64,32,128]{2,1,0:T(8,128)S(1)}, f32[64,32,128]{2,1,0:T(8,128)}, u32[]{:S(2)}) copy-start(f32[64,32,128]{2,1,0:T(8,128)} %param.15) | copy-start | bytes 3145732
  7.1 1.2 collective-permute-start.16
  8.3 8.9 %collective-permute-start.17 = (f32[64,64]{1,0:T(8,128)S(1)}, f32[64,64]{1,0:T(8,128)S(1)}, u32[]{:S(2)}, u32[]{:S(2)}) collective-permute-start(f32[64,64]{1,0:T(8,128)S(1)} %add.83), channel_id=1, source_target_pairs={{0,32},{16,48},{32,0},{48,16},{64,96},{80,112},{96,64},{112,80},{1... | collective-permute-start | bytes 49160 | tf_op jit(solution)/shard_map/ppermute | solution.py:37
  10.9 99.1 %collective-permute-start.11 = (f32[3,64,2,128]{3,2,1,0:T(2,128)}, f32[3,64,2,128]{3,2,1,0:T(2,128)}, u32[]{:S(2)}, u32[]{:S(2)}) collective-permute-start(f32[3,64,2,128]{3,2,1,0:T(2,128)} %get-tuple-element.51), channel_id=1, source_target_pairs={{1,0},{2,1},{3,2},{4,3},{5,4},{6,5},{7,6},{8,7},{9,8},{10,9},{11,1... | collective-permute-start | bytes 589832 | tf_op jit(solution)/shard_map/ppermute | solution.py:25
  17.2 7.0 %copy-start.6 = (f32[1,64,32,128]{3,2,1,0:T(8,128)}, f32[1,64,32,128]{3,2,1,0:T(8,128)S(1)}, u32[]{:S(2)}) copy-start(f32[1,64,32,128]{3,2,1,0:T(8,128)S(1)} %slice.152) | copy-start | bytes 3145732
  17.3 6.1 %collective-permute-start.18 = (f32[64,64]{1,0:T(8,128)S(1)}, f32[64,64]{1,0:T(8,128)S(1)}, u32[]{:S(2)}, u32[]{:S(2)}) collective-permute-start(f32[64,64]{1,0:T(8,128)S(1)} %add.84), channel_id=1, source_target_pairs={{0,64},{16,80},{32,96},{48,112},{64,0},{80,16},{96,32},{112,48},{1... | collective-permute-start | bytes 49160 | tf_op jit(solution)/shard_map/ppermute | solution.py:37
  21.3 32.1 %collective-permute-start.3 = (f32[5,64,2,128]{3,2,1,0:T(2,128)}, f32[5,64,2,128]{3,2,1,0:T(2,128)S(1)}, u32[]{:S(2)}, u32[]{:S(2)}) collective-permute-start(f32[5,64,2,128]{3,2,1,0:T(2,128)} %get-tuple-element.47), channel_id=1, source_target_pairs={{1,0},{2,1},{3,2},{4,3},{5,4},{6,5},{7,6},{8,7},{9,8},{10,9},{11,1... | collective-permute-start | bytes 983048 | tf_op jit(solution)/shard_map/ppermute | solution.py:25
  22.9 30.6 %collective-permute-start = (f32[5,64,2,128]{3,2,1,0:T(2,128)}, f32[5,64,2,128]{3,2,1,0:T(2,128)}, u32[]{:S(2)}, u32[]{:S(2)}) collective-permute-start(f32[5,64,2,128]{3,2,1,0:T(2,128)} %get-tuple-element.46), channel_id=1, source_target_pairs={{0,1},{1,2},{2,3},{3,4},{4,5},{5,6},{6,7},{7,8},{8,9},{9,10},{10,1... | collective-permute-start | bytes 983048 | tf_op jit(solution)/shard_map/ppermute | solution.py:24
  23.4 7.8 %collective-permute-start.19 = (f32[64,64]{1,0:T(8,128)S(1)}, f32[64,64]{1,0:T(8,128)S(1)}, u32[]{:S(2)}, u32[]{:S(2)}) collective-permute-start(f32[64,64]{1,0:T(8,128)S(1)} %add.85), channel_id=1, source_target_pairs={{0,1},{1,0},{2,3},{3,2},{4,5},{5,4},{6,7},{7,6},{8,9},{9,8},{10,11... | collective-permute-start | bytes 49160 | tf_op jit(solution)/shard_map/ppermute | solution.py:37
  24.2 17.7 %copy-start.4 = (f32[4]{0:T(128)S(1)}, f32[4]{0:T(128)}, u32[]{:S(2)}) copy-start(f32[4]{0:T(128)} %param.16) | copy-start | bytes 52
  24.2 17.8 %copy-start.13 = (f32[48]{0:T(128)S(1)}, f32[48]{0:T(128)}, u32[]{:S(2)}) copy-start(f32[48]{0:T(128)} %param.18) | copy-start | bytes 580
  24.2 29.2 %collective-permute-start.2 = (f32[5,2,32,128]{3,2,1,0:T(8,128)}, f32[5,2,32,128]{3,2,1,0:T(8,128)}, u32[]{:S(2)}, u32[]{:S(2)}) collective-permute-start(f32[5,2,32,128]{3,2,1,0:T(8,128)} %get-tuple-element.45), channel_id=1, source_target_pairs={{16,0},{32,16},{48,32},{64,48},{80,64},{96,80},{112,96},{0,112},{1... | collective-permute-start | bytes 491528 | tf_op jit(solution)/shard_map/ppermute | solution.py:23
  31.2 5.4 %collective-permute-start.20 = (f32[64,64]{1,0:T(8,128)S(1)}, f32[64,64]{1,0:T(8,128)S(1)}, u32[]{:S(2)}, u32[]{:S(2)}) collective-permute-start(f32[64,64]{1,0:T(8,128)S(1)} %add.86), channel_id=1, source_target_pairs={{0,2},{1,3},{2,0},{3,1},{4,6},{5,7},{6,4},{7,5},{8,10},{9,11},{10,... | collective-permute-start | bytes 49160 | tf_op jit(solution)/shard_map/ppermute | solution.py:37
  36.6 3.9 %collective-permute-start.21 = (f32[64,64]{1,0:T(8,128)S(1)}, f32[64,64]{1,0:T(8,128)S(1)}, u32[]{:S(2)}, u32[]{:S(2)}) collective-permute-start(f32[64,64]{1,0:T(8,128)S(1)} %add.87), channel_id=1, source_target_pairs={{0,4},{1,5},{2,6},{3,7},{4,0},{5,1},{6,2},{7,3},{8,12},{9,13},{10,... | collective-permute-start | bytes 49160 | tf_op jit(solution)/shard_map/ppermute | solution.py:37
  40.5 5.4 %collective-permute-start.22 = (f32[64,64]{1,0:T(8,128)S(1)}, f32[64,64]{1,0:T(8,128)S(1)}, u32[]{:S(2)}, u32[]{:S(2)}) collective-permute-start(f32[64,64]{1,0:T(8,128)S(1)} %add.88), channel_id=1, source_target_pairs={{0,8},{1,9},{2,10},{3,11},{4,12},{5,13},{6,14},{7,15},{8,0},{9,1},... | collective-permute-start | bytes 49160 | tf_op jit(solution)/shard_map/ppermute | solution.py:37
  46.0 7.5 %collective-permute-start.1 = (f32[5,2,32,128]{3,2,1,0:T(8,128)}, f32[5,2,32,128]{3,2,1,0:T(8,128)}, u32[]{:S(2)}, u32[]{:S(2)}) collective-permute-start(f32[5,2,32,128]{3,2,1,0:T(8,128)} %get-tuple-element.44), channel_id=1, source_target_pairs={{0,16},{16,32},{32,48},{48,64},{64,80},{80,96},{96,112},{112,0},{1... | collective-permute-start | bytes 491528 | tf_op jit(solution)/shard_map/ppermute | solution.py:22
  53.4 4.4 %copy-start.11 = (f32[64,64]{1,0:T(8,128)}, f32[64,64]{1,0:T(8,128)S(1)}, u32[]{:S(2)}) copy-start(f32[64,64]{1,0:T(8,128)S(1)} %cholesky.17) | copy-start | bytes 49156
  70.3 10.9 %collective-permute-start.7 = (f32[1,64,2,128]{3,2,1,0:T(2,128)S(1)}, f32[1,64,2,128]{3,2,1,0:T(2,128)S(1)}, u32[]{:S(2)}, u32[]{:S(2)}) collective-permute-start(f32[1,64,2,128]{3,2,1,0:T(2,128)S(1)} %get-tuple-element.59), channel_id=1, source_target_pairs={{1,0},{2,1},{3,2},{4,3},{5,4},{6,5},{7,6},{8,7},{9,8},{10,9},{11,1... | collective-permute-start | bytes 196616 | tf_op jit(solution)/shard_map/ppermute | solution.py:25
  71.5 9.6 %collective-permute-start.4 = (f32[1,64,2,128]{3,2,1,0:T(2,128)S(1)}, f32[1,64,2,128]{3,2,1,0:T(2,128)S(1)}, u32[]{:S(2)}, u32[]{:S(2)}) collective-permute-start(f32[1,64,2,128]{3,2,1,0:T(2,128)S(1)} %get-tuple-element.58), channel_id=1, source_target_pairs={{0,1},{1,2},{2,3},{3,4},{4,5},{5,6},{6,7},{7,8},{8,9},{9,10},{10,1... | collective-permute-start | bytes 196616 | tf_op jit(solution)/shard_map/ppermute | solution.py:24
  72.6 4.3 %collective-permute-start.6 = (f32[1,2,32,128]{3,2,1,0:T(8,128)S(1)}, f32[1,2,32,128]{3,2,1,0:T(8,128)S(1)}, u32[]{:S(2)}, u32[]{:S(2)}) collective-permute-start(f32[1,2,32,128]{3,2,1,0:T(8,128)S(1)} %get-tuple-element.57), channel_id=1, source_target_pairs={{16,0},{32,16},{48,32},{64,48},{80,64},{96,80},{112,96},{0,112},{1... | collective-permute-start | bytes 98312 | tf_op jit(solution)/shard_map/ppermute | solution.py:23
  75.2 4.6 %collective-permute-start.5 = (f32[1,2,32,128]{3,2,1,0:T(8,128)S(1)}, f32[1,2,32,128]{3,2,1,0:T(8,128)S(1)}, u32[]{:S(2)}, u32[]{:S(2)}) collective-permute-start(f32[1,2,32,128]{3,2,1,0:T(8,128)S(1)} %get-tuple-element.56), channel_id=1, source_target_pairs={{0,16},{16,32},{32,48},{48,64},{64,80},{80,96},{96,112},{112,0},{1... | collective-permute-start | bytes 98312 | tf_op jit(solution)/shard_map/ppermute | solution.py:22
  76.8 33.2 %collective-permute-start.8 = (f32[3,64,2,128]{3,2,1,0:T(2,128)}, f32[3,64,2,128]{3,2,1,0:T(2,128)}, u32[]{:S(2)}, u32[]{:S(2)}) collective-permute-start(f32[3,64,2,128]{3,2,1,0:T(2,128)} %get-tuple-element.50), channel_id=1, source_target_pairs={{0,1},{1,2},{2,3},{3,4},{4,5},{5,6},{6,7},{7,8},{8,9},{9,10},{10,1... | collective-permute-start | bytes 589832 | tf_op jit(solution)/shard_map/ppermute | solution.py:24
  79.8 30.3 %collective-permute-start.10 = (f32[3,2,32,128]{3,2,1,0:T(8,128)}, f32[3,2,32,128]{3,2,1,0:T(8,128)}, u32[]{:S(2)}, u32[]{:S(2)}) collective-permute-start(f32[3,2,32,128]{3,2,1,0:T(8,128)} %get-tuple-element.49), channel_id=1, source_target_pairs={{16,0},{32,16},{48,32},{64,48},{80,64},{96,80},{112,96},{0,112},{1... | collective-permute-start | bytes 294920 | tf_op jit(solution)/shard_map/ppermute | solution.py:23
  81.2 28.9 %collective-permute-start.9 = (f32[3,2,32,128]{3,2,1,0:T(8,128)}, f32[3,2,32,128]{3,2,1,0:T(8,128)}, u32[]{:S(2)}, u32[]{:S(2)}) collective-permute-start(f32[3,2,32,128]{3,2,1,0:T(8,128)} %get-tuple-element.48), channel_id=1, source_target_pairs={{0,16},{16,32},{32,48},{48,64},{64,80},{80,96},{96,112},{112,0},{1... | collective-permute-start | bytes 294920 | tf_op jit(solution)/shard_map/ppermute | solution.py:22
  81.4 10.5 %copy-start.14 = (s32[64]{0:T(128)S(1)}, s32[64]{0:T(128)}, u32[]{:S(2)}) copy-start(s32[64]{0:T(128)} %iota_multiply_fusion.1) | copy-start | bytes 772
  81.4 10.9 %copy-start.15 = (s32[16]{0:T(128)S(1)}, s32[16]{0:T(128)}, u32[]{:S(2)}) copy-start(s32[16]{0:T(128)} %iota_multiply_fusion) | copy-start | bytes 196
  91.0 1.0 copy-start.2
  92.0 18.1 %slice-start = ((f32[4,64,32,128]{3,2,1,0:T(8,128)}), f32[3,64,32,128]{3,2,1,0:T(8,128)S(1)}, s32[]{:S(2)}) async-start(f32[4,64,32,128]{3,2,1,0:T(8,128)} %param.13), calls=%async_computation | async-start | bytes 6291456 | tf_op jit(solution)/shard_map/slice | solution.py:257
  93.4 4.1 %copy-start.12 = (f32[64,64]{1,0:T(8,128)S(1)}, f32[64,64]{1,0:T(8,128)}, u32[]{:S(2)}) copy-start(f32[64,64]{1,0:T(8,128)} %copy-done.11) | copy-start | bytes 49156
  97.5 1.2 collective-permute-start.23
  99.4 6.2 %collective-permute-start.24 = (f32[65]{0:T(128)S(1)}, f32[65]{0:T(128)S(1)}, u32[]{:S(2)}, u32[]{:S(2)}) collective-permute-start(f32[65]{0:T(128)S(1)} %fusion.34), channel_id=1, source_target_pairs={{0,32},{16,48},{32,0},{48,16},{64,96},{80,112},{96,64},{112,80},{1... | collective-permute-start | bytes 788 | tf_op jit(solution)/shard_map/ppermute | solution.py:37
  105.6 8.3 %collective-permute-start.25 = (f32[65]{0:T(128)S(1)}, f32[65]{0:T(128)S(1)}, u32[]{:S(2)}, u32[]{:S(2)}) collective-permute-start(f32[65]{0:T(128)S(1)} %add.92), channel_id=1, source_target_pairs={{0,64},{16,80},{32,96},{48,112},{64,0},{80,16},{96,32},{112,48},{1... | collective-permute-start | bytes 788 | tf_op jit(solution)/shard_map/ppermute | solution.py:37
  113.9 24.2 %collective-permute-start.26 = (f32[65]{0:T(128)S(1)}, f32[65]{0:T(128)S(1)}, u32[]{:S(2)}, u32[]{:S(2)}) collective-permute-start(f32[65]{0:T(128)S(1)} %add.93), channel_id=1, source_target_pairs={{0,1},{1,0},{2,3},{3,2},{4,5},{5,4},{6,7},{7,6},{8,9},{9,8},{10,11... | collective-permute-start | bytes 788 | tf_op jit(solution)/shard_map/ppermute | solution.py:37
  138.1 5.2 %collective-permute-start.27 = (f32[65]{0:T(128)S(1)}, f32[65]{0:T(128)S(1)}, u32[]{:S(2)}, u32[]{:S(2)}) collective-permute-start(f32[65]{0:T(128)S(1)} %add.94), channel_id=1, source_target_pairs={{0,2},{1,3},{2,0},{3,1},{4,6},{5,7},{6,4},{7,5},{8,10},{9,11},{10,... | collective-permute-start | bytes 788 | tf_op jit(solution)/shard_map/ppermute | solution.py:37
  143.2 4.8 %collective-permute-start.28 = (f32[65]{0:T(128)S(1)}, f32[65]{0:T(128)S(1)}, u32[]{:S(2)}, u32[]{:S(2)}) collective-permute-start(f32[65]{0:T(128)S(1)} %add.95), channel_id=1, source_target_pairs={{0,4},{1,5},{2,6},{3,7},{4,0},{5,1},{6,2},{7,3},{8,12},{9,13},{10,... | collective-permute-start | bytes 788 | tf_op jit(solution)/shard_map/ppermute | solution.py:37
  144.0 31.0 %collective-permute-start.15 = (f32[3,64,2,128]{3,2,1,0:T(2,128)}, f32[3,64,2,128]{3,2,1,0:T(2,128)}, u32[]{:S(2)}, u32[]{:S(2)}) collective-permute-start(f32[3,64,2,128]{3,2,1,0:T(2,128)} %get-tuple-element.55), channel_id=1, source_target_pairs={{1,0},{2,1},{3,2},{4,3},{5,4},{6,5},{7,6},{8,7},{9,8},{10,9},{11,1... | collective-permute-start | bytes 589832 | tf_op jit(solution)/shard_map/ppermute | solution.py:25
  148.1 27.0 %collective-permute-start.12 = (f32[3,64,2,128]{3,2,1,0:T(2,128)}, f32[3,64,2,128]{3,2,1,0:T(2,128)}, u32[]{:S(2)}, u32[]{:S(2)}) collective-permute-start(f32[3,64,2,128]{3,2,1,0:T(2,128)} %get-tuple-element.54), channel_id=1, source_target_pairs={{0,1},{1,2},{2,3},{3,4},{4,5},{5,6},{6,7},{7,8},{8,9},{9,10},{10,1... | collective-permute-start | bytes 589832 | tf_op jit(solution)/shard_map/ppermute | solution.py:24
  148.1 5.1 %collective-permute-start.29 = (f32[65]{0:T(128)S(1)}, f32[65]{0:T(128)}, u32[]{:S(2)}, u32[]{:S(2)}) collective-permute-start(f32[65]{0:T(128)S(1)} %add.96), channel_id=1, source_target_pairs={{0,8},{1,9},{2,10},{3,11},{4,12},{5,13},{6,14},{7,15},{8,0},{9,1},... | collective-permute-start | bytes 788 | tf_op jit(solution)/shard_map/ppermute | solution.py:37
  150.5 24.5 %collective-permute-start.14 = (f32[3,2,32,128]{3,2,1,0:T(8,128)}, f32[3,2,32,128]{3,2,1,0:T(8,128)}, u32[]{:S(2)}, u32[]{:S(2)}) collective-permute-start(f32[3,2,32,128]{3,2,1,0:T(8,128)} %get-tuple-element.53), channel_id=1, source_target_pairs={{16,0},{32,16},{48,32},{64,48},{80,64},{96,80},{112,96},{0,112},{1... | collective-permute-start | bytes 294920 | tf_op jit(solution)/shard_map/ppermute | solution.py:23
  150.6 24.5 %collective-permute-start.13 = (f32[3,2,32,128]{3,2,1,0:T(8,128)}, f32[3,2,32,128]{3,2,1,0:T(8,128)}, u32[]{:S(2)}, u32[]{:S(2)}) collective-permute-start(f32[3,2,32,128]{3,2,1,0:T(8,128)} %get-tuple-element.52), channel_id=1, source_target_pairs={{0,16},{16,32},{32,48},{48,64},{64,80},{80,96},{96,112},{112,0},{1... | collective-permute-start | bytes 294920 | tf_op jit(solution)/shard_map/ppermute | solution.py:22
  151.2 11.5 %copy-start.10 = (f32[65,65]{1,0:T(8,128)S(1)}, f32[65,65]{1,0:T(8,128)}, u32[]{:S(2)}) copy-start(f32[65,65]{1,0:T(8,128)} %scatter.10) | copy-start | bytes 50704
  163.7 2.2 %copy-start.1 = (bf16[64,32,1024]{2,0,1:T(8,128)(2,1)S(1)}, bf16[64,32,1024]{2,0,1:T(8,128)(2,1)}, u32[]{:S(2)}) copy-start(bf16[64,32,1024]{2,0,1:T(8,128)(2,1)} %copy-done) | copy-start | bytes 12582916
  178.8 23.9 %copy-start.3 = (f32[1,64,32,128]{3,2,1,0:T(8,128)S(1)}, f32[1,64,32,128]{3,2,1,0:T(8,128)}, u32[]{:S(2)}) copy-start(f32[1,64,32,128]{3,2,1,0:T(8,128)} %copy-done.2) | copy-start | bytes 3145732

commit v2 on v1

--- a/solution.py
+++ b/solution.py
@@ -234,8 +234,9 @@
     basis_ext = basis_rows(mix_ext, static)
 
     coeffs = jnp.concatenate([velocity, diffusivity[None]], 0)
-    first = halo(jnp.concatenate([scalars[:1], coeffs], 0))
-    coeff_pad = first[1:]
+    count = scalars.shape[0]
+    first = halo(jnp.concatenate([scalars, coeffs], 0))
+    coeff_pad = first[count:]
     middle0 = stencil_step(first[:1], coeff_pad, diff_scale[:1])
     result0 = stencil_step(halo(middle0), coeff_pad, diff_scale[:1])
 
@@ -254,8 +255,7 @@
     cross_g = moments[:width] * weight
     self_g = moments[width]
 
-    rest = halo(scalars[1:])
-    middle_r = stencil_step(rest, coeff_pad, diff_scale[1:])
+    middle_r = stencil_step(first[1:count], coeff_pad, diff_scale[1:])
     result_r = stencil_step(halo(middle_r), coeff_pad, diff_scale[1:])
     result = jnp.concatenate([result0, result_r], 0)
 

time: 207 us -> 210 us (1.014)
  waiting for transfers between devices: 26.4 us -> 35.2 us
  starting transfers between devices: 36.6 us -> 29.8 us
  local copies, waits for them, and re-layouts: 17.4 us -> 23.2 us
  other arithmetic: 41.5 us -> 38 us
    ppermute x4 -> x3, starting transfers between devices: 13.1 us -> 7.9 us  [halo(): high_y = lax.ppermute(block[:, :, :width], 'gy', by)]
    ppermute x14, waiting for transfers between devices: 24.1 us -> 28.9 us  [butterfly_sum(): value = value + lax.ppermute(value, axis, pairs)]
    slice x4 -> x2, local copies, waits for them, and re-layouts: 2.87 us -> 7.5 us  [the longest x1 4.45 us: per_device(): middle_r = stencil_step(first[1:count], coeff_pad, diff_scale[1:])]
    ppermute x4 -> x3, starting transfers between devices: 4.07 us -> 0.01 us  [halo(): high_x = lax.ppermute(block[:, :width], 'gx', bx)]
    ppermute x14, starting transfers between devices: 15.7 us -> 19.4 us  [butterfly_sum(): value = value + lax.ppermute(value, axis, pairs)]
    unnamed x34 -> x26, local copies, waits for them, and re-layouts: 8.54 us -> 11.4 us
    ppermute x4 -> x3, starting transfers between devices: 3.18 us -> 0.94 us  [halo(): low_y = lax.ppermute(block[:, :, ny - width:], 'gy', fy)]
    ppermute x4 -> x3, waiting for transfers between devices: 0.01 us -> 2.12 us  [halo(): low_y = lax.ppermute(block[:, :, ny - width:], 'gy', fy)]
  transfers between devices with their start and end apart: 30 -> 26, of which waited for: 10 -> 14; matrix products, arithmetic and copies ran while one was open for 23% -> 15% of each run, Pallas kernels for 25% -> 16%
where the time goes in v2:
time: 210 us; the launch traced here: 209 us
  Pallas kernels  75.8 us (36%)
  other arithmetic  38 us (18%)
  waiting for transfers between devices  35.2 us (17%)
  starting transfers between devices  29.8 us (14%)
  local copies, waits for them, and re-layouts  23.2 us (11%)
  matrix products  5.04 us (2%)
  between operations  2.38 us (1%)
    pallas_call x4, Pallas kernels, stencil_step(): pl.pallas_call(stencil_body, out_shape=jax.ShapeDtypeStruct((count, nx, n...  66.7 us
    ppermute x14, waiting for transfers between devices, butterfly_sum(): value = value + lax.ppermute(value, axis, pairs)  28.9 us
    ppermute x14, starting transfers between devices, butterfly_sum(): value = value + lax.ppermute(value, axis, pairs)  19.4 us
    unnamed x26, local copies, waits for them, and re-layouts  11.4 us
    concatenate x3, other arithmetic, halo(): jnp.concatenate([jnp.pad(low_y, edge), rows, jnp.pad(high_y, edge)], axis=2)  10.7 us
    ppermute x3, starting transfers between devices, halo(): high_y = lax.ppermute(block[:, :, :width], 'gy', by)  7.9 us
    pallas_call x1, Pallas kernels, basis_rows(): pl.pallas_call(basis_body, out_shape=jax.ShapeDtypeStruct((rows, span, co...  7.52 us
    another operation x3, other arithmetic, per_device(): lower_static = jnp.linalg.cholesky(gram_static)  6.51 us
  transfers between devices with their start and end apart: 26, of which 14 were waited for; matrix products, arithmetic and copies ran while one was open for 15% of the time, Pallas kernels for 16%

profile of v2, /device:TPU:0, one launch (start us, length us, event | category | flops | bytes accessed | tf_op | source)
XLA Modules:
  0.0 209.4 jit_solution(7009891082763010978)
XLA Ops:
  0.6 3.7 %copy_dynamic-update-slice_fusion = bf16[64,32,1024]{2,0,1:T(8,128)(2,1)S(1)} fusion(bf16[48,32,1024]{2,1,0:T(8,128)(2,1)} %param.17), kind=kLoop, calls=%fused_computation.13 | loop fusion | bytes 6291456
  4.4 0.6 copy_dynamic-update-slice_fusion.1
  5.0 1.2 convolution_bitcast_fusion.1
  6.2 0.9 copy-done
  7.1 1.2 collective-permute-done.12
  8.3 1.7 collective-permute-start.13
  10.0 2.2 %collective-permute-done.13 = f32[64,64]{1,0:T(8,128)S(1)} collective-permute-done((f32[64,64]{1,0:T(8,128)S(1)}, f32[64,64]{1,0:T(8,128)S(1)}, u32[]{:S(2)}, u32[]{:S(2)}) %collective-permute-start.13) | collective-permute-done | bytes 16416 | tf_op jit(solution)/shard_map/ppermute | solution.py:37
  12.2 3.3 %collective-permute-start.14 = (f32[64,64]{1,0:T(8,128)S(1)}, f32[64,64]{1,0:T(8,128)S(1)}, u32[]{:S(2)}, u32[]{:S(2)}) collective-permute-start(f32[64,64]{1,0:T(8,128)S(1)} %add.80), channel_id=1, source_target_pairs={{0,64},{16,80},{32,96},{48,112},{64,0},{80,16},{96,32},{112,48},{1... | collective-permute-start | bytes 49160 | tf_op jit(solution)/shard_map/ppermute | solution.py:37
  15.5 2.1 %collective-permute-done.14 = f32[64,64]{1,0:T(8,128)S(1)} collective-permute-done((f32[64,64]{1,0:T(8,128)S(1)}, f32[64,64]{1,0:T(8,128)S(1)}, u32[]{:S(2)}, u32[]{:S(2)}) %collective-permute-start.14) | collective-permute-done | bytes 16416 | tf_op jit(solution)/shard_map/ppermute | solution.py:37
  17.7 2.0 collective-permute-start.15
  19.7 1.5 pad_maximum_fusion.3
  21.2 4.7 %collective-permute-start.3 = (f32[8,64,2,128]{3,2,1,0:T(2,128)}, f32[8,64,2,128]{3,2,1,0:T(2,128)}, u32[]{:S(2)}, u32[]{:S(2)}) collective-permute-start(f32[8,64,2,128]{3,2,1,0:T(2,128)} %get-tuple-element.47), channel_id=1, source_target_pairs={{1,0},{2,1},{3,2},{4,3},{5,4},{6,5},{7,6},{8,7},{9,8},{10,9},{11,1... | collective-permute-start | bytes 1572872 | tf_op jit(solution)/shard_map/ppermute | solution.py:25
  25.9 1.0 collective-permute-start.16
  26.9 0.8 pad_maximum_fusion.5
  28.2 9.3 %collective-permute-done.16 = f32[64,64]{1,0:T(8,128)S(1)} collective-permute-done((f32[64,64]{1,0:T(8,128)S(1)}, f32[64,64]{1,0:T(8,128)S(1)}, u32[]{:S(2)}, u32[]{:S(2)}) %collective-permute-start.16) | collective-permute-done | bytes 16416 | tf_op jit(solution)/shard_map/ppermute | solution.py:37
  37.5 1.4 collective-permute-start.17
  38.9 2.6 %collective-permute-done.17 = f32[64,64]{1,0:T(8,128)S(1)} collective-permute-done((f32[64,64]{1,0:T(8,128)S(1)}, f32[64,64]{1,0:T(8,128)S(1)}, u32[]{:S(2)}, u32[]{:S(2)}) %collective-permute-start.17) | collective-permute-done | bytes 16416 | tf_op jit(solution)/shard_map/ppermute | solution.py:37
  41.5 2.9 %collective-permute-start.18 = (f32[64,64]{1,0:T(8,128)S(1)}, f32[64,64]{1,0:T(8,128)S(1)}, u32[]{:S(2)}, u32[]{:S(2)}) collective-permute-start(f32[64,64]{1,0:T(8,128)S(1)} %add.84), channel_id=1, source_target_pairs={{0,8},{1,9},{2,10},{3,11},{4,12},{5,13},{6,14},{7,15},{8,0},{9,1},... | collective-permute-start | bytes 49160 | tf_op jit(solution)/shard_map/ppermute | solution.py:37
  44.5 2.4 %collective-permute-done.18 = f32[64,64]{1,0:T(8,128)S(1)} collective-permute-done((f32[64,64]{1,0:T(8,128)S(1)}, f32[64,64]{1,0:T(8,128)S(1)}, u32[]{:S(2)}, u32[]{:S(2)}) %collective-permute-start.18) | collective-permute-done | bytes 16416 | tf_op jit(solution)/shard_map/ppermute | solution.py:37
  47.1 5.8 %cholesky.17 = f32[64,64]{1,0:T(8,128)S(1)} custom-call(f32[64,64]{1,0:T(8,128)S(1)} %fusion.12), custom_call_target="Cholesky" | custom-call | tf_op jit(solution)/shard_map/jit(cholesky)/cholesky | solution.py:227
  53.0 6.7 %select_maximum_fusion = f32[8,68,36,128]{3,2,1,0:T(8,128)S(1)} fusion(f32[8,64,2,128]{3,2,1,0:T(2,128)} %collective-permute-done.3, f32[8,64,2,128]{3,2,1,0:T(2,128)} %collective-permute-done, f32[8,2,32,128]{3,2,1,0:T(8,128)S(1)} %collective-permute-done.2, f32[1,64,32,128]{3,2,1,0:T(8,128)} %bitcast.60, f32[3,64,32,128]{3,2,1,0:T(8,128)S(1)} %copy-done.7, ...), kind=kLoop, calls=%fused_computation | loop fusion | flops 25067520 | bytes 19988480 | tf_op jit(solution)/shard_map/concatenate | solution.py:28
  59.8 3.0 %slice.153.coeff_ref = f32[4,68,36,128]{3,2,1,0:T(8,128)} slice(f32[8,68,36,128]{3,2,1,0:T(8,128)S(1)} %select_maximum_fusion), slice={[4:8], [0:68], [0:36], [0:128]} | slice | bytes 10027008 | tf_op jit(solution)/shard_map/slice | solution.py:239
  62.8 2.8 %copy-done.5 = f32[8,68,36,128]{3,2,1,0:T(8,128)} copy-done((f32[8,68,36,128]{3,2,1,0:T(8,128)}, f32[8,68,36,128]{3,2,1,0:T(8,128)S(1)}, u32[]{:S(2)}) %copy-start.5) | copy-done | bytes 10027032
  65.7 9.5 %shard_map.94 = f32[1,64,32,128]{3,2,1,0:T(8,128)S(1)} custom-call(f32[1]{0:T(128)S(1)} %bitcast.58, f32[1,68,36,128]{3,2,1,0:T(8,128)S(1)} %slice.152.conc_ref, f32[4,68,36,128]{3,2,1,0:T(8,128)} %slice.153.coeff_ref), custom_call_target="tpu_custom_call" | custom-call | flops 20971520 | bytes 7315456 | tf_op jit(solution)/shard_map/pallas_call | solution.py:160
  75.3 1.4 collective-permute-start.7
  76.7 0.7 collective-permute-start.4
  78.0 1.1 collective-permute-done.6
  79.0 3.1 %collective-permute-done.5 = f32[1,2,32,128]{3,2,1,0:T(8,128)S(1)} collective-permute-done((f32[1,2,32,128]{3,2,1,0:T(8,128)S(1)}, f32[1,2,32,128]{3,2,1,0:T(8,128)S(1)}, u32[]{:S(2)}, u32[]{:S(2)}) %collective-permute-start.5) | collective-permute-done | bytes 32800 | tf_op jit(solution)/shard_map/ppermute | solution.py:22
  82.1 2.1 %collective-permute-done.4 = f32[1,64,2,128]{3,2,1,0:T(2,128)S(1)} collective-permute-done((f32[1,64,2,128]{3,2,1,0:T(2,128)S(1)}, f32[1,64,2,128]{3,2,1,0:T(2,128)S(1)}, u32[]{:S(2)}, u32[]{:S(2)}) %collective-permute-start.4) | collective-permute-done | bytes 65568 | tf_op jit(solution)/shard_map/ppermute | solution.py:24
  84.5 9.5 %shard_map.95 = f32[1,64,32,128]{3,2,1,0:T(8,128)S(1)} custom-call(f32[1]{0:T(128)S(1)} %bitcast.59, f32[1,68,36,128]{3,2,1,0:T(8,128)S(1)} %select_maximum_fusion.4.conc_ref, f32[4,68,36,128]{3,2,1,0:T(8,128)} %slice.153.coeff_ref), custom_call_target="tpu_custom_call" | custom-call | flops 20971520 | bytes 7315456 | tf_op jit(solution)/shard_map/pallas_call | solution.py:160
  94.0 1.0 copy-done.2
  95.4 0.9 multiply_reduce_fusion
  96.5 3.3 %fusion = f32[64]{0:T(128)S(1)} fusion(bf16[64,32,1024]{2,0,1:T(8,128)(2,1)} %copy-done, f32[32,1024]{1,0:T(8,128)S(1)} %mul.85), kind=kLoop, calls=%fused_computation.6 | loop fusion | flops 6291392 | bytes 4325632 | tf_op jit(solution)/shard_map/reduce_sum | solution.py:252
  99.8 0.7 pad_maximum_fusion.7
  100.6 0.6 compare_reduce_fusion
  101.7 0.7 fusion.32
  102.4 1.6 collective-permute-start.20
  104.0 0.7 select_bitcast_fusion
  104.7 1.3 collective-permute-done.20
  106.0 3.2 %collective-permute-start.21 = (f32[65]{0:T(128)S(1)}, f32[65]{0:T(128)S(1)}, u32[]{:S(2)}, u32[]{:S(2)}) collective-permute-start(f32[65]{0:T(128)S(1)} %add.88), channel_id=1, source_target_pairs={{0,64},{16,80},{32,96},{48,112},{64,0},{80,16},{96,32},{112,48},{1... | collective-permute-start | bytes 788 | tf_op jit(solution)/shard_map/ppermute | solution.py:37
  109.2 5.5 %custom-call.8 = f32[1,64,64]{1,2,0:T(8,128)} custom-call(f32[1,64,64]{2,1,0:T(8,128)S(1)} %get-tuple-element.42), custom_call_target="InvertDiagBlocksLowerTriangular" | custom-call | tf_op jit(solution)/shard_map/triangular_solve | solution.py:229
  114.7 0.6 scatter.10
  115.4 4.5 %slice.158.conc_ref = f32[3,68,36,128]{3,2,1,0:T(8,128)} slice(f32[8,68,36,128]{3,2,1,0:T(8,128)} %copy-done.5), slice={[1:4], [0:68], [0:36], [0:128]} | slice | bytes 7520256 | tf_op jit(solution)/shard_map/slice | solution.py:258
  119.8 23.8 %shard_map.96 = f32[3,64,32,128]{3,2,1,0:T(8,128)S(1)} custom-call(f32[3]{0:T(128)S(1)} %slice.143.scale_ref, f32[3,68,36,128]{3,2,1,0:T(8,128)} %slice.158.conc_ref, f32[4,68,36,128]{3,2,1,0:T(8,128)} %slice.153.coeff_ref), custom_call_target="tpu_custom_call" | custom-call | flops 62914560 | bytes 11919360 | tf_op jit(solution)/shard_map/pallas_call | solution.py:160
  144.1 0.9 fusion.25
  145.0 3.9 %collective-permute-done.23 = f32[65]{0:T(128)S(1)} collective-permute-done((f32[65]{0:T(128)S(1)}, f32[65]{0:T(128)S(1)}, u32[]{:S(2)}, u32[]{:S(2)}) %collective-permute-start.23) | collective-permute-done | bytes 292 | tf_op jit(solution)/shard_map/ppermute | solution.py:37
  148.9 0.7 fusion.24
  149.6 1.8 collective-permute-start.11
  151.6 0.8 collective-permute-done.24
  152.4 1.9 collective-permute-start.25
  155.0 2.5 %collective-permute-done.25 = f32[65]{0:T(128)} collective-permute-done((f32[65]{0:T(128)S(1)}, f32[65]{0:T(128)}, u32[]{:S(2)}, u32[]{:S(2)}) %collective-permute-start.25) | collective-permute-done | bytes 292 | tf_op jit(solution)/shard_map/ppermute | solution.py:37
  157.5 0.7 add_multiply_fusion
  158.1 0.7 slice.151
  158.8 1.5 multiply_reduce_fusion.2
  160.3 1.0 multiply_reduce_fusion.1
  161.3 3.5 %fusion.1 = f32[32,1024]{1,0:T(8,128)S(1)} fusion(bf16[64,32,1024]{2,0,1:T(8,128)(2,1)} %copy-done, f32[64]{0:T(128)S(1)} %get-tuple-element.61), kind=kLoop, calls=%fused_computation.7 | loop fusion | flops 6258688 | bytes 4325632 | tf_op jit(solution)/shard_map/reduce_sum | solution.py:272
  166.2 0.7 fusion.5.last_ref
  167.3 0.7 copy.15
  168.0 2.2 %copy-done.1 = bf16[64,32,1024]{2,0,1:T(8,128)(2,1)S(1)} copy-done((bf16[64,32,1024]{2,0,1:T(8,128)(2,1)S(1)}, bf16[64,32,1024]{2,0,1:T(8,128)(2,1)}, u32[]{:S(2)}) %copy-start.1) | copy-done | bytes 4194328
  170.2 7.5 %shard_map.98._ = f32[65,32,1024]{2,1,0:T(8,128)} custom-call(bf16[3,65,64]{2,1,0:T(8,128)(2,1)S(1)} %pad_maximum_fusion.6.mix_ref, bf16[32,64,1024]{2,1,0:T(8,128)(2,1)S(1)} %bitcast.57), custom_call_target="tpu_custom_call" | custom-call | flops 817889280 | bytes 12713984 | tf_op jit(solution)/shard_map/pallas_call | solution.py:198
  177.7 1.6 shard_map.99
  179.3 3.8 %select_maximum_fusion.2.conc_ref = f32[3,68,36,128]{3,2,1,0:T(8,128)} fusion(f32[3,64,2,128]{3,2,1,0:T(2,128)} %collective-permute-done.11, f32[3,64,2,128]{3,2,1,0:T(2,128)} %collective-permute-done.8, f32[3,2,32,128]{3,2,1,0:T(8,128)} %collective-permute-done.10, f32[3,64,32,128]{3,2,1,0:T(8,128)S(1)} %shard_map.96, ...), kind=kLoop, calls=%fused_computation.9 | loop fusion | flops 7520256 | bytes 7495680 | tf_op jit(solution)/shard_map/concatenate | solution.py:28
  183.1 23.9 %shard_map.97 = f32[3,64,32,128]{3,2,1,0:T(8,128)S(1)} custom-call(f32[3]{0:T(128)S(1)} %slice.143.scale_ref, f32[3,68,36,128]{3,2,1,0:T(8,128)} %select_maximum_fusion.2.conc_ref, f32[4,68,36,128]{3,2,1,0:T(8,128)} %slice.153.coeff_ref), custom_call_target="tpu_custom_call" | custom-call | flops 62914560 | bytes 11919360 | tf_op jit(solution)/shard_map/pallas_call | solution.py:160
  207.0 2.5 %pad_maximum_fusion = f32[4,64,32,128]{3,2,1,0:T(8,128)} fusion(f32[3,64,32,128]{3,2,1,0:T(8,128)S(1)} %shard_map.97, f32[1,64,32,128]{3,2,1,0:T(8,128)S(1)} %copy-done.3), kind=kLoop, calls=%fused_computation.8 | loop fusion | flops 1048576 | bytes 8388608 | tf_op jit(solution)/shard_map/concatenate | solution.py:260
  (76 shorter events, 4.4 us)
Async XLA Ops:
  0.6 3.7 %copy-start.9 = (bf16[16,32,1024]{2,1,0:T(8,128)(2,1)S(1)}, bf16[16,32,1024]{2,1,0:T(8,128)(2,1)}, u32[]{:S(2)}) copy-start(bf16[16,32,1024]{2,1,0:T(8,128)(2,1)} %param.19) | copy-start | bytes 3145732
  5.0 2.1 %copy-start = (bf16[64,32,1024]{2,0,1:T(8,128)(2,1)}, bf16[64,32,1024]{2,0,1:T(8,128)(2,1)S(1)}, u32[]{:S(2)}) copy-start(bf16[64,32,1024]{2,0,1:T(8,128)(2,1)S(1)} %copy_dynamic-update-slice_fusion.1) | copy-start | bytes 12582916
  5.0 14.7 %copy-start.6 = (f32[4,64,32,128]{3,2,1,0:T(8,128)S(1)}, f32[4,64,32,128]{3,2,1,0:T(8,128)}, u32[]{:S(2)}) copy-start(f32[4,64,32,128]{3,2,1,0:T(8,128)} %param.13) | copy-start | bytes 12582916
  5.0 14.7 %copy-start.7 = (f32[3,64,32,128]{3,2,1,0:T(8,128)S(1)}, f32[3,64,32,128]{3,2,1,0:T(8,128)}, u32[]{:S(2)}) copy-start(f32[3,64,32,128]{3,2,1,0:T(8,128)} %param.14) | copy-start | bytes 9437188
  5.0 14.7 %copy-start.8 = (f32[64,32,128]{2,1,0:T(8,128)S(1)}, f32[64,32,128]{2,1,0:T(8,128)}, u32[]{:S(2)}) copy-start(f32[64,32,128]{2,1,0:T(8,128)} %param.15) | copy-start | bytes 3145732
  7.1 1.2 collective-permute-start.12
  8.3 3.9 %collective-permute-start.13 = (f32[64,64]{1,0:T(8,128)S(1)}, f32[64,64]{1,0:T(8,128)S(1)}, u32[]{:S(2)}, u32[]{:S(2)}) collective-permute-start(f32[64,64]{1,0:T(8,128)S(1)} %add.79), channel_id=1, source_target_pairs={{0,32},{16,48},{32,0},{48,16},{64,96},{80,112},{96,64},{112,80},{1... | collective-permute-start | bytes 49160 | tf_op jit(solution)/shard_map/ppermute | solution.py:37
  12.2 5.4 %collective-permute-start.14 = (f32[64,64]{1,0:T(8,128)S(1)}, f32[64,64]{1,0:T(8,128)S(1)}, u32[]{:S(2)}, u32[]{:S(2)}) collective-permute-start(f32[64,64]{1,0:T(8,128)S(1)} %add.80), channel_id=1, source_target_pairs={{0,64},{16,80},{32,96},{48,112},{64,0},{80,16},{96,32},{112,48},{1... | collective-permute-start | bytes 49160 | tf_op jit(solution)/shard_map/ppermute | solution.py:37
  17.7 8.2 %collective-permute-start.15 = (f32[64,64]{1,0:T(8,128)S(1)}, f32[64,64]{1,0:T(8,128)S(1)}, u32[]{:S(2)}, u32[]{:S(2)}) collective-permute-start(f32[64,64]{1,0:T(8,128)S(1)} %add.81), channel_id=1, source_target_pairs={{0,1},{1,0},{2,3},{3,2},{4,5},{5,4},{6,7},{7,6},{8,9},{9,8},{10,11... | collective-permute-start | bytes 49160 | tf_op jit(solution)/shard_map/ppermute | solution.py:37
  21.2 31.8 %collective-permute-start.3 = (f32[8,64,2,128]{3,2,1,0:T(2,128)}, f32[8,64,2,128]{3,2,1,0:T(2,128)}, u32[]{:S(2)}, u32[]{:S(2)}) collective-permute-start(f32[8,64,2,128]{3,2,1,0:T(2,128)} %get-tuple-element.47), channel_id=1, source_target_pairs={{1,0},{2,1},{3,2},{4,3},{5,4},{6,5},{7,6},{8,7},{9,8},{10,9},{11,1... | collective-permute-start | bytes 1572872 | tf_op jit(solution)/shard_map/ppermute | solution.py:25
  25.9 27.1 %collective-permute-start = (f32[8,64,2,128]{3,2,1,0:T(2,128)}, f32[8,64,2,128]{3,2,1,0:T(2,128)}, u32[]{:S(2)}, u32[]{:S(2)}) collective-permute-start(f32[8,64,2,128]{3,2,1,0:T(2,128)} %get-tuple-element.46), channel_id=1, source_target_pairs={{0,1},{1,2},{2,3},{3,4},{4,5},{5,6},{6,7},{7,8},{8,9},{9,10},{10,1... | collective-permute-start | bytes 1572872 | tf_op jit(solution)/shard_map/ppermute | solution.py:24
  25.9 18.6 %copy-start.4 = (f32[4]{0:T(128)S(1)}, f32[4]{0:T(128)}, u32[]{:S(2)}) copy-start(f32[4]{0:T(128)} %param.16) | copy-start | bytes 52
  25.9 18.6 %copy-start.11 = (f32[48]{0:T(128)S(1)}, f32[48]{0:T(128)}, u32[]{:S(2)}) copy-start(f32[48]{0:T(128)} %param.18) | copy-start | bytes 580
  25.9 11.6 %collective-permute-start.16 = (f32[64,64]{1,0:T(8,128)S(1)}, f32[64,64]{1,0:T(8,128)S(1)}, u32[]{:S(2)}, u32[]{:S(2)}) collective-permute-start(f32[64,64]{1,0:T(8,128)S(1)} %add.82), channel_id=1, source_target_pairs={{0,2},{1,3},{2,0},{3,1},{4,6},{5,7},{6,4},{7,5},{8,10},{9,11},{10,... | collective-permute-start | bytes 49160 | tf_op jit(solution)/shard_map/ppermute | solution.py:37
  27.7 25.2 %collective-permute-start.2 = (f32[8,2,32,128]{3,2,1,0:T(8,128)}, f32[8,2,32,128]{3,2,1,0:T(8,128)S(1)}, u32[]{:S(2)}, u32[]{:S(2)}) collective-permute-start(f32[8,2,32,128]{3,2,1,0:T(8,128)} %get-tuple-element.45), channel_id=1, source_target_pairs={{16,0},{32,16},{48,32},{64,48},{80,64},{96,80},{112,96},{0,112},{1... | collective-permute-start | bytes 786440 | tf_op jit(solution)/shard_map/ppermute | solution.py:23
  27.7 25.3 %collective-permute-start.1 = (f32[8,2,32,128]{3,2,1,0:T(8,128)}, f32[8,2,32,128]{3,2,1,0:T(8,128)}, u32[]{:S(2)}, u32[]{:S(2)}) collective-permute-start(f32[8,2,32,128]{3,2,1,0:T(8,128)} %get-tuple-element.44), channel_id=1, source_target_pairs={{0,16},{16,32},{32,48},{48,64},{64,80},{80,96},{96,112},{112,0},{1... | collective-permute-start | bytes 786440 | tf_op jit(solution)/shard_map/ppermute | solution.py:22
  37.5 4.0 %collective-permute-start.17 = (f32[64,64]{1,0:T(8,128)S(1)}, f32[64,64]{1,0:T(8,128)S(1)}, u32[]{:S(2)}, u32[]{:S(2)}) collective-permute-start(f32[64,64]{1,0:T(8,128)S(1)} %add.83), channel_id=1, source_target_pairs={{0,4},{1,5},{2,6},{3,7},{4,0},{5,1},{6,2},{7,3},{8,12},{9,13},{10,... | collective-permute-start | bytes 49160 | tf_op jit(solution)/shard_map/ppermute | solution.py:37
  41.5 5.4 %collective-permute-start.18 = (f32[64,64]{1,0:T(8,128)S(1)}, f32[64,64]{1,0:T(8,128)S(1)}, u32[]{:S(2)}, u32[]{:S(2)}) collective-permute-start(f32[64,64]{1,0:T(8,128)S(1)} %add.84), channel_id=1, source_target_pairs={{0,8},{1,9},{2,10},{3,11},{4,12},{5,13},{6,14},{7,15},{8,0},{9,1},... | collective-permute-start | bytes 49160 | tf_op jit(solution)/shard_map/ppermute | solution.py:37
  59.7 5.9 %copy-start.5 = (f32[8,68,36,128]{3,2,1,0:T(8,128)}, f32[8,68,36,128]{3,2,1,0:T(8,128)S(1)}, u32[]{:S(2)}) copy-start(f32[8,68,36,128]{3,2,1,0:T(8,128)S(1)} %select_maximum_fusion) | copy-start | bytes 30081028
  75.3 6.8 %collective-permute-start.7 = (f32[1,64,2,128]{3,2,1,0:T(2,128)S(1)}, f32[1,64,2,128]{3,2,1,0:T(2,128)S(1)}, u32[]{:S(2)}, u32[]{:S(2)}) collective-permute-start(f32[1,64,2,128]{3,2,1,0:T(2,128)S(1)} %get-tuple-element.55), channel_id=1, source_target_pairs={{1,0},{2,1},{3,2},{4,3},{5,4},{6,5},{7,6},{8,7},{9,8},{10,9},{11,1... | collective-permute-start | bytes 196616 | tf_op jit(solution)/shard_map/ppermute | solution.py:25
  76.7 7.6 %collective-permute-start.4 = (f32[1,64,2,128]{3,2,1,0:T(2,128)S(1)}, f32[1,64,2,128]{3,2,1,0:T(2,128)S(1)}, u32[]{:S(2)}, u32[]{:S(2)}) collective-permute-start(f32[1,64,2,128]{3,2,1,0:T(2,128)S(1)} %get-tuple-element.54), channel_id=1, source_target_pairs={{0,1},{1,2},{2,3},{3,4},{4,5},{5,6},{6,7},{7,8},{8,9},{9,10},{10,1... | collective-permute-start | bytes 196616 | tf_op jit(solution)/shard_map/ppermute | solution.py:24
  77.4 1.6 collective-permute-start.6
  77.4 4.7 %collective-permute-start.5 = (f32[1,2,32,128]{3,2,1,0:T(8,128)S(1)}, f32[1,2,32,128]{3,2,1,0:T(8,128)S(1)}, u32[]{:S(2)}, u32[]{:S(2)}) collective-permute-start(f32[1,2,32,128]{3,2,1,0:T(8,128)S(1)} %get-tuple-element.52), channel_id=1, source_target_pairs={{0,16},{16,32},{32,48},{48,64},{64,80},{80,96},{96,112},{112,0},{1... | collective-permute-start | bytes 98312 | tf_op jit(solution)/shard_map/ppermute | solution.py:22
  94.0 1.0 copy-start.2
  100.5 1.2 collective-permute-start.19
  102.4 3.6 %collective-permute-start.20 = (f32[65]{0:T(128)S(1)}, f32[65]{0:T(128)S(1)}, u32[]{:S(2)}, u32[]{:S(2)}) collective-permute-start(f32[65]{0:T(128)S(1)} %fusion.32), channel_id=1, source_target_pairs={{0,32},{16,48},{32,0},{48,16},{64,96},{80,112},{96,64},{112,80},{1... | collective-permute-start | bytes 788 | tf_op jit(solution)/shard_map/ppermute | solution.py:37
  106.0 13.8 %collective-permute-start.21 = (f32[65]{0:T(128)S(1)}, f32[65]{0:T(128)S(1)}, u32[]{:S(2)}, u32[]{:S(2)}) collective-permute-start(f32[65]{0:T(128)S(1)} %add.88), channel_id=1, source_target_pairs={{0,64},{16,80},{32,96},{48,112},{64,0},{80,16},{96,32},{112,48},{1... | collective-permute-start | bytes 788 | tf_op jit(solution)/shard_map/ppermute | solution.py:37
  119.8 23.8 %collective-permute-start.22 = (f32[65]{0:T(128)S(1)}, f32[65]{0:T(128)S(1)}, u32[]{:S(2)}, u32[]{:S(2)}) collective-permute-start(f32[65]{0:T(128)S(1)} %add.89), channel_id=1, source_target_pairs={{0,1},{1,0},{2,3},{3,2},{4,5},{5,4},{6,7},{7,6},{8,9},{9,8},{10,11... | collective-permute-start | bytes 788 | tf_op jit(solution)/shard_map/ppermute | solution.py:37
  143.7 5.2 %collective-permute-start.23 = (f32[65]{0:T(128)S(1)}, f32[65]{0:T(128)S(1)}, u32[]{:S(2)}, u32[]{:S(2)}) collective-permute-start(f32[65]{0:T(128)S(1)} %add.90), channel_id=1, source_target_pairs={{0,2},{1,3},{2,0},{3,1},{4,6},{5,7},{6,4},{7,5},{8,10},{9,11},{10,... | collective-permute-start | bytes 788 | tf_op jit(solution)/shard_map/ppermute | solution.py:37
  148.9 3.6 %collective-permute-start.24 = (f32[65]{0:T(128)S(1)}, f32[65]{0:T(128)S(1)}, u32[]{:S(2)}, u32[]{:S(2)}) collective-permute-start(f32[65]{0:T(128)S(1)} %add.91), channel_id=1, source_target_pairs={{0,4},{1,5},{2,6},{3,7},{4,0},{5,1},{6,2},{7,3},{8,12},{9,13},{10,... | collective-permute-start | bytes 788 | tf_op jit(solution)/shard_map/ppermute | solution.py:37
  149.6 29.7 %collective-permute-start.11 = (f32[3,64,2,128]{3,2,1,0:T(2,128)}, f32[3,64,2,128]{3,2,1,0:T(2,128)}, u32[]{:S(2)}, u32[]{:S(2)}) collective-permute-start(f32[3,64,2,128]{3,2,1,0:T(2,128)} %get-tuple-element.51), channel_id=1, source_target_pairs={{1,0},{2,1},{3,2},{4,3},{5,4},{6,5},{7,6},{8,7},{9,8},{10,9},{11,1... | collective-permute-start | bytes 589832 | tf_op jit(solution)/shard_map/ppermute | solution.py:25
  151.4 27.9 %collective-permute-start.8 = (f32[3,64,2,128]{3,2,1,0:T(2,128)}, f32[3,64,2,128]{3,2,1,0:T(2,128)}, u32[]{:S(2)}, u32[]{:S(2)}) collective-permute-start(f32[3,64,2,128]{3,2,1,0:T(2,128)} %get-tuple-element.50), channel_id=1, source_target_pairs={{0,1},{1,2},{2,3},{3,4},{4,5},{5,6},{6,7},{7,8},{8,9},{9,10},{10,1... | collective-permute-start | bytes 589832 | tf_op jit(solution)/shard_map/ppermute | solution.py:24
  152.4 5.0 %collective-permute-start.25 = (f32[65]{0:T(128)S(1)}, f32[65]{0:T(128)}, u32[]{:S(2)}, u32[]{:S(2)}) collective-permute-start(f32[65]{0:T(128)S(1)} %add.92), channel_id=1, source_target_pairs={{0,8},{1,9},{2,10},{3,11},{4,12},{5,13},{6,14},{7,15},{8,0},{9,1},... | collective-permute-start | bytes 788 | tf_op jit(solution)/shard_map/ppermute | solution.py:37
  154.3 24.9 %collective-permute-start.10 = (f32[3,2,32,128]{3,2,1,0:T(8,128)}, f32[3,2,32,128]{3,2,1,0:T(8,128)}, u32[]{:S(2)}, u32[]{:S(2)}) collective-permute-start(f32[3,2,32,128]{3,2,1,0:T(8,128)} %get-tuple-element.49), channel_id=1, source_target_pairs={{16,0},{32,16},{48,32},{64,48},{80,64},{96,80},{112,96},{0,112},{1... | collective-permute-start | bytes 294920 | tf_op jit(solution)/shard_map/ppermute | solution.py:23
  154.3 24.9 %collective-permute-start.9 = (f32[3,2,32,128]{3,2,1,0:T(8,128)}, f32[3,2,32,128]{3,2,1,0:T(8,128)}, u32[]{:S(2)}, u32[]{:S(2)}) collective-permute-start(f32[3,2,32,128]{3,2,1,0:T(8,128)} %get-tuple-element.48), channel_id=1, source_target_pairs={{0,16},{16,32},{32,48},{48,64},{64,80},{80,96},{96,112},{112,0},{1... | collective-permute-start | bytes 294920 | tf_op jit(solution)/shard_map/ppermute | solution.py:22
  155.0 12.0 %copy-start.10 = (f32[65,65]{1,0:T(8,128)S(1)}, f32[65,65]{1,0:T(8,128)}, u32[]{:S(2)}) copy-start(f32[65,65]{1,0:T(8,128)} %scatter.10) | copy-start | bytes 50704
  168.0 2.2 %copy-start.1 = (bf16[64,32,1024]{2,0,1:T(8,128)(2,1)S(1)}, bf16[64,32,1024]{2,0,1:T(8,128)(2,1)}, u32[]{:S(2)}) copy-start(bf16[64,32,1024]{2,0,1:T(8,128)(2,1)} %copy-done) | copy-start | bytes 12582916
  183.1 23.9 %copy-start.3 = (f32[1,64,32,128]{3,2,1,0:T(8,128)S(1)}, f32[1,64,32,128]{3,2,1,0:T(8,128)}, u32[]{:S(2)}) copy-start(f32[1,64,32,128]{3,2,1,0:T(8,128)} %copy-done.2) | copy-start | bytes 3145732

commit v3 on v1

--- a/solution.py
+++ b/solution.py
@@ -223,6 +223,11 @@
     local_gram = lax.dot_general(
         static, static, (((1, 2), (1, 2)), ((), ())), preferred_element_type=jnp.float32
     )
+    coeffs = jnp.concatenate([velocity, diffusivity[None]], 0)
+    first = halo(jnp.concatenate([scalars[:1], coeffs], 0))
+    coeff_pad = first[1:]
+    middle0 = stencil_step(first[:1], coeff_pad, diff_scale[:1])
+    local_gram, middle0 = lax.optimization_barrier((local_gram, middle0))
     gram_static = butterfly_sum(local_gram) * (weight[:, None] * weight[None, :]) / total_rows
     lower_static = jnp.linalg.cholesky(gram_static)
     width = rank + snaps
@@ -233,10 +238,6 @@
     mix_ext = jnp.concatenate([mix, jnp.zeros((1, width), jnp.float32)], 0)
     basis_ext = basis_rows(mix_ext, static)
 
-    coeffs = jnp.concatenate([velocity, diffusivity[None]], 0)
-    first = halo(jnp.concatenate([scalars[:1], coeffs], 0))
-    coeff_pad = first[1:]
-    middle0 = stencil_step(first[:1], coeff_pad, diff_scale[:1])
     result0 = stencil_step(halo(middle0), coeff_pad, diff_scale[:1])
 
     coarse = result0[0, ::2]

time: 207 us -> 206 us (level)
  starting transfers between devices: 36.6 us -> 49.9 us
  waiting for transfers between devices: 26.4 us -> 15.2 us
    ppermute x14, waiting for transfers between devices: 24.1 us -> 11 us  [butterfly_sum(): value = value + lax.ppermute(value, axis, pairs)]
    ppermute x4, starting transfers between devices: 4.07 us -> 11.3 us  [halo(): high_x = lax.ppermute(block[:, :width], 'gx', bx)]
    ppermute x4, starting transfers between devices: 13.1 us -> 18.1 us  [halo(): high_y = lax.ppermute(block[:, :, :width], 'gy', by)]
    ppermute x4, waiting for transfers between devices: 0.01 us -> 3.49 us  [halo(): high_y = lax.ppermute(block[:, :, :width], 'gy', by)]
    unnamed x34 -> x32, local copies, waits for them, and re-layouts: 8.54 us -> 7.07 us
  transfers between devices with their start and end apart: 30 -> 30, of which waited for: 10 -> 6; matrix products, arithmetic and copies ran while one was open for 23% -> 21% of each run, Pallas kernels for 25% -> 21%
where the time goes in v3:
time: 206 us
  Pallas kernels  75.8 us (37%)
  starting transfers between devices  49.9 us (24%)
  other arithmetic  40.2 us (20%)
  local copies, waits for them, and re-layouts  18.5 us (9%)
  waiting for transfers between devices  15.2 us (7%)
  matrix products  3.54 us (2%)
  between operations  2.42 us (1%)
    pallas_call x4, Pallas kernels, stencil_step(): pl.pallas_call(stencil_body, out_shape=jax.ShapeDtypeStruct((count, nx, n...  66.7 us
    ppermute x4, starting transfers between devices, halo(): high_y = lax.ppermute(block[:, :, :width], 'gy', by)  18.1 us
    ppermute x14, starting transfers between devices, butterfly_sum(): value = value + lax.ppermute(value, axis, pairs)  16.9 us
    ppermute x4, starting transfers between devices, halo(): high_x = lax.ppermute(block[:, :width], 'gx', bx)  11.3 us
    ppermute x14, waiting for transfers between devices, butterfly_sum(): value = value + lax.ppermute(value, axis, pairs)  11 us
    concatenate x4, other arithmetic, halo(): jnp.concatenate([jnp.pad(low_y, edge), rows, jnp.pad(high_y, edge)], axis=2)  10.8 us
    pallas_call x1, Pallas kernels, basis_rows(): pl.pallas_call(basis_body, out_shape=jax.ShapeDtypeStruct((rows, span, co...  7.53 us
    another operation x3, other arithmetic, per_device(): lower_static = jnp.linalg.cholesky(gram_static)  7.29 us
  transfers between devices with their start and end apart: 30, of which 6 were waited for; matrix products, arithmetic and copies ran while one was open for 21% of the time, Pallas kernels for 21%

profile of v3, /device:TPU:0, one launch (start us, length us, event | category | flops | bytes accessed | tf_op | source)
XLA Modules:
  0.0 205.6 jit_solution(17257566197804791747)
XLA Ops:
  0.7 1.4 slice.152
  2.1 1.1 pad_maximum_fusion.5
  3.3 2.9 %collective-permute-start.2 = (f32[5,2,32,128]{3,2,1,0:T(8,128)S(1)}, f32[5,2,32,128]{3,2,1,0:T(8,128)S(1)}, u32[]{:S(2)}, u32[]{:S(2)}) collective-permute-start(f32[5,2,32,128]{3,2,1,0:T(8,128)S(1)} %get-tuple-element.49), channel_id=1, source_target_pairs={{16,0},{32,16},{48,32},{64,48},{80,64},{96,80},{112,96},{0,112},{1... | collective-permute-start | bytes 491528 | tf_op jit(solution)/shard_map/ppermute | solution.py:23
  6.5 2.1 %collective-permute-start = (f32[5,64,2,128]{3,2,1,0:T(2,128)S(1)}, f32[5,64,2,128]{3,2,1,0:T(2,128)S(1)}, u32[]{:S(2)}, u32[]{:S(2)}) collective-permute-start(f32[5,64,2,128]{3,2,1,0:T(2,128)S(1)} %get-tuple-element.50), channel_id=1, source_target_pairs={{0,1},{1,2},{2,3},{3,4},{4,5},{5,6},{6,7},{7,8},{8,9},{9,10},{10,1... | collective-permute-start | bytes 983048 | tf_op jit(solution)/shard_map/ppermute | solution.py:24
  8.6 4.4 %collective-permute-start.3 = (f32[5,64,2,128]{3,2,1,0:T(2,128)S(1)}, f32[5,64,2,128]{3,2,1,0:T(2,128)S(1)}, u32[]{:S(2)}, u32[]{:S(2)}) collective-permute-start(f32[5,64,2,128]{3,2,1,0:T(2,128)S(1)} %get-tuple-element.51), channel_id=1, source_target_pairs={{1,0},{2,1},{3,2},{4,3},{5,4},{6,5},{7,6},{8,7},{9,8},{10,9},{11,1... | collective-permute-start | bytes 983048 | tf_op jit(solution)/shard_map/ppermute | solution.py:25
  13.0 0.9 fusion.25
  13.9 1.7 copy_dynamic-update-slice_fusion
  15.6 0.6 copy_dynamic-update-slice_fusion.1
  16.2 1.2 convolution_bitcast_fusion.1
  17.5 0.8 copy-done
  18.2 0.7 fusion.24
  18.9 0.6 collective-permute-done
  19.5 2.9 %select_maximum_fusion = f32[5,68,36,128]{3,2,1,0:T(8,128)S(1)} fusion(f32[5,64,2,128]{3,2,1,0:T(2,128)S(1)} %collective-permute-done.3, f32[5,64,2,128]{3,2,1,0:T(2,128)S(1)} %collective-permute-done, f32[5,2,32,128]{3,2,1,0:T(8,128)S(1)} %collective-permute-done.2, f32[1,64,32,128]{3,2,1,0:T(8,128)S(1)} %bitcast.62, f32[3,64,32,128]{3,2,1,0:T(8,128)S(1)} %copy-done.5, ...), kind=kLoop, calls=%fused_computation.4 | loop fusion | flops 15667200 | bytes 12492800 | tf_op jit(solution)/shard_map/concatenate | solution.py:28
  22.6 2.8 %slice.177.coeff_ref = f32[4,68,36,128]{3,2,1,0:T(8,128)} slice(f32[5,68,36,128]{3,2,1,0:T(8,128)S(1)} %select_maximum_fusion), slice={[1:5], [0:68], [0:36], [0:128]} | slice | bytes 10027008 | tf_op jit(solution)/shard_map/slice | solution.py:228
  25.4 9.5 %shard_map.94 = f32[1,64,32,128]{3,2,1,0:T(8,128)S(1)} custom-call(f32[1]{0:T(128)S(1)} %bitcast.58, f32[1,68,36,128]{3,2,1,0:T(8,128)S(1)} %slice.176.conc_ref, f32[4,68,36,128]{3,2,1,0:T(8,128)} %slice.177.coeff_ref), custom_call_target="tpu_custom_call" | custom-call | flops 20971520 | bytes 7315456 | tf_op jit(solution)/shard_map/pallas_call | solution.py:160
  35.5 2.5 %collective-permute-start.6 = (f32[1,2,32,128]{3,2,1,0:T(8,128)S(1)}, f32[1,2,32,128]{3,2,1,0:T(8,128)S(1)}, u32[]{:S(2)}, u32[]{:S(2)}) collective-permute-start(f32[1,2,32,128]{3,2,1,0:T(8,128)S(1)} %get-tuple-element.61), channel_id=1, source_target_pairs={{16,0},{32,16},{48,32},{64,48},{80,64},{96,80},{112,96},{0,112},{1... | collective-permute-start | bytes 98312 | tf_op jit(solution)/shard_map/ppermute | solution.py:23
  38.0 5.3 %collective-permute-start.7 = (f32[1,64,2,128]{3,2,1,0:T(2,128)S(1)}, f32[1,64,2,128]{3,2,1,0:T(2,128)S(1)}, u32[]{:S(2)}, u32[]{:S(2)}) collective-permute-start(f32[1,64,2,128]{3,2,1,0:T(2,128)S(1)} %get-tuple-element.63), channel_id=1, source_target_pairs={{1,0},{2,1},{3,2},{4,3},{5,4},{6,5},{7,6},{8,7},{9,8},{10,9},{11,1... | collective-permute-start | bytes 196616 | tf_op jit(solution)/shard_map/ppermute | solution.py:25
  43.9 3.5 %collective-permute-done.17 = f32[64,64]{1,0:T(8,128)S(1)} collective-permute-done((f32[64,64]{1,0:T(8,128)S(1)}, f32[64,64]{1,0:T(8,128)S(1)}, u32[]{:S(2)}, u32[]{:S(2)}) %collective-permute-start.17) | collective-permute-done | bytes 16416 | tf_op jit(solution)/shard_map/ppermute | solution.py:37
  47.4 3.0 %collective-permute-start.10 = (f32[3,2,32,128]{3,2,1,0:T(8,128)}, f32[3,2,32,128]{3,2,1,0:T(8,128)}, u32[]{:S(2)}, u32[]{:S(2)}) collective-permute-start(f32[3,2,32,128]{3,2,1,0:T(8,128)} %get-tuple-element.53), channel_id=1, source_target_pairs={{16,0},{32,16},{48,32},{64,48},{80,64},{96,80},{112,96},{0,112},{1... | collective-permute-start | bytes 294920 | tf_op jit(solution)/shard_map/ppermute | solution.py:23
  50.4 0.6 collective-permute-start.18
  51.1 9.5 %shard_map.95 = f32[1,64,32,128]{3,2,1,0:T(8,128)S(1)} custom-call(f32[1]{0:T(128)S(1)} %bitcast.59, f32[1,68,36,128]{3,2,1,0:T(8,128)S(1)} %select_maximum_fusion.6.conc_ref, f32[4,68,36,128]{3,2,1,0:T(8,128)} %slice.177.coeff_ref), custom_call_target="tpu_custom_call" | custom-call | flops 20971520 | bytes 7315456 | tf_op jit(solution)/shard_map/pallas_call | solution.py:160
  60.7 1.0 copy-done.2
  62.0 0.9 multiply_reduce_fusion
  63.0 0.8 mul.85
  63.8 3.3 %fusion = f32[64]{0:T(128)S(1)} fusion(bf16[64,32,1024]{2,0,1:T(8,128)(2,1)} %copy-done, f32[32,1024]{1,0:T(8,128)} %mul.85), kind=kLoop, calls=%fused_computation.2 | loop fusion | flops 6291392 | bytes 4325632 | tf_op jit(solution)/shard_map/reduce_sum | solution.py:252
  67.1 0.7 pad_maximum_fusion.7
  67.9 5.3 %collective-permute-start.11 = (f32[3,64,2,128]{3,2,1,0:T(2,128)S(1)}, f32[3,64,2,128]{3,2,1,0:T(2,128)S(1)}, u32[]{:S(2)}, u32[]{:S(2)}) collective-permute-start(f32[3,64,2,128]{3,2,1,0:T(2,128)S(1)} %copy-done.11), channel_id=1, source_target_pairs={{1,0},{2,1},{3,2},{4,3},{5,4},{6,5},{7,6},{8,7},{9,8},{10,9},{11,1... | collective-permute-start | bytes 589832 | tf_op jit(solution)/shard_map/ppermute | solution.py:25
  73.4 0.7 fusion.34
  74.6 3.5 %collective-permute-done.11 = f32[3,64,2,128]{3,2,1,0:T(2,128)S(1)} collective-permute-done((f32[3,64,2,128]{3,2,1,0:T(2,128)S(1)}, f32[3,64,2,128]{3,2,1,0:T(2,128)S(1)}, u32[]{:S(2)}, u32[]{:S(2)}) %collective-permute-start.11) | collective-permute-done | bytes 196640 | tf_op jit(solution)/shard_map/ppermute | solution.py:25
  78.1 3.8 %select_maximum_fusion.4.conc_ref = f32[3,68,36,128]{3,2,1,0:T(8,128)} fusion(f32[3,64,2,128]{3,2,1,0:T(2,128)S(1)} %collective-permute-done.11, f32[3,64,2,128]{3,2,1,0:T(2,128)} %collective-permute-done.8, f32[3,2,32,128]{3,2,1,0:T(8,128)} %collective-permute-done.10, f32[3,64,32,128]{3,2,1,0:T(8,128)S(1)} %slice-done, ...), kind=kLoop, calls=%fused_computation.11 | loop fusion | flops 7520256 | bytes 7495680 | tf_op jit(solution)/shard_map/concatenate | solution.py:28
  81.9 3.1 %collective-permute-start.25 = (f32[65]{0:T(128)S(1)}, f32[65]{0:T(128)S(1)}, u32[]{:S(2)}, u32[]{:S(2)}) collective-permute-start(f32[65]{0:T(128)S(1)} %add.92), channel_id=1, source_target_pairs={{0,64},{16,80},{32,96},{48,112},{64,0},{80,16},{96,32},{112,48},{1... | collective-permute-start | bytes 788 | tf_op jit(solution)/shard_map/ppermute | solution.py:37
  85.0 23.8 %shard_map.96 = f32[3,64,32,128]{3,2,1,0:T(8,128)S(1)} custom-call(f32[3]{0:T(128)S(1)} %slice.163.scale_ref, f32[3,68,36,128]{3,2,1,0:T(8,128)} %select_maximum_fusion.4.conc_ref, f32[4,68,36,128]{3,2,1,0:T(8,128)} %slice.177.coeff_ref), custom_call_target="tpu_custom_call" | custom-call | flops 62914560 | bytes 11919360 | tf_op jit(solution)/shard_map/pallas_call | solution.py:160
  109.0 0.8 collective-permute-start.26
  109.8 0.9 fusion.27
  110.7 1.9 collective-permute-done.26
  112.6 3.4 %collective-permute-start.27 = (f32[65]{0:T(128)S(1)}, f32[65]{0:T(128)S(1)}, u32[]{:S(2)}, u32[]{:S(2)}) collective-permute-start(f32[65]{0:T(128)S(1)} %add.94), channel_id=1, source_target_pairs={{0,2},{1,3},{2,0},{3,1},{4,6},{5,7},{6,4},{7,5},{8,10},{9,11},{10,... | collective-permute-start | bytes 788 | tf_op jit(solution)/shard_map/ppermute | solution.py:37
  116.2 0.7 fusion.26
  116.9 0.8 collective-permute-done.27
  117.7 1.2 collective-permute-start.28
  118.9 3.0 %collective-permute-start.14 = (f32[3,2,32,128]{3,2,1,0:T(8,128)}, f32[3,2,32,128]{3,2,1,0:T(8,128)}, u32[]{:S(2)}, u32[]{:S(2)}) collective-permute-start(f32[3,2,32,128]{3,2,1,0:T(8,128)} %get-tuple-element.57), channel_id=1, source_target_pairs={{16,0},{32,16},{48,32},{64,48},{80,64},{96,80},{112,96},{0,112},{1... | collective-permute-start | bytes 294920 | tf_op jit(solution)/shard_map/ppermute | solution.py:23
  121.9 1.0 collective-permute-start.12
  122.9 6.4 %collective-permute-start.29 = (f32[65]{0:T(128)S(1)}, f32[65]{0:T(128)S(1)}, u32[]{:S(2)}, u32[]{:S(2)}) collective-permute-start(f32[65]{0:T(128)S(1)} %add.96), channel_id=1, source_target_pairs={{0,8},{1,9},{2,10},{3,11},{4,12},{5,13},{6,14},{7,15},{8,0},{9,1},... | collective-permute-start | bytes 788 | tf_op jit(solution)/shard_map/ppermute | solution.py:37
  129.3 0.8 reshape.146
  130.0 0.6 copy-done.13
  130.7 3.1 %collective-permute-start.15 = (f32[3,64,2,128]{3,2,1,0:T(2,128)}, f32[3,64,2,128]{3,2,1,0:T(2,128)S(1)}, u32[]{:S(2)}, u32[]{:S(2)}) collective-permute-start(f32[3,64,2,128]{3,2,1,0:T(2,128)} %get-tuple-element.59), channel_id=1, source_target_pairs={{1,0},{2,1},{3,2},{4,3},{5,4},{6,5},{7,6},{8,7},{9,8},{10,9},{11,1... | collective-permute-start | bytes 589832 | tf_op jit(solution)/shard_map/ppermute | solution.py:25
  133.7 0.8 add.88
  134.6 0.6 slice.175
  135.2 4.8 %collective-permute-done.22 = f32[64,64]{1,0:T(8,128)S(1)} collective-permute-done((f32[64,64]{1,0:T(8,128)S(1)}, f32[64,64]{1,0:T(8,128)S(1)}, u32[]{:S(2)}, u32[]{:S(2)}) %collective-permute-start.22) | collective-permute-done | bytes 16416 | tf_op jit(solution)/shard_map/ppermute | solution.py:37
  140.1 0.7 copy.13
  140.8 1.4 fusion.12
  142.1 6.6 %cholesky.17 = f32[64,64]{1,0:T(8,128)S(1)} custom-call(f32[64,64]{1,0:T(8,128)} %fusion.12), custom_call_target="Cholesky" | custom-call | tf_op jit(solution)/shard_map/jit(cholesky)/cholesky | solution.py:232
  148.8 0.7 compare_reduce_fusion
  149.4 1.3 select_bitcast_fusion
  150.7 5.7 %custom-call.8 = f32[1,64,64]{1,2,0:T(8,128)S(1)} custom-call(f32[1,64,64]{2,1,0:T(8,128)} %get-tuple-element.46), custom_call_target="InvertDiagBlocksLowerTriangular" | custom-call | tf_op jit(solution)/shard_map/triangular_solve | solution.py:234
  156.4 0.8 multiply_reduce_fusion.2
  158.7 3.5 %fusion.1 = f32[32,1024]{1,0:T(8,128)S(1)} fusion(bf16[64,32,1024]{2,0,1:T(8,128)(2,1)} %copy-done, f32[64]{0:T(128)S(1)} %get-tuple-element.69), kind=kLoop, calls=%fused_computation.3 | loop fusion | flops 6258688 | bytes 4325632 | tf_op jit(solution)/shard_map/reduce_sum | solution.py:273
  162.2 0.7 fusion.5.last_ref
  163.3 0.7 copy.15
  164.0 2.2 %copy-done.1 = bf16[64,32,1024]{2,0,1:T(8,128)(2,1)S(1)} copy-done((bf16[64,32,1024]{2,0,1:T(8,128)(2,1)S(1)}, bf16[64,32,1024]{2,0,1:T(8,128)(2,1)}, u32[]{:S(2)}) %copy-start.1) | copy-done | bytes 4194328
  166.2 7.5 %shard_map.98._ = f32[65,32,1024]{2,1,0:T(8,128)} custom-call(bf16[3,65,64]{2,1,0:T(8,128)(2,1)S(1)} %pad_maximum_fusion.6.mix_ref, bf16[32,64,1024]{2,1,0:T(8,128)(2,1)S(1)} %bitcast.57), custom_call_target="tpu_custom_call" | custom-call | flops 817889280 | bytes 12713984 | tf_op jit(solution)/shard_map/pallas_call | solution.py:198
  173.7 1.6 shard_map.99
  175.3 3.9 %select_maximum_fusion.2.conc_ref = f32[3,68,36,128]{3,2,1,0:T(8,128)} fusion(f32[3,64,2,128]{3,2,1,0:T(2,128)S(1)} %collective-permute-done.15, f32[3,64,2,128]{3,2,1,0:T(2,128)} %collective-permute-done.12, f32[3,2,32,128]{3,2,1,0:T(8,128)} %collective-permute-done.14, f32[3,64,32,128]{3,2,1,0:T(8,128)S(1)} %shard_map.96, ...), kind=kLoop, calls=%fused_computation.9 | loop fusion | flops 7520256 | bytes 7495680 | tf_op jit(solution)/shard_map/concatenate | solution.py:28
  179.2 23.9 %shard_map.97 = f32[3,64,32,128]{3,2,1,0:T(8,128)S(1)} custom-call(f32[3]{0:T(128)S(1)} %slice.163.scale_ref, f32[3,68,36,128]{3,2,1,0:T(8,128)} %select_maximum_fusion.2.conc_ref, f32[4,68,36,128]{3,2,1,0:T(8,128)} %slice.177.coeff_ref), custom_call_target="tpu_custom_call" | custom-call | flops 62914560 | bytes 11919360 | tf_op jit(solution)/shard_map/pallas_call | solution.py:160
  203.1 2.5 %pad_maximum_fusion = f32[4,64,32,128]{3,2,1,0:T(8,128)} fusion(f32[3,64,32,128]{3,2,1,0:T(8,128)S(1)} %shard_map.97, f32[1,64,32,128]{3,2,1,0:T(8,128)S(1)} %copy-done.3), kind=kLoop, calls=%fused_computation.8 | loop fusion | flops 1048576 | bytes 8388608 | tf_op jit(solution)/shard_map/concatenate | solution.py:261
  (95 shorter events, 3.9 us)
Async XLA Ops:
  0.6 5.6 %copy-start.5 = (f32[3,64,32,128]{3,2,1,0:T(8,128)S(1)}, f32[3,64,32,128]{3,2,1,0:T(8,128)}, u32[]{:S(2)}) copy-start(f32[3,64,32,128]{3,2,1,0:T(8,128)} %param.14) | copy-start | bytes 9437188
  0.6 5.6 %copy-start.7 = (f32[64,32,128]{2,1,0:T(8,128)S(1)}, f32[64,32,128]{2,1,0:T(8,128)}, u32[]{:S(2)}) copy-start(f32[64,32,128]{2,1,0:T(8,128)} %param.15) | copy-start | bytes 3145732
  2.1 11.8 %copy-start.8 = (bf16[48,32,1024]{2,1,0:T(8,128)(2,1)S(1)}, bf16[48,32,1024]{2,1,0:T(8,128)(2,1)}, u32[]{:S(2)}) copy-start(bf16[48,32,1024]{2,1,0:T(8,128)(2,1)} %param.17) | copy-start | bytes 9437188
  3.3 9.7 %copy-start.6 = (f32[4,64,32,128]{3,2,1,0:T(8,128)S(1)}, f32[4,64,32,128]{3,2,1,0:T(8,128)}, u32[]{:S(2)}) copy-start(f32[4,64,32,128]{3,2,1,0:T(8,128)} %param.13) | copy-start | bytes 12582916
  3.3 15.6 %collective-permute-start.1 = (f32[5,2,32,128]{3,2,1,0:T(8,128)S(1)}, f32[5,2,32,128]{3,2,1,0:T(8,128)S(1)}, u32[]{:S(2)}, u32[]{:S(2)}) collective-permute-start(f32[5,2,32,128]{3,2,1,0:T(8,128)S(1)} %get-tuple-element.48), channel_id=1, source_target_pairs={{0,16},{16,32},{32,48},{48,64},{64,80},{80,96},{96,112},{112,0},{1... | collective-permute-start | bytes 491528 | tf_op jit(solution)/shard_map/ppermute | solution.py:22
  3.3 15.6 %collective-permute-start.2 = (f32[5,2,32,128]{3,2,1,0:T(8,128)S(1)}, f32[5,2,32,128]{3,2,1,0:T(8,128)S(1)}, u32[]{:S(2)}, u32[]{:S(2)}) collective-permute-start(f32[5,2,32,128]{3,2,1,0:T(8,128)S(1)} %get-tuple-element.49), channel_id=1, source_target_pairs={{16,0},{32,16},{48,32},{64,48},{80,64},{96,80},{112,96},{0,112},{1... | collective-permute-start | bytes 491528 | tf_op jit(solution)/shard_map/ppermute | solution.py:23
  6.5 9.1 %copy-start.9 = (bf16[16,32,1024]{2,1,0:T(8,128)(2,1)S(1)}, bf16[16,32,1024]{2,1,0:T(8,128)(2,1)}, u32[]{:S(2)}) copy-start(bf16[16,32,1024]{2,1,0:T(8,128)(2,1)} %param.19) | copy-start | bytes 3145732
  6.5 13.0 %collective-permute-start = (f32[5,64,2,128]{3,2,1,0:T(2,128)S(1)}, f32[5,64,2,128]{3,2,1,0:T(2,128)S(1)}, u32[]{:S(2)}, u32[]{:S(2)}) collective-permute-start(f32[5,64,2,128]{3,2,1,0:T(2,128)S(1)} %get-tuple-element.50), channel_id=1, source_target_pairs={{0,1},{1,2},{2,3},{3,4},{4,5},{5,6},{6,7},{7,8},{8,9},{9,10},{10,1... | collective-permute-start | bytes 983048 | tf_op jit(solution)/shard_map/ppermute | solution.py:24
  8.6 10.9 %collective-permute-start.3 = (f32[5,64,2,128]{3,2,1,0:T(2,128)S(1)}, f32[5,64,2,128]{3,2,1,0:T(2,128)S(1)}, u32[]{:S(2)}, u32[]{:S(2)}) collective-permute-start(f32[5,64,2,128]{3,2,1,0:T(2,128)S(1)} %get-tuple-element.51), channel_id=1, source_target_pairs={{1,0},{2,1},{3,2},{4,3},{5,4},{6,5},{7,6},{8,7},{9,8},{10,9},{11,1... | collective-permute-start | bytes 983048 | tf_op jit(solution)/shard_map/ppermute | solution.py:25
  16.2 2.0 copy-start
  22.6 2.8 %copy-start.4 = (f32[4]{0:T(128)S(1)}, f32[4]{0:T(128)}, u32[]{:S(2)}) copy-start(f32[4]{0:T(128)} %param.16) | copy-start | bytes 52
  34.9 8.5 %collective-permute-start.16 = (f32[64,64]{1,0:T(8,128)S(1)}, f32[64,64]{1,0:T(8,128)S(1)}, u32[]{:S(2)}, u32[]{:S(2)}) collective-permute-start(f32[64,64]{1,0:T(8,128)S(1)} %convolution_bitcast_fusion.1), channel_id=1, source_target_pairs={{0,16},{16,0},{32,48},{48,32},{64,80},{80,64},{96,112},{112,96},{1... | collective-permute-start | bytes 49160 | tf_op jit(solution)/shard_map/ppermute | solution.py:37
  35.0 12.3 %collective-permute-start.5 = (f32[1,2,32,128]{3,2,1,0:T(8,128)S(1)}, f32[1,2,32,128]{3,2,1,0:T(8,128)S(1)}, u32[]{:S(2)}, u32[]{:S(2)}) collective-permute-start(f32[1,2,32,128]{3,2,1,0:T(8,128)S(1)} %get-tuple-element.60), channel_id=1, source_target_pairs={{0,16},{16,32},{32,48},{48,64},{64,80},{80,96},{96,112},{112,0},{1... | collective-permute-start | bytes 98312 | tf_op jit(solution)/shard_map/ppermute | solution.py:22
  35.5 14.8 %collective-permute-start.6 = (f32[1,2,32,128]{3,2,1,0:T(8,128)S(1)}, f32[1,2,32,128]{3,2,1,0:T(8,128)S(1)}, u32[]{:S(2)}, u32[]{:S(2)}) collective-permute-start(f32[1,2,32,128]{3,2,1,0:T(8,128)S(1)} %get-tuple-element.61), channel_id=1, source_target_pairs={{16,0},{32,16},{48,32},{64,48},{80,64},{96,80},{112,96},{0,112},{1... | collective-permute-start | bytes 98312 | tf_op jit(solution)/shard_map/ppermute | solution.py:23
  38.0 12.3 %collective-permute-start.4 = (f32[1,64,2,128]{3,2,1,0:T(2,128)S(1)}, f32[1,64,2,128]{3,2,1,0:T(2,128)S(1)}, u32[]{:S(2)}, u32[]{:S(2)}) collective-permute-start(f32[1,64,2,128]{3,2,1,0:T(2,128)S(1)} %get-tuple-element.62), channel_id=1, source_target_pairs={{0,1},{1,2},{2,3},{3,4},{4,5},{5,6},{6,7},{7,8},{8,9},{9,10},{10,1... | collective-permute-start | bytes 196616 | tf_op jit(solution)/shard_map/ppermute | solution.py:24
  38.0 12.9 %collective-permute-start.7 = (f32[1,64,2,128]{3,2,1,0:T(2,128)S(1)}, f32[1,64,2,128]{3,2,1,0:T(2,128)S(1)}, u32[]{:S(2)}, u32[]{:S(2)}) collective-permute-start(f32[1,64,2,128]{3,2,1,0:T(2,128)S(1)} %get-tuple-element.63), channel_id=1, source_target_pairs={{1,0},{2,1},{3,2},{4,3},{5,4},{6,5},{7,6},{8,7},{9,8},{10,9},{11,1... | collective-permute-start | bytes 196616 | tf_op jit(solution)/shard_map/ppermute | solution.py:25
  43.4 4.0 %collective-permute-start.17 = (f32[64,64]{1,0:T(8,128)S(1)}, f32[64,64]{1,0:T(8,128)S(1)}, u32[]{:S(2)}, u32[]{:S(2)}) collective-permute-start(f32[64,64]{1,0:T(8,128)S(1)} %add.83), channel_id=1, source_target_pairs={{0,32},{16,48},{32,0},{48,16},{64,96},{80,112},{96,64},{112,80},{1... | collective-permute-start | bytes 49160 | tf_op jit(solution)/shard_map/ppermute | solution.py:37
  47.4 26.7 %collective-permute-start.9 = (f32[3,2,32,128]{3,2,1,0:T(8,128)}, f32[3,2,32,128]{3,2,1,0:T(8,128)}, u32[]{:S(2)}, u32[]{:S(2)}) collective-permute-start(f32[3,2,32,128]{3,2,1,0:T(8,128)} %get-tuple-element.52), channel_id=1, source_target_pairs={{0,16},{16,32},{32,48},{48,64},{64,80},{80,96},{96,112},{112,0},{1... | collective-permute-start | bytes 294920 | tf_op jit(solution)/shard_map/ppermute | solution.py:22
  47.4 27.2 %collective-permute-start.10 = (f32[3,2,32,128]{3,2,1,0:T(8,128)}, f32[3,2,32,128]{3,2,1,0:T(8,128)}, u32[]{:S(2)}, u32[]{:S(2)}) collective-permute-start(f32[3,2,32,128]{3,2,1,0:T(8,128)} %get-tuple-element.53), channel_id=1, source_target_pairs={{16,0},{32,16},{48,32},{64,48},{80,64},{96,80},{112,96},{0,112},{1... | collective-permute-start | bytes 294920 | tf_op jit(solution)/shard_map/ppermute | solution.py:23
  50.3 24.2 %collective-permute-start.8 = (f32[3,64,2,128]{3,2,1,0:T(2,128)}, f32[3,64,2,128]{3,2,1,0:T(2,128)}, u32[]{:S(2)}, u32[]{:S(2)}) collective-permute-start(f32[3,64,2,128]{3,2,1,0:T(2,128)} %get-tuple-element.54), channel_id=1, source_target_pairs={{0,1},{1,2},{2,3},{3,4},{4,5},{5,6},{6,7},{7,8},{8,9},{9,10},{10,1... | collective-permute-start | bytes 589832 | tf_op jit(solution)/shard_map/ppermute | solution.py:24
  50.4 17.5 %collective-permute-start.18 = (f32[64,64]{1,0:T(8,128)S(1)}, f32[64,64]{1,0:T(8,128)S(1)}, u32[]{:S(2)}, u32[]{:S(2)}) collective-permute-start(f32[64,64]{1,0:T(8,128)S(1)} %add.84), channel_id=1, source_target_pairs={{0,64},{16,80},{32,96},{48,112},{64,0},{80,16},{96,32},{112,48},{1... | collective-permute-start | bytes 49160 | tf_op jit(solution)/shard_map/ppermute | solution.py:37
  60.7 1.0 copy-start.2
  61.7 6.2 %copy-start.14 = (f32[48]{0:T(128)S(1)}, f32[48]{0:T(128)}, u32[]{:S(2)}) copy-start(f32[48]{0:T(128)} %param.18) | copy-start | bytes 580
  61.7 16.4 %slice-start = ((f32[4,64,32,128]{3,2,1,0:T(8,128)}), f32[3,64,32,128]{3,2,1,0:T(8,128)S(1)}, s32[]{:S(2)}) async-start(f32[4,64,32,128]{3,2,1,0:T(8,128)} %param.13), calls=%async_computation | async-start | bytes 6291456 | tf_op jit(solution)/shard_map/slice | solution.py:258
  63.8 4.1 %copy-start.11 = (f32[3,64,2,128]{3,2,1,0:T(2,128)S(1)}, f32[3,64,2,128]{3,2,1,0:T(2,128)}, u32[]{:S(2)}) copy-start(f32[3,64,2,128]{3,2,1,0:T(2,128)} %get-tuple-element.55) | copy-start | bytes 589828
  67.8 5.4 %collective-permute-start.23 = (f32[65]{0:T(128)S(1)}, f32[65]{0:T(128)S(1)}, u32[]{:S(2)}, u32[]{:S(2)}) collective-permute-start(f32[65]{0:T(128)S(1)} %pad_maximum_fusion.7), channel_id=1, source_target_pairs={{0,16},{16,0},{32,48},{48,32},{64,80},{80,64},{96,112},{112,96},{1... | collective-permute-start | bytes 788 | tf_op jit(solution)/shard_map/ppermute | solution.py:37
  67.9 10.1 %collective-permute-start.11 = (f32[3,64,2,128]{3,2,1,0:T(2,128)S(1)}, f32[3,64,2,128]{3,2,1,0:T(2,128)S(1)}, u32[]{:S(2)}, u32[]{:S(2)}) collective-permute-start(f32[3,64,2,128]{3,2,1,0:T(2,128)S(1)} %copy-done.11), channel_id=1, source_target_pairs={{1,0},{2,1},{3,2},{4,3},{5,4},{6,5},{7,6},{8,7},{9,8},{10,9},{11,1... | collective-permute-start | bytes 589832 | tf_op jit(solution)/shard_map/ppermute | solution.py:25
  73.3 35.6 %collective-permute-start.19 = (f32[64,64]{1,0:T(8,128)S(1)}, f32[64,64]{1,0:T(8,128)S(1)}, u32[]{:S(2)}, u32[]{:S(2)}) collective-permute-start(f32[64,64]{1,0:T(8,128)S(1)} %add.85), channel_id=1, source_target_pairs={{0,1},{1,0},{2,3},{3,2},{4,5},{5,4},{6,7},{7,6},{8,9},{9,8},{10,11... | collective-permute-start | bytes 49160 | tf_op jit(solution)/shard_map/ppermute | solution.py:37
  74.1 7.8 %collective-permute-start.24 = (f32[65]{0:T(128)S(1)}, f32[65]{0:T(128)S(1)}, u32[]{:S(2)}, u32[]{:S(2)}) collective-permute-start(f32[65]{0:T(128)S(1)} %fusion.34), channel_id=1, source_target_pairs={{0,32},{16,48},{32,0},{48,16},{64,96},{80,112},{96,64},{112,80},{1... | collective-permute-start | bytes 788 | tf_op jit(solution)/shard_map/ppermute | solution.py:37
  81.9 27.1 %collective-permute-start.25 = (f32[65]{0:T(128)S(1)}, f32[65]{0:T(128)S(1)}, u32[]{:S(2)}, u32[]{:S(2)}) collective-permute-start(f32[65]{0:T(128)S(1)} %add.92), channel_id=1, source_target_pairs={{0,64},{16,80},{32,96},{48,112},{64,0},{80,16},{96,32},{112,48},{1... | collective-permute-start | bytes 788 | tf_op jit(solution)/shard_map/ppermute | solution.py:37
  108.9 7.2 %collective-permute-start.20 = (f32[64,64]{1,0:T(8,128)S(1)}, f32[64,64]{1,0:T(8,128)S(1)}, u32[]{:S(2)}, u32[]{:S(2)}) collective-permute-start(f32[64,64]{1,0:T(8,128)S(1)} %add.86), channel_id=1, source_target_pairs={{0,2},{1,3},{2,0},{3,1},{4,6},{5,7},{6,4},{7,5},{8,10},{9,11},{10,... | collective-permute-start | bytes 49160 | tf_op jit(solution)/shard_map/ppermute | solution.py:37
  109.0 3.6 %collective-permute-start.26 = (f32[65]{0:T(128)S(1)}, f32[65]{0:T(128)S(1)}, u32[]{:S(2)}, u32[]{:S(2)}) collective-permute-start(f32[65]{0:T(128)S(1)} %add.93), channel_id=1, source_target_pairs={{0,1},{1,0},{2,3},{3,2},{4,5},{5,4},{6,7},{7,6},{8,9},{9,8},{10,11... | collective-permute-start | bytes 788 | tf_op jit(solution)/shard_map/ppermute | solution.py:37
  112.6 5.1 %collective-permute-start.27 = (f32[65]{0:T(128)S(1)}, f32[65]{0:T(128)S(1)}, u32[]{:S(2)}, u32[]{:S(2)}) collective-permute-start(f32[65]{0:T(128)S(1)} %add.94), channel_id=1, source_target_pairs={{0,2},{1,3},{2,0},{3,1},{4,6},{5,7},{6,4},{7,5},{8,10},{9,11},{10,... | collective-permute-start | bytes 788 | tf_op jit(solution)/shard_map/ppermute | solution.py:37
  116.1 14.0 %collective-permute-start.21 = (f32[64,64]{1,0:T(8,128)S(1)}, f32[64,64]{1,0:T(8,128)S(1)}, u32[]{:S(2)}, u32[]{:S(2)}) collective-permute-start(f32[64,64]{1,0:T(8,128)S(1)} %add.87), channel_id=1, source_target_pairs={{0,4},{1,5},{2,6},{3,7},{4,0},{5,1},{6,2},{7,3},{8,12},{9,13},{10,... | collective-permute-start | bytes 49160 | tf_op jit(solution)/shard_map/ppermute | solution.py:37
  117.7 5.2 %collective-permute-start.28 = (f32[65]{0:T(128)S(1)}, f32[65]{0:T(128)S(1)}, u32[]{:S(2)}, u32[]{:S(2)}) collective-permute-start(f32[65]{0:T(128)S(1)} %add.95), channel_id=1, source_target_pairs={{0,4},{1,5},{2,6},{3,7},{4,0},{5,1},{6,2},{7,3},{8,12},{9,13},{10,... | collective-permute-start | bytes 788 | tf_op jit(solution)/shard_map/ppermute | solution.py:37
  118.9 56.4 %collective-permute-start.13 = (f32[3,2,32,128]{3,2,1,0:T(8,128)}, f32[3,2,32,128]{3,2,1,0:T(8,128)}, u32[]{:S(2)}, u32[]{:S(2)}) collective-permute-start(f32[3,2,32,128]{3,2,1,0:T(8,128)} %get-tuple-element.56), channel_id=1, source_target_pairs={{0,16},{16,32},{32,48},{48,64},{64,80},{80,96},{96,112},{112,0},{1... | collective-permute-start | bytes 294920 | tf_op jit(solution)/shard_map/ppermute | solution.py:22
  118.9 56.4 %collective-permute-start.14 = (f32[3,2,32,128]{3,2,1,0:T(8,128)}, f32[3,2,32,128]{3,2,1,0:T(8,128)}, u32[]{:S(2)}, u32[]{:S(2)}) collective-permute-start(f32[3,2,32,128]{3,2,1,0:T(8,128)} %get-tuple-element.57), channel_id=1, source_target_pairs={{16,0},{32,16},{48,32},{64,48},{80,64},{96,80},{112,96},{0,112},{1... | collective-permute-start | bytes 294920 | tf_op jit(solution)/shard_map/ppermute | solution.py:23
  121.9 53.4 %collective-permute-start.12 = (f32[3,64,2,128]{3,2,1,0:T(2,128)}, f32[3,64,2,128]{3,2,1,0:T(2,128)}, u32[]{:S(2)}, u32[]{:S(2)}) collective-permute-start(f32[3,64,2,128]{3,2,1,0:T(2,128)} %get-tuple-element.58), channel_id=1, source_target_pairs={{0,1},{1,2},{2,3},{3,4},{4,5},{5,6},{6,7},{7,8},{8,9},{9,10},{10,1... | collective-permute-start | bytes 589832 | tf_op jit(solution)/shard_map/ppermute | solution.py:24
  122.9 11.6 %collective-permute-start.29 = (f32[65]{0:T(128)S(1)}, f32[65]{0:T(128)S(1)}, u32[]{:S(2)}, u32[]{:S(2)}) collective-permute-start(f32[65]{0:T(128)S(1)} %add.96), channel_id=1, source_target_pairs={{0,8},{1,9},{2,10},{3,11},{4,12},{5,13},{6,14},{7,15},{8,0},{9,1},... | collective-permute-start | bytes 788 | tf_op jit(solution)/shard_map/ppermute | solution.py:37
  130.0 32.2 %copy-start.10 = (f32[1,32,1024]{2,1,0:T(8,128)S(1)}, f32[1,32,1024]{2,1,0:T(8,128)}, u32[]{:S(2)}) copy-start(f32[1,32,1024]{2,1,0:T(8,128)} %reshape.146) | copy-start | bytes 393220
  130.0 0.6 copy-start.13
  130.7 44.7 %collective-permute-start.15 = (f32[3,64,2,128]{3,2,1,0:T(2,128)}, f32[3,64,2,128]{3,2,1,0:T(2,128)S(1)}, u32[]{:S(2)}, u32[]{:S(2)}) collective-permute-start(f32[3,64,2,128]{3,2,1,0:T(2,128)} %get-tuple-element.59), channel_id=1, source_target_pairs={{1,0},{2,1},{3,2},{4,3},{5,4},{6,5},{7,6},{8,7},{9,8},{10,9},{11,1... | collective-permute-start | bytes 589832 | tf_op jit(solution)/shard_map/ppermute | solution.py:25
  134.5 5.5 %collective-permute-start.22 = (f32[64,64]{1,0:T(8,128)S(1)}, f32[64,64]{1,0:T(8,128)S(1)}, u32[]{:S(2)}, u32[]{:S(2)}) collective-permute-start(f32[64,64]{1,0:T(8,128)S(1)} %add.88), channel_id=1, source_target_pairs={{0,8},{1,9},{2,10},{3,11},{4,12},{5,13},{6,14},{7,15},{8,0},{9,1},... | collective-permute-start | bytes 49160 | tf_op jit(solution)/shard_map/ppermute | solution.py:37
  158.4 4.5 %copy-start.12 = (f32[64,64]{1,0:T(8,128)S(1)}, f32[64,64]{1,0:T(8,128)}, u32[]{:S(2)}) copy-start(f32[64,64]{1,0:T(8,128)} %get-tuple-element.47) | copy-start | bytes 49156
  164.0 2.2 %copy-start.1 = (bf16[64,32,1024]{2,0,1:T(8,128)(2,1)S(1)}, bf16[64,32,1024]{2,0,1:T(8,128)(2,1)}, u32[]{:S(2)}) copy-start(bf16[64,32,1024]{2,0,1:T(8,128)(2,1)} %copy-done) | copy-start | bytes 12582916
  179.2 23.9 %copy-start.3 = (f32[1,64,32,128]{3,2,1,0:T(8,128)S(1)}, f32[1,64,32,128]{3,2,1,0:T(8,128)}, u32[]{:S(2)}) copy-start(f32[1,64,32,128]{3,2,1,0:T(8,128)} %copy-done.2) | copy-start | bytes 3145732

commit v4 on v3

--- a/solution.py
+++ b/solution.py
@@ -224,8 +224,9 @@
         static, static, (((1, 2), (1, 2)), ((), ())), preferred_element_type=jnp.float32
     )
     coeffs = jnp.concatenate([velocity, diffusivity[None]], 0)
-    first = halo(jnp.concatenate([scalars[:1], coeffs], 0))
-    coeff_pad = first[1:]
+    count = scalars.shape[0]
+    first = halo(jnp.concatenate([scalars, coeffs], 0))
+    coeff_pad = first[count:]
     middle0 = stencil_step(first[:1], coeff_pad, diff_scale[:1])
     local_gram, middle0 = lax.optimization_barrier((local_gram, middle0))
     gram_static = butterfly_sum(local_gram) * (weight[:, None] * weight[None, :]) / total_rows
@@ -255,8 +256,7 @@
     cross_g = moments[:width] * weight
     self_g = moments[width]
 
-    rest = halo(scalars[1:])
-    middle_r = stencil_step(rest, coeff_pad, diff_scale[1:])
+    middle_r = stencil_step(first[1:count], coeff_pad, diff_scale[1:])
     result_r = stencil_step(halo(middle_r), coeff_pad, diff_scale[1:])
     result = jnp.concatenate([result0, result_r], 0)
 

time: 206 us -> 197 us (0.956)
  starting transfers between devices: 49.9 us -> 40.4 us
  other arithmetic: 40.2 us -> 36.4 us
    ppermute x4 -> x3, waiting for transfers between devices: 0.61 us -> 6.81 us  [halo(): low_y = lax.ppermute(block[:, :, ny - width:], 'gy', fy)]
    ppermute x4 -> x3, starting transfers between devices: 18.1 us -> 14.1 us  [halo(): high_y = lax.ppermute(block[:, :, :width], 'gy', by)]
    ppermute x4 -> x3, waiting for transfers between devices: 3.49 us -> 0.01 us  [halo(): high_y = lax.ppermute(block[:, :, :width], 'gy', by)]
    slice x4 -> x2, local copies, waits for them, and re-layouts: 4.24 us -> 7.55 us  [the longest x1 4.45 us: per_device(): middle_r = stencil_step(first[1:count], coeff_pad, diff_scale[1:])]
    ppermute x4 -> x3, starting transfers between devices: 11.3 us -> 8.53 us  [halo(): high_x = lax.ppermute(block[:, :width], 'gx', bx)]
    ppermute x14, starting transfers between devices: 16.9 us -> 14.2 us  [butterfly_sum(): value = value + lax.ppermute(value, axis, pairs)]
    unnamed x32 -> x26, local copies, waits for them, and re-layouts: 7.07 us -> 9.14 us
    concatenate x4 -> x3, other arithmetic: 10.8 us -> 8.92 us  [halo(): jnp.concatenate([jnp.pad(low_y, edge), rows, jnp.pad(high_y, edge)], axis=2)]
  transfers between devices with their start and end apart: 30 -> 26, of which waited for: 6 -> 6; matrix products, arithmetic and copies ran while one was open for 21% -> 19% of each run, Pallas kernels for 21% -> 22%
where the time goes in v4:
time: 197 us
  Pallas kernels  76.3 us (39%)
  starting transfers between devices  40.4 us (21%)
  other arithmetic  36.4 us (18%)
  local copies, waits for them, and re-layouts  20.3 us (10%)
  waiting for transfers between devices  17.1 us (9%)
  matrix products  3.54 us (2%)
  between operations  2.4 us (1%)
    pallas_call x4, Pallas kernels, stencil_step(): pl.pallas_call(stencil_body, out_shape=jax.ShapeDtypeStruct((count, nx, n...  67.2 us
    ppermute x14, starting transfers between devices, butterfly_sum(): value = value + lax.ppermute(value, axis, pairs)  14.2 us
    ppermute x3, starting transfers between devices, halo(): high_y = lax.ppermute(block[:, :, :width], 'gy', by)  14.1 us
    ppermute x14, waiting for transfers between devices, butterfly_sum(): value = value + lax.ppermute(value, axis, pairs)  10.3 us
    unnamed x26, local copies, waits for them, and re-layouts  9.14 us
    concatenate x3, other arithmetic, halo(): jnp.concatenate([jnp.pad(low_y, edge), rows, jnp.pad(high_y, edge)], axis=2)  8.92 us
    ppermute x3, starting transfers between devices, halo(): high_x = lax.ppermute(block[:, :width], 'gx', bx)  8.53 us
    pallas_call x1, Pallas kernels, basis_rows(): pl.pallas_call(basis_body, out_shape=jax.ShapeDtypeStruct((rows, span, co...  7.53 us
  transfers between devices with their start and end apart: 26, of which 6 were waited for; matrix products, arithmetic and copies ran while one was open for 19% of the time, Pallas kernels for 22%

profile of v4, /device:TPU:0, one launch (start us, length us, event | category | flops | bytes accessed | tf_op | source)
XLA Modules:
  0.0 196.6 jit_solution(14729798048110056612)
XLA Ops:
  0.7 1.3 pad_maximum_fusion.5
  2.0 2.9 %collective-permute-start.2 = (f32[8,2,32,128]{3,2,1,0:T(8,128)S(1)}, f32[8,2,32,128]{3,2,1,0:T(8,128)S(1)}, u32[]{:S(2)}, u32[]{:S(2)}) collective-permute-start(f32[8,2,32,128]{3,2,1,0:T(8,128)S(1)} %get-tuple-element.49), channel_id=1, source_target_pairs={{16,0},{32,16},{48,32},{64,48},{80,64},{96,80},{112,96},{0,112},{1... | collective-permute-start | bytes 786440 | tf_op jit(solution)/shard_map/ppermute | solution.py:23
  4.9 0.5 pad_maximum_fusion.3
  5.4 2.1 %collective-permute-start = (f32[8,64,2,128]{3,2,1,0:T(2,128)S(1)}, f32[8,64,2,128]{3,2,1,0:T(2,128)S(1)}, u32[]{:S(2)}, u32[]{:S(2)}) collective-permute-start(f32[8,64,2,128]{3,2,1,0:T(2,128)S(1)} %get-tuple-element.50), channel_id=1, source_target_pairs={{0,1},{1,2},{2,3},{3,4},{4,5},{5,6},{6,7},{7,8},{8,9},{9,10},{10,1... | collective-permute-start | bytes 1572872 | tf_op jit(solution)/shard_map/ppermute | solution.py:24
  7.5 4.4 %collective-permute-start.3 = (f32[8,64,2,128]{3,2,1,0:T(2,128)S(1)}, f32[8,64,2,128]{3,2,1,0:T(2,128)S(1)}, u32[]{:S(2)}, u32[]{:S(2)}) collective-permute-start(f32[8,64,2,128]{3,2,1,0:T(2,128)S(1)} %get-tuple-element.51), channel_id=1, source_target_pairs={{1,0},{2,1},{3,2},{4,3},{5,4},{6,5},{7,6},{8,7},{9,8},{10,9},{11,1... | collective-permute-start | bytes 1572872 | tf_op jit(solution)/shard_map/ppermute | solution.py:25
  11.9 1.7 copy_dynamic-update-slice_fusion
  13.7 0.6 copy_dynamic-update-slice_fusion.1
  14.3 1.2 convolution_bitcast_fusion.1
  15.5 0.8 copy-done
  16.3 6.8 %collective-permute-done = f32[8,64,2,128]{3,2,1,0:T(2,128)S(1)} collective-permute-done((f32[8,64,2,128]{3,2,1,0:T(2,128)S(1)}, f32[8,64,2,128]{3,2,1,0:T(2,128)S(1)}, u32[]{:S(2)}, u32[]{:S(2)}) %collective-permute-start) | collective-permute-done | bytes 524320 | tf_op jit(solution)/shard_map/ppermute | solution.py:24
  23.1 4.9 %select_maximum_fusion = f32[8,68,36,128]{3,2,1,0:T(8,128)S(1)} fusion(f32[8,64,2,128]{3,2,1,0:T(2,128)S(1)} %collective-permute-done.3, f32[8,64,2,128]{3,2,1,0:T(2,128)S(1)} %collective-permute-done, f32[8,2,32,128]{3,2,1,0:T(8,128)S(1)} %collective-permute-done.2, f32[1,64,32,128]{3,2,1,0:T(8,128)S(1)} %bitcast.62, f32[3,64,32,128]{3,2,1,0:T(8,128)S(1)} %copy-done.7, ...), kind=kLoop, calls=%fused_computation | loop fusion | flops 25067520 | bytes 19988480 | tf_op jit(solution)/shard_map/concatenate | solution.py:28
  28.1 3.1 %slice.153.coeff_ref = f32[4,68,36,128]{3,2,1,0:T(8,128)} slice(f32[8,68,36,128]{3,2,1,0:T(8,128)S(1)} %select_maximum_fusion), slice={[4:8], [0:68], [0:36], [0:128]} | slice | bytes 10027008 | tf_op jit(solution)/shard_map/slice | solution.py:229
  31.2 2.7 %copy-done.5 = f32[8,68,36,128]{3,2,1,0:T(8,128)} copy-done((f32[8,68,36,128]{3,2,1,0:T(8,128)}, f32[8,68,36,128]{3,2,1,0:T(8,128)S(1)}, u32[]{:S(2)}) %copy-start.5) | copy-done | bytes 10027032
  33.9 10.0 %shard_map.94 = f32[1,64,32,128]{3,2,1,0:T(8,128)S(1)} custom-call(f32[1]{0:T(128)S(1)} %bitcast.58, f32[1,68,36,128]{3,2,1,0:T(8,128)S(1)} %slice.152.conc_ref, f32[4,68,36,128]{3,2,1,0:T(8,128)} %slice.153.coeff_ref), custom_call_target="tpu_custom_call" | custom-call | flops 20971520 | bytes 7315456 | tf_op jit(solution)/shard_map/pallas_call | solution.py:160
  44.0 0.5 collective-permute-start.5
  44.5 2.6 %collective-permute-start.6 = (f32[1,2,32,128]{3,2,1,0:T(8,128)S(1)}, f32[1,2,32,128]{3,2,1,0:T(8,128)S(1)}, u32[]{:S(2)}, u32[]{:S(2)}) collective-permute-start(f32[1,2,32,128]{3,2,1,0:T(8,128)S(1)} %get-tuple-element.57), channel_id=1, source_target_pairs={{16,0},{32,16},{48,32},{64,48},{80,64},{96,80},{112,96},{0,112},{1... | collective-permute-start | bytes 98312 | tf_op jit(solution)/shard_map/ppermute | solution.py:23
  47.2 5.3 %collective-permute-start.7 = (f32[1,64,2,128]{3,2,1,0:T(2,128)S(1)}, f32[1,64,2,128]{3,2,1,0:T(2,128)S(1)}, u32[]{:S(2)}, u32[]{:S(2)}) collective-permute-start(f32[1,64,2,128]{3,2,1,0:T(2,128)S(1)} %get-tuple-element.59), channel_id=1, source_target_pairs={{1,0},{2,1},{3,2},{4,3},{5,4},{6,5},{7,6},{8,7},{9,8},{10,9},{11,1... | collective-permute-start | bytes 196616 | tf_op jit(solution)/shard_map/ppermute | solution.py:25
  52.5 0.3 collective-permute-start.13
  52.8 3.7 %collective-permute-done.13 = f32[64,64]{1,0:T(8,128)S(1)} collective-permute-done((f32[64,64]{1,0:T(8,128)S(1)}, f32[64,64]{1,0:T(8,128)S(1)}, u32[]{:S(2)}, u32[]{:S(2)}) %collective-permute-start.13) | collective-permute-done | bytes 16416 | tf_op jit(solution)/shard_map/ppermute | solution.py:37
  56.5 1.8 collective-permute-start.14
  58.4 0.2 select_maximum_fusion.4.conc_ref
  58.6 9.5 %shard_map.95 = f32[1,64,32,128]{3,2,1,0:T(8,128)S(1)} custom-call(f32[1]{0:T(128)S(1)} %bitcast.59, f32[1,68,36,128]{3,2,1,0:T(8,128)S(1)} %select_maximum_fusion.4.conc_ref, f32[4,68,36,128]{3,2,1,0:T(8,128)} %slice.153.coeff_ref), custom_call_target="tpu_custom_call" | custom-call | flops 20971520 | bytes 7315456 | tf_op jit(solution)/shard_map/pallas_call | solution.py:160
  68.1 1.0 copy-done.2
  69.1 0.4 fusion.2
  69.5 0.9 multiply_reduce_fusion
  70.6 3.3 %fusion = f32[64]{0:T(128)S(1)} fusion(bf16[64,32,1024]{2,0,1:T(8,128)(2,1)} %copy-done, f32[32,1024]{1,0:T(8,128)S(1)} %mul.85), kind=kLoop, calls=%fused_computation.6 | loop fusion | flops 6291392 | bytes 4325632 | tf_op jit(solution)/shard_map/reduce_sum | solution.py:253
  73.9 0.7 pad_maximum_fusion.7
  74.8 1.0 collective-permute-done.19
  75.8 0.7 fusion.32
  76.6 0.7 collective-permute-start.20
  77.3 4.5 %slice.154.conc_ref = f32[3,68,36,128]{3,2,1,0:T(8,128)} slice(f32[8,68,36,128]{3,2,1,0:T(8,128)} %copy-done.5), slice={[1:4], [0:68], [0:36], [0:128]} | slice | bytes 7520256 | tf_op jit(solution)/shard_map/slice | solution.py:259
  81.8 1.8 collective-permute-start.21
  83.6 23.8 %shard_map.96 = f32[3,64,32,128]{3,2,1,0:T(8,128)S(1)} custom-call(f32[3]{0:T(128)S(1)} %slice.143.scale_ref, f32[3,68,36,128]{3,2,1,0:T(8,128)} %slice.154.conc_ref, f32[4,68,36,128]{3,2,1,0:T(8,128)} %slice.153.coeff_ref), custom_call_target="tpu_custom_call" | custom-call | flops 62914560 | bytes 11919360 | tf_op jit(solution)/shard_map/pallas_call | solution.py:160
  107.6 1.1 collective-permute-start.22
  108.7 0.9 fusion.25
  109.6 1.7 collective-permute-done.22
  111.2 3.4 %collective-permute-start.23 = (f32[65]{0:T(128)S(1)}, f32[65]{0:T(128)S(1)}, u32[]{:S(2)}, u32[]{:S(2)}) collective-permute-start(f32[65]{0:T(128)S(1)} %add.90), channel_id=1, source_target_pairs={{0,2},{1,3},{2,0},{3,1},{4,6},{5,7},{6,4},{7,5},{8,10},{9,11},{10,... | collective-permute-start | bytes 788 | tf_op jit(solution)/shard_map/ppermute | solution.py:37
  114.7 0.6 add.83
  115.3 0.7 fusion.24
  116.0 0.3 collective-permute-done.23
  116.3 1.8 collective-permute-start.24
  118.1 3.0 %collective-permute-start.10 = (f32[3,2,32,128]{3,2,1,0:T(8,128)}, f32[3,2,32,128]{3,2,1,0:T(8,128)}, u32[]{:S(2)}, u32[]{:S(2)}) collective-permute-start(f32[3,2,32,128]{3,2,1,0:T(8,128)} %get-tuple-element.53), channel_id=1, source_target_pairs={{16,0},{32,16},{48,32},{64,48},{80,64},{96,80},{112,96},{0,112},{1... | collective-permute-start | bytes 294920 | tf_op jit(solution)/shard_map/ppermute | solution.py:23
  121.0 1.0 collective-permute-start.8
  122.0 2.4 %collective-permute-start.25 = (f32[65]{0:T(128)S(1)}, f32[65]{0:T(128)}, u32[]{:S(2)}, u32[]{:S(2)}) collective-permute-start(f32[65]{0:T(128)S(1)} %add.92), channel_id=1, source_target_pairs={{0,8},{1,9},{2,10},{3,11},{4,12},{5,13},{6,14},{7,15},{8,0},{9,1},... | collective-permute-start | bytes 788 | tf_op jit(solution)/shard_map/ppermute | solution.py:37
  124.5 4.4 %collective-permute-start.11 = (f32[3,64,2,128]{3,2,1,0:T(2,128)}, f32[3,64,2,128]{3,2,1,0:T(2,128)}, u32[]{:S(2)}, u32[]{:S(2)}) collective-permute-start(f32[3,64,2,128]{3,2,1,0:T(2,128)} %get-tuple-element.55), channel_id=1, source_target_pairs={{1,0},{2,1},{3,2},{4,3},{5,4},{6,5},{7,6},{8,7},{9,8},{10,9},{11,1... | collective-permute-start | bytes 589832 | tf_op jit(solution)/shard_map/ppermute | solution.py:25
  128.9 0.8 add.84
  129.7 0.7 collective-permute-start.18
  130.4 0.7 add_multiply_fusion
  131.1 0.6 slice.151
  131.7 3.5 %collective-permute-done.18 = f32[64,64]{1,0:T(8,128)S(1)} collective-permute-done((f32[64,64]{1,0:T(8,128)S(1)}, f32[64,64]{1,0:T(8,128)S(1)}, u32[]{:S(2)}, u32[]{:S(2)}) %collective-permute-start.18) | collective-permute-done | bytes 16416 | tf_op jit(solution)/shard_map/ppermute | solution.py:37
  135.3 5.8 %cholesky.17 = f32[64,64]{1,0:T(8,128)S(1)} custom-call(f32[64,64]{1,0:T(8,128)S(1)} %fusion.12), custom_call_target="Cholesky" | custom-call | tf_op jit(solution)/shard_map/jit(cholesky)/cholesky | solution.py:233
  141.2 0.6 compare_reduce_fusion
  141.9 0.7 select_bitcast_fusion
  142.5 4.9 %custom-call.8 = f32[1,64,64]{1,2,0:T(8,128)S(1)} custom-call(f32[1,64,64]{2,1,0:T(8,128)S(1)} %get-tuple-element.46), custom_call_target="InvertDiagBlocksLowerTriangular" | custom-call | tf_op jit(solution)/shard_map/triangular_solve | solution.py:235
  147.4 0.8 multiply_reduce_fusion.2
  149.8 3.5 %fusion.1 = f32[32,1024]{1,0:T(8,128)S(1)} fusion(bf16[64,32,1024]{2,0,1:T(8,128)(2,1)} %copy-done, f32[64]{0:T(128)S(1)} %get-tuple-element.65), kind=kLoop, calls=%fused_computation.7 | loop fusion | flops 6258688 | bytes 4325632 | tf_op jit(solution)/shard_map/reduce_sum | solution.py:273
  153.3 0.7 fusion.5.last_ref
  154.4 0.7 copy.15
  155.1 2.2 %copy-done.1 = bf16[64,32,1024]{2,0,1:T(8,128)(2,1)S(1)} copy-done((bf16[64,32,1024]{2,0,1:T(8,128)(2,1)S(1)}, bf16[64,32,1024]{2,0,1:T(8,128)(2,1)}, u32[]{:S(2)}) %copy-start.1) | copy-done | bytes 4194328
  157.3 7.5 %shard_map.98._ = f32[65,32,1024]{2,1,0:T(8,128)} custom-call(bf16[3,65,64]{2,1,0:T(8,128)(2,1)S(1)} %pad_maximum_fusion.6.mix_ref, bf16[32,64,1024]{2,1,0:T(8,128)(2,1)S(1)} %bitcast.57), custom_call_target="tpu_custom_call" | custom-call | flops 817889280 | bytes 12713984 | tf_op jit(solution)/shard_map/pallas_call | solution.py:198
  164.8 1.6 shard_map.99
  166.4 3.8 %select_maximum_fusion.2.conc_ref = f32[3,68,36,128]{3,2,1,0:T(8,128)} fusion(f32[3,64,2,128]{3,2,1,0:T(2,128)} %collective-permute-done.11, f32[3,64,2,128]{3,2,1,0:T(2,128)} %collective-permute-done.8, f32[3,2,32,128]{3,2,1,0:T(8,128)} %collective-permute-done.10, f32[3,64,32,128]{3,2,1,0:T(8,128)S(1)} %shard_map.96, ...), kind=kLoop, calls=%fused_computation.9 | loop fusion | flops 7520256 | bytes 7495680 | tf_op jit(solution)/shard_map/concatenate | solution.py:28
  170.2 23.9 %shard_map.97 = f32[3,64,32,128]{3,2,1,0:T(8,128)S(1)} custom-call(f32[3]{0:T(128)S(1)} %slice.143.scale_ref, f32[3,68,36,128]{3,2,1,0:T(8,128)} %select_maximum_fusion.2.conc_ref, f32[4,68,36,128]{3,2,1,0:T(8,128)} %slice.153.coeff_ref), custom_call_target="tpu_custom_call" | custom-call | flops 62914560 | bytes 11919360 | tf_op jit(solution)/shard_map/pallas_call | solution.py:160
  194.1 2.5 %pad_maximum_fusion = f32[4,64,32,128]{3,2,1,0:T(8,128)} fusion(f32[3,64,32,128]{3,2,1,0:T(8,128)S(1)} %shard_map.97, f32[1,64,32,128]{3,2,1,0:T(8,128)S(1)} %copy-done.3), kind=kLoop, calls=%fused_computation.8 | loop fusion | flops 1048576 | bytes 8388608 | tf_op jit(solution)/shard_map/concatenate | solution.py:261
  (76 shorter events, 1.7 us)
Async XLA Ops:
  0.6 4.3 %copy-start.6 = (f32[4,64,32,128]{3,2,1,0:T(8,128)S(1)}, f32[4,64,32,128]{3,2,1,0:T(8,128)}, u32[]{:S(2)}) copy-start(f32[4,64,32,128]{3,2,1,0:T(8,128)} %param.13) | copy-start | bytes 12582916
  0.6 4.3 %copy-start.7 = (f32[3,64,32,128]{3,2,1,0:T(8,128)S(1)}, f32[3,64,32,128]{3,2,1,0:T(8,128)}, u32[]{:S(2)}) copy-start(f32[3,64,32,128]{3,2,1,0:T(8,128)} %param.14) | copy-start | bytes 9437188
  0.7 4.3 %copy-start.8 = (f32[64,32,128]{2,1,0:T(8,128)S(1)}, f32[64,32,128]{2,1,0:T(8,128)}, u32[]{:S(2)}) copy-start(f32[64,32,128]{2,1,0:T(8,128)} %param.15) | copy-start | bytes 3145732
  2.0 14.3 %collective-permute-start.1 = (f32[8,2,32,128]{3,2,1,0:T(8,128)S(1)}, f32[8,2,32,128]{3,2,1,0:T(8,128)S(1)}, u32[]{:S(2)}, u32[]{:S(2)}) collective-permute-start(f32[8,2,32,128]{3,2,1,0:T(8,128)S(1)} %get-tuple-element.48), channel_id=1, source_target_pairs={{0,16},{16,32},{32,48},{48,64},{64,80},{80,96},{96,112},{112,0},{1... | collective-permute-start | bytes 786440 | tf_op jit(solution)/shard_map/ppermute | solution.py:22
  2.0 9.9 %copy-start.9 = (bf16[48,32,1024]{2,1,0:T(8,128)(2,1)S(1)}, bf16[48,32,1024]{2,1,0:T(8,128)(2,1)}, u32[]{:S(2)}) copy-start(bf16[48,32,1024]{2,1,0:T(8,128)(2,1)} %param.17) | copy-start | bytes 9437188
  2.0 14.3 %collective-permute-start.2 = (f32[8,2,32,128]{3,2,1,0:T(8,128)S(1)}, f32[8,2,32,128]{3,2,1,0:T(8,128)S(1)}, u32[]{:S(2)}, u32[]{:S(2)}) collective-permute-start(f32[8,2,32,128]{3,2,1,0:T(8,128)S(1)} %get-tuple-element.49), channel_id=1, source_target_pairs={{16,0},{32,16},{48,32},{64,48},{80,64},{96,80},{112,96},{0,112},{1... | collective-permute-start | bytes 786440 | tf_op jit(solution)/shard_map/ppermute | solution.py:23
  5.4 8.3 %copy-start.10 = (bf16[16,32,1024]{2,1,0:T(8,128)(2,1)S(1)}, bf16[16,32,1024]{2,1,0:T(8,128)(2,1)}, u32[]{:S(2)}) copy-start(bf16[16,32,1024]{2,1,0:T(8,128)(2,1)} %param.19) | copy-start | bytes 3145732
  5.4 17.7 %collective-permute-start = (f32[8,64,2,128]{3,2,1,0:T(2,128)S(1)}, f32[8,64,2,128]{3,2,1,0:T(2,128)S(1)}, u32[]{:S(2)}, u32[]{:S(2)}) collective-permute-start(f32[8,64,2,128]{3,2,1,0:T(2,128)S(1)} %get-tuple-element.50), channel_id=1, source_target_pairs={{0,1},{1,2},{2,3},{3,4},{4,5},{5,6},{6,7},{7,8},{8,9},{9,10},{10,1... | collective-permute-start | bytes 1572872 | tf_op jit(solution)/shard_map/ppermute | solution.py:24
  7.5 15.6 %collective-permute-start.3 = (f32[8,64,2,128]{3,2,1,0:T(2,128)S(1)}, f32[8,64,2,128]{3,2,1,0:T(2,128)S(1)}, u32[]{:S(2)}, u32[]{:S(2)}) collective-permute-start(f32[8,64,2,128]{3,2,1,0:T(2,128)S(1)} %get-tuple-element.51), channel_id=1, source_target_pairs={{1,0},{2,1},{3,2},{4,3},{5,4},{6,5},{7,6},{8,7},{9,8},{10,9},{11,1... | collective-permute-start | bytes 1572872 | tf_op jit(solution)/shard_map/ppermute | solution.py:25
  14.3 2.0 %copy-start = (bf16[64,32,1024]{2,0,1:T(8,128)(2,1)}, bf16[64,32,1024]{2,0,1:T(8,128)(2,1)S(1)}, u32[]{:S(2)}) copy-start(bf16[64,32,1024]{2,0,1:T(8,128)(2,1)S(1)} %copy_dynamic-update-slice_fusion.1) | copy-start | bytes 12582916
  28.0 5.9 %copy-start.5 = (f32[8,68,36,128]{3,2,1,0:T(8,128)}, f32[8,68,36,128]{3,2,1,0:T(8,128)S(1)}, u32[]{:S(2)}) copy-start(f32[8,68,36,128]{3,2,1,0:T(8,128)S(1)} %select_maximum_fusion) | copy-start | bytes 30081028
  28.1 5.8 %copy-start.4 = (f32[4]{0:T(128)S(1)}, f32[4]{0:T(128)}, u32[]{:S(2)}) copy-start(f32[4]{0:T(128)} %param.16) | copy-start | bytes 52
  43.9 8.7 %collective-permute-start.12 = (f32[64,64]{1,0:T(8,128)S(1)}, f32[64,64]{1,0:T(8,128)S(1)}, u32[]{:S(2)}, u32[]{:S(2)}) collective-permute-start(f32[64,64]{1,0:T(8,128)S(1)} %convolution_bitcast_fusion.1), channel_id=1, source_target_pairs={{0,16},{16,0},{32,48},{48,32},{64,80},{80,64},{96,112},{112,96},{1... | collective-permute-start | bytes 49160 | tf_op jit(solution)/shard_map/ppermute | solution.py:37
  44.0 14.3 %collective-permute-start.5 = (f32[1,2,32,128]{3,2,1,0:T(8,128)S(1)}, f32[1,2,32,128]{3,2,1,0:T(8,128)S(1)}, u32[]{:S(2)}, u32[]{:S(2)}) collective-permute-start(f32[1,2,32,128]{3,2,1,0:T(8,128)S(1)} %get-tuple-element.56), channel_id=1, source_target_pairs={{0,16},{16,32},{32,48},{48,64},{64,80},{80,96},{96,112},{112,0},{1... | collective-permute-start | bytes 98312 | tf_op jit(solution)/shard_map/ppermute | solution.py:22
  44.5 13.8 %collective-permute-start.6 = (f32[1,2,32,128]{3,2,1,0:T(8,128)S(1)}, f32[1,2,32,128]{3,2,1,0:T(8,128)S(1)}, u32[]{:S(2)}, u32[]{:S(2)}) collective-permute-start(f32[1,2,32,128]{3,2,1,0:T(8,128)S(1)} %get-tuple-element.57), channel_id=1, source_target_pairs={{16,0},{32,16},{48,32},{64,48},{80,64},{96,80},{112,96},{0,112},{1... | collective-permute-start | bytes 98312 | tf_op jit(solution)/shard_map/ppermute | solution.py:23
  47.2 11.2 %collective-permute-start.4 = (f32[1,64,2,128]{3,2,1,0:T(2,128)S(1)}, f32[1,64,2,128]{3,2,1,0:T(2,128)S(1)}, u32[]{:S(2)}, u32[]{:S(2)}) collective-permute-start(f32[1,64,2,128]{3,2,1,0:T(2,128)S(1)} %get-tuple-element.58), channel_id=1, source_target_pairs={{0,1},{1,2},{2,3},{3,4},{4,5},{5,6},{6,7},{7,8},{8,9},{9,10},{10,1... | collective-permute-start | bytes 196616 | tf_op jit(solution)/shard_map/ppermute | solution.py:24
  47.2 11.2 %collective-permute-start.7 = (f32[1,64,2,128]{3,2,1,0:T(2,128)S(1)}, f32[1,64,2,128]{3,2,1,0:T(2,128)S(1)}, u32[]{:S(2)}, u32[]{:S(2)}) collective-permute-start(f32[1,64,2,128]{3,2,1,0:T(2,128)S(1)} %get-tuple-element.59), channel_id=1, source_target_pairs={{1,0},{2,1},{3,2},{4,3},{5,4},{6,5},{7,6},{8,7},{9,8},{10,9},{11,1... | collective-permute-start | bytes 196616 | tf_op jit(solution)/shard_map/ppermute | solution.py:25
  52.5 4.0 %collective-permute-start.13 = (f32[64,64]{1,0:T(8,128)S(1)}, f32[64,64]{1,0:T(8,128)S(1)}, u32[]{:S(2)}, u32[]{:S(2)}) collective-permute-start(f32[64,64]{1,0:T(8,128)S(1)} %add.79), channel_id=1, source_target_pairs={{0,32},{16,48},{32,0},{48,16},{64,96},{80,112},{96,64},{112,80},{1... | collective-permute-start | bytes 49160 | tf_op jit(solution)/shard_map/ppermute | solution.py:37
  56.5 18.1 %collective-permute-start.14 = (f32[64,64]{1,0:T(8,128)S(1)}, f32[64,64]{1,0:T(8,128)S(1)}, u32[]{:S(2)}, u32[]{:S(2)}) collective-permute-start(f32[64,64]{1,0:T(8,128)S(1)} %add.80), channel_id=1, source_target_pairs={{0,64},{16,80},{32,96},{48,112},{64,0},{80,16},{96,32},{112,48},{1... | collective-permute-start | bytes 49160 | tf_op jit(solution)/shard_map/ppermute | solution.py:37
  68.1 1.0 copy-start.2
  69.1 8.2 %copy-start.11 = (f32[48]{0:T(128)S(1)}, f32[48]{0:T(128)}, u32[]{:S(2)}) copy-start(f32[48]{0:T(128)} %param.18) | copy-start | bytes 580
  74.7 1.2 collective-permute-start.19
  74.7 32.7 %collective-permute-start.15 = (f32[64,64]{1,0:T(8,128)S(1)}, f32[64,64]{1,0:T(8,128)S(1)}, u32[]{:S(2)}, u32[]{:S(2)}) collective-permute-start(f32[64,64]{1,0:T(8,128)S(1)} %add.81), channel_id=1, source_target_pairs={{0,1},{1,0},{2,3},{3,2},{4,5},{5,4},{6,7},{7,6},{8,9},{9,8},{10,11... | collective-permute-start | bytes 49160 | tf_op jit(solution)/shard_map/ppermute | solution.py:37
  76.6 5.2 %collective-permute-start.20 = (f32[65]{0:T(128)S(1)}, f32[65]{0:T(128)S(1)}, u32[]{:S(2)}, u32[]{:S(2)}) collective-permute-start(f32[65]{0:T(128)S(1)} %fusion.32), channel_id=1, source_target_pairs={{0,32},{16,48},{32,0},{48,16},{64,96},{80,112},{96,64},{112,80},{1... | collective-permute-start | bytes 788 | tf_op jit(solution)/shard_map/ppermute | solution.py:37
  81.8 25.8 %collective-permute-start.21 = (f32[65]{0:T(128)S(1)}, f32[65]{0:T(128)S(1)}, u32[]{:S(2)}, u32[]{:S(2)}) collective-permute-start(f32[65]{0:T(128)S(1)} %add.88), channel_id=1, source_target_pairs={{0,64},{16,80},{32,96},{48,112},{64,0},{80,16},{96,32},{112,48},{1... | collective-permute-start | bytes 788 | tf_op jit(solution)/shard_map/ppermute | solution.py:37
  107.5 7.2 %collective-permute-start.16 = (f32[64,64]{1,0:T(8,128)S(1)}, f32[64,64]{1,0:T(8,128)S(1)}, u32[]{:S(2)}, u32[]{:S(2)}) collective-permute-start(f32[64,64]{1,0:T(8,128)S(1)} %add.82), channel_id=1, source_target_pairs={{0,2},{1,3},{2,0},{3,1},{4,6},{5,7},{6,4},{7,5},{8,10},{9,11},{10,... | collective-permute-start | bytes 49160 | tf_op jit(solution)/shard_map/ppermute | solution.py:37
  107.6 3.6 %collective-permute-start.22 = (f32[65]{0:T(128)S(1)}, f32[65]{0:T(128)S(1)}, u32[]{:S(2)}, u32[]{:S(2)}) collective-permute-start(f32[65]{0:T(128)S(1)} %add.89), channel_id=1, source_target_pairs={{0,1},{1,0},{2,3},{3,2},{4,5},{5,4},{6,7},{7,6},{8,9},{9,8},{10,11... | collective-permute-start | bytes 788 | tf_op jit(solution)/shard_map/ppermute | solution.py:37
  111.2 5.1 %collective-permute-start.23 = (f32[65]{0:T(128)S(1)}, f32[65]{0:T(128)S(1)}, u32[]{:S(2)}, u32[]{:S(2)}) collective-permute-start(f32[65]{0:T(128)S(1)} %add.90), channel_id=1, source_target_pairs={{0,2},{1,3},{2,0},{3,1},{4,6},{5,7},{6,4},{7,5},{8,10},{9,11},{10,... | collective-permute-start | bytes 788 | tf_op jit(solution)/shard_map/ppermute | solution.py:37
  115.3 9.2 %collective-permute-start.17 = (f32[64,64]{1,0:T(8,128)}, f32[64,64]{1,0:T(8,128)}, u32[]{:S(2)}, u32[]{:S(2)}) collective-permute-start(f32[64,64]{1,0:T(8,128)} %add.83), channel_id=1, source_target_pairs={{0,4},{1,5},{2,6},{3,7},{4,0},{5,1},{6,2},{7,3},{8,12},{9,13},{10,... | collective-permute-start | bytes 49160 | tf_op jit(solution)/shard_map/ppermute | solution.py:37
  116.3 5.7 %collective-permute-start.24 = (f32[65]{0:T(128)S(1)}, f32[65]{0:T(128)S(1)}, u32[]{:S(2)}, u32[]{:S(2)}) collective-permute-start(f32[65]{0:T(128)S(1)} %add.91), channel_id=1, source_target_pairs={{0,4},{1,5},{2,6},{3,7},{4,0},{5,1},{6,2},{7,3},{8,12},{9,13},{10,... | collective-permute-start | bytes 788 | tf_op jit(solution)/shard_map/ppermute | solution.py:37
  118.1 48.3 %collective-permute-start.9 = (f32[3,2,32,128]{3,2,1,0:T(8,128)}, f32[3,2,32,128]{3,2,1,0:T(8,128)}, u32[]{:S(2)}, u32[]{:S(2)}) collective-permute-start(f32[3,2,32,128]{3,2,1,0:T(8,128)} %get-tuple-element.52), channel_id=1, source_target_pairs={{0,16},{16,32},{32,48},{48,64},{64,80},{80,96},{96,112},{112,0},{1... | collective-permute-start | bytes 294920 | tf_op jit(solution)/shard_map/ppermute | solution.py:22
  118.1 48.3 %collective-permute-start.10 = (f32[3,2,32,128]{3,2,1,0:T(8,128)}, f32[3,2,32,128]{3,2,1,0:T(8,128)}, u32[]{:S(2)}, u32[]{:S(2)}) collective-permute-start(f32[3,2,32,128]{3,2,1,0:T(8,128)} %get-tuple-element.53), channel_id=1, source_target_pairs={{16,0},{32,16},{48,32},{64,48},{80,64},{96,80},{112,96},{0,112},{1... | collective-permute-start | bytes 294920 | tf_op jit(solution)/shard_map/ppermute | solution.py:23
  121.0 45.4 %collective-permute-start.8 = (f32[3,64,2,128]{3,2,1,0:T(2,128)}, f32[3,64,2,128]{3,2,1,0:T(2,128)}, u32[]{:S(2)}, u32[]{:S(2)}) collective-permute-start(f32[3,64,2,128]{3,2,1,0:T(2,128)} %get-tuple-element.54), channel_id=1, source_target_pairs={{0,1},{1,2},{2,3},{3,4},{4,5},{5,6},{6,7},{7,8},{8,9},{9,10},{10,1... | collective-permute-start | bytes 589832 | tf_op jit(solution)/shard_map/ppermute | solution.py:24
  122.0 7.6 %collective-permute-start.25 = (f32[65]{0:T(128)S(1)}, f32[65]{0:T(128)}, u32[]{:S(2)}, u32[]{:S(2)}) collective-permute-start(f32[65]{0:T(128)S(1)} %add.92), channel_id=1, source_target_pairs={{0,8},{1,9},{2,10},{3,11},{4,12},{5,13},{6,14},{7,15},{8,0},{9,1},... | collective-permute-start | bytes 788 | tf_op jit(solution)/shard_map/ppermute | solution.py:37
  124.5 41.9 %collective-permute-start.11 = (f32[3,64,2,128]{3,2,1,0:T(2,128)}, f32[3,64,2,128]{3,2,1,0:T(2,128)}, u32[]{:S(2)}, u32[]{:S(2)}) collective-permute-start(f32[3,64,2,128]{3,2,1,0:T(2,128)} %get-tuple-element.55), channel_id=1, source_target_pairs={{1,0},{2,1},{3,2},{4,3},{5,4},{6,5},{7,6},{8,7},{9,8},{10,9},{11,1... | collective-permute-start | bytes 589832 | tf_op jit(solution)/shard_map/ppermute | solution.py:25
  129.7 5.5 %collective-permute-start.18 = (f32[64,64]{1,0:T(8,128)S(1)}, f32[64,64]{1,0:T(8,128)S(1)}, u32[]{:S(2)}, u32[]{:S(2)}) collective-permute-start(f32[64,64]{1,0:T(8,128)S(1)} %add.84), channel_id=1, source_target_pairs={{0,8},{1,9},{2,10},{3,11},{4,12},{5,13},{6,14},{7,15},{8,0},{9,1},... | collective-permute-start | bytes 49160 | tf_op jit(solution)/shard_map/ppermute | solution.py:37
  155.1 2.2 %copy-start.1 = (bf16[64,32,1024]{2,0,1:T(8,128)(2,1)S(1)}, bf16[64,32,1024]{2,0,1:T(8,128)(2,1)}, u32[]{:S(2)}) copy-start(bf16[64,32,1024]{2,0,1:T(8,128)(2,1)} %copy-done) | copy-start | bytes 12582916
  170.2 23.9 %copy-start.3 = (f32[1,64,32,128]{3,2,1,0:T(8,128)S(1)}, f32[1,64,32,128]{3,2,1,0:T(8,128)}, u32[]{:S(2)}) copy-start(f32[1,64,32,128]{3,2,1,0:T(8,128)} %copy-done.2) | copy-start | bytes 3145732

commit v5 on v4

--- a/solution.py
+++ b/solution.py
@@ -124,16 +124,17 @@
         def f1(d):
             return k(0, d, 0) * c(d, 0)
 
-        slope = (8.0 * (f1(1) - f1(-1)) - (f1(2) - f1(-2))) / 12.0
+        slope = 8.0 * (f1(1) - f1(-1)) - (f1(2) - f1(-2))
 
         def f2(d):
             return k(1, 0, d) * c(0, d)
 
-        slope = slope + (8.0 * (f2(1) - f2(-1)) - (f2(2) - f2(-2))) / 12.0
+        slope = slope + (8.0 * (f2(1) - f2(-1)) - (f2(2) - f2(-2)))
         f3 = k(2, 0, 0) * center
         slope = slope + (
             8.0 * (shifted(f3, 1) - shifted(f3, -1)) - (shifted(f3, 2) - shifted(f3, -2))
-        ) / 12.0
+        )
+        slope = slope * (1.0 / 12.0)
         kmid = k(3, 0, 0)
         spread = (kmid + k(3, 1, 0)) * 0.5 * (c(1, 0) - center) - (kmid + k(3, -1, 0)) * 0.5 * (
             center - c(-1, 0)

time: 197 us -> 197 us (level)
  no operation moved by 1% of the time
where the time goes in v5:
time: 197 us
  Pallas kernels  76.3 us (39%)
  starting transfers between devices  40.4 us (21%)
  other arithmetic  36.4 us (18%)
  local copies, waits for them, and re-layouts  20.3 us (10%)
  waiting for transfers between devices  17.1 us (9%)
  matrix products  3.54 us (2%)
  between operations  2.4 us (1%)
    pallas_call x4, Pallas kernels, stencil_step(): pl.pallas_call(stencil_body, out_shape=jax.ShapeDtypeStruct((count, nx, n...  67.2 us
    ppermute x14, starting transfers between devices, butterfly_sum(): value = value + lax.ppermute(value, axis, pairs)  14.2 us
    ppermute x3, starting transfers between devices, halo(): high_y = lax.ppermute(block[:, :, :width], 'gy', by)  14.1 us
    ppermute x14, waiting for transfers between devices, butterfly_sum(): value = value + lax.ppermute(value, axis, pairs)  10.3 us
    unnamed x26, local copies, waits for them, and re-layouts  9.14 us
    concatenate x3, other arithmetic, halo(): jnp.concatenate([jnp.pad(low_y, edge), rows, jnp.pad(high_y, edge)], axis=2)  8.92 us
    ppermute x3, starting transfers between devices, halo(): high_x = lax.ppermute(block[:, :width], 'gx', bx)  8.53 us
    pallas_call x1, Pallas kernels, basis_rows(): pl.pallas_call(basis_body, out_shape=jax.ShapeDtypeStruct((rows, span, co...  7.52 us
  transfers between devices with their start and end apart: 26, of which 6 were waited for; matrix products, arithmetic and copies ran while one was open for 19% of the time, Pallas kernels for 22%

profile of v5, /device:TPU:0, one launch (start us, length us, event | category | flops | bytes accessed | tf_op | source)
XLA Modules:
  0.0 196.6 jit_solution(17966017794726366102)
XLA Ops:
  0.7 1.3 pad_maximum_fusion.5
  2.0 2.9 %collective-permute-start.2 = (f32[8,2,32,128]{3,2,1,0:T(8,128)S(1)}, f32[8,2,32,128]{3,2,1,0:T(8,128)S(1)}, u32[]{:S(2)}, u32[]{:S(2)}) collective-permute-start(f32[8,2,32,128]{3,2,1,0:T(8,128)S(1)} %get-tuple-element.49), channel_id=1, source_target_pairs={{16,0},{32,16},{48,32},{64,48},{80,64},{96,80},{112,96},{0,112},{1... | collective-permute-start | bytes 786440 | tf_op jit(solution)/shard_map/ppermute | solution.py:23
  4.9 0.5 pad_maximum_fusion.3
  5.4 2.1 %collective-permute-start = (f32[8,64,2,128]{3,2,1,0:T(2,128)S(1)}, f32[8,64,2,128]{3,2,1,0:T(2,128)S(1)}, u32[]{:S(2)}, u32[]{:S(2)}) collective-permute-start(f32[8,64,2,128]{3,2,1,0:T(2,128)S(1)} %get-tuple-element.50), channel_id=1, source_target_pairs={{0,1},{1,2},{2,3},{3,4},{4,5},{5,6},{6,7},{7,8},{8,9},{9,10},{10,1... | collective-permute-start | bytes 1572872 | tf_op jit(solution)/shard_map/ppermute | solution.py:24
  7.5 4.4 %collective-permute-start.3 = (f32[8,64,2,128]{3,2,1,0:T(2,128)S(1)}, f32[8,64,2,128]{3,2,1,0:T(2,128)S(1)}, u32[]{:S(2)}, u32[]{:S(2)}) collective-permute-start(f32[8,64,2,128]{3,2,1,0:T(2,128)S(1)} %get-tuple-element.51), channel_id=1, source_target_pairs={{1,0},{2,1},{3,2},{4,3},{5,4},{6,5},{7,6},{8,7},{9,8},{10,9},{11,1... | collective-permute-start | bytes 1572872 | tf_op jit(solution)/shard_map/ppermute | solution.py:25
  11.9 1.7 copy_dynamic-update-slice_fusion
  13.7 0.6 copy_dynamic-update-slice_fusion.1
  14.3 1.2 convolution_bitcast_fusion.1
  15.5 0.8 copy-done
  16.3 6.8 %collective-permute-done = f32[8,64,2,128]{3,2,1,0:T(2,128)S(1)} collective-permute-done((f32[8,64,2,128]{3,2,1,0:T(2,128)S(1)}, f32[8,64,2,128]{3,2,1,0:T(2,128)S(1)}, u32[]{:S(2)}, u32[]{:S(2)}) %collective-permute-start) | collective-permute-done | bytes 524320 | tf_op jit(solution)/shard_map/ppermute | solution.py:24
  23.1 4.9 %select_maximum_fusion = f32[8,68,36,128]{3,2,1,0:T(8,128)S(1)} fusion(f32[8,64,2,128]{3,2,1,0:T(2,128)S(1)} %collective-permute-done.3, f32[8,64,2,128]{3,2,1,0:T(2,128)S(1)} %collective-permute-done, f32[8,2,32,128]{3,2,1,0:T(8,128)S(1)} %collective-permute-done.2, f32[1,64,32,128]{3,2,1,0:T(8,128)S(1)} %bitcast.62, f32[3,64,32,128]{3,2,1,0:T(8,128)S(1)} %copy-done.7, ...), kind=kLoop, calls=%fused_computation | loop fusion | flops 25067520 | bytes 19988480 | tf_op jit(solution)/shard_map/concatenate | solution.py:28
  28.1 3.1 %slice.153.coeff_ref = f32[4,68,36,128]{3,2,1,0:T(8,128)} slice(f32[8,68,36,128]{3,2,1,0:T(8,128)S(1)} %select_maximum_fusion), slice={[4:8], [0:68], [0:36], [0:128]} | slice | bytes 10027008 | tf_op jit(solution)/shard_map/slice | solution.py:230
  31.2 2.7 %copy-done.5 = f32[8,68,36,128]{3,2,1,0:T(8,128)} copy-done((f32[8,68,36,128]{3,2,1,0:T(8,128)}, f32[8,68,36,128]{3,2,1,0:T(8,128)S(1)}, u32[]{:S(2)}) %copy-start.5) | copy-done | bytes 10027032
  33.9 10.0 %shard_map.94 = f32[1,64,32,128]{3,2,1,0:T(8,128)S(1)} custom-call(f32[1]{0:T(128)S(1)} %bitcast.58, f32[1,68,36,128]{3,2,1,0:T(8,128)S(1)} %slice.152.conc_ref, f32[4,68,36,128]{3,2,1,0:T(8,128)} %slice.153.coeff_ref), custom_call_target="tpu_custom_call" | custom-call | flops 20971520 | bytes 7315456 | tf_op jit(solution)/shard_map/pallas_call | solution.py:161
  44.1 0.5 collective-permute-start.5
  44.6 2.6 %collective-permute-start.6 = (f32[1,2,32,128]{3,2,1,0:T(8,128)S(1)}, f32[1,2,32,128]{3,2,1,0:T(8,128)S(1)}, u32[]{:S(2)}, u32[]{:S(2)}) collective-permute-start(f32[1,2,32,128]{3,2,1,0:T(8,128)S(1)} %get-tuple-element.57), channel_id=1, source_target_pairs={{16,0},{32,16},{48,32},{64,48},{80,64},{96,80},{112,96},{0,112},{1... | collective-permute-start | bytes 98312 | tf_op jit(solution)/shard_map/ppermute | solution.py:23
  47.3 5.3 %collective-permute-start.7 = (f32[1,64,2,128]{3,2,1,0:T(2,128)S(1)}, f32[1,64,2,128]{3,2,1,0:T(2,128)S(1)}, u32[]{:S(2)}, u32[]{:S(2)}) collective-permute-start(f32[1,64,2,128]{3,2,1,0:T(2,128)S(1)} %get-tuple-element.59), channel_id=1, source_target_pairs={{1,0},{2,1},{3,2},{4,3},{5,4},{6,5},{7,6},{8,7},{9,8},{10,9},{11,1... | collective-permute-start | bytes 196616 | tf_op jit(solution)/shard_map/ppermute | solution.py:25
  52.6 0.3 collective-permute-start.13
  52.9 3.7 %collective-permute-done.13 = f32[64,64]{1,0:T(8,128)S(1)} collective-permute-done((f32[64,64]{1,0:T(8,128)S(1)}, f32[64,64]{1,0:T(8,128)S(1)}, u32[]{:S(2)}, u32[]{:S(2)}) %collective-permute-start.13) | collective-permute-done | bytes 16416 | tf_op jit(solution)/shard_map/ppermute | solution.py:37
  56.6 1.8 collective-permute-start.14
  58.4 0.2 select_maximum_fusion.4.conc_ref
  58.7 9.5 %shard_map.95 = f32[1,64,32,128]{3,2,1,0:T(8,128)S(1)} custom-call(f32[1]{0:T(128)S(1)} %bitcast.59, f32[1,68,36,128]{3,2,1,0:T(8,128)S(1)} %select_maximum_fusion.4.conc_ref, f32[4,68,36,128]{3,2,1,0:T(8,128)} %slice.153.coeff_ref), custom_call_target="tpu_custom_call" | custom-call | flops 20971520 | bytes 7315456 | tf_op jit(solution)/shard_map/pallas_call | solution.py:161
  68.2 1.0 copy-done.2
  69.2 0.4 fusion.2
  69.6 0.9 multiply_reduce_fusion
  70.7 3.3 %fusion = f32[64]{0:T(128)S(1)} fusion(bf16[64,32,1024]{2,0,1:T(8,128)(2,1)} %copy-done, f32[32,1024]{1,0:T(8,128)S(1)} %mul.85), kind=kLoop, calls=%fused_computation.6 | loop fusion | flops 6291392 | bytes 4325632 | tf_op jit(solution)/shard_map/reduce_sum | solution.py:254
  74.0 0.7 pad_maximum_fusion.7
  74.9 1.0 collective-permute-done.19
  75.9 0.7 fusion.32
  76.6 0.7 collective-permute-start.20
  77.4 4.5 %slice.154.conc_ref = f32[3,68,36,128]{3,2,1,0:T(8,128)} slice(f32[8,68,36,128]{3,2,1,0:T(8,128)} %copy-done.5), slice={[1:4], [0:68], [0:36], [0:128]} | slice | bytes 7520256 | tf_op jit(solution)/shard_map/slice | solution.py:260
  81.9 1.8 collective-permute-start.21
  83.7 23.8 %shard_map.96 = f32[3,64,32,128]{3,2,1,0:T(8,128)S(1)} custom-call(f32[3]{0:T(128)S(1)} %slice.143.scale_ref, f32[3,68,36,128]{3,2,1,0:T(8,128)} %slice.154.conc_ref, f32[4,68,36,128]{3,2,1,0:T(8,128)} %slice.153.coeff_ref), custom_call_target="tpu_custom_call" | custom-call | flops 62914560 | bytes 11919360 | tf_op jit(solution)/shard_map/pallas_call | solution.py:161
  107.7 1.1 collective-permute-start.22
  108.7 0.9 fusion.25
  109.6 1.7 collective-permute-done.22
  111.3 3.4 %collective-permute-start.23 = (f32[65]{0:T(128)S(1)}, f32[65]{0:T(128)S(1)}, u32[]{:S(2)}, u32[]{:S(2)}) collective-permute-start(f32[65]{0:T(128)S(1)} %add.90), channel_id=1, source_target_pairs={{0,2},{1,3},{2,0},{3,1},{4,6},{5,7},{6,4},{7,5},{8,10},{9,11},{10,... | collective-permute-start | bytes 788 | tf_op jit(solution)/shard_map/ppermute | solution.py:37
  114.7 0.6 add.83
  115.4 0.7 fusion.24
  116.1 0.3 collective-permute-done.23
  116.4 1.8 collective-permute-start.24
  118.1 3.0 %collective-permute-start.10 = (f32[3,2,32,128]{3,2,1,0:T(8,128)}, f32[3,2,32,128]{3,2,1,0:T(8,128)}, u32[]{:S(2)}, u32[]{:S(2)}) collective-permute-start(f32[3,2,32,128]{3,2,1,0:T(8,128)} %get-tuple-element.53), channel_id=1, source_target_pairs={{16,0},{32,16},{48,32},{64,48},{80,64},{96,80},{112,96},{0,112},{1... | collective-permute-start | bytes 294920 | tf_op jit(solution)/shard_map/ppermute | solution.py:23
  121.1 1.0 collective-permute-start.8
  122.1 2.4 %collective-permute-start.25 = (f32[65]{0:T(128)S(1)}, f32[65]{0:T(128)}, u32[]{:S(2)}, u32[]{:S(2)}) collective-permute-start(f32[65]{0:T(128)S(1)} %add.92), channel_id=1, source_target_pairs={{0,8},{1,9},{2,10},{3,11},{4,12},{5,13},{6,14},{7,15},{8,0},{9,1},... | collective-permute-start | bytes 788 | tf_op jit(solution)/shard_map/ppermute | solution.py:37
  124.6 4.4 %collective-permute-start.11 = (f32[3,64,2,128]{3,2,1,0:T(2,128)}, f32[3,64,2,128]{3,2,1,0:T(2,128)}, u32[]{:S(2)}, u32[]{:S(2)}) collective-permute-start(f32[3,64,2,128]{3,2,1,0:T(2,128)} %get-tuple-element.55), channel_id=1, source_target_pairs={{1,0},{2,1},{3,2},{4,3},{5,4},{6,5},{7,6},{8,7},{9,8},{10,9},{11,1... | collective-permute-start | bytes 589832 | tf_op jit(solution)/shard_map/ppermute | solution.py:25
  129.0 0.8 add.84
  129.7 0.7 collective-permute-start.18
  130.4 0.7 add_multiply_fusion
  131.1 0.6 slice.151
  131.7 3.5 %collective-permute-done.18 = f32[64,64]{1,0:T(8,128)S(1)} collective-permute-done((f32[64,64]{1,0:T(8,128)S(1)}, f32[64,64]{1,0:T(8,128)S(1)}, u32[]{:S(2)}, u32[]{:S(2)}) %collective-permute-start.18) | collective-permute-done | bytes 16416 | tf_op jit(solution)/shard_map/ppermute | solution.py:37
  135.4 5.8 %cholesky.17 = f32[64,64]{1,0:T(8,128)S(1)} custom-call(f32[64,64]{1,0:T(8,128)S(1)} %fusion.12), custom_call_target="Cholesky" | custom-call | tf_op jit(solution)/shard_map/jit(cholesky)/cholesky | solution.py:234
  141.3 0.6 compare_reduce_fusion
  141.9 0.7 select_bitcast_fusion
  142.6 4.9 %custom-call.8 = f32[1,64,64]{1,2,0:T(8,128)S(1)} custom-call(f32[1,64,64]{2,1,0:T(8,128)S(1)} %get-tuple-element.46), custom_call_target="InvertDiagBlocksLowerTriangular" | custom-call | tf_op jit(solution)/shard_map/triangular_solve | solution.py:236
  147.5 0.8 multiply_reduce_fusion.2
  149.8 3.5 %fusion.1 = f32[32,1024]{1,0:T(8,128)S(1)} fusion(bf16[64,32,1024]{2,0,1:T(8,128)(2,1)} %copy-done, f32[64]{0:T(128)S(1)} %get-tuple-element.65), kind=kLoop, calls=%fused_computation.7 | loop fusion | flops 6258688 | bytes 4325632 | tf_op jit(solution)/shard_map/reduce_sum | solution.py:274
  153.4 0.7 fusion.5.last_ref
  154.5 0.7 copy.15
  155.2 2.2 %copy-done.1 = bf16[64,32,1024]{2,0,1:T(8,128)(2,1)S(1)} copy-done((bf16[64,32,1024]{2,0,1:T(8,128)(2,1)S(1)}, bf16[64,32,1024]{2,0,1:T(8,128)(2,1)}, u32[]{:S(2)}) %copy-start.1) | copy-done | bytes 4194328
  157.4 7.5 %shard_map.98._ = f32[65,32,1024]{2,1,0:T(8,128)} custom-call(bf16[3,65,64]{2,1,0:T(8,128)(2,1)S(1)} %pad_maximum_fusion.6.mix_ref, bf16[32,64,1024]{2,1,0:T(8,128)(2,1)S(1)} %bitcast.57), custom_call_target="tpu_custom_call" | custom-call | flops 817889280 | bytes 12713984 | tf_op jit(solution)/shard_map/pallas_call | solution.py:199
  164.9 1.6 shard_map.99
  166.5 3.8 %select_maximum_fusion.2.conc_ref = f32[3,68,36,128]{3,2,1,0:T(8,128)} fusion(f32[3,64,2,128]{3,2,1,0:T(2,128)} %collective-permute-done.11, f32[3,64,2,128]{3,2,1,0:T(2,128)} %collective-permute-done.8, f32[3,2,32,128]{3,2,1,0:T(8,128)} %collective-permute-done.10, f32[3,64,32,128]{3,2,1,0:T(8,128)S(1)} %shard_map.96, ...), kind=kLoop, calls=%fused_computation.9 | loop fusion | flops 7520256 | bytes 7495680 | tf_op jit(solution)/shard_map/concatenate | solution.py:28
  170.3 23.9 %shard_map.97 = f32[3,64,32,128]{3,2,1,0:T(8,128)S(1)} custom-call(f32[3]{0:T(128)S(1)} %slice.143.scale_ref, f32[3,68,36,128]{3,2,1,0:T(8,128)} %select_maximum_fusion.2.conc_ref, f32[4,68,36,128]{3,2,1,0:T(8,128)} %slice.153.coeff_ref), custom_call_target="tpu_custom_call" | custom-call | flops 62914560 | bytes 11919360 | tf_op jit(solution)/shard_map/pallas_call | solution.py:161
  194.2 2.5 %pad_maximum_fusion = f32[4,64,32,128]{3,2,1,0:T(8,128)} fusion(f32[3,64,32,128]{3,2,1,0:T(8,128)S(1)} %shard_map.97, f32[1,64,32,128]{3,2,1,0:T(8,128)S(1)} %copy-done.3), kind=kLoop, calls=%fused_computation.8 | loop fusion | flops 1048576 | bytes 8388608 | tf_op jit(solution)/shard_map/concatenate | solution.py:262
  (76 shorter events, 1.7 us)
Async XLA Ops:
  0.6 4.3 %copy-start.6 = (f32[4,64,32,128]{3,2,1,0:T(8,128)S(1)}, f32[4,64,32,128]{3,2,1,0:T(8,128)}, u32[]{:S(2)}) copy-start(f32[4,64,32,128]{3,2,1,0:T(8,128)} %param.13) | copy-start | bytes 12582916
  0.6 4.3 %copy-start.7 = (f32[3,64,32,128]{3,2,1,0:T(8,128)S(1)}, f32[3,64,32,128]{3,2,1,0:T(8,128)}, u32[]{:S(2)}) copy-start(f32[3,64,32,128]{3,2,1,0:T(8,128)} %param.14) | copy-start | bytes 9437188
  0.7 4.3 %copy-start.8 = (f32[64,32,128]{2,1,0:T(8,128)S(1)}, f32[64,32,128]{2,1,0:T(8,128)}, u32[]{:S(2)}) copy-start(f32[64,32,128]{2,1,0:T(8,128)} %param.15) | copy-start | bytes 3145732
  2.0 14.3 %collective-permute-start.1 = (f32[8,2,32,128]{3,2,1,0:T(8,128)S(1)}, f32[8,2,32,128]{3,2,1,0:T(8,128)S(1)}, u32[]{:S(2)}, u32[]{:S(2)}) collective-permute-start(f32[8,2,32,128]{3,2,1,0:T(8,128)S(1)} %get-tuple-element.48), channel_id=1, source_target_pairs={{0,16},{16,32},{32,48},{48,64},{64,80},{80,96},{96,112},{112,0},{1... | collective-permute-start | bytes 786440 | tf_op jit(solution)/shard_map/ppermute | solution.py:22
  2.0 9.9 %copy-start.9 = (bf16[48,32,1024]{2,1,0:T(8,128)(2,1)S(1)}, bf16[48,32,1024]{2,1,0:T(8,128)(2,1)}, u32[]{:S(2)}) copy-start(bf16[48,32,1024]{2,1,0:T(8,128)(2,1)} %param.17) | copy-start | bytes 9437188
  2.0 14.3 %collective-permute-start.2 = (f32[8,2,32,128]{3,2,1,0:T(8,128)S(1)}, f32[8,2,32,128]{3,2,1,0:T(8,128)S(1)}, u32[]{:S(2)}, u32[]{:S(2)}) collective-permute-start(f32[8,2,32,128]{3,2,1,0:T(8,128)S(1)} %get-tuple-element.49), channel_id=1, source_target_pairs={{16,0},{32,16},{48,32},{64,48},{80,64},{96,80},{112,96},{0,112},{1... | collective-permute-start | bytes 786440 | tf_op jit(solution)/shard_map/ppermute | solution.py:23
  5.4 8.3 %copy-start.10 = (bf16[16,32,1024]{2,1,0:T(8,128)(2,1)S(1)}, bf16[16,32,1024]{2,1,0:T(8,128)(2,1)}, u32[]{:S(2)}) copy-start(bf16[16,32,1024]{2,1,0:T(8,128)(2,1)} %param.19) | copy-start | bytes 3145732
  5.4 17.7 %collective-permute-start = (f32[8,64,2,128]{3,2,1,0:T(2,128)S(1)}, f32[8,64,2,128]{3,2,1,0:T(2,128)S(1)}, u32[]{:S(2)}, u32[]{:S(2)}) collective-permute-start(f32[8,64,2,128]{3,2,1,0:T(2,128)S(1)} %get-tuple-element.50), channel_id=1, source_target_pairs={{0,1},{1,2},{2,3},{3,4},{4,5},{5,6},{6,7},{7,8},{8,9},{9,10},{10,1... | collective-permute-start | bytes 1572872 | tf_op jit(solution)/shard_map/ppermute | solution.py:24
  7.5 15.6 %collective-permute-start.3 = (f32[8,64,2,128]{3,2,1,0:T(2,128)S(1)}, f32[8,64,2,128]{3,2,1,0:T(2,128)S(1)}, u32[]{:S(2)}, u32[]{:S(2)}) collective-permute-start(f32[8,64,2,128]{3,2,1,0:T(2,128)S(1)} %get-tuple-element.51), channel_id=1, source_target_pairs={{1,0},{2,1},{3,2},{4,3},{5,4},{6,5},{7,6},{8,7},{9,8},{10,9},{11,1... | collective-permute-start | bytes 1572872 | tf_op jit(solution)/shard_map/ppermute | solution.py:25
  14.3 2.0 %copy-start = (bf16[64,32,1024]{2,0,1:T(8,128)(2,1)}, bf16[64,32,1024]{2,0,1:T(8,128)(2,1)S(1)}, u32[]{:S(2)}) copy-start(bf16[64,32,1024]{2,0,1:T(8,128)(2,1)S(1)} %copy_dynamic-update-slice_fusion.1) | copy-start | bytes 12582916
  28.0 5.9 %copy-start.5 = (f32[8,68,36,128]{3,2,1,0:T(8,128)}, f32[8,68,36,128]{3,2,1,0:T(8,128)S(1)}, u32[]{:S(2)}) copy-start(f32[8,68,36,128]{3,2,1,0:T(8,128)S(1)} %select_maximum_fusion) | copy-start | bytes 30081028
  28.1 5.8 %copy-start.4 = (f32[4]{0:T(128)S(1)}, f32[4]{0:T(128)}, u32[]{:S(2)}) copy-start(f32[4]{0:T(128)} %param.16) | copy-start | bytes 52
  43.9 8.7 %collective-permute-start.12 = (f32[64,64]{1,0:T(8,128)S(1)}, f32[64,64]{1,0:T(8,128)S(1)}, u32[]{:S(2)}, u32[]{:S(2)}) collective-permute-start(f32[64,64]{1,0:T(8,128)S(1)} %convolution_bitcast_fusion.1), channel_id=1, source_target_pairs={{0,16},{16,0},{32,48},{48,32},{64,80},{80,64},{96,112},{112,96},{1... | collective-permute-start | bytes 49160 | tf_op jit(solution)/shard_map/ppermute | solution.py:37
  44.1 14.3 %collective-permute-start.5 = (f32[1,2,32,128]{3,2,1,0:T(8,128)S(1)}, f32[1,2,32,128]{3,2,1,0:T(8,128)S(1)}, u32[]{:S(2)}, u32[]{:S(2)}) collective-permute-start(f32[1,2,32,128]{3,2,1,0:T(8,128)S(1)} %get-tuple-element.56), channel_id=1, source_target_pairs={{0,16},{16,32},{32,48},{48,64},{64,80},{80,96},{96,112},{112,0},{1... | collective-permute-start | bytes 98312 | tf_op jit(solution)/shard_map/ppermute | solution.py:22
  44.6 13.8 %collective-permute-start.6 = (f32[1,2,32,128]{3,2,1,0:T(8,128)S(1)}, f32[1,2,32,128]{3,2,1,0:T(8,128)S(1)}, u32[]{:S(2)}, u32[]{:S(2)}) collective-permute-start(f32[1,2,32,128]{3,2,1,0:T(8,128)S(1)} %get-tuple-element.57), channel_id=1, source_target_pairs={{16,0},{32,16},{48,32},{64,48},{80,64},{96,80},{112,96},{0,112},{1... | collective-permute-start | bytes 98312 | tf_op jit(solution)/shard_map/ppermute | solution.py:23
  47.3 11.2 %collective-permute-start.4 = (f32[1,64,2,128]{3,2,1,0:T(2,128)S(1)}, f32[1,64,2,128]{3,2,1,0:T(2,128)S(1)}, u32[]{:S(2)}, u32[]{:S(2)}) collective-permute-start(f32[1,64,2,128]{3,2,1,0:T(2,128)S(1)} %get-tuple-element.58), channel_id=1, source_target_pairs={{0,1},{1,2},{2,3},{3,4},{4,5},{5,6},{6,7},{7,8},{8,9},{9,10},{10,1... | collective-permute-start | bytes 196616 | tf_op jit(solution)/shard_map/ppermute | solution.py:24
  47.3 11.2 %collective-permute-start.7 = (f32[1,64,2,128]{3,2,1,0:T(2,128)S(1)}, f32[1,64,2,128]{3,2,1,0:T(2,128)S(1)}, u32[]{:S(2)}, u32[]{:S(2)}) collective-permute-start(f32[1,64,2,128]{3,2,1,0:T(2,128)S(1)} %get-tuple-element.59), channel_id=1, source_target_pairs={{1,0},{2,1},{3,2},{4,3},{5,4},{6,5},{7,6},{8,7},{9,8},{10,9},{11,1... | collective-permute-start | bytes 196616 | tf_op jit(solution)/shard_map/ppermute | solution.py:25
  52.6 4.0 %collective-permute-start.13 = (f32[64,64]{1,0:T(8,128)S(1)}, f32[64,64]{1,0:T(8,128)S(1)}, u32[]{:S(2)}, u32[]{:S(2)}) collective-permute-start(f32[64,64]{1,0:T(8,128)S(1)} %add.79), channel_id=1, source_target_pairs={{0,32},{16,48},{32,0},{48,16},{64,96},{80,112},{96,64},{112,80},{1... | collective-permute-start | bytes 49160 | tf_op jit(solution)/shard_map/ppermute | solution.py:37
  56.6 18.1 %collective-permute-start.14 = (f32[64,64]{1,0:T(8,128)S(1)}, f32[64,64]{1,0:T(8,128)S(1)}, u32[]{:S(2)}, u32[]{:S(2)}) collective-permute-start(f32[64,64]{1,0:T(8,128)S(1)} %add.80), channel_id=1, source_target_pairs={{0,64},{16,80},{32,96},{48,112},{64,0},{80,16},{96,32},{112,48},{1... | collective-permute-start | bytes 49160 | tf_op jit(solution)/shard_map/ppermute | solution.py:37
  68.2 1.0 copy-start.2
  69.2 8.2 %copy-start.11 = (f32[48]{0:T(128)S(1)}, f32[48]{0:T(128)}, u32[]{:S(2)}) copy-start(f32[48]{0:T(128)} %param.18) | copy-start | bytes 580
  74.7 1.2 collective-permute-start.19
  74.8 32.7 %collective-permute-start.15 = (f32[64,64]{1,0:T(8,128)S(1)}, f32[64,64]{1,0:T(8,128)S(1)}, u32[]{:S(2)}, u32[]{:S(2)}) collective-permute-start(f32[64,64]{1,0:T(8,128)S(1)} %add.81), channel_id=1, source_target_pairs={{0,1},{1,0},{2,3},{3,2},{4,5},{5,4},{6,7},{7,6},{8,9},{9,8},{10,11... | collective-permute-start | bytes 49160 | tf_op jit(solution)/shard_map/ppermute | solution.py:37
  76.6 5.2 %collective-permute-start.20 = (f32[65]{0:T(128)S(1)}, f32[65]{0:T(128)S(1)}, u32[]{:S(2)}, u32[]{:S(2)}) collective-permute-start(f32[65]{0:T(128)S(1)} %fusion.32), channel_id=1, source_target_pairs={{0,32},{16,48},{32,0},{48,16},{64,96},{80,112},{96,64},{112,80},{1... | collective-permute-start | bytes 788 | tf_op jit(solution)/shard_map/ppermute | solution.py:37
  81.9 25.8 %collective-permute-start.21 = (f32[65]{0:T(128)S(1)}, f32[65]{0:T(128)S(1)}, u32[]{:S(2)}, u32[]{:S(2)}) collective-permute-start(f32[65]{0:T(128)S(1)} %add.88), channel_id=1, source_target_pairs={{0,64},{16,80},{32,96},{48,112},{64,0},{80,16},{96,32},{112,48},{1... | collective-permute-start | bytes 788 | tf_op jit(solution)/shard_map/ppermute | solution.py:37
  107.5 7.2 %collective-permute-start.16 = (f32[64,64]{1,0:T(8,128)S(1)}, f32[64,64]{1,0:T(8,128)S(1)}, u32[]{:S(2)}, u32[]{:S(2)}) collective-permute-start(f32[64,64]{1,0:T(8,128)S(1)} %add.82), channel_id=1, source_target_pairs={{0,2},{1,3},{2,0},{3,1},{4,6},{5,7},{6,4},{7,5},{8,10},{9,11},{10,... | collective-permute-start | bytes 49160 | tf_op jit(solution)/shard_map/ppermute | solution.py:37
  107.7 3.6 %collective-permute-start.22 = (f32[65]{0:T(128)S(1)}, f32[65]{0:T(128)S(1)}, u32[]{:S(2)}, u32[]{:S(2)}) collective-permute-start(f32[65]{0:T(128)S(1)} %add.89), channel_id=1, source_target_pairs={{0,1},{1,0},{2,3},{3,2},{4,5},{5,4},{6,7},{7,6},{8,9},{9,8},{10,11... | collective-permute-start | bytes 788 | tf_op jit(solution)/shard_map/ppermute | solution.py:37
  111.3 5.1 %collective-permute-start.23 = (f32[65]{0:T(128)S(1)}, f32[65]{0:T(128)S(1)}, u32[]{:S(2)}, u32[]{:S(2)}) collective-permute-start(f32[65]{0:T(128)S(1)} %add.90), channel_id=1, source_target_pairs={{0,2},{1,3},{2,0},{3,1},{4,6},{5,7},{6,4},{7,5},{8,10},{9,11},{10,... | collective-permute-start | bytes 788 | tf_op jit(solution)/shard_map/ppermute | solution.py:37
  115.4 9.2 %collective-permute-start.17 = (f32[64,64]{1,0:T(8,128)}, f32[64,64]{1,0:T(8,128)}, u32[]{:S(2)}, u32[]{:S(2)}) collective-permute-start(f32[64,64]{1,0:T(8,128)} %add.83), channel_id=1, source_target_pairs={{0,4},{1,5},{2,6},{3,7},{4,0},{5,1},{6,2},{7,3},{8,12},{9,13},{10,... | collective-permute-start | bytes 49160 | tf_op jit(solution)/shard_map/ppermute | solution.py:37
  116.4 5.7 %collective-permute-start.24 = (f32[65]{0:T(128)S(1)}, f32[65]{0:T(128)S(1)}, u32[]{:S(2)}, u32[]{:S(2)}) collective-permute-start(f32[65]{0:T(128)S(1)} %add.91), channel_id=1, source_target_pairs={{0,4},{1,5},{2,6},{3,7},{4,0},{5,1},{6,2},{7,3},{8,12},{9,13},{10,... | collective-permute-start | bytes 788 | tf_op jit(solution)/shard_map/ppermute | solution.py:37
  118.1 48.3 %collective-permute-start.9 = (f32[3,2,32,128]{3,2,1,0:T(8,128)}, f32[3,2,32,128]{3,2,1,0:T(8,128)}, u32[]{:S(2)}, u32[]{:S(2)}) collective-permute-start(f32[3,2,32,128]{3,2,1,0:T(8,128)} %get-tuple-element.52), channel_id=1, source_target_pairs={{0,16},{16,32},{32,48},{48,64},{64,80},{80,96},{96,112},{112,0},{1... | collective-permute-start | bytes 294920 | tf_op jit(solution)/shard_map/ppermute | solution.py:22
  118.1 48.3 %collective-permute-start.10 = (f32[3,2,32,128]{3,2,1,0:T(8,128)}, f32[3,2,32,128]{3,2,1,0:T(8,128)}, u32[]{:S(2)}, u32[]{:S(2)}) collective-permute-start(f32[3,2,32,128]{3,2,1,0:T(8,128)} %get-tuple-element.53), channel_id=1, source_target_pairs={{16,0},{32,16},{48,32},{64,48},{80,64},{96,80},{112,96},{0,112},{1... | collective-permute-start | bytes 294920 | tf_op jit(solution)/shard_map/ppermute | solution.py:23
  121.1 45.4 %collective-permute-start.8 = (f32[3,64,2,128]{3,2,1,0:T(2,128)}, f32[3,64,2,128]{3,2,1,0:T(2,128)}, u32[]{:S(2)}, u32[]{:S(2)}) collective-permute-start(f32[3,64,2,128]{3,2,1,0:T(2,128)} %get-tuple-element.54), channel_id=1, source_target_pairs={{0,1},{1,2},{2,3},{3,4},{4,5},{5,6},{6,7},{7,8},{8,9},{9,10},{10,1... | collective-permute-start | bytes 589832 | tf_op jit(solution)/shard_map/ppermute | solution.py:24
  122.1 7.6 %collective-permute-start.25 = (f32[65]{0:T(128)S(1)}, f32[65]{0:T(128)}, u32[]{:S(2)}, u32[]{:S(2)}) collective-permute-start(f32[65]{0:T(128)S(1)} %add.92), channel_id=1, source_target_pairs={{0,8},{1,9},{2,10},{3,11},{4,12},{5,13},{6,14},{7,15},{8,0},{9,1},... | collective-permute-start | bytes 788 | tf_op jit(solution)/shard_map/ppermute | solution.py:37
  124.6 41.9 %collective-permute-start.11 = (f32[3,64,2,128]{3,2,1,0:T(2,128)}, f32[3,64,2,128]{3,2,1,0:T(2,128)}, u32[]{:S(2)}, u32[]{:S(2)}) collective-permute-start(f32[3,64,2,128]{3,2,1,0:T(2,128)} %get-tuple-element.55), channel_id=1, source_target_pairs={{1,0},{2,1},{3,2},{4,3},{5,4},{6,5},{7,6},{8,7},{9,8},{10,9},{11,1... | collective-permute-start | bytes 589832 | tf_op jit(solution)/shard_map/ppermute | solution.py:25
  129.7 5.5 %collective-permute-start.18 = (f32[64,64]{1,0:T(8,128)S(1)}, f32[64,64]{1,0:T(8,128)S(1)}, u32[]{:S(2)}, u32[]{:S(2)}) collective-permute-start(f32[64,64]{1,0:T(8,128)S(1)} %add.84), channel_id=1, source_target_pairs={{0,8},{1,9},{2,10},{3,11},{4,12},{5,13},{6,14},{7,15},{8,0},{9,1},... | collective-permute-start | bytes 49160 | tf_op jit(solution)/shard_map/ppermute | solution.py:37
  155.2 2.2 %copy-start.1 = (bf16[64,32,1024]{2,0,1:T(8,128)(2,1)S(1)}, bf16[64,32,1024]{2,0,1:T(8,128)(2,1)}, u32[]{:S(2)}) copy-start(bf16[64,32,1024]{2,0,1:T(8,128)(2,1)} %copy-done) | copy-start | bytes 12582916
  170.3 23.9 %copy-start.3 = (f32[1,64,32,128]{3,2,1,0:T(8,128)S(1)}, f32[1,64,32,128]{3,2,1,0:T(8,128)}, u32[]{:S(2)}) copy-start(f32[1,64,32,128]{3,2,1,0:T(8,128)} %copy-done.2) | copy-start | bytes 3145732

commit v6 on v5

--- a/solution.py
+++ b/solution.py
@@ -6,6 +6,7 @@
 from jax.experimental.pallas import tpu as pltpu
 
 time_step = 0.25
+ALIGN = 8
 
 
 def ring(axis):
@@ -25,7 +26,10 @@
     high_y = lax.ppermute(block[:, :, :width], "gy", by)
     rows = jnp.concatenate([low_x, block, high_x], axis=1)
     edge = ((0, 0), (width, width), (0, 0), (0, 0))
-    return jnp.concatenate([jnp.pad(low_y, edge), rows, jnp.pad(high_y, edge)], axis=2)
+    gap = jnp.zeros(rows.shape[:2] + (ALIGN - width,) + rows.shape[3:], rows.dtype)
+    return jnp.concatenate(
+        [gap, jnp.pad(low_y, edge), rows, jnp.pad(high_y, edge), gap], axis=2
+    )
 
 
 def butterfly_sum(value):
@@ -114,10 +118,10 @@
 
     def row(i, carry):
         def c(dx, dy):
-            return conc_ref[0, i + 2 + dx, pl.ds(2 + dy, rows), :]
+            return conc_ref[0, i + 2 + dx, pl.ds(ALIGN + dy, rows), :]
 
         def k(field, dx, dy):
-            return coeff_ref[field, i + 2 + dx, pl.ds(2 + dy, rows), :]
+            return coeff_ref[field, i + 2 + dx, pl.ds(ALIGN + dy, rows), :]
 
         center = c(0, 0)
 
@@ -157,7 +161,7 @@
 
 def stencil_step(conc_pad, coeff_pad, scale):
     count, px, py, depth = conc_pad.shape
-    nx, ny = px - 4, py - 4
+    nx, ny = px - 4, py - 2 * ALIGN
     return pl.pallas_call(
         stencil_body,
         out_shape=jax.ShapeDtypeStruct((count, nx, ny, depth), jnp.float32),

time: 197 us -> 249 us (1.26)
  local copies, waits for them, and re-layouts: 20.3 us -> 73.5 us
  waiting for transfers between devices: 17.1 us -> 12 us
    concatenate x0 -> x3, local copies, waits for them, and re-layouts: none -> 46.4 us  [halo(): jnp.concatenate([gap, jnp.pad(low_y, edge), rows, jnp.pad(high_y, edge),...]
    ppermute x3, waiting for transfers between devices: 6.81 us -> 1.76 us  [halo(): low_y = lax.ppermute(block[:, :, ny - width:], 'gy', fy)]
    ppermute x14, starting transfers between devices: 14.2 us -> 18 us  [butterfly_sum(): value = value + lax.ppermute(value, axis, pairs)]
    ppermute x3, starting transfers between devices: 8.53 us -> 4.86 us  [halo(): high_x = lax.ppermute(block[:, :width], 'gx', bx)]
    slice x1, local copies, waits for them, and re-layouts: 3.09 us -> 6.28 us  [per_device(): coeff_pad = first[count:]]
    pad x0 -> x6, local copies, waits for them, and re-layouts: none -> 3.12 us  [the longest x3 1.91 us: halo(): jnp.pad(high_y, edge)]
    unnamed x26, local copies, waits for them, and re-layouts: 9.14 us -> 6.41 us
    concatenate x3 -> x4, other arithmetic: 8.92 us -> 9.9 us  [the longest x3 7.12 us: halo(): rows = jnp.concatenate([low_x, block, high_x], axis=1)]
  transfers between devices with their start and end apart: 26 -> 26, of which waited for: 6 -> 7; matrix products, arithmetic and copies ran while one was open for 19% -> 19% of each run, Pallas kernels for 22% -> 18%
where the time goes in v6:
time: 249 us; the launch traced here: 247 us
  Pallas kernels  78 us (31%)
  local copies, waits for them, and re-layouts  73.5 us (30%)
  starting transfers between devices  42.2 us (17%)
  other arithmetic  35.7 us (14%)
  waiting for transfers between devices  12 us (5%)
  matrix products  3.54 us (1%)
    pallas_call x4, Pallas kernels, stencil_step(): pl.pallas_call(stencil_body, out_shape=jax.ShapeDtypeStruct((count, nx, n...  68.7 us
    concatenate x3, local copies, waits for them, and re-layouts, halo(): jnp.concatenate([gap, jnp.pad(low_y, edge), rows, jnp.pad(high_y, edge),...  46.4 us
    ppermute x14, starting transfers between devices, butterfly_sum(): value = value + lax.ppermute(value, axis, pairs)  18 us
    ppermute x3, starting transfers between devices, halo(): high_y = lax.ppermute(block[:, :, :width], 'gy', by)  15.2 us
    ppermute x14, waiting for transfers between devices, butterfly_sum(): value = value + lax.ppermute(value, axis, pairs)  8.23 us
    pallas_call x1, Pallas kernels, basis_rows(): pl.pallas_call(basis_body, out_shape=jax.ShapeDtypeStruct((rows, span, co...  7.65 us
    concatenate x3, other arithmetic, halo(): rows = jnp.concatenate([low_x, block, high_x], axis=1)  7.12 us
    another operation x3, other arithmetic, per_device(): lower_static = jnp.linalg.cholesky(gram_static)  6.52 us
  transfers between devices with their start and end apart: 26, of which 7 were waited for; matrix products, arithmetic and copies ran while one was open for 19% of the time, Pallas kernels for 18%

profile of v6, /device:TPU:0, one launch (start us, length us, event | category | flops | bytes accessed | tf_op | source)
XLA Modules:
  0.0 247.3 jit_solution(12735949518925442105)
XLA Ops:
  0.7 2.8 %pad_maximum_fusion.4 = (f32[8,64,2,128]{3,2,1,0:T(2,128)S(1)}, f32[8,64,2,128]{3,2,1,0:T(2,128)S(1)}) fusion(f32[1,64,32,128]{3,2,1,0:T(8,128)} %bitcast.60, f32[3,64,32,128]{3,2,1,0:T(8,128)} %param.14, f32[4,64,32,128]{3,2,1,0:T(8,128)} %param.13), kind=kLoop, calls=%fused_computation.13 | loop fusion | flops 524288 | bytes 9437184 | tf_op jit(solution)/shard_map/concatenate | solution.py:233
  3.5 2.1 collective-permute-start
  5.6 2.4 collective-permute-start.2
  8.0 6.2 %collective-permute-start.3 = (f32[8,64,2,128]{3,2,1,0:T(2,128)S(1)}, f32[8,64,2,128]{3,2,1,0:T(2,128)S(1)}, u32[]{:S(2)}, u32[]{:S(2)}) collective-permute-start(f32[8,64,2,128]{3,2,1,0:T(2,128)S(1)} %get-tuple-element.48), channel_id=1, source_target_pairs={{1,0},{2,1},{3,2},{4,3},{5,4},{6,5},{7,6},{8,7},{9,8},{10,9},{11,1... | collective-permute-start | bytes 1572872 | tf_op jit(solution)/shard_map/ppermute | solution.py:26
  14.2 1.7 copy_dynamic-update-slice_fusion
  16.6 1.2 convolution_bitcast_fusion.1
  17.8 0.8 copy-done
  18.6 4.0 %pad_maximum_fusion = f32[8,68,32,128]{3,2,1,0:T(8,128)} fusion(f32[8,2,32,128]{3,2,1,0:T(8,128)S(1)} %collective-permute-done.2, f32[1,64,32,128]{3,2,1,0:T(8,128)S(1)} %bitcast.62, f32[3,64,32,128]{3,2,1,0:T(8,128)S(1)} %copy-done.6, f32[4,64,32,128]{3,2,1,0:T(8,128)S(1)} %copy-done.5, f32[8,2,32,128]{3,2,1,0:T(8,128)S(1)} %collective-permute-done.1), kind=kLoop, calls=%fused_computation.2 | loop fusion | flops 8912896 | bytes 17825792 | tf_op jit(solution)/shard_map/concatenate | solution.py:27
  22.8 2.0 collective-permute-done.3
  25.2 32.1 %concatenate.45 = f32[8,68,48,128]{3,2,1,0:T(8,128)} concatenate(f32[8,68,6,128]{3,2,1,0:T(8,128)S(1)} %broadcast_in_dim.13, f32[8,68,2,128]{3,2,1,0:T(2,128)S(1)} %pad.37, f32[8,68,32,128]{3,2,1,0:T(8,128)} %pad_maximum_fusion, f32[8,68,2,128]{3,2,1,0:T(2,128)S(1)} %pad.38, f32[8,68,6,128]{3,2,1,0:T(8,128)S(1)} %broadcast_in_dim.13), dimensions={2} | concatenate | bytes 26738688 | tf_op jit(solution)/shard_map/concatenate | solution.py:30
  57.3 6.3 %slice.153.coeff_ref = f32[4,68,48,128]{3,2,1,0:T(8,128)} slice(f32[8,68,48,128]{3,2,1,0:T(8,128)} %concatenate.45), slice={[4:8], [0:68], [0:48], [0:128]} | slice | bytes 13369344 | tf_op jit(solution)/shard_map/slice | solution.py:234
  63.6 1.5 slice.152.conc_ref
  65.1 9.8 %shard_map.94 = f32[1,64,32,128]{3,2,1,0:T(8,128)S(1)} custom-call(f32[1]{0:T(128)S(1)} %bitcast.58, f32[1,68,48,128]{3,2,1,0:T(8,128)S(1)} %slice.152.conc_ref, f32[4,68,48,128]{3,2,1,0:T(8,128)} %slice.153.coeff_ref), custom_call_target="tpu_custom_call" | custom-call | flops 20971520 | bytes 9404416 | tf_op jit(solution)/shard_map/pallas_call | solution.py:165
  75.0 2.5 %collective-permute-start.6 = (f32[1,2,32,128]{3,2,1,0:T(8,128)S(1)}, f32[1,2,32,128]{3,2,1,0:T(8,128)S(1)}, u32[]{:S(2)}, u32[]{:S(2)}) collective-permute-start(f32[1,2,32,128]{3,2,1,0:T(8,128)S(1)} %get-tuple-element.59), channel_id=1, source_target_pairs={{16,0},{32,16},{48,32},{64,48},{80,64},{96,80},{112,96},{0,112},{1... | collective-permute-start | bytes 98312 | tf_op jit(solution)/shard_map/ppermute | solution.py:24
  77.6 5.6 %collective-permute-start.7 = (f32[1,64,2,128]{3,2,1,0:T(2,128)S(1)}, f32[1,64,2,128]{3,2,1,0:T(2,128)S(1)}, u32[]{:S(2)}, u32[]{:S(2)}) collective-permute-start(f32[1,64,2,128]{3,2,1,0:T(2,128)S(1)} %get-tuple-element.56), channel_id=1, source_target_pairs={{1,0},{2,1},{3,2},{4,3},{5,4},{6,5},{7,6},{8,7},{9,8},{10,9},{11,1... | collective-permute-start | bytes 196616 | tf_op jit(solution)/shard_map/ppermute | solution.py:26
  83.2 0.8 collective-permute-start.13
  84.1 1.8 collective-permute-done.4
  86.0 1.1 concatenate.47.conc_ref
  87.1 10.3 %shard_map.95 = f32[1,64,32,128]{3,2,1,0:T(8,128)S(1)} custom-call(f32[1]{0:T(128)S(1)} %bitcast.59, f32[1,68,48,128]{3,2,1,0:T(8,128)S(1)} %concatenate.47.conc_ref, f32[4,68,48,128]{3,2,1,0:T(8,128)} %slice.153.coeff_ref), custom_call_target="tpu_custom_call" | custom-call | flops 20971520 | bytes 9404416 | tf_op jit(solution)/shard_map/pallas_call | solution.py:165
  97.5 1.0 copy-done.2
  98.8 0.9 multiply_reduce_fusion
  99.9 3.3 %fusion = f32[64]{0:T(128)S(1)} fusion(bf16[64,32,1024]{2,0,1:T(8,128)(2,1)} %copy-done, f32[32,1024]{1,0:T(8,128)S(1)} %mul.85), kind=kLoop, calls=%fused_computation.3 | loop fusion | flops 6291392 | bytes 4325632 | tf_op jit(solution)/shard_map/reduce_sum | solution.py:258
  103.2 0.7 pad_maximum_fusion.10
  104.0 2.4 collective-permute-start.14
  106.4 0.7 fusion.32
  107.1 1.6 collective-permute-start.20
  108.8 5.0 %slice.154.conc_ref = f32[3,68,48,128]{3,2,1,0:T(8,128)} slice(f32[8,68,48,128]{3,2,1,0:T(8,128)} %concatenate.45), slice={[1:4], [0:68], [0:48], [0:128]} | slice | bytes 10027008 | tf_op jit(solution)/shard_map/slice | solution.py:264
  113.8 1.6 collective-permute-start.21
  115.5 24.2 %shard_map.96 = f32[3,64,32,128]{3,2,1,0:T(8,128)S(1)} custom-call(f32[3]{0:T(128)S(1)} %slice.143.scale_ref, f32[3,68,48,128]{3,2,1,0:T(8,128)} %slice.154.conc_ref, f32[4,68,48,128]{3,2,1,0:T(8,128)} %slice.153.coeff_ref), custom_call_target="tpu_custom_call" | custom-call | flops 62914560 | bytes 14843904 | tf_op jit(solution)/shard_map/pallas_call | solution.py:165
  139.8 2.0 collective-permute-start.22
  141.8 0.9 fusion.24
  142.7 1.0 collective-permute-done.15
  143.7 0.6 add.82
  144.5 3.3 %collective-permute-start.23 = (f32[65]{0:T(128)S(1)}, f32[65]{0:T(128)S(1)}, u32[]{:S(2)}, u32[]{:S(2)}) collective-permute-start(f32[65]{0:T(128)S(1)} %add.90), channel_id=1, source_target_pairs={{0,2},{1,3},{2,0},{3,1},{4,6},{5,7},{6,4},{7,5},{8,10},{9,11},{10,... | collective-permute-start | bytes 788 | tf_op jit(solution)/shard_map/ppermute | solution.py:41
  147.9 0.7 fusion.25
  148.6 1.5 collective-permute-done.23
  150.1 1.0 collective-permute-start.24
  151.1 1.4 collective-permute-start.8
  153.0 0.6 collective-permute-done.24
  153.6 4.5 %collective-permute-start.25 = (f32[65]{0:T(128)S(1)}, f32[65]{0:T(128)}, u32[]{:S(2)}, u32[]{:S(2)}) collective-permute-start(f32[65]{0:T(128)S(1)} %add.92), channel_id=1, source_target_pairs={{0,8},{1,9},{2,10},{3,11},{4,12},{5,13},{6,14},{7,15},{8,0},{9,1},... | collective-permute-start | bytes 788 | tf_op jit(solution)/shard_map/ppermute | solution.py:41
  158.3 3.4 %collective-permute-start.11 = (f32[3,64,2,128]{3,2,1,0:T(2,128)}, f32[3,64,2,128]{3,2,1,0:T(2,128)}, u32[]{:S(2)}, u32[]{:S(2)}) collective-permute-start(f32[3,64,2,128]{3,2,1,0:T(2,128)} %get-tuple-element.52), channel_id=1, source_target_pairs={{1,0},{2,1},{3,2},{4,3},{5,4},{6,5},{7,6},{8,7},{9,8},{10,9},{11,1... | collective-permute-start | bytes 589832 | tf_op jit(solution)/shard_map/ppermute | solution.py:26
  161.7 0.8 add.83
  162.6 0.7 add_multiply_fusion
  163.3 0.6 slice.151
  163.9 3.0 %collective-permute-done.17 = f32[64,64]{1,0:T(8,128)S(1)} collective-permute-done((f32[64,64]{1,0:T(8,128)S(1)}, f32[64,64]{1,0:T(8,128)S(1)}, u32[]{:S(2)}, u32[]{:S(2)}) %collective-permute-start.17) | collective-permute-done | bytes 16416 | tf_op jit(solution)/shard_map/ppermute | solution.py:41
  167.1 3.0 %pad_maximum_fusion.2 = f32[3,68,32,128]{3,2,1,0:T(8,128)} fusion(f32[3,2,32,128]{3,2,1,0:T(8,128)} %collective-permute-done.10, f32[3,64,32,128]{3,2,1,0:T(8,128)S(1)} %shard_map.96, f32[3,2,32,128]{3,2,1,0:T(8,128)} %collective-permute-done.9), kind=kLoop, calls=%fused_computation.6 | loop fusion | flops 1671168 | bytes 6684672 | tf_op jit(solution)/shard_map/concatenate | solution.py:27
  170.1 2.1 collective-permute-done.18
  172.4 5.8 %cholesky.17 = f32[64,64]{1,0:T(8,128)S(1)} custom-call(f32[64,64]{1,0:T(8,128)S(1)} %fusion.12), custom_call_target="Cholesky" | custom-call | tf_op jit(solution)/shard_map/jit(cholesky)/cholesky | solution.py:238
  178.3 0.6 compare_reduce_fusion
  179.0 0.7 select_bitcast_fusion
  179.6 4.9 %custom-call.8 = f32[1,64,64]{1,2,0:T(8,128)S(1)} custom-call(f32[1,64,64]{2,1,0:T(8,128)S(1)} %get-tuple-element.46), custom_call_target="InvertDiagBlocksLowerTriangular" | custom-call | tf_op jit(solution)/shard_map/triangular_solve | solution.py:240
  184.5 0.8 multiply_reduce_fusion.2
  185.5 3.5 %fusion.1 = f32[32,1024]{1,0:T(8,128)S(1)} fusion(bf16[64,32,1024]{2,0,1:T(8,128)(2,1)} %copy-done, f32[64]{0:T(128)S(1)} %get-tuple-element.65), kind=kLoop, calls=%fused_computation.4 | loop fusion | flops 6258688 | bytes 4325632 | tf_op jit(solution)/shard_map/reduce_sum | solution.py:278
  190.8 0.7 copy.15
  191.5 2.2 copy-done.1
  193.7 7.6 %shard_map.98._ = f32[65,32,1024]{2,1,0:T(8,128)} custom-call(bf16[3,65,64]{2,1,0:T(8,128)(2,1)S(1)} %pad_maximum_fusion.9.mix_ref, bf16[32,64,1024]{2,1,0:T(8,128)(2,1)S(1)} %bitcast.57), custom_call_target="tpu_custom_call" | custom-call | flops 817889280 | bytes 12713984 | tf_op jit(solution)/shard_map/pallas_call | solution.py:203
  201.3 0.7 fusion.5.last_ref
  202.0 1.7 shard_map.99
  203.7 1.0 pad.41
  204.7 1.7 pad.42
  206.4 0.9 broadcast_in_dim.15
  207.4 13.2 %concatenate.49.conc_ref = f32[3,68,48,128]{3,2,1,0:T(8,128)} concatenate(f32[3,68,6,128]{3,2,1,0:T(8,128)} %broadcast_in_dim.15, f32[3,68,2,128]{3,2,1,0:T(2,128)S(1)} %pad.41, f32[3,68,32,128]{3,2,1,0:T(8,128)S(1)} %copy-done.7, f32[3,68,2,128]{3,2,1,0:T(2,128)} %pad.42, f32[3,68,6,128]{3,2,1,0:T(8,128)} %broadcast_in_dim.15), dimensions={2} | concatenate | bytes 10027008 | tf_op jit(solution)/shard_map/concatenate | solution.py:30
  220.5 24.3 %shard_map.97 = f32[3,64,32,128]{3,2,1,0:T(8,128)S(1)} custom-call(f32[3]{0:T(128)S(1)} %slice.143.scale_ref, f32[3,68,48,128]{3,2,1,0:T(8,128)} %concatenate.49.conc_ref, f32[4,68,48,128]{3,2,1,0:T(8,128)} %slice.153.coeff_ref), custom_call_target="tpu_custom_call" | custom-call | flops 62914560 | bytes 14843904 | tf_op jit(solution)/shard_map/pallas_call | solution.py:165
  244.8 2.5 pad_maximum_fusion.1
  (88 shorter events, 4.3 us)
Async XLA Ops:
  0.6 4.9 %copy-start.5 = (f32[4,64,32,128]{3,2,1,0:T(8,128)S(1)}, f32[4,64,32,128]{3,2,1,0:T(8,128)}, u32[]{:S(2)}) copy-start(f32[4,64,32,128]{3,2,1,0:T(8,128)} %param.13) | copy-start | bytes 12582916
  0.6 4.9 %copy-start.6 = (f32[3,64,32,128]{3,2,1,0:T(8,128)S(1)}, f32[3,64,32,128]{3,2,1,0:T(8,128)}, u32[]{:S(2)}) copy-start(f32[3,64,32,128]{3,2,1,0:T(8,128)} %param.14) | copy-start | bytes 9437188
  0.7 4.9 %copy-start.8 = (f32[64,32,128]{2,1,0:T(8,128)S(1)}, f32[64,32,128]{2,1,0:T(8,128)}, u32[]{:S(2)}) copy-start(f32[64,32,128]{2,1,0:T(8,128)} %param.15) | copy-start | bytes 3145732
  3.5 10.8 %copy-start.9 = (bf16[48,32,1024]{2,1,0:T(8,128)(2,1)S(1)}, bf16[48,32,1024]{2,1,0:T(8,128)(2,1)}, u32[]{:S(2)}) copy-start(bf16[48,32,1024]{2,1,0:T(8,128)(2,1)} %param.17) | copy-start | bytes 9437188
  3.5 19.2 %collective-permute-start = (f32[8,64,2,128]{3,2,1,0:T(2,128)S(1)}, f32[8,64,2,128]{3,2,1,0:T(2,128)S(1)}, u32[]{:S(2)}, u32[]{:S(2)}) collective-permute-start(f32[8,64,2,128]{3,2,1,0:T(2,128)S(1)} %get-tuple-element.49), channel_id=1, source_target_pairs={{0,1},{1,2},{2,3},{3,4},{4,5},{5,6},{6,7},{7,8},{8,9},{9,10},{10,1... | collective-permute-start | bytes 1572872 | tf_op jit(solution)/shard_map/ppermute | solution.py:25
  5.6 10.3 %copy-start.10 = (bf16[16,32,1024]{2,1,0:T(8,128)(2,1)S(1)}, bf16[16,32,1024]{2,1,0:T(8,128)(2,1)}, u32[]{:S(2)}) copy-start(bf16[16,32,1024]{2,1,0:T(8,128)(2,1)} %param.19) | copy-start | bytes 3145732
  5.6 13.0 %collective-permute-start.2 = (f32[8,2,32,128]{3,2,1,0:T(8,128)S(1)}, f32[8,2,32,128]{3,2,1,0:T(8,128)S(1)}, u32[]{:S(2)}, u32[]{:S(2)}) collective-permute-start(f32[8,2,32,128]{3,2,1,0:T(8,128)S(1)} %get-tuple-element.51), channel_id=1, source_target_pairs={{16,0},{32,16},{48,32},{64,48},{80,64},{96,80},{112,96},{0,112},{1... | collective-permute-start | bytes 786440 | tf_op jit(solution)/shard_map/ppermute | solution.py:24
  8.0 10.6 %collective-permute-start.1 = (f32[8,2,32,128]{3,2,1,0:T(8,128)S(1)}, f32[8,2,32,128]{3,2,1,0:T(8,128)S(1)}, u32[]{:S(2)}, u32[]{:S(2)}) collective-permute-start(f32[8,2,32,128]{3,2,1,0:T(8,128)S(1)} %get-tuple-element.50), channel_id=1, source_target_pairs={{0,16},{16,32},{32,48},{48,64},{64,80},{80,96},{96,112},{112,0},{1... | collective-permute-start | bytes 786440 | tf_op jit(solution)/shard_map/ppermute | solution.py:23
  8.0 16.8 %collective-permute-start.3 = (f32[8,64,2,128]{3,2,1,0:T(2,128)S(1)}, f32[8,64,2,128]{3,2,1,0:T(2,128)S(1)}, u32[]{:S(2)}, u32[]{:S(2)}) collective-permute-start(f32[8,64,2,128]{3,2,1,0:T(2,128)S(1)} %get-tuple-element.48), channel_id=1, source_target_pairs={{1,0},{2,1},{3,2},{4,3},{5,4},{6,5},{7,6},{8,7},{9,8},{10,9},{11,1... | collective-permute-start | bytes 1572872 | tf_op jit(solution)/shard_map/ppermute | solution.py:26
  16.6 2.0 copy-start
  57.3 7.8 %copy-start.4 = (f32[4]{0:T(128)S(1)}, f32[4]{0:T(128)}, u32[]{:S(2)}) copy-start(f32[4]{0:T(128)} %param.16) | copy-start | bytes 52
  75.0 9.1 %collective-permute-start.6 = (f32[1,2,32,128]{3,2,1,0:T(8,128)S(1)}, f32[1,2,32,128]{3,2,1,0:T(8,128)S(1)}, u32[]{:S(2)}, u32[]{:S(2)}) collective-permute-start(f32[1,2,32,128]{3,2,1,0:T(8,128)S(1)} %get-tuple-element.59), channel_id=1, source_target_pairs={{16,0},{32,16},{48,32},{64,48},{80,64},{96,80},{112,96},{0,112},{1... | collective-permute-start | bytes 98312 | tf_op jit(solution)/shard_map/ppermute | solution.py:24
  77.5 6.6 %collective-permute-start.5 = (f32[1,2,32,128]{3,2,1,0:T(8,128)S(1)}, f32[1,2,32,128]{3,2,1,0:T(8,128)S(1)}, u32[]{:S(2)}, u32[]{:S(2)}) collective-permute-start(f32[1,2,32,128]{3,2,1,0:T(8,128)S(1)} %get-tuple-element.58), channel_id=1, source_target_pairs={{0,16},{16,32},{32,48},{48,64},{64,80},{80,96},{96,112},{112,0},{1... | collective-permute-start | bytes 98312 | tf_op jit(solution)/shard_map/ppermute | solution.py:23
  77.5 5.7 %collective-permute-start.12 = (f32[64,64]{1,0:T(8,128)S(1)}, f32[64,64]{1,0:T(8,128)S(1)}, u32[]{:S(2)}, u32[]{:S(2)}) collective-permute-start(f32[64,64]{1,0:T(8,128)S(1)} %convolution_bitcast_fusion.1), channel_id=1, source_target_pairs={{0,16},{16,0},{32,48},{48,32},{64,80},{80,64},{96,112},{112,96},{1... | collective-permute-start | bytes 49160 | tf_op jit(solution)/shard_map/ppermute | solution.py:41
  77.6 8.3 %collective-permute-start.4 = (f32[1,64,2,128]{3,2,1,0:T(2,128)S(1)}, f32[1,64,2,128]{3,2,1,0:T(2,128)S(1)}, u32[]{:S(2)}, u32[]{:S(2)}) collective-permute-start(f32[1,64,2,128]{3,2,1,0:T(2,128)S(1)} %get-tuple-element.57), channel_id=1, source_target_pairs={{0,1},{1,2},{2,3},{3,4},{4,5},{5,6},{6,7},{7,8},{8,9},{9,10},{10,1... | collective-permute-start | bytes 196616 | tf_op jit(solution)/shard_map/ppermute | solution.py:25
  77.6 8.3 %collective-permute-start.7 = (f32[1,64,2,128]{3,2,1,0:T(2,128)S(1)}, f32[1,64,2,128]{3,2,1,0:T(2,128)S(1)}, u32[]{:S(2)}, u32[]{:S(2)}) collective-permute-start(f32[1,64,2,128]{3,2,1,0:T(2,128)S(1)} %get-tuple-element.56), channel_id=1, source_target_pairs={{1,0},{2,1},{3,2},{4,3},{5,4},{6,5},{7,6},{8,7},{9,8},{10,9},{11,1... | collective-permute-start | bytes 196616 | tf_op jit(solution)/shard_map/ppermute | solution.py:26
  83.2 20.8 %collective-permute-start.13 = (f32[64,64]{1,0:T(8,128)S(1)}, f32[64,64]{1,0:T(8,128)S(1)}, u32[]{:S(2)}, u32[]{:S(2)}) collective-permute-start(f32[64,64]{1,0:T(8,128)S(1)} %add.79), channel_id=1, source_target_pairs={{0,32},{16,48},{32,0},{48,16},{64,96},{80,112},{96,64},{112,80},{1... | collective-permute-start | bytes 49160 | tf_op jit(solution)/shard_map/ppermute | solution.py:41
  97.5 1.0 copy-start.2
  98.4 10.4 %copy-start.11 = (f32[48]{0:T(128)S(1)}, f32[48]{0:T(128)}, u32[]{:S(2)}) copy-start(f32[48]{0:T(128)} %param.18) | copy-start | bytes 580
  104.0 2.5 collective-permute-start.19
  104.0 35.7 %collective-permute-start.14 = (f32[64,64]{1,0:T(8,128)S(1)}, f32[64,64]{1,0:T(8,128)S(1)}, u32[]{:S(2)}, u32[]{:S(2)}) collective-permute-start(f32[64,64]{1,0:T(8,128)S(1)} %add.80), channel_id=1, source_target_pairs={{0,64},{16,80},{32,96},{48,112},{64,0},{80,16},{96,32},{112,48},{1... | collective-permute-start | bytes 49160 | tf_op jit(solution)/shard_map/ppermute | solution.py:41
  107.1 6.7 %collective-permute-start.20 = (f32[65]{0:T(128)S(1)}, f32[65]{0:T(128)S(1)}, u32[]{:S(2)}, u32[]{:S(2)}) collective-permute-start(f32[65]{0:T(128)S(1)} %fusion.32), channel_id=1, source_target_pairs={{0,32},{16,48},{32,0},{48,16},{64,96},{80,112},{96,64},{112,80},{1... | collective-permute-start | bytes 788 | tf_op jit(solution)/shard_map/ppermute | solution.py:41
  113.8 26.0 %collective-permute-start.21 = (f32[65]{0:T(128)S(1)}, f32[65]{0:T(128)S(1)}, u32[]{:S(2)}, u32[]{:S(2)}) collective-permute-start(f32[65]{0:T(128)S(1)} %add.88), channel_id=1, source_target_pairs={{0,64},{16,80},{32,96},{48,112},{64,0},{80,16},{96,32},{112,48},{1... | collective-permute-start | bytes 788 | tf_op jit(solution)/shard_map/ppermute | solution.py:41
  139.7 4.0 %collective-permute-start.15 = (f32[64,64]{1,0:T(8,128)S(1)}, f32[64,64]{1,0:T(8,128)S(1)}, u32[]{:S(2)}, u32[]{:S(2)}) collective-permute-start(f32[64,64]{1,0:T(8,128)S(1)} %add.81), channel_id=1, source_target_pairs={{0,1},{1,0},{2,3},{3,2},{4,5},{5,4},{6,7},{7,6},{8,9},{9,8},{10,11... | collective-permute-start | bytes 49160 | tf_op jit(solution)/shard_map/ppermute | solution.py:41
  139.8 4.7 %collective-permute-start.22 = (f32[65]{0:T(128)S(1)}, f32[65]{0:T(128)S(1)}, u32[]{:S(2)}, u32[]{:S(2)}) collective-permute-start(f32[65]{0:T(128)S(1)} %add.89), channel_id=1, source_target_pairs={{0,1},{1,0},{2,3},{3,2},{4,5},{5,4},{6,7},{7,6},{8,9},{9,8},{10,11... | collective-permute-start | bytes 788 | tf_op jit(solution)/shard_map/ppermute | solution.py:41
  144.3 14.0 %collective-permute-start.16 = (f32[64,64]{1,0:T(8,128)}, f32[64,64]{1,0:T(8,128)}, u32[]{:S(2)}, u32[]{:S(2)}) collective-permute-start(f32[64,64]{1,0:T(8,128)} %add.82), channel_id=1, source_target_pairs={{0,2},{1,3},{2,0},{3,1},{4,6},{5,7},{6,4},{7,5},{8,10},{9,11},{10,... | collective-permute-start | bytes 49160 | tf_op jit(solution)/shard_map/ppermute | solution.py:41
  144.5 5.5 %collective-permute-start.23 = (f32[65]{0:T(128)S(1)}, f32[65]{0:T(128)S(1)}, u32[]{:S(2)}, u32[]{:S(2)}) collective-permute-start(f32[65]{0:T(128)S(1)} %add.90), channel_id=1, source_target_pairs={{0,2},{1,3},{2,0},{3,1},{4,6},{5,7},{6,4},{7,5},{8,10},{9,11},{10,... | collective-permute-start | bytes 788 | tf_op jit(solution)/shard_map/ppermute | solution.py:41
  150.1 3.6 %collective-permute-start.24 = (f32[65]{0:T(128)S(1)}, f32[65]{0:T(128)S(1)}, u32[]{:S(2)}, u32[]{:S(2)}) collective-permute-start(f32[65]{0:T(128)S(1)} %add.91), channel_id=1, source_target_pairs={{0,4},{1,5},{2,6},{3,7},{4,0},{5,1},{6,2},{7,3},{8,12},{9,13},{10,... | collective-permute-start | bytes 788 | tf_op jit(solution)/shard_map/ppermute | solution.py:41
  151.1 52.6 %collective-permute-start.8 = (f32[3,64,2,128]{3,2,1,0:T(2,128)}, f32[3,64,2,128]{3,2,1,0:T(2,128)}, u32[]{:S(2)}, u32[]{:S(2)}) collective-permute-start(f32[3,64,2,128]{3,2,1,0:T(2,128)} %get-tuple-element.53), channel_id=1, source_target_pairs={{0,1},{1,2},{2,3},{3,4},{4,5},{5,6},{6,7},{7,8},{8,9},{9,10},{10,1... | collective-permute-start | bytes 589832 | tf_op jit(solution)/shard_map/ppermute | solution.py:25
  152.5 14.6 %collective-permute-start.10 = (f32[3,2,32,128]{3,2,1,0:T(8,128)}, f32[3,2,32,128]{3,2,1,0:T(8,128)}, u32[]{:S(2)}, u32[]{:S(2)}) collective-permute-start(f32[3,2,32,128]{3,2,1,0:T(8,128)} %get-tuple-element.55), channel_id=1, source_target_pairs={{16,0},{32,16},{48,32},{64,48},{80,64},{96,80},{112,96},{0,112},{1... | collective-permute-start | bytes 294920 | tf_op jit(solution)/shard_map/ppermute | solution.py:24
  152.5 14.6 %collective-permute-start.9 = (f32[3,2,32,128]{3,2,1,0:T(8,128)}, f32[3,2,32,128]{3,2,1,0:T(8,128)}, u32[]{:S(2)}, u32[]{:S(2)}) collective-permute-start(f32[3,2,32,128]{3,2,1,0:T(8,128)} %get-tuple-element.54), channel_id=1, source_target_pairs={{0,16},{16,32},{32,48},{48,64},{64,80},{80,96},{96,112},{112,0},{1... | collective-permute-start | bytes 294920 | tf_op jit(solution)/shard_map/ppermute | solution.py:23
  153.6 8.8 %collective-permute-start.25 = (f32[65]{0:T(128)S(1)}, f32[65]{0:T(128)}, u32[]{:S(2)}, u32[]{:S(2)}) collective-permute-start(f32[65]{0:T(128)S(1)} %add.92), channel_id=1, source_target_pairs={{0,8},{1,9},{2,10},{3,11},{4,12},{5,13},{6,14},{7,15},{8,0},{9,1},... | collective-permute-start | bytes 788 | tf_op jit(solution)/shard_map/ppermute | solution.py:41
  158.3 46.4 %collective-permute-start.11 = (f32[3,64,2,128]{3,2,1,0:T(2,128)}, f32[3,64,2,128]{3,2,1,0:T(2,128)}, u32[]{:S(2)}, u32[]{:S(2)}) collective-permute-start(f32[3,64,2,128]{3,2,1,0:T(2,128)} %get-tuple-element.52), channel_id=1, source_target_pairs={{1,0},{2,1},{3,2},{4,3},{5,4},{6,5},{7,6},{8,7},{9,8},{10,9},{11,1... | collective-permute-start | bytes 589832 | tf_op jit(solution)/shard_map/ppermute | solution.py:26
  162.5 4.3 %collective-permute-start.17 = (f32[64,64]{1,0:T(8,128)S(1)}, f32[64,64]{1,0:T(8,128)S(1)}, u32[]{:S(2)}, u32[]{:S(2)}) collective-permute-start(f32[64,64]{1,0:T(8,128)S(1)} %add.83), channel_id=1, source_target_pairs={{0,4},{1,5},{2,6},{3,7},{4,0},{5,1},{6,2},{7,3},{8,12},{9,13},{10,... | collective-permute-start | bytes 49160 | tf_op jit(solution)/shard_map/ppermute | solution.py:41
  166.8 5.4 %collective-permute-start.18 = (f32[64,64]{1,0:T(8,128)S(1)}, f32[64,64]{1,0:T(8,128)S(1)}, u32[]{:S(2)}, u32[]{:S(2)}) collective-permute-start(f32[64,64]{1,0:T(8,128)S(1)} %add.84), channel_id=1, source_target_pairs={{0,8},{1,9},{2,10},{3,11},{4,12},{5,13},{6,14},{7,15},{8,0},{9,1},... | collective-permute-start | bytes 49160 | tf_op jit(solution)/shard_map/ppermute | solution.py:41
  191.5 2.2 copy-start.1
  202.0 5.4 %copy-start.7 = (f32[3,68,32,128]{3,2,1,0:T(8,128)S(1)}, f32[3,68,32,128]{3,2,1,0:T(8,128)}, u32[]{:S(2)}) copy-start(f32[3,68,32,128]{3,2,1,0:T(8,128)} %pad_maximum_fusion.2) | copy-start | bytes 10027012
  220.5 24.3 %copy-start.3 = (f32[1,64,32,128]{3,2,1,0:T(8,128)S(1)}, f32[1,64,32,128]{3,2,1,0:T(8,128)}, u32[]{:S(2)}) copy-start(f32[1,64,32,128]{3,2,1,0:T(8,128)} %copy-done.2) | copy-start | bytes 3145732

commit v7 on v5

--- a/solution.py
+++ b/solution.py
@@ -152,7 +152,7 @@
         out_ref[0, i] = center + time_step * (scale * spread - slope)
         return carry
 
-    lax.fori_loop(0, out_ref.shape[1], row, 0)
+    lax.fori_loop(0, out_ref.shape[1], row, 0, unroll=4)
 
 
 def stencil_step(conc_pad, coeff_pad, scale):

time: 197 us -> 171 us (0.87)
  Pallas kernels: 76.3 us -> 50.1 us
    pallas_call x4, Pallas kernels: 67.2 us -> 41 us  [stencil_step(): pl.pallas_call(stencil_body, out_shape=jax.ShapeDtypeStruct((count, nx, n...]
  transfers between devices with their start and end apart: 26 -> 26, of which waited for: 6 -> 6; matrix products, arithmetic and copies ran while one was open for 19% -> 22% of each run, Pallas kernels for 22% -> 17%
where the time goes in v7:
time: 171 us; the launch traced here: 170 us
  Pallas kernels  50.1 us (29%)
  starting transfers between devices  40.4 us (24%)
  other arithmetic  36.4 us (21%)
  local copies, waits for them, and re-layouts  20.3 us (12%)
  waiting for transfers between devices  17.1 us (10%)
  matrix products  3.54 us (2%)
  between operations  2.4 us (1%)
    pallas_call x4, Pallas kernels, stencil_step(): pl.pallas_call(stencil_body, out_shape=jax.ShapeDtypeStruct((count, nx, n...  41 us
    ppermute x14, starting transfers between devices, butterfly_sum(): value = value + lax.ppermute(value, axis, pairs)  14.2 us
    ppermute x3, starting transfers between devices, halo(): high_y = lax.ppermute(block[:, :, :width], 'gy', by)  14.1 us
    ppermute x14, waiting for transfers between devices, butterfly_sum(): value = value + lax.ppermute(value, axis, pairs)  10.3 us
    unnamed x26, local copies, waits for them, and re-layouts  9.14 us
    concatenate x3, other arithmetic, halo(): jnp.concatenate([jnp.pad(low_y, edge), rows, jnp.pad(high_y, edge)], axis=2)  8.92 us
    ppermute x3, starting transfers between devices, halo(): high_x = lax.ppermute(block[:, :width], 'gx', bx)  8.53 us
    pallas_call x1, Pallas kernels, basis_rows(): pl.pallas_call(basis_body, out_shape=jax.ShapeDtypeStruct((rows, span, co...  7.52 us
  transfers between devices with their start and end apart: 26, of which 6 were waited for; matrix products, arithmetic and copies ran while one was open for 22% of the time, Pallas kernels for 17%

profile of v7, /device:TPU:0, one launch (start us, length us, event | category | flops | bytes accessed | tf_op | source)
XLA Modules:
  0.0 170.4 jit_solution(9605518574129560785)
XLA Ops:
  0.7 1.3 pad_maximum_fusion.5
  2.0 2.9 %collective-permute-start.2 = (f32[8,2,32,128]{3,2,1,0:T(8,128)S(1)}, f32[8,2,32,128]{3,2,1,0:T(8,128)S(1)}, u32[]{:S(2)}, u32[]{:S(2)}) collective-permute-start(f32[8,2,32,128]{3,2,1,0:T(8,128)S(1)} %get-tuple-element.49), channel_id=1, source_target_pairs={{16,0},{32,16},{48,32},{64,48},{80,64},{96,80},{112,96},{0,112},{1... | collective-permute-start | bytes 786440 | tf_op jit(solution)/shard_map/ppermute | solution.py:23
  4.9 0.5 pad_maximum_fusion.3
  5.4 2.1 %collective-permute-start = (f32[8,64,2,128]{3,2,1,0:T(2,128)S(1)}, f32[8,64,2,128]{3,2,1,0:T(2,128)S(1)}, u32[]{:S(2)}, u32[]{:S(2)}) collective-permute-start(f32[8,64,2,128]{3,2,1,0:T(2,128)S(1)} %get-tuple-element.50), channel_id=1, source_target_pairs={{0,1},{1,2},{2,3},{3,4},{4,5},{5,6},{6,7},{7,8},{8,9},{9,10},{10,1... | collective-permute-start | bytes 1572872 | tf_op jit(solution)/shard_map/ppermute | solution.py:24
  7.5 4.4 %collective-permute-start.3 = (f32[8,64,2,128]{3,2,1,0:T(2,128)S(1)}, f32[8,64,2,128]{3,2,1,0:T(2,128)S(1)}, u32[]{:S(2)}, u32[]{:S(2)}) collective-permute-start(f32[8,64,2,128]{3,2,1,0:T(2,128)S(1)} %get-tuple-element.51), channel_id=1, source_target_pairs={{1,0},{2,1},{3,2},{4,3},{5,4},{6,5},{7,6},{8,7},{9,8},{10,9},{11,1... | collective-permute-start | bytes 1572872 | tf_op jit(solution)/shard_map/ppermute | solution.py:25
  11.9 1.7 %copy_dynamic-update-slice_fusion = bf16[64,32,1024]{2,0,1:T(8,128)(2,1)S(1)} fusion(bf16[48,32,1024]{2,1,0:T(8,128)(2,1)S(1)} %copy-done.9), kind=kLoop, calls=%fused_computation.13 | loop fusion | bytes 6291456
  13.7 0.6 copy_dynamic-update-slice_fusion.1
  14.3 1.2 convolution_bitcast_fusion.1
  15.5 0.8 copy-done
  16.3 6.8 %collective-permute-done = f32[8,64,2,128]{3,2,1,0:T(2,128)S(1)} collective-permute-done((f32[8,64,2,128]{3,2,1,0:T(2,128)S(1)}, f32[8,64,2,128]{3,2,1,0:T(2,128)S(1)}, u32[]{:S(2)}, u32[]{:S(2)}) %collective-permute-start) | collective-permute-done | bytes 524320 | tf_op jit(solution)/shard_map/ppermute | solution.py:24
  23.1 4.9 %select_maximum_fusion = f32[8,68,36,128]{3,2,1,0:T(8,128)S(1)} fusion(f32[8,64,2,128]{3,2,1,0:T(2,128)S(1)} %collective-permute-done.3, f32[8,64,2,128]{3,2,1,0:T(2,128)S(1)} %collective-permute-done, f32[8,2,32,128]{3,2,1,0:T(8,128)S(1)} %collective-permute-done.2, f32[1,64,32,128]{3,2,1,0:T(8,128)S(1)} %bitcast.62, f32[3,64,32,128]{3,2,1,0:T(8,128)S(1)} %copy-done.7, ...), kind=kLoop, calls=%fused_computation | loop fusion | flops 25067520 | bytes 19988480 | tf_op jit(solution)/shard_map/concatenate | solution.py:28
  28.1 3.1 %slice.153.coeff_ref = f32[4,68,36,128]{3,2,1,0:T(8,128)} slice(f32[8,68,36,128]{3,2,1,0:T(8,128)S(1)} %select_maximum_fusion), slice={[4:8], [0:68], [0:36], [0:128]} | slice | bytes 10027008 | tf_op jit(solution)/shard_map/slice | solution.py:230
  31.2 2.7 %copy-done.5 = f32[8,68,36,128]{3,2,1,0:T(8,128)} copy-done((f32[8,68,36,128]{3,2,1,0:T(8,128)}, f32[8,68,36,128]{3,2,1,0:T(8,128)S(1)}, u32[]{:S(2)}) %copy-start.5) | copy-done | bytes 10027032
  33.9 6.6 %shard_map.94 = f32[1,64,32,128]{3,2,1,0:T(8,128)S(1)} custom-call(f32[1]{0:T(128)S(1)} %bitcast.58, f32[1,68,36,128]{3,2,1,0:T(8,128)S(1)} %slice.152.conc_ref, f32[4,68,36,128]{3,2,1,0:T(8,128)} %slice.153.coeff_ref), custom_call_target="tpu_custom_call" | custom-call | flops 20971520 | bytes 7315456 | tf_op jit(solution)/shard_map/pallas_call | solution.py:161
  40.6 0.5 collective-permute-start.5
  41.1 2.6 %collective-permute-start.6 = (f32[1,2,32,128]{3,2,1,0:T(8,128)S(1)}, f32[1,2,32,128]{3,2,1,0:T(8,128)S(1)}, u32[]{:S(2)}, u32[]{:S(2)}) collective-permute-start(f32[1,2,32,128]{3,2,1,0:T(8,128)S(1)} %get-tuple-element.57), channel_id=1, source_target_pairs={{16,0},{32,16},{48,32},{64,48},{80,64},{96,80},{112,96},{0,112},{1... | collective-permute-start | bytes 98312 | tf_op jit(solution)/shard_map/ppermute | solution.py:23
  43.8 5.3 %collective-permute-start.7 = (f32[1,64,2,128]{3,2,1,0:T(2,128)S(1)}, f32[1,64,2,128]{3,2,1,0:T(2,128)S(1)}, u32[]{:S(2)}, u32[]{:S(2)}) collective-permute-start(f32[1,64,2,128]{3,2,1,0:T(2,128)S(1)} %get-tuple-element.59), channel_id=1, source_target_pairs={{1,0},{2,1},{3,2},{4,3},{5,4},{6,5},{7,6},{8,7},{9,8},{10,9},{11,1... | collective-permute-start | bytes 196616 | tf_op jit(solution)/shard_map/ppermute | solution.py:25
  49.2 0.3 collective-permute-start.13
  49.4 3.7 %collective-permute-done.13 = f32[64,64]{1,0:T(8,128)S(1)} collective-permute-done((f32[64,64]{1,0:T(8,128)S(1)}, f32[64,64]{1,0:T(8,128)S(1)}, u32[]{:S(2)}, u32[]{:S(2)}) %collective-permute-start.13) | collective-permute-done | bytes 16416 | tf_op jit(solution)/shard_map/ppermute | solution.py:37
  53.2 1.8 %collective-permute-start.14 = (f32[64,64]{1,0:T(8,128)S(1)}, f32[64,64]{1,0:T(8,128)S(1)}, u32[]{:S(2)}, u32[]{:S(2)}) collective-permute-start(f32[64,64]{1,0:T(8,128)S(1)} %add.80), channel_id=1, source_target_pairs={{0,64},{16,80},{32,96},{48,112},{64,0},{80,16},{96,32},{112,48},{1... | collective-permute-start | bytes 49160 | tf_op jit(solution)/shard_map/ppermute | solution.py:37
  55.0 0.2 select_maximum_fusion.4.conc_ref
  55.2 6.3 %shard_map.95 = f32[1,64,32,128]{3,2,1,0:T(8,128)S(1)} custom-call(f32[1]{0:T(128)S(1)} %bitcast.59, f32[1,68,36,128]{3,2,1,0:T(8,128)S(1)} %select_maximum_fusion.4.conc_ref, f32[4,68,36,128]{3,2,1,0:T(8,128)} %slice.153.coeff_ref), custom_call_target="tpu_custom_call" | custom-call | flops 20971520 | bytes 7315456 | tf_op jit(solution)/shard_map/pallas_call | solution.py:161
  61.5 1.0 copy-done.2
  62.5 0.4 fusion.2
  62.9 0.9 multiply_reduce_fusion
  64.0 3.3 %fusion = f32[64]{0:T(128)S(1)} fusion(bf16[64,32,1024]{2,0,1:T(8,128)(2,1)} %copy-done, f32[32,1024]{1,0:T(8,128)S(1)} %mul.85), kind=kLoop, calls=%fused_computation.6 | loop fusion | flops 6291392 | bytes 4325632 | tf_op jit(solution)/shard_map/reduce_sum | solution.py:254
  67.3 0.7 pad_maximum_fusion.7
  68.2 1.0 collective-permute-done.19
  69.2 0.7 fusion.32
  69.9 0.7 collective-permute-start.20
  70.7 4.5 %slice.154.conc_ref = f32[3,68,36,128]{3,2,1,0:T(8,128)} slice(f32[8,68,36,128]{3,2,1,0:T(8,128)} %copy-done.5), slice={[1:4], [0:68], [0:36], [0:128]} | slice | bytes 7520256 | tf_op jit(solution)/shard_map/slice | solution.py:260
  75.1 1.8 %collective-permute-start.21 = (f32[65]{0:T(128)S(1)}, f32[65]{0:T(128)S(1)}, u32[]{:S(2)}, u32[]{:S(2)}) collective-permute-start(f32[65]{0:T(128)S(1)} %add.88), channel_id=1, source_target_pairs={{0,64},{16,80},{32,96},{48,112},{64,0},{80,16},{96,32},{112,48},{1... | collective-permute-start | bytes 788 | tf_op jit(solution)/shard_map/ppermute | solution.py:37
  77.0 14.1 %shard_map.96 = f32[3,64,32,128]{3,2,1,0:T(8,128)S(1)} custom-call(f32[3]{0:T(128)S(1)} %slice.143.scale_ref, f32[3,68,36,128]{3,2,1,0:T(8,128)} %slice.154.conc_ref, f32[4,68,36,128]{3,2,1,0:T(8,128)} %slice.153.coeff_ref), custom_call_target="tpu_custom_call" | custom-call | flops 62914560 | bytes 11919360 | tf_op jit(solution)/shard_map/pallas_call | solution.py:161
  91.2 1.1 collective-permute-start.22
  92.3 0.9 fusion.25
  93.2 1.7 collective-permute-done.22
  94.9 3.4 %collective-permute-start.23 = (f32[65]{0:T(128)S(1)}, f32[65]{0:T(128)S(1)}, u32[]{:S(2)}, u32[]{:S(2)}) collective-permute-start(f32[65]{0:T(128)S(1)} %add.90), channel_id=1, source_target_pairs={{0,2},{1,3},{2,0},{3,1},{4,6},{5,7},{6,4},{7,5},{8,10},{9,11},{10,... | collective-permute-start | bytes 788 | tf_op jit(solution)/shard_map/ppermute | solution.py:37
  98.3 0.6 add.83
  98.9 0.7 fusion.24
  99.6 0.3 collective-permute-done.23
  99.9 1.8 %collective-permute-start.24 = (f32[65]{0:T(128)S(1)}, f32[65]{0:T(128)S(1)}, u32[]{:S(2)}, u32[]{:S(2)}) collective-permute-start(f32[65]{0:T(128)S(1)} %add.91), channel_id=1, source_target_pairs={{0,4},{1,5},{2,6},{3,7},{4,0},{5,1},{6,2},{7,3},{8,12},{9,13},{10,... | collective-permute-start | bytes 788 | tf_op jit(solution)/shard_map/ppermute | solution.py:37
  101.7 3.0 %collective-permute-start.10 = (f32[3,2,32,128]{3,2,1,0:T(8,128)}, f32[3,2,32,128]{3,2,1,0:T(8,128)}, u32[]{:S(2)}, u32[]{:S(2)}) collective-permute-start(f32[3,2,32,128]{3,2,1,0:T(8,128)} %get-tuple-element.53), channel_id=1, source_target_pairs={{16,0},{32,16},{48,32},{64,48},{80,64},{96,80},{112,96},{0,112},{1... | collective-permute-start | bytes 294920 | tf_op jit(solution)/shard_map/ppermute | solution.py:23
  104.7 1.0 collective-permute-start.8
  105.6 2.4 %collective-permute-start.25 = (f32[65]{0:T(128)S(1)}, f32[65]{0:T(128)}, u32[]{:S(2)}, u32[]{:S(2)}) collective-permute-start(f32[65]{0:T(128)S(1)} %add.92), channel_id=1, source_target_pairs={{0,8},{1,9},{2,10},{3,11},{4,12},{5,13},{6,14},{7,15},{8,0},{9,1},... | collective-permute-start | bytes 788 | tf_op jit(solution)/shard_map/ppermute | solution.py:37
  108.1 4.4 %collective-permute-start.11 = (f32[3,64,2,128]{3,2,1,0:T(2,128)}, f32[3,64,2,128]{3,2,1,0:T(2,128)}, u32[]{:S(2)}, u32[]{:S(2)}) collective-permute-start(f32[3,64,2,128]{3,2,1,0:T(2,128)} %get-tuple-element.55), channel_id=1, source_target_pairs={{1,0},{2,1},{3,2},{4,3},{5,4},{6,5},{7,6},{8,7},{9,8},{10,9},{11,1... | collective-permute-start | bytes 589832 | tf_op jit(solution)/shard_map/ppermute | solution.py:25
  112.5 0.8 add.84
  113.3 0.7 collective-permute-start.18
  114.0 0.7 add_multiply_fusion
  114.7 0.6 slice.151
  115.3 3.5 %collective-permute-done.18 = f32[64,64]{1,0:T(8,128)S(1)} collective-permute-done((f32[64,64]{1,0:T(8,128)S(1)}, f32[64,64]{1,0:T(8,128)S(1)}, u32[]{:S(2)}, u32[]{:S(2)}) %collective-permute-start.18) | collective-permute-done | bytes 16416 | tf_op jit(solution)/shard_map/ppermute | solution.py:37
  119.0 5.8 %cholesky.17 = f32[64,64]{1,0:T(8,128)S(1)} custom-call(f32[64,64]{1,0:T(8,128)S(1)} %fusion.12), custom_call_target="Cholesky" | custom-call | tf_op jit(solution)/shard_map/jit(cholesky)/cholesky | solution.py:234
  124.8 0.6 compare_reduce_fusion
  125.5 0.7 select_bitcast_fusion
  126.2 4.9 %custom-call.8 = f32[1,64,64]{1,2,0:T(8,128)S(1)} custom-call(f32[1,64,64]{2,1,0:T(8,128)S(1)} %get-tuple-element.46), custom_call_target="InvertDiagBlocksLowerTriangular" | custom-call | tf_op jit(solution)/shard_map/triangular_solve | solution.py:236
  131.0 0.8 multiply_reduce_fusion.2
  133.4 3.5 %fusion.1 = f32[32,1024]{1,0:T(8,128)S(1)} fusion(bf16[64,32,1024]{2,0,1:T(8,128)(2,1)} %copy-done, f32[64]{0:T(128)S(1)} %get-tuple-element.65), kind=kLoop, calls=%fused_computation.7 | loop fusion | flops 6258688 | bytes 4325632 | tf_op jit(solution)/shard_map/reduce_sum | solution.py:274
  136.9 0.7 fusion.5.last_ref
  138.0 0.7 copy.15
  138.7 2.2 %copy-done.1 = bf16[64,32,1024]{2,0,1:T(8,128)(2,1)S(1)} copy-done((bf16[64,32,1024]{2,0,1:T(8,128)(2,1)S(1)}, bf16[64,32,1024]{2,0,1:T(8,128)(2,1)}, u32[]{:S(2)}) %copy-start.1) | copy-done | bytes 4194328
  140.9 7.5 %shard_map.98._ = f32[65,32,1024]{2,1,0:T(8,128)} custom-call(bf16[3,65,64]{2,1,0:T(8,128)(2,1)S(1)} %pad_maximum_fusion.6.mix_ref, bf16[32,64,1024]{2,1,0:T(8,128)(2,1)S(1)} %bitcast.57), custom_call_target="tpu_custom_call" | custom-call | flops 817889280 | bytes 12713984 | tf_op jit(solution)/shard_map/pallas_call | solution.py:199
  148.4 1.6 shard_map.99
  150.0 3.8 %select_maximum_fusion.2.conc_ref = f32[3,68,36,128]{3,2,1,0:T(8,128)} fusion(f32[3,64,2,128]{3,2,1,0:T(2,128)} %collective-permute-done.11, f32[3,64,2,128]{3,2,1,0:T(2,128)} %collective-permute-done.8, f32[3,2,32,128]{3,2,1,0:T(8,128)} %collective-permute-done.10, f32[3,64,32,128]{3,2,1,0:T(8,128)S(1)} %shard_map.96, ...), kind=kLoop, calls=%fused_computation.9 | loop fusion | flops 7520256 | bytes 7495680 | tf_op jit(solution)/shard_map/concatenate | solution.py:28
  153.8 14.1 %shard_map.97 = f32[3,64,32,128]{3,2,1,0:T(8,128)S(1)} custom-call(f32[3]{0:T(128)S(1)} %slice.143.scale_ref, f32[3,68,36,128]{3,2,1,0:T(8,128)} %select_maximum_fusion.2.conc_ref, f32[4,68,36,128]{3,2,1,0:T(8,128)} %slice.153.coeff_ref), custom_call_target="tpu_custom_call" | custom-call | flops 62914560 | bytes 11919360 | tf_op jit(solution)/shard_map/pallas_call | solution.py:161
  168.0 2.5 %pad_maximum_fusion = f32[4,64,32,128]{3,2,1,0:T(8,128)} fusion(f32[3,64,32,128]{3,2,1,0:T(8,128)S(1)} %shard_map.97, f32[1,64,32,128]{3,2,1,0:T(8,128)S(1)} %copy-done.3), kind=kLoop, calls=%fused_computation.8 | loop fusion | flops 1048576 | bytes 8388608 | tf_op jit(solution)/shard_map/concatenate | solution.py:262
  (76 shorter events, 1.7 us)
Async XLA Ops:
  0.6 4.3 %copy-start.6 = (f32[4,64,32,128]{3,2,1,0:T(8,128)S(1)}, f32[4,64,32,128]{3,2,1,0:T(8,128)}, u32[]{:S(2)}) copy-start(f32[4,64,32,128]{3,2,1,0:T(8,128)} %param.13) | copy-start | bytes 12582916
  0.6 4.3 %copy-start.7 = (f32[3,64,32,128]{3,2,1,0:T(8,128)S(1)}, f32[3,64,32,128]{3,2,1,0:T(8,128)}, u32[]{:S(2)}) copy-start(f32[3,64,32,128]{3,2,1,0:T(8,128)} %param.14) | copy-start | bytes 9437188
  0.7 4.3 %copy-start.8 = (f32[64,32,128]{2,1,0:T(8,128)S(1)}, f32[64,32,128]{2,1,0:T(8,128)}, u32[]{:S(2)}) copy-start(f32[64,32,128]{2,1,0:T(8,128)} %param.15) | copy-start | bytes 3145732
  2.0 14.3 %collective-permute-start.1 = (f32[8,2,32,128]{3,2,1,0:T(8,128)S(1)}, f32[8,2,32,128]{3,2,1,0:T(8,128)S(1)}, u32[]{:S(2)}, u32[]{:S(2)}) collective-permute-start(f32[8,2,32,128]{3,2,1,0:T(8,128)S(1)} %get-tuple-element.48), channel_id=1, source_target_pairs={{0,16},{16,32},{32,48},{48,64},{64,80},{80,96},{96,112},{112,0},{1... | collective-permute-start | bytes 786440 | tf_op jit(solution)/shard_map/ppermute | solution.py:22
  2.0 9.9 %copy-start.9 = (bf16[48,32,1024]{2,1,0:T(8,128)(2,1)S(1)}, bf16[48,32,1024]{2,1,0:T(8,128)(2,1)}, u32[]{:S(2)}) copy-start(bf16[48,32,1024]{2,1,0:T(8,128)(2,1)} %param.17) | copy-start | bytes 9437188
  2.0 14.3 %collective-permute-start.2 = (f32[8,2,32,128]{3,2,1,0:T(8,128)S(1)}, f32[8,2,32,128]{3,2,1,0:T(8,128)S(1)}, u32[]{:S(2)}, u32[]{:S(2)}) collective-permute-start(f32[8,2,32,128]{3,2,1,0:T(8,128)S(1)} %get-tuple-element.49), channel_id=1, source_target_pairs={{16,0},{32,16},{48,32},{64,48},{80,64},{96,80},{112,96},{0,112},{1... | collective-permute-start | bytes 786440 | tf_op jit(solution)/shard_map/ppermute | solution.py:23
  5.4 8.3 %copy-start.10 = (bf16[16,32,1024]{2,1,0:T(8,128)(2,1)S(1)}, bf16[16,32,1024]{2,1,0:T(8,128)(2,1)}, u32[]{:S(2)}) copy-start(bf16[16,32,1024]{2,1,0:T(8,128)(2,1)} %param.19) | copy-start | bytes 3145732
  5.4 17.7 %collective-permute-start = (f32[8,64,2,128]{3,2,1,0:T(2,128)S(1)}, f32[8,64,2,128]{3,2,1,0:T(2,128)S(1)}, u32[]{:S(2)}, u32[]{:S(2)}) collective-permute-start(f32[8,64,2,128]{3,2,1,0:T(2,128)S(1)} %get-tuple-element.50), channel_id=1, source_target_pairs={{0,1},{1,2},{2,3},{3,4},{4,5},{5,6},{6,7},{7,8},{8,9},{9,10},{10,1... | collective-permute-start | bytes 1572872 | tf_op jit(solution)/shard_map/ppermute | solution.py:24
  7.5 15.6 %collective-permute-start.3 = (f32[8,64,2,128]{3,2,1,0:T(2,128)S(1)}, f32[8,64,2,128]{3,2,1,0:T(2,128)S(1)}, u32[]{:S(2)}, u32[]{:S(2)}) collective-permute-start(f32[8,64,2,128]{3,2,1,0:T(2,128)S(1)} %get-tuple-element.51), channel_id=1, source_target_pairs={{1,0},{2,1},{3,2},{4,3},{5,4},{6,5},{7,6},{8,7},{9,8},{10,9},{11,1... | collective-permute-start | bytes 1572872 | tf_op jit(solution)/shard_map/ppermute | solution.py:25
  14.3 2.0 %copy-start = (bf16[64,32,1024]{2,0,1:T(8,128)(2,1)}, bf16[64,32,1024]{2,0,1:T(8,128)(2,1)S(1)}, u32[]{:S(2)}) copy-start(bf16[64,32,1024]{2,0,1:T(8,128)(2,1)S(1)} %copy_dynamic-update-slice_fusion.1) | copy-start | bytes 12582916
  28.0 5.9 %copy-start.5 = (f32[8,68,36,128]{3,2,1,0:T(8,128)}, f32[8,68,36,128]{3,2,1,0:T(8,128)S(1)}, u32[]{:S(2)}) copy-start(f32[8,68,36,128]{3,2,1,0:T(8,128)S(1)} %select_maximum_fusion) | copy-start | bytes 30081028
  28.1 5.8 %copy-start.4 = (f32[4]{0:T(128)S(1)}, f32[4]{0:T(128)}, u32[]{:S(2)}) copy-start(f32[4]{0:T(128)} %param.16) | copy-start | bytes 52
  40.5 8.7 %collective-permute-start.12 = (f32[64,64]{1,0:T(8,128)S(1)}, f32[64,64]{1,0:T(8,128)S(1)}, u32[]{:S(2)}, u32[]{:S(2)}) collective-permute-start(f32[64,64]{1,0:T(8,128)S(1)} %convolution_bitcast_fusion.1), channel_id=1, source_target_pairs={{0,16},{16,0},{32,48},{48,32},{64,80},{80,64},{96,112},{112,96},{1... | collective-permute-start | bytes 49160 | tf_op jit(solution)/shard_map/ppermute | solution.py:37
  40.6 14.3 %collective-permute-start.5 = (f32[1,2,32,128]{3,2,1,0:T(8,128)S(1)}, f32[1,2,32,128]{3,2,1,0:T(8,128)S(1)}, u32[]{:S(2)}, u32[]{:S(2)}) collective-permute-start(f32[1,2,32,128]{3,2,1,0:T(8,128)S(1)} %get-tuple-element.56), channel_id=1, source_target_pairs={{0,16},{16,32},{32,48},{48,64},{64,80},{80,96},{96,112},{112,0},{1... | collective-permute-start | bytes 98312 | tf_op jit(solution)/shard_map/ppermute | solution.py:22
  41.1 13.8 %collective-permute-start.6 = (f32[1,2,32,128]{3,2,1,0:T(8,128)S(1)}, f32[1,2,32,128]{3,2,1,0:T(8,128)S(1)}, u32[]{:S(2)}, u32[]{:S(2)}) collective-permute-start(f32[1,2,32,128]{3,2,1,0:T(8,128)S(1)} %get-tuple-element.57), channel_id=1, source_target_pairs={{16,0},{32,16},{48,32},{64,48},{80,64},{96,80},{112,96},{0,112},{1... | collective-permute-start | bytes 98312 | tf_op jit(solution)/shard_map/ppermute | solution.py:23
  43.8 11.2 %collective-permute-start.4 = (f32[1,64,2,128]{3,2,1,0:T(2,128)S(1)}, f32[1,64,2,128]{3,2,1,0:T(2,128)S(1)}, u32[]{:S(2)}, u32[]{:S(2)}) collective-permute-start(f32[1,64,2,128]{3,2,1,0:T(2,128)S(1)} %get-tuple-element.58), channel_id=1, source_target_pairs={{0,1},{1,2},{2,3},{3,4},{4,5},{5,6},{6,7},{7,8},{8,9},{9,10},{10,1... | collective-permute-start | bytes 196616 | tf_op jit(solution)/shard_map/ppermute | solution.py:24
  43.8 11.2 %collective-permute-start.7 = (f32[1,64,2,128]{3,2,1,0:T(2,128)S(1)}, f32[1,64,2,128]{3,2,1,0:T(2,128)S(1)}, u32[]{:S(2)}, u32[]{:S(2)}) collective-permute-start(f32[1,64,2,128]{3,2,1,0:T(2,128)S(1)} %get-tuple-element.59), channel_id=1, source_target_pairs={{1,0},{2,1},{3,2},{4,3},{5,4},{6,5},{7,6},{8,7},{9,8},{10,9},{11,1... | collective-permute-start | bytes 196616 | tf_op jit(solution)/shard_map/ppermute | solution.py:25
  49.2 4.0 %collective-permute-start.13 = (f32[64,64]{1,0:T(8,128)S(1)}, f32[64,64]{1,0:T(8,128)S(1)}, u32[]{:S(2)}, u32[]{:S(2)}) collective-permute-start(f32[64,64]{1,0:T(8,128)S(1)} %add.79), channel_id=1, source_target_pairs={{0,32},{16,48},{32,0},{48,16},{64,96},{80,112},{96,64},{112,80},{1... | collective-permute-start | bytes 49160 | tf_op jit(solution)/shard_map/ppermute | solution.py:37
  53.2 14.9 %collective-permute-start.14 = (f32[64,64]{1,0:T(8,128)S(1)}, f32[64,64]{1,0:T(8,128)S(1)}, u32[]{:S(2)}, u32[]{:S(2)}) collective-permute-start(f32[64,64]{1,0:T(8,128)S(1)} %add.80), channel_id=1, source_target_pairs={{0,64},{16,80},{32,96},{48,112},{64,0},{80,16},{96,32},{112,48},{1... | collective-permute-start | bytes 49160 | tf_op jit(solution)/shard_map/ppermute | solution.py:37
  61.5 1.0 copy-start.2
  62.5 8.2 %copy-start.11 = (f32[48]{0:T(128)S(1)}, f32[48]{0:T(128)}, u32[]{:S(2)}) copy-start(f32[48]{0:T(128)} %param.18) | copy-start | bytes 580
  68.0 1.2 collective-permute-start.19
  68.1 23.0 %collective-permute-start.15 = (f32[64,64]{1,0:T(8,128)S(1)}, f32[64,64]{1,0:T(8,128)S(1)}, u32[]{:S(2)}, u32[]{:S(2)}) collective-permute-start(f32[64,64]{1,0:T(8,128)S(1)} %add.81), channel_id=1, source_target_pairs={{0,1},{1,0},{2,3},{3,2},{4,5},{5,4},{6,7},{7,6},{8,9},{9,8},{10,11... | collective-permute-start | bytes 49160 | tf_op jit(solution)/shard_map/ppermute | solution.py:37
  69.9 5.2 %collective-permute-start.20 = (f32[65]{0:T(128)S(1)}, f32[65]{0:T(128)S(1)}, u32[]{:S(2)}, u32[]{:S(2)}) collective-permute-start(f32[65]{0:T(128)S(1)} %fusion.32), channel_id=1, source_target_pairs={{0,32},{16,48},{32,0},{48,16},{64,96},{80,112},{96,64},{112,80},{1... | collective-permute-start | bytes 788 | tf_op jit(solution)/shard_map/ppermute | solution.py:37
  75.1 16.0 %collective-permute-start.21 = (f32[65]{0:T(128)S(1)}, f32[65]{0:T(128)S(1)}, u32[]{:S(2)}, u32[]{:S(2)}) collective-permute-start(f32[65]{0:T(128)S(1)} %add.88), channel_id=1, source_target_pairs={{0,64},{16,80},{32,96},{48,112},{64,0},{80,16},{96,32},{112,48},{1... | collective-permute-start | bytes 788 | tf_op jit(solution)/shard_map/ppermute | solution.py:37
  91.1 7.2 %collective-permute-start.16 = (f32[64,64]{1,0:T(8,128)S(1)}, f32[64,64]{1,0:T(8,128)S(1)}, u32[]{:S(2)}, u32[]{:S(2)}) collective-permute-start(f32[64,64]{1,0:T(8,128)S(1)} %add.82), channel_id=1, source_target_pairs={{0,2},{1,3},{2,0},{3,1},{4,6},{5,7},{6,4},{7,5},{8,10},{9,11},{10,... | collective-permute-start | bytes 49160 | tf_op jit(solution)/shard_map/ppermute | solution.py:37
  91.2 3.6 %collective-permute-start.22 = (f32[65]{0:T(128)S(1)}, f32[65]{0:T(128)S(1)}, u32[]{:S(2)}, u32[]{:S(2)}) collective-permute-start(f32[65]{0:T(128)S(1)} %add.89), channel_id=1, source_target_pairs={{0,1},{1,0},{2,3},{3,2},{4,5},{5,4},{6,7},{7,6},{8,9},{9,8},{10,11... | collective-permute-start | bytes 788 | tf_op jit(solution)/shard_map/ppermute | solution.py:37
  94.9 5.1 %collective-permute-start.23 = (f32[65]{0:T(128)S(1)}, f32[65]{0:T(128)S(1)}, u32[]{:S(2)}, u32[]{:S(2)}) collective-permute-start(f32[65]{0:T(128)S(1)} %add.90), channel_id=1, source_target_pairs={{0,2},{1,3},{2,0},{3,1},{4,6},{5,7},{6,4},{7,5},{8,10},{9,11},{10,... | collective-permute-start | bytes 788 | tf_op jit(solution)/shard_map/ppermute | solution.py:37
  98.9 9.2 %collective-permute-start.17 = (f32[64,64]{1,0:T(8,128)}, f32[64,64]{1,0:T(8,128)}, u32[]{:S(2)}, u32[]{:S(2)}) collective-permute-start(f32[64,64]{1,0:T(8,128)} %add.83), channel_id=1, source_target_pairs={{0,4},{1,5},{2,6},{3,7},{4,0},{5,1},{6,2},{7,3},{8,12},{9,13},{10,... | collective-permute-start | bytes 49160 | tf_op jit(solution)/shard_map/ppermute | solution.py:37
  99.9 5.7 %collective-permute-start.24 = (f32[65]{0:T(128)S(1)}, f32[65]{0:T(128)S(1)}, u32[]{:S(2)}, u32[]{:S(2)}) collective-permute-start(f32[65]{0:T(128)S(1)} %add.91), channel_id=1, source_target_pairs={{0,4},{1,5},{2,6},{3,7},{4,0},{5,1},{6,2},{7,3},{8,12},{9,13},{10,... | collective-permute-start | bytes 788 | tf_op jit(solution)/shard_map/ppermute | solution.py:37
  101.7 48.3 %collective-permute-start.9 = (f32[3,2,32,128]{3,2,1,0:T(8,128)}, f32[3,2,32,128]{3,2,1,0:T(8,128)}, u32[]{:S(2)}, u32[]{:S(2)}) collective-permute-start(f32[3,2,32,128]{3,2,1,0:T(8,128)} %get-tuple-element.52), channel_id=1, source_target_pairs={{0,16},{16,32},{32,48},{48,64},{64,80},{80,96},{96,112},{112,0},{1... | collective-permute-start | bytes 294920 | tf_op jit(solution)/shard_map/ppermute | solution.py:22
  101.7 48.3 %collective-permute-start.10 = (f32[3,2,32,128]{3,2,1,0:T(8,128)}, f32[3,2,32,128]{3,2,1,0:T(8,128)}, u32[]{:S(2)}, u32[]{:S(2)}) collective-permute-start(f32[3,2,32,128]{3,2,1,0:T(8,128)} %get-tuple-element.53), channel_id=1, source_target_pairs={{16,0},{32,16},{48,32},{64,48},{80,64},{96,80},{112,96},{0,112},{1... | collective-permute-start | bytes 294920 | tf_op jit(solution)/shard_map/ppermute | solution.py:23
  104.7 45.4 %collective-permute-start.8 = (f32[3,64,2,128]{3,2,1,0:T(2,128)}, f32[3,64,2,128]{3,2,1,0:T(2,128)}, u32[]{:S(2)}, u32[]{:S(2)}) collective-permute-start(f32[3,64,2,128]{3,2,1,0:T(2,128)} %get-tuple-element.54), channel_id=1, source_target_pairs={{0,1},{1,2},{2,3},{3,4},{4,5},{5,6},{6,7},{7,8},{8,9},{9,10},{10,1... | collective-permute-start | bytes 589832 | tf_op jit(solution)/shard_map/ppermute | solution.py:24
  105.6 7.6 %collective-permute-start.25 = (f32[65]{0:T(128)S(1)}, f32[65]{0:T(128)}, u32[]{:S(2)}, u32[]{:S(2)}) collective-permute-start(f32[65]{0:T(128)S(1)} %add.92), channel_id=1, source_target_pairs={{0,8},{1,9},{2,10},{3,11},{4,12},{5,13},{6,14},{7,15},{8,0},{9,1},... | collective-permute-start | bytes 788 | tf_op jit(solution)/shard_map/ppermute | solution.py:37
  108.1 41.9 %collective-permute-start.11 = (f32[3,64,2,128]{3,2,1,0:T(2,128)}, f32[3,64,2,128]{3,2,1,0:T(2,128)}, u32[]{:S(2)}, u32[]{:S(2)}) collective-permute-start(f32[3,64,2,128]{3,2,1,0:T(2,128)} %get-tuple-element.55), channel_id=1, source_target_pairs={{1,0},{2,1},{3,2},{4,3},{5,4},{6,5},{7,6},{8,7},{9,8},{10,9},{11,1... | collective-permute-start | bytes 589832 | tf_op jit(solution)/shard_map/ppermute | solution.py:25
  113.3 5.5 %collective-permute-start.18 = (f32[64,64]{1,0:T(8,128)S(1)}, f32[64,64]{1,0:T(8,128)S(1)}, u32[]{:S(2)}, u32[]{:S(2)}) collective-permute-start(f32[64,64]{1,0:T(8,128)S(1)} %add.84), channel_id=1, source_target_pairs={{0,8},{1,9},{2,10},{3,11},{4,12},{5,13},{6,14},{7,15},{8,0},{9,1},... | collective-permute-start | bytes 49160 | tf_op jit(solution)/shard_map/ppermute | solution.py:37
  138.7 2.2 %copy-start.1 = (bf16[64,32,1024]{2,0,1:T(8,128)(2,1)S(1)}, bf16[64,32,1024]{2,0,1:T(8,128)(2,1)}, u32[]{:S(2)}) copy-start(bf16[64,32,1024]{2,0,1:T(8,128)(2,1)} %copy-done) | copy-start | bytes 12582916
  153.8 14.2 %copy-start.3 = (f32[1,64,32,128]{3,2,1,0:T(8,128)S(1)}, f32[1,64,32,128]{3,2,1,0:T(8,128)}, u32[]{:S(2)}) copy-start(f32[1,64,32,128]{3,2,1,0:T(8,128)} %copy-done.2) | copy-start | bytes 3145732

commit v8 on v7

--- a/solution.py
+++ b/solution.py
@@ -152,7 +152,7 @@
         out_ref[0, i] = center + time_step * (scale * spread - slope)
         return carry
 
-    lax.fori_loop(0, out_ref.shape[1], row, 0, unroll=4)
+    lax.fori_loop(0, out_ref.shape[1], row, 0, unroll=8)
 
 
 def stencil_step(conc_pad, coeff_pad, scale):

time: 171 us -> 167 us (0.977)
  Pallas kernels: 50.1 us -> 46 us
    pallas_call x4, Pallas kernels: 41 us -> 36.9 us  [stencil_step(): pl.pallas_call(stencil_body, out_shape=jax.ShapeDtypeStruct((count, nx, n...]
  transfers between devices with their start and end apart: 26 -> 26, of which waited for: 6 -> 6; matrix products, arithmetic and copies ran while one was open for 22% -> 23% of each run, Pallas kernels for 17% -> 16%
where the time goes in v8:
time: 167 us; the launch traced here: 166 us
  Pallas kernels  46 us (28%)
  starting transfers between devices  40.6 us (24%)
  other arithmetic  36.4 us (22%)
  local copies, waits for them, and re-layouts  20.3 us (12%)
  waiting for transfers between devices  17.1 us (10%)
  matrix products  3.54 us (2%)
  between operations  2.4 us (1%)
    pallas_call x4, Pallas kernels, stencil_step(): pl.pallas_call(stencil_body, out_shape=jax.ShapeDtypeStruct((count, nx, n...  36.9 us
    ppermute x14, starting transfers between devices, butterfly_sum(): value = value + lax.ppermute(value, axis, pairs)  14.4 us
    ppermute x3, starting transfers between devices, halo(): high_y = lax.ppermute(block[:, :, :width], 'gy', by)  14.1 us
    ppermute x14, waiting for transfers between devices, butterfly_sum(): value = value + lax.ppermute(value, axis, pairs)  10.3 us
    unnamed x26, local copies, waits for them, and re-layouts  9.14 us
    concatenate x3, other arithmetic, halo(): jnp.concatenate([jnp.pad(low_y, edge), rows, jnp.pad(high_y, edge)], axis=2)  8.92 us
    ppermute x3, starting transfers between devices, halo(): high_x = lax.ppermute(block[:, :width], 'gx', bx)  8.53 us
    pallas_call x1, Pallas kernels, basis_rows(): pl.pallas_call(basis_body, out_shape=jax.ShapeDtypeStruct((rows, span, co...  7.53 us
  transfers between devices with their start and end apart: 26, of which 6 were waited for; matrix products, arithmetic and copies ran while one was open for 23% of the time, Pallas kernels for 16%

profile of v8, /device:TPU:0, one launch (start us, length us, event | category | flops | bytes accessed | tf_op | source)
XLA Modules:
  0.0 166.5 jit_solution(7811758064083170743)
XLA Ops:
  0.7 1.3 pad_maximum_fusion.5
  2.0 2.9 %collective-permute-start.2 = (f32[8,2,32,128]{3,2,1,0:T(8,128)S(1)}, f32[8,2,32,128]{3,2,1,0:T(8,128)S(1)}, u32[]{:S(2)}, u32[]{:S(2)}) collective-permute-start(f32[8,2,32,128]{3,2,1,0:T(8,128)S(1)} %get-tuple-element.49), channel_id=1, source_target_pairs={{16,0},{32,16},{48,32},{64,48},{80,64},{96,80},{112,96},{0,112},{1... | collective-permute-start | bytes 786440 | tf_op jit(solution)/shard_map/ppermute | solution.py:23
  4.9 0.5 pad_maximum_fusion.3
  5.4 2.1 %collective-permute-start = (f32[8,64,2,128]{3,2,1,0:T(2,128)S(1)}, f32[8,64,2,128]{3,2,1,0:T(2,128)S(1)}, u32[]{:S(2)}, u32[]{:S(2)}) collective-permute-start(f32[8,64,2,128]{3,2,1,0:T(2,128)S(1)} %get-tuple-element.50), channel_id=1, source_target_pairs={{0,1},{1,2},{2,3},{3,4},{4,5},{5,6},{6,7},{7,8},{8,9},{9,10},{10,1... | collective-permute-start | bytes 1572872 | tf_op jit(solution)/shard_map/ppermute | solution.py:24
  7.5 4.4 %collective-permute-start.3 = (f32[8,64,2,128]{3,2,1,0:T(2,128)S(1)}, f32[8,64,2,128]{3,2,1,0:T(2,128)S(1)}, u32[]{:S(2)}, u32[]{:S(2)}) collective-permute-start(f32[8,64,2,128]{3,2,1,0:T(2,128)S(1)} %get-tuple-element.51), channel_id=1, source_target_pairs={{1,0},{2,1},{3,2},{4,3},{5,4},{6,5},{7,6},{8,7},{9,8},{10,9},{11,1... | collective-permute-start | bytes 1572872 | tf_op jit(solution)/shard_map/ppermute | solution.py:25
  11.9 1.7 %copy_dynamic-update-slice_fusion = bf16[64,32,1024]{2,0,1:T(8,128)(2,1)S(1)} fusion(bf16[48,32,1024]{2,1,0:T(8,128)(2,1)S(1)} %copy-done.9), kind=kLoop, calls=%fused_computation.13 | loop fusion | bytes 6291456
  13.7 0.6 copy_dynamic-update-slice_fusion.1
  14.3 1.2 convolution_bitcast_fusion.1
  15.5 0.8 copy-done
  16.3 6.8 %collective-permute-done = f32[8,64,2,128]{3,2,1,0:T(2,128)S(1)} collective-permute-done((f32[8,64,2,128]{3,2,1,0:T(2,128)S(1)}, f32[8,64,2,128]{3,2,1,0:T(2,128)S(1)}, u32[]{:S(2)}, u32[]{:S(2)}) %collective-permute-start) | collective-permute-done | bytes 524320 | tf_op jit(solution)/shard_map/ppermute | solution.py:24
  23.1 4.9 %select_maximum_fusion = f32[8,68,36,128]{3,2,1,0:T(8,128)S(1)} fusion(f32[8,64,2,128]{3,2,1,0:T(2,128)S(1)} %collective-permute-done.3, f32[8,64,2,128]{3,2,1,0:T(2,128)S(1)} %collective-permute-done, f32[8,2,32,128]{3,2,1,0:T(8,128)S(1)} %collective-permute-done.2, f32[1,64,32,128]{3,2,1,0:T(8,128)S(1)} %bitcast.62, f32[3,64,32,128]{3,2,1,0:T(8,128)S(1)} %copy-done.7, ...), kind=kLoop, calls=%fused_computation | loop fusion | flops 25067520 | bytes 19988480 | tf_op jit(solution)/shard_map/concatenate | solution.py:28
  28.1 3.1 %slice.153.coeff_ref = f32[4,68,36,128]{3,2,1,0:T(8,128)} slice(f32[8,68,36,128]{3,2,1,0:T(8,128)S(1)} %select_maximum_fusion), slice={[4:8], [0:68], [0:36], [0:128]} | slice | bytes 10027008 | tf_op jit(solution)/shard_map/slice | solution.py:230
  31.2 2.7 %copy-done.5 = f32[8,68,36,128]{3,2,1,0:T(8,128)} copy-done((f32[8,68,36,128]{3,2,1,0:T(8,128)}, f32[8,68,36,128]{3,2,1,0:T(8,128)S(1)}, u32[]{:S(2)}) %copy-start.5) | copy-done | bytes 10027032
  33.9 6.1 %shard_map.94 = f32[1,64,32,128]{3,2,1,0:T(8,128)S(1)} custom-call(f32[1]{0:T(128)S(1)} %bitcast.58, f32[1,68,36,128]{3,2,1,0:T(8,128)S(1)} %slice.152.conc_ref, f32[4,68,36,128]{3,2,1,0:T(8,128)} %slice.153.coeff_ref), custom_call_target="tpu_custom_call" | custom-call | flops 20971520 | bytes 7315456 | tf_op jit(solution)/shard_map/pallas_call | solution.py:161
  40.2 0.5 collective-permute-start.5
  40.7 2.6 %collective-permute-start.6 = (f32[1,2,32,128]{3,2,1,0:T(8,128)S(1)}, f32[1,2,32,128]{3,2,1,0:T(8,128)S(1)}, u32[]{:S(2)}, u32[]{:S(2)}) collective-permute-start(f32[1,2,32,128]{3,2,1,0:T(8,128)S(1)} %get-tuple-element.57), channel_id=1, source_target_pairs={{16,0},{32,16},{48,32},{64,48},{80,64},{96,80},{112,96},{0,112},{1... | collective-permute-start | bytes 98312 | tf_op jit(solution)/shard_map/ppermute | solution.py:23
  43.3 5.3 %collective-permute-start.7 = (f32[1,64,2,128]{3,2,1,0:T(2,128)S(1)}, f32[1,64,2,128]{3,2,1,0:T(2,128)S(1)}, u32[]{:S(2)}, u32[]{:S(2)}) collective-permute-start(f32[1,64,2,128]{3,2,1,0:T(2,128)S(1)} %get-tuple-element.59), channel_id=1, source_target_pairs={{1,0},{2,1},{3,2},{4,3},{5,4},{6,5},{7,6},{8,7},{9,8},{10,9},{11,1... | collective-permute-start | bytes 196616 | tf_op jit(solution)/shard_map/ppermute | solution.py:25
  48.7 0.3 collective-permute-start.13
  48.9 3.7 %collective-permute-done.13 = f32[64,64]{1,0:T(8,128)S(1)} collective-permute-done((f32[64,64]{1,0:T(8,128)S(1)}, f32[64,64]{1,0:T(8,128)S(1)}, u32[]{:S(2)}, u32[]{:S(2)}) %collective-permute-start.13) | collective-permute-done | bytes 16416 | tf_op jit(solution)/shard_map/ppermute | solution.py:37
  52.7 1.8 %collective-permute-start.14 = (f32[64,64]{1,0:T(8,128)S(1)}, f32[64,64]{1,0:T(8,128)S(1)}, u32[]{:S(2)}, u32[]{:S(2)}) collective-permute-start(f32[64,64]{1,0:T(8,128)S(1)} %add.80), channel_id=1, source_target_pairs={{0,64},{16,80},{32,96},{48,112},{64,0},{80,16},{96,32},{112,48},{1... | collective-permute-start | bytes 49160 | tf_op jit(solution)/shard_map/ppermute | solution.py:37
  54.5 0.2 select_maximum_fusion.4.conc_ref
  54.7 5.8 %shard_map.95 = f32[1,64,32,128]{3,2,1,0:T(8,128)S(1)} custom-call(f32[1]{0:T(128)S(1)} %bitcast.59, f32[1,68,36,128]{3,2,1,0:T(8,128)S(1)} %select_maximum_fusion.4.conc_ref, f32[4,68,36,128]{3,2,1,0:T(8,128)} %slice.153.coeff_ref), custom_call_target="tpu_custom_call" | custom-call | flops 20971520 | bytes 7315456 | tf_op jit(solution)/shard_map/pallas_call | solution.py:161
  60.5 1.0 copy-done.2
  61.5 0.4 fusion.2
  61.9 0.9 multiply_reduce_fusion
  62.9 3.3 %fusion = f32[64]{0:T(128)S(1)} fusion(bf16[64,32,1024]{2,0,1:T(8,128)(2,1)} %copy-done, f32[32,1024]{1,0:T(8,128)S(1)} %mul.85), kind=kLoop, calls=%fused_computation.6 | loop fusion | flops 6291392 | bytes 4325632 | tf_op jit(solution)/shard_map/reduce_sum | solution.py:254
  66.3 0.7 pad_maximum_fusion.7
  67.2 1.0 collective-permute-done.19
  68.2 0.7 fusion.32
  68.9 0.9 collective-permute-start.20
  69.9 4.5 %slice.154.conc_ref = f32[3,68,36,128]{3,2,1,0:T(8,128)} slice(f32[8,68,36,128]{3,2,1,0:T(8,128)} %copy-done.5), slice={[1:4], [0:68], [0:36], [0:128]} | slice | bytes 7520256 | tf_op jit(solution)/shard_map/slice | solution.py:260
  74.3 1.8 %collective-permute-start.21 = (f32[65]{0:T(128)S(1)}, f32[65]{0:T(128)S(1)}, u32[]{:S(2)}, u32[]{:S(2)}) collective-permute-start(f32[65]{0:T(128)S(1)} %add.88), channel_id=1, source_target_pairs={{0,64},{16,80},{32,96},{48,112},{64,0},{80,16},{96,32},{112,48},{1... | collective-permute-start | bytes 788 | tf_op jit(solution)/shard_map/ppermute | solution.py:37
  76.2 12.5 %shard_map.96 = f32[3,64,32,128]{3,2,1,0:T(8,128)S(1)} custom-call(f32[3]{0:T(128)S(1)} %slice.143.scale_ref, f32[3,68,36,128]{3,2,1,0:T(8,128)} %slice.154.conc_ref, f32[4,68,36,128]{3,2,1,0:T(8,128)} %slice.153.coeff_ref), custom_call_target="tpu_custom_call" | custom-call | flops 62914560 | bytes 11919360 | tf_op jit(solution)/shard_map/pallas_call | solution.py:161
  88.8 1.1 collective-permute-start.22
  89.9 0.9 fusion.25
  90.8 1.7 %collective-permute-done.22 = f32[65]{0:T(128)S(1)} collective-permute-done((f32[65]{0:T(128)S(1)}, f32[65]{0:T(128)S(1)}, u32[]{:S(2)}, u32[]{:S(2)}) %collective-permute-start.22) | collective-permute-done | bytes 292 | tf_op jit(solution)/shard_map/ppermute | solution.py:37
  92.5 3.4 %collective-permute-start.23 = (f32[65]{0:T(128)S(1)}, f32[65]{0:T(128)S(1)}, u32[]{:S(2)}, u32[]{:S(2)}) collective-permute-start(f32[65]{0:T(128)S(1)} %add.90), channel_id=1, source_target_pairs={{0,2},{1,3},{2,0},{3,1},{4,6},{5,7},{6,4},{7,5},{8,10},{9,11},{10,... | collective-permute-start | bytes 788 | tf_op jit(solution)/shard_map/ppermute | solution.py:37
  95.9 0.6 add.83
  96.5 0.7 fusion.24
  97.2 0.3 collective-permute-done.23
  97.6 1.8 %collective-permute-start.24 = (f32[65]{0:T(128)S(1)}, f32[65]{0:T(128)S(1)}, u32[]{:S(2)}, u32[]{:S(2)}) collective-permute-start(f32[65]{0:T(128)S(1)} %add.91), channel_id=1, source_target_pairs={{0,4},{1,5},{2,6},{3,7},{4,0},{5,1},{6,2},{7,3},{8,12},{9,13},{10,... | collective-permute-start | bytes 788 | tf_op jit(solution)/shard_map/ppermute | solution.py:37
  99.3 3.0 %collective-permute-start.10 = (f32[3,2,32,128]{3,2,1,0:T(8,128)}, f32[3,2,32,128]{3,2,1,0:T(8,128)}, u32[]{:S(2)}, u32[]{:S(2)}) collective-permute-start(f32[3,2,32,128]{3,2,1,0:T(8,128)} %get-tuple-element.53), channel_id=1, source_target_pairs={{16,0},{32,16},{48,32},{64,48},{80,64},{96,80},{112,96},{0,112},{1... | collective-permute-start | bytes 294920 | tf_op jit(solution)/shard_map/ppermute | solution.py:23
  102.3 1.0 collective-permute-start.8
  103.3 2.4 %collective-permute-start.25 = (f32[65]{0:T(128)S(1)}, f32[65]{0:T(128)}, u32[]{:S(2)}, u32[]{:S(2)}) collective-permute-start(f32[65]{0:T(128)S(1)} %add.92), channel_id=1, source_target_pairs={{0,8},{1,9},{2,10},{3,11},{4,12},{5,13},{6,14},{7,15},{8,0},{9,1},... | collective-permute-start | bytes 788 | tf_op jit(solution)/shard_map/ppermute | solution.py:37
  105.7 4.4 %collective-permute-start.11 = (f32[3,64,2,128]{3,2,1,0:T(2,128)}, f32[3,64,2,128]{3,2,1,0:T(2,128)}, u32[]{:S(2)}, u32[]{:S(2)}) collective-permute-start(f32[3,64,2,128]{3,2,1,0:T(2,128)} %get-tuple-element.55), channel_id=1, source_target_pairs={{1,0},{2,1},{3,2},{4,3},{5,4},{6,5},{7,6},{8,7},{9,8},{10,9},{11,1... | collective-permute-start | bytes 589832 | tf_op jit(solution)/shard_map/ppermute | solution.py:25
  110.1 0.8 add.84
  110.9 0.7 collective-permute-start.18
  111.6 0.7 add_multiply_fusion
  112.3 0.6 slice.151
  112.9 3.5 %collective-permute-done.18 = f32[64,64]{1,0:T(8,128)S(1)} collective-permute-done((f32[64,64]{1,0:T(8,128)S(1)}, f32[64,64]{1,0:T(8,128)S(1)}, u32[]{:S(2)}, u32[]{:S(2)}) %collective-permute-start.18) | collective-permute-done | bytes 16416 | tf_op jit(solution)/shard_map/ppermute | solution.py:37
  116.6 5.8 %cholesky.17 = f32[64,64]{1,0:T(8,128)S(1)} custom-call(f32[64,64]{1,0:T(8,128)S(1)} %fusion.12), custom_call_target="Cholesky" | custom-call | tf_op jit(solution)/shard_map/jit(cholesky)/cholesky | solution.py:234
  122.5 0.6 compare_reduce_fusion
  123.1 0.7 select_bitcast_fusion
  123.8 4.9 %custom-call.8 = f32[1,64,64]{1,2,0:T(8,128)S(1)} custom-call(f32[1,64,64]{2,1,0:T(8,128)S(1)} %get-tuple-element.46), custom_call_target="InvertDiagBlocksLowerTriangular" | custom-call | tf_op jit(solution)/shard_map/triangular_solve | solution.py:236
  128.7 0.8 multiply_reduce_fusion.2
  131.0 3.5 %fusion.1 = f32[32,1024]{1,0:T(8,128)S(1)} fusion(bf16[64,32,1024]{2,0,1:T(8,128)(2,1)} %copy-done, f32[64]{0:T(128)S(1)} %get-tuple-element.65), kind=kLoop, calls=%fused_computation.7 | loop fusion | flops 6258688 | bytes 4325632 | tf_op jit(solution)/shard_map/reduce_sum | solution.py:274
  134.6 0.7 fusion.5.last_ref
  135.6 0.7 copy.15
  136.3 2.2 %copy-done.1 = bf16[64,32,1024]{2,0,1:T(8,128)(2,1)S(1)} copy-done((bf16[64,32,1024]{2,0,1:T(8,128)(2,1)S(1)}, bf16[64,32,1024]{2,0,1:T(8,128)(2,1)}, u32[]{:S(2)}) %copy-start.1) | copy-done | bytes 4194328
  138.5 7.5 %shard_map.98._ = f32[65,32,1024]{2,1,0:T(8,128)} custom-call(bf16[3,65,64]{2,1,0:T(8,128)(2,1)S(1)} %pad_maximum_fusion.6.mix_ref, bf16[32,64,1024]{2,1,0:T(8,128)(2,1)S(1)} %bitcast.57), custom_call_target="tpu_custom_call" | custom-call | flops 817889280 | bytes 12713984 | tf_op jit(solution)/shard_map/pallas_call | solution.py:199
  146.1 1.6 shard_map.99
  147.6 3.8 %select_maximum_fusion.2.conc_ref = f32[3,68,36,128]{3,2,1,0:T(8,128)} fusion(f32[3,64,2,128]{3,2,1,0:T(2,128)} %collective-permute-done.11, f32[3,64,2,128]{3,2,1,0:T(2,128)} %collective-permute-done.8, f32[3,2,32,128]{3,2,1,0:T(8,128)} %collective-permute-done.10, f32[3,64,32,128]{3,2,1,0:T(8,128)S(1)} %shard_map.96, ...), kind=kLoop, calls=%fused_computation.9 | loop fusion | flops 7520256 | bytes 7495680 | tf_op jit(solution)/shard_map/concatenate | solution.py:28
  151.4 12.6 %shard_map.97 = f32[3,64,32,128]{3,2,1,0:T(8,128)S(1)} custom-call(f32[3]{0:T(128)S(1)} %slice.143.scale_ref, f32[3,68,36,128]{3,2,1,0:T(8,128)} %select_maximum_fusion.2.conc_ref, f32[4,68,36,128]{3,2,1,0:T(8,128)} %slice.153.coeff_ref), custom_call_target="tpu_custom_call" | custom-call | flops 62914560 | bytes 11919360 | tf_op jit(solution)/shard_map/pallas_call | solution.py:161
  164.0 2.5 %pad_maximum_fusion = f32[4,64,32,128]{3,2,1,0:T(8,128)} fusion(f32[3,64,32,128]{3,2,1,0:T(8,128)S(1)} %shard_map.97, f32[1,64,32,128]{3,2,1,0:T(8,128)S(1)} %copy-done.3), kind=kLoop, calls=%fused_computation.8 | loop fusion | flops 1048576 | bytes 8388608 | tf_op jit(solution)/shard_map/concatenate | solution.py:262
  (76 shorter events, 1.7 us)
Async XLA Ops:
  0.6 4.3 %copy-start.6 = (f32[4,64,32,128]{3,2,1,0:T(8,128)S(1)}, f32[4,64,32,128]{3,2,1,0:T(8,128)}, u32[]{:S(2)}) copy-start(f32[4,64,32,128]{3,2,1,0:T(8,128)} %param.13) | copy-start | bytes 12582916
  0.6 4.3 %copy-start.7 = (f32[3,64,32,128]{3,2,1,0:T(8,128)S(1)}, f32[3,64,32,128]{3,2,1,0:T(8,128)}, u32[]{:S(2)}) copy-start(f32[3,64,32,128]{3,2,1,0:T(8,128)} %param.14) | copy-start | bytes 9437188
  0.7 4.3 %copy-start.8 = (f32[64,32,128]{2,1,0:T(8,128)S(1)}, f32[64,32,128]{2,1,0:T(8,128)}, u32[]{:S(2)}) copy-start(f32[64,32,128]{2,1,0:T(8,128)} %param.15) | copy-start | bytes 3145732
  2.0 14.3 %collective-permute-start.1 = (f32[8,2,32,128]{3,2,1,0:T(8,128)S(1)}, f32[8,2,32,128]{3,2,1,0:T(8,128)S(1)}, u32[]{:S(2)}, u32[]{:S(2)}) collective-permute-start(f32[8,2,32,128]{3,2,1,0:T(8,128)S(1)} %get-tuple-element.48), channel_id=1, source_target_pairs={{0,16},{16,32},{32,48},{48,64},{64,80},{80,96},{96,112},{112,0},{1... | collective-permute-start | bytes 786440 | tf_op jit(solution)/shard_map/ppermute | solution.py:22
  2.0 9.9 %copy-start.9 = (bf16[48,32,1024]{2,1,0:T(8,128)(2,1)S(1)}, bf16[48,32,1024]{2,1,0:T(8,128)(2,1)}, u32[]{:S(2)}) copy-start(bf16[48,32,1024]{2,1,0:T(8,128)(2,1)} %param.17) | copy-start | bytes 9437188
  2.0 14.3 %collective-permute-start.2 = (f32[8,2,32,128]{3,2,1,0:T(8,128)S(1)}, f32[8,2,32,128]{3,2,1,0:T(8,128)S(1)}, u32[]{:S(2)}, u32[]{:S(2)}) collective-permute-start(f32[8,2,32,128]{3,2,1,0:T(8,128)S(1)} %get-tuple-element.49), channel_id=1, source_target_pairs={{16,0},{32,16},{48,32},{64,48},{80,64},{96,80},{112,96},{0,112},{1... | collective-permute-start | bytes 786440 | tf_op jit(solution)/shard_map/ppermute | solution.py:23
  5.4 8.3 %copy-start.10 = (bf16[16,32,1024]{2,1,0:T(8,128)(2,1)S(1)}, bf16[16,32,1024]{2,1,0:T(8,128)(2,1)}, u32[]{:S(2)}) copy-start(bf16[16,32,1024]{2,1,0:T(8,128)(2,1)} %param.19) | copy-start | bytes 3145732
  5.4 17.7 %collective-permute-start = (f32[8,64,2,128]{3,2,1,0:T(2,128)S(1)}, f32[8,64,2,128]{3,2,1,0:T(2,128)S(1)}, u32[]{:S(2)}, u32[]{:S(2)}) collective-permute-start(f32[8,64,2,128]{3,2,1,0:T(2,128)S(1)} %get-tuple-element.50), channel_id=1, source_target_pairs={{0,1},{1,2},{2,3},{3,4},{4,5},{5,6},{6,7},{7,8},{8,9},{9,10},{10,1... | collective-permute-start | bytes 1572872 | tf_op jit(solution)/shard_map/ppermute | solution.py:24
  7.5 15.6 %collective-permute-start.3 = (f32[8,64,2,128]{3,2,1,0:T(2,128)S(1)}, f32[8,64,2,128]{3,2,1,0:T(2,128)S(1)}, u32[]{:S(2)}, u32[]{:S(2)}) collective-permute-start(f32[8,64,2,128]{3,2,1,0:T(2,128)S(1)} %get-tuple-element.51), channel_id=1, source_target_pairs={{1,0},{2,1},{3,2},{4,3},{5,4},{6,5},{7,6},{8,7},{9,8},{10,9},{11,1... | collective-permute-start | bytes 1572872 | tf_op jit(solution)/shard_map/ppermute | solution.py:25
  14.3 2.0 %copy-start = (bf16[64,32,1024]{2,0,1:T(8,128)(2,1)}, bf16[64,32,1024]{2,0,1:T(8,128)(2,1)S(1)}, u32[]{:S(2)}) copy-start(bf16[64,32,1024]{2,0,1:T(8,128)(2,1)S(1)} %copy_dynamic-update-slice_fusion.1) | copy-start | bytes 12582916
  28.0 5.9 %copy-start.5 = (f32[8,68,36,128]{3,2,1,0:T(8,128)}, f32[8,68,36,128]{3,2,1,0:T(8,128)S(1)}, u32[]{:S(2)}) copy-start(f32[8,68,36,128]{3,2,1,0:T(8,128)S(1)} %select_maximum_fusion) | copy-start | bytes 30081028
  28.1 5.8 %copy-start.4 = (f32[4]{0:T(128)S(1)}, f32[4]{0:T(128)}, u32[]{:S(2)}) copy-start(f32[4]{0:T(128)} %param.16) | copy-start | bytes 52
  40.0 8.7 %collective-permute-start.12 = (f32[64,64]{1,0:T(8,128)S(1)}, f32[64,64]{1,0:T(8,128)S(1)}, u32[]{:S(2)}, u32[]{:S(2)}) collective-permute-start(f32[64,64]{1,0:T(8,128)S(1)} %convolution_bitcast_fusion.1), channel_id=1, source_target_pairs={{0,16},{16,0},{32,48},{48,32},{64,80},{80,64},{96,112},{112,96},{1... | collective-permute-start | bytes 49160 | tf_op jit(solution)/shard_map/ppermute | solution.py:37
  40.2 14.3 %collective-permute-start.5 = (f32[1,2,32,128]{3,2,1,0:T(8,128)S(1)}, f32[1,2,32,128]{3,2,1,0:T(8,128)S(1)}, u32[]{:S(2)}, u32[]{:S(2)}) collective-permute-start(f32[1,2,32,128]{3,2,1,0:T(8,128)S(1)} %get-tuple-element.56), channel_id=1, source_target_pairs={{0,16},{16,32},{32,48},{48,64},{64,80},{80,96},{96,112},{112,0},{1... | collective-permute-start | bytes 98312 | tf_op jit(solution)/shard_map/ppermute | solution.py:22
  40.7 13.8 %collective-permute-start.6 = (f32[1,2,32,128]{3,2,1,0:T(8,128)S(1)}, f32[1,2,32,128]{3,2,1,0:T(8,128)S(1)}, u32[]{:S(2)}, u32[]{:S(2)}) collective-permute-start(f32[1,2,32,128]{3,2,1,0:T(8,128)S(1)} %get-tuple-element.57), channel_id=1, source_target_pairs={{16,0},{32,16},{48,32},{64,48},{80,64},{96,80},{112,96},{0,112},{1... | collective-permute-start | bytes 98312 | tf_op jit(solution)/shard_map/ppermute | solution.py:23
  43.3 11.2 %collective-permute-start.4 = (f32[1,64,2,128]{3,2,1,0:T(2,128)S(1)}, f32[1,64,2,128]{3,2,1,0:T(2,128)S(1)}, u32[]{:S(2)}, u32[]{:S(2)}) collective-permute-start(f32[1,64,2,128]{3,2,1,0:T(2,128)S(1)} %get-tuple-element.58), channel_id=1, source_target_pairs={{0,1},{1,2},{2,3},{3,4},{4,5},{5,6},{6,7},{7,8},{8,9},{9,10},{10,1... | collective-permute-start | bytes 196616 | tf_op jit(solution)/shard_map/ppermute | solution.py:24
  43.3 11.2 %collective-permute-start.7 = (f32[1,64,2,128]{3,2,1,0:T(2,128)S(1)}, f32[1,64,2,128]{3,2,1,0:T(2,128)S(1)}, u32[]{:S(2)}, u32[]{:S(2)}) collective-permute-start(f32[1,64,2,128]{3,2,1,0:T(2,128)S(1)} %get-tuple-element.59), channel_id=1, source_target_pairs={{1,0},{2,1},{3,2},{4,3},{5,4},{6,5},{7,6},{8,7},{9,8},{10,9},{11,1... | collective-permute-start | bytes 196616 | tf_op jit(solution)/shard_map/ppermute | solution.py:25
  48.7 4.0 %collective-permute-start.13 = (f32[64,64]{1,0:T(8,128)S(1)}, f32[64,64]{1,0:T(8,128)S(1)}, u32[]{:S(2)}, u32[]{:S(2)}) collective-permute-start(f32[64,64]{1,0:T(8,128)S(1)} %add.79), channel_id=1, source_target_pairs={{0,32},{16,48},{32,0},{48,16},{64,96},{80,112},{96,64},{112,80},{1... | collective-permute-start | bytes 49160 | tf_op jit(solution)/shard_map/ppermute | solution.py:37
  52.7 14.4 %collective-permute-start.14 = (f32[64,64]{1,0:T(8,128)S(1)}, f32[64,64]{1,0:T(8,128)S(1)}, u32[]{:S(2)}, u32[]{:S(2)}) collective-permute-start(f32[64,64]{1,0:T(8,128)S(1)} %add.80), channel_id=1, source_target_pairs={{0,64},{16,80},{32,96},{48,112},{64,0},{80,16},{96,32},{112,48},{1... | collective-permute-start | bytes 49160 | tf_op jit(solution)/shard_map/ppermute | solution.py:37
  60.5 1.0 copy-start.2
  61.5 8.4 %copy-start.11 = (f32[48]{0:T(128)S(1)}, f32[48]{0:T(128)}, u32[]{:S(2)}) copy-start(f32[48]{0:T(128)} %param.18) | copy-start | bytes 580
  67.0 1.2 collective-permute-start.19
  67.1 21.6 %collective-permute-start.15 = (f32[64,64]{1,0:T(8,128)S(1)}, f32[64,64]{1,0:T(8,128)S(1)}, u32[]{:S(2)}, u32[]{:S(2)}) collective-permute-start(f32[64,64]{1,0:T(8,128)S(1)} %add.81), channel_id=1, source_target_pairs={{0,1},{1,0},{2,3},{3,2},{4,5},{5,4},{6,7},{7,6},{8,9},{9,8},{10,11... | collective-permute-start | bytes 49160 | tf_op jit(solution)/shard_map/ppermute | solution.py:37
  68.9 5.4 %collective-permute-start.20 = (f32[65]{0:T(128)S(1)}, f32[65]{0:T(128)S(1)}, u32[]{:S(2)}, u32[]{:S(2)}) collective-permute-start(f32[65]{0:T(128)S(1)} %fusion.32), channel_id=1, source_target_pairs={{0,32},{16,48},{32,0},{48,16},{64,96},{80,112},{96,64},{112,80},{1... | collective-permute-start | bytes 788 | tf_op jit(solution)/shard_map/ppermute | solution.py:37
  74.3 14.5 %collective-permute-start.21 = (f32[65]{0:T(128)S(1)}, f32[65]{0:T(128)S(1)}, u32[]{:S(2)}, u32[]{:S(2)}) collective-permute-start(f32[65]{0:T(128)S(1)} %add.88), channel_id=1, source_target_pairs={{0,64},{16,80},{32,96},{48,112},{64,0},{80,16},{96,32},{112,48},{1... | collective-permute-start | bytes 788 | tf_op jit(solution)/shard_map/ppermute | solution.py:37
  88.7 7.2 %collective-permute-start.16 = (f32[64,64]{1,0:T(8,128)S(1)}, f32[64,64]{1,0:T(8,128)S(1)}, u32[]{:S(2)}, u32[]{:S(2)}) collective-permute-start(f32[64,64]{1,0:T(8,128)S(1)} %add.82), channel_id=1, source_target_pairs={{0,2},{1,3},{2,0},{3,1},{4,6},{5,7},{6,4},{7,5},{8,10},{9,11},{10,... | collective-permute-start | bytes 49160 | tf_op jit(solution)/shard_map/ppermute | solution.py:37
  88.8 3.6 %collective-permute-start.22 = (f32[65]{0:T(128)S(1)}, f32[65]{0:T(128)S(1)}, u32[]{:S(2)}, u32[]{:S(2)}) collective-permute-start(f32[65]{0:T(128)S(1)} %add.89), channel_id=1, source_target_pairs={{0,1},{1,0},{2,3},{3,2},{4,5},{5,4},{6,7},{7,6},{8,9},{9,8},{10,11... | collective-permute-start | bytes 788 | tf_op jit(solution)/shard_map/ppermute | solution.py:37
  92.5 5.1 %collective-permute-start.23 = (f32[65]{0:T(128)S(1)}, f32[65]{0:T(128)S(1)}, u32[]{:S(2)}, u32[]{:S(2)}) collective-permute-start(f32[65]{0:T(128)S(1)} %add.90), channel_id=1, source_target_pairs={{0,2},{1,3},{2,0},{3,1},{4,6},{5,7},{6,4},{7,5},{8,10},{9,11},{10,... | collective-permute-start | bytes 788 | tf_op jit(solution)/shard_map/ppermute | solution.py:37
  96.5 9.2 %collective-permute-start.17 = (f32[64,64]{1,0:T(8,128)}, f32[64,64]{1,0:T(8,128)}, u32[]{:S(2)}, u32[]{:S(2)}) collective-permute-start(f32[64,64]{1,0:T(8,128)} %add.83), channel_id=1, source_target_pairs={{0,4},{1,5},{2,6},{3,7},{4,0},{5,1},{6,2},{7,3},{8,12},{9,13},{10,... | collective-permute-start | bytes 49160 | tf_op jit(solution)/shard_map/ppermute | solution.py:37
  97.6 5.7 %collective-permute-start.24 = (f32[65]{0:T(128)S(1)}, f32[65]{0:T(128)S(1)}, u32[]{:S(2)}, u32[]{:S(2)}) collective-permute-start(f32[65]{0:T(128)S(1)} %add.91), channel_id=1, source_target_pairs={{0,4},{1,5},{2,6},{3,7},{4,0},{5,1},{6,2},{7,3},{8,12},{9,13},{10,... | collective-permute-start | bytes 788 | tf_op jit(solution)/shard_map/ppermute | solution.py:37
  99.3 48.3 %collective-permute-start.9 = (f32[3,2,32,128]{3,2,1,0:T(8,128)}, f32[3,2,32,128]{3,2,1,0:T(8,128)}, u32[]{:S(2)}, u32[]{:S(2)}) collective-permute-start(f32[3,2,32,128]{3,2,1,0:T(8,128)} %get-tuple-element.52), channel_id=1, source_target_pairs={{0,16},{16,32},{32,48},{48,64},{64,80},{80,96},{96,112},{112,0},{1... | collective-permute-start | bytes 294920 | tf_op jit(solution)/shard_map/ppermute | solution.py:22
  99.3 48.3 %collective-permute-start.10 = (f32[3,2,32,128]{3,2,1,0:T(8,128)}, f32[3,2,32,128]{3,2,1,0:T(8,128)}, u32[]{:S(2)}, u32[]{:S(2)}) collective-permute-start(f32[3,2,32,128]{3,2,1,0:T(8,128)} %get-tuple-element.53), channel_id=1, source_target_pairs={{16,0},{32,16},{48,32},{64,48},{80,64},{96,80},{112,96},{0,112},{1... | collective-permute-start | bytes 294920 | tf_op jit(solution)/shard_map/ppermute | solution.py:23
  102.3 45.4 %collective-permute-start.8 = (f32[3,64,2,128]{3,2,1,0:T(2,128)}, f32[3,64,2,128]{3,2,1,0:T(2,128)}, u32[]{:S(2)}, u32[]{:S(2)}) collective-permute-start(f32[3,64,2,128]{3,2,1,0:T(2,128)} %get-tuple-element.54), channel_id=1, source_target_pairs={{0,1},{1,2},{2,3},{3,4},{4,5},{5,6},{6,7},{7,8},{8,9},{9,10},{10,1... | collective-permute-start | bytes 589832 | tf_op jit(solution)/shard_map/ppermute | solution.py:24
  103.3 7.6 %collective-permute-start.25 = (f32[65]{0:T(128)S(1)}, f32[65]{0:T(128)}, u32[]{:S(2)}, u32[]{:S(2)}) collective-permute-start(f32[65]{0:T(128)S(1)} %add.92), channel_id=1, source_target_pairs={{0,8},{1,9},{2,10},{3,11},{4,12},{5,13},{6,14},{7,15},{8,0},{9,1},... | collective-permute-start | bytes 788 | tf_op jit(solution)/shard_map/ppermute | solution.py:37
  105.7 41.9 %collective-permute-start.11 = (f32[3,64,2,128]{3,2,1,0:T(2,128)}, f32[3,64,2,128]{3,2,1,0:T(2,128)}, u32[]{:S(2)}, u32[]{:S(2)}) collective-permute-start(f32[3,64,2,128]{3,2,1,0:T(2,128)} %get-tuple-element.55), channel_id=1, source_target_pairs={{1,0},{2,1},{3,2},{4,3},{5,4},{6,5},{7,6},{8,7},{9,8},{10,9},{11,1... | collective-permute-start | bytes 589832 | tf_op jit(solution)/shard_map/ppermute | solution.py:25
  110.9 5.5 %collective-permute-start.18 = (f32[64,64]{1,0:T(8,128)S(1)}, f32[64,64]{1,0:T(8,128)S(1)}, u32[]{:S(2)}, u32[]{:S(2)}) collective-permute-start(f32[64,64]{1,0:T(8,128)S(1)} %add.84), channel_id=1, source_target_pairs={{0,8},{1,9},{2,10},{3,11},{4,12},{5,13},{6,14},{7,15},{8,0},{9,1},... | collective-permute-start | bytes 49160 | tf_op jit(solution)/shard_map/ppermute | solution.py:37
  136.3 2.2 %copy-start.1 = (bf16[64,32,1024]{2,0,1:T(8,128)(2,1)S(1)}, bf16[64,32,1024]{2,0,1:T(8,128)(2,1)}, u32[]{:S(2)}) copy-start(bf16[64,32,1024]{2,0,1:T(8,128)(2,1)} %copy-done) | copy-start | bytes 12582916
  151.4 12.6 %copy-start.3 = (f32[1,64,32,128]{3,2,1,0:T(8,128)S(1)}, f32[1,64,32,128]{3,2,1,0:T(8,128)}, u32[]{:S(2)}) copy-start(f32[1,64,32,128]{3,2,1,0:T(8,128)} %copy-done.2) | copy-start | bytes 3145732

commit v9 on v8

--- a/solution.py
+++ b/solution.py
@@ -152,7 +152,7 @@
         out_ref[0, i] = center + time_step * (scale * spread - slope)
         return carry
 
-    lax.fori_loop(0, out_ref.shape[1], row, 0, unroll=8)
+    lax.fori_loop(0, out_ref.shape[1], row, 0, unroll=16)
 
 
 def stencil_step(conc_pad, coeff_pad, scale):

time: 167 us -> 165 us (0.988)
  Pallas kernels: 46 us -> 44.2 us
    pallas_call x4, Pallas kernels: 36.9 us -> 35.1 us  [stencil_step(): pl.pallas_call(stencil_body, out_shape=jax.ShapeDtypeStruct((count, nx, n...]
where the time goes in v9:
time: 165 us
  Pallas kernels  44.2 us (27%)
  starting transfers between devices  41 us (25%)
  other arithmetic  36.4 us (22%)
  local copies, waits for them, and re-layouts  20.3 us (12%)
  waiting for transfers between devices  16.8 us (10%)
  matrix products  3.54 us (2%)
  between operations  2.4 us (1%)
    pallas_call x4, Pallas kernels, stencil_step(): pl.pallas_call(stencil_body, out_shape=jax.ShapeDtypeStruct((count, nx, n...  35.1 us
    ppermute x14, starting transfers between devices, butterfly_sum(): value = value + lax.ppermute(value, axis, pairs)  14.5 us
    ppermute x3, starting transfers between devices, halo(): high_y = lax.ppermute(block[:, :, :width], 'gy', by)  14.2 us
    ppermute x14, waiting for transfers between devices, butterfly_sum(): value = value + lax.ppermute(value, axis, pairs)  9.95 us
    unnamed x26, local copies, waits for them, and re-layouts  9.14 us
    concatenate x3, other arithmetic, halo(): jnp.concatenate([jnp.pad(low_y, edge), rows, jnp.pad(high_y, edge)], axis=2)  8.92 us
    ppermute x3, starting transfers between devices, halo(): high_x = lax.ppermute(block[:, :width], 'gx', bx)  8.53 us
    pallas_call x1, Pallas kernels, basis_rows(): pl.pallas_call(basis_body, out_shape=jax.ShapeDtypeStruct((rows, span, co...  7.52 us
  transfers between devices with their start and end apart: 26, of which 6 were waited for; matrix products, arithmetic and copies ran while one was open for 23% of the time, Pallas kernels for 16%

profile of v9, /device:TPU:0, one launch (start us, length us, event | category | flops | bytes accessed | tf_op | source)
XLA Modules:
  0.0 164.7 jit_solution(13811600203550664898)
XLA Ops:
  0.7 1.3 pad_maximum_fusion.5
  2.0 2.9 %collective-permute-start.2 = (f32[8,2,32,128]{3,2,1,0:T(8,128)S(1)}, f32[8,2,32,128]{3,2,1,0:T(8,128)S(1)}, u32[]{:S(2)}, u32[]{:S(2)}) collective-permute-start(f32[8,2,32,128]{3,2,1,0:T(8,128)S(1)} %get-tuple-element.49), channel_id=1, source_target_pairs={{16,0},{32,16},{48,32},{64,48},{80,64},{96,80},{112,96},{0,112},{1... | collective-permute-start | bytes 786440 | tf_op jit(solution)/shard_map/ppermute | solution.py:23
  4.9 0.5 pad_maximum_fusion.3
  5.4 2.1 %collective-permute-start = (f32[8,64,2,128]{3,2,1,0:T(2,128)S(1)}, f32[8,64,2,128]{3,2,1,0:T(2,128)S(1)}, u32[]{:S(2)}, u32[]{:S(2)}) collective-permute-start(f32[8,64,2,128]{3,2,1,0:T(2,128)S(1)} %get-tuple-element.50), channel_id=1, source_target_pairs={{0,1},{1,2},{2,3},{3,4},{4,5},{5,6},{6,7},{7,8},{8,9},{9,10},{10,1... | collective-permute-start | bytes 1572872 | tf_op jit(solution)/shard_map/ppermute | solution.py:24
  7.5 4.4 %collective-permute-start.3 = (f32[8,64,2,128]{3,2,1,0:T(2,128)S(1)}, f32[8,64,2,128]{3,2,1,0:T(2,128)S(1)}, u32[]{:S(2)}, u32[]{:S(2)}) collective-permute-start(f32[8,64,2,128]{3,2,1,0:T(2,128)S(1)} %get-tuple-element.51), channel_id=1, source_target_pairs={{1,0},{2,1},{3,2},{4,3},{5,4},{6,5},{7,6},{8,7},{9,8},{10,9},{11,1... | collective-permute-start | bytes 1572872 | tf_op jit(solution)/shard_map/ppermute | solution.py:25
  11.9 1.7 %copy_dynamic-update-slice_fusion = bf16[64,32,1024]{2,0,1:T(8,128)(2,1)S(1)} fusion(bf16[48,32,1024]{2,1,0:T(8,128)(2,1)S(1)} %copy-done.9), kind=kLoop, calls=%fused_computation.13 | loop fusion | bytes 6291456
  13.7 0.6 copy_dynamic-update-slice_fusion.1
  14.3 1.2 convolution_bitcast_fusion.1
  15.5 0.8 copy-done
  16.3 6.8 %collective-permute-done = f32[8,64,2,128]{3,2,1,0:T(2,128)S(1)} collective-permute-done((f32[8,64,2,128]{3,2,1,0:T(2,128)S(1)}, f32[8,64,2,128]{3,2,1,0:T(2,128)S(1)}, u32[]{:S(2)}, u32[]{:S(2)}) %collective-permute-start) | collective-permute-done | bytes 524320 | tf_op jit(solution)/shard_map/ppermute | solution.py:24
  23.1 4.9 %select_maximum_fusion = f32[8,68,36,128]{3,2,1,0:T(8,128)S(1)} fusion(f32[8,64,2,128]{3,2,1,0:T(2,128)S(1)} %collective-permute-done.3, f32[8,64,2,128]{3,2,1,0:T(2,128)S(1)} %collective-permute-done, f32[8,2,32,128]{3,2,1,0:T(8,128)S(1)} %collective-permute-done.2, f32[1,64,32,128]{3,2,1,0:T(8,128)S(1)} %bitcast.62, f32[3,64,32,128]{3,2,1,0:T(8,128)S(1)} %copy-done.7, ...), kind=kLoop, calls=%fused_computation | loop fusion | flops 25067520 | bytes 19988480 | tf_op jit(solution)/shard_map/concatenate | solution.py:28
  28.1 3.1 %slice.153.coeff_ref = f32[4,68,36,128]{3,2,1,0:T(8,128)} slice(f32[8,68,36,128]{3,2,1,0:T(8,128)S(1)} %select_maximum_fusion), slice={[4:8], [0:68], [0:36], [0:128]} | slice | bytes 10027008 | tf_op jit(solution)/shard_map/slice | solution.py:230
  31.2 2.7 %copy-done.5 = f32[8,68,36,128]{3,2,1,0:T(8,128)} copy-done((f32[8,68,36,128]{3,2,1,0:T(8,128)}, f32[8,68,36,128]{3,2,1,0:T(8,128)S(1)}, u32[]{:S(2)}) %copy-start.5) | copy-done | bytes 10027032
  33.9 5.8 %shard_map.94 = f32[1,64,32,128]{3,2,1,0:T(8,128)S(1)} custom-call(f32[1]{0:T(128)S(1)} %bitcast.58, f32[1,68,36,128]{3,2,1,0:T(8,128)S(1)} %slice.152.conc_ref, f32[4,68,36,128]{3,2,1,0:T(8,128)} %slice.153.coeff_ref), custom_call_target="tpu_custom_call" | custom-call | flops 20971520 | bytes 7315456 | tf_op jit(solution)/shard_map/pallas_call | solution.py:161
  39.9 0.5 collective-permute-start.5
  40.4 2.6 %collective-permute-start.6 = (f32[1,2,32,128]{3,2,1,0:T(8,128)S(1)}, f32[1,2,32,128]{3,2,1,0:T(8,128)S(1)}, u32[]{:S(2)}, u32[]{:S(2)}) collective-permute-start(f32[1,2,32,128]{3,2,1,0:T(8,128)S(1)} %get-tuple-element.57), channel_id=1, source_target_pairs={{16,0},{32,16},{48,32},{64,48},{80,64},{96,80},{112,96},{0,112},{1... | collective-permute-start | bytes 98312 | tf_op jit(solution)/shard_map/ppermute | solution.py:23
  43.1 5.3 %collective-permute-start.7 = (f32[1,64,2,128]{3,2,1,0:T(2,128)S(1)}, f32[1,64,2,128]{3,2,1,0:T(2,128)S(1)}, u32[]{:S(2)}, u32[]{:S(2)}) collective-permute-start(f32[1,64,2,128]{3,2,1,0:T(2,128)S(1)} %get-tuple-element.59), channel_id=1, source_target_pairs={{1,0},{2,1},{3,2},{4,3},{5,4},{6,5},{7,6},{8,7},{9,8},{10,9},{11,1... | collective-permute-start | bytes 196616 | tf_op jit(solution)/shard_map/ppermute | solution.py:25
  48.4 0.3 collective-permute-start.13
  48.7 3.7 %collective-permute-done.13 = f32[64,64]{1,0:T(8,128)S(1)} collective-permute-done((f32[64,64]{1,0:T(8,128)S(1)}, f32[64,64]{1,0:T(8,128)S(1)}, u32[]{:S(2)}, u32[]{:S(2)}) %collective-permute-start.13) | collective-permute-done | bytes 16416 | tf_op jit(solution)/shard_map/ppermute | solution.py:37
  52.4 1.8 %collective-permute-start.14 = (f32[64,64]{1,0:T(8,128)S(1)}, f32[64,64]{1,0:T(8,128)S(1)}, u32[]{:S(2)}, u32[]{:S(2)}) collective-permute-start(f32[64,64]{1,0:T(8,128)S(1)} %add.80), channel_id=1, source_target_pairs={{0,64},{16,80},{32,96},{48,112},{64,0},{80,16},{96,32},{112,48},{1... | collective-permute-start | bytes 49160 | tf_op jit(solution)/shard_map/ppermute | solution.py:37
  54.5 5.5 %shard_map.95 = f32[1,64,32,128]{3,2,1,0:T(8,128)S(1)} custom-call(f32[1]{0:T(128)S(1)} %bitcast.59, f32[1,68,36,128]{3,2,1,0:T(8,128)S(1)} %select_maximum_fusion.4.conc_ref, f32[4,68,36,128]{3,2,1,0:T(8,128)} %slice.153.coeff_ref), custom_call_target="tpu_custom_call" | custom-call | flops 20971520 | bytes 7315456 | tf_op jit(solution)/shard_map/pallas_call | solution.py:161
  60.0 1.0 copy-done.2
  61.0 0.4 fusion.2
  61.4 0.9 multiply_reduce_fusion
  62.5 3.3 %fusion = f32[64]{0:T(128)S(1)} fusion(bf16[64,32,1024]{2,0,1:T(8,128)(2,1)} %copy-done, f32[32,1024]{1,0:T(8,128)S(1)} %mul.85), kind=kLoop, calls=%fused_computation.6 | loop fusion | flops 6291392 | bytes 4325632 | tf_op jit(solution)/shard_map/reduce_sum | solution.py:254
  65.8 0.7 pad_maximum_fusion.7
  66.6 0.3 collective-permute-start.15
  66.9 0.8 collective-permute-done.19
  67.7 0.7 fusion.32
  68.5 0.7 collective-permute-start.20
  69.2 4.5 %slice.154.conc_ref = f32[3,68,36,128]{3,2,1,0:T(8,128)} slice(f32[8,68,36,128]{3,2,1,0:T(8,128)} %copy-done.5), slice={[1:4], [0:68], [0:36], [0:128]} | slice | bytes 7520256 | tf_op jit(solution)/shard_map/slice | solution.py:260
  73.7 1.8 %collective-permute-start.21 = (f32[65]{0:T(128)S(1)}, f32[65]{0:T(128)S(1)}, u32[]{:S(2)}, u32[]{:S(2)}) collective-permute-start(f32[65]{0:T(128)S(1)} %add.88), channel_id=1, source_target_pairs={{0,64},{16,80},{32,96},{48,112},{64,0},{80,16},{96,32},{112,48},{1... | collective-permute-start | bytes 788 | tf_op jit(solution)/shard_map/ppermute | solution.py:37
  75.5 11.8 %shard_map.96 = f32[3,64,32,128]{3,2,1,0:T(8,128)S(1)} custom-call(f32[3]{0:T(128)S(1)} %slice.143.scale_ref, f32[3,68,36,128]{3,2,1,0:T(8,128)} %slice.154.conc_ref, f32[4,68,36,128]{3,2,1,0:T(8,128)} %slice.153.coeff_ref), custom_call_target="tpu_custom_call" | custom-call | flops 62914560 | bytes 11919360 | tf_op jit(solution)/shard_map/pallas_call | solution.py:161
  87.5 1.2 collective-permute-start.22
  88.8 0.9 fusion.25
  89.7 1.5 collective-permute-done.22
  91.2 3.5 %collective-permute-start.23 = (f32[65]{0:T(128)S(1)}, f32[65]{0:T(128)S(1)}, u32[]{:S(2)}, u32[]{:S(2)}) collective-permute-start(f32[65]{0:T(128)S(1)} %add.90), channel_id=1, source_target_pairs={{0,2},{1,3},{2,0},{3,1},{4,6},{5,7},{6,4},{7,5},{8,10},{9,11},{10,... | collective-permute-start | bytes 788 | tf_op jit(solution)/shard_map/ppermute | solution.py:37
  94.7 0.6 add.83
  95.3 0.7 fusion.24
  96.0 0.2 collective-permute-done.23
  96.2 1.8 %collective-permute-start.24 = (f32[65]{0:T(128)S(1)}, f32[65]{0:T(128)S(1)}, u32[]{:S(2)}, u32[]{:S(2)}) collective-permute-start(f32[65]{0:T(128)S(1)} %add.91), channel_id=1, source_target_pairs={{0,4},{1,5},{2,6},{3,7},{4,0},{5,1},{6,2},{7,3},{8,12},{9,13},{10,... | collective-permute-start | bytes 788 | tf_op jit(solution)/shard_map/ppermute | solution.py:37
  98.1 3.0 %collective-permute-start.10 = (f32[3,2,32,128]{3,2,1,0:T(8,128)}, f32[3,2,32,128]{3,2,1,0:T(8,128)}, u32[]{:S(2)}, u32[]{:S(2)}) collective-permute-start(f32[3,2,32,128]{3,2,1,0:T(8,128)} %get-tuple-element.53), channel_id=1, source_target_pairs={{16,0},{32,16},{48,32},{64,48},{80,64},{96,80},{112,96},{0,112},{1... | collective-permute-start | bytes 294920 | tf_op jit(solution)/shard_map/ppermute | solution.py:23
  101.0 1.1 collective-permute-start.8
  102.1 2.3 %collective-permute-start.25 = (f32[65]{0:T(128)S(1)}, f32[65]{0:T(128)}, u32[]{:S(2)}, u32[]{:S(2)}) collective-permute-start(f32[65]{0:T(128)S(1)} %add.92), channel_id=1, source_target_pairs={{0,8},{1,9},{2,10},{3,11},{4,12},{5,13},{6,14},{7,15},{8,0},{9,1},... | collective-permute-start | bytes 788 | tf_op jit(solution)/shard_map/ppermute | solution.py:37
  104.5 4.5 %collective-permute-start.11 = (f32[3,64,2,128]{3,2,1,0:T(2,128)}, f32[3,64,2,128]{3,2,1,0:T(2,128)}, u32[]{:S(2)}, u32[]{:S(2)}) collective-permute-start(f32[3,64,2,128]{3,2,1,0:T(2,128)} %get-tuple-element.55), channel_id=1, source_target_pairs={{1,0},{2,1},{3,2},{4,3},{5,4},{6,5},{7,6},{8,7},{9,8},{10,9},{11,1... | collective-permute-start | bytes 589832 | tf_op jit(solution)/shard_map/ppermute | solution.py:25
  109.0 0.8 add.84
  109.8 0.6 collective-permute-start.18
  110.4 0.7 add_multiply_fusion
  111.1 0.6 slice.151
  111.7 3.6 %collective-permute-done.18 = f32[64,64]{1,0:T(8,128)S(1)} collective-permute-done((f32[64,64]{1,0:T(8,128)S(1)}, f32[64,64]{1,0:T(8,128)S(1)}, u32[]{:S(2)}, u32[]{:S(2)}) %collective-permute-start.18) | collective-permute-done | bytes 16416 | tf_op jit(solution)/shard_map/ppermute | solution.py:37
  115.4 5.8 %cholesky.17 = f32[64,64]{1,0:T(8,128)S(1)} custom-call(f32[64,64]{1,0:T(8,128)S(1)} %fusion.12), custom_call_target="Cholesky" | custom-call | tf_op jit(solution)/shard_map/jit(cholesky)/cholesky | solution.py:234
  121.3 0.6 compare_reduce_fusion
  122.0 0.7 select_bitcast_fusion
  122.6 4.9 %custom-call.8 = f32[1,64,64]{1,2,0:T(8,128)S(1)} custom-call(f32[1,64,64]{2,1,0:T(8,128)S(1)} %get-tuple-element.46), custom_call_target="InvertDiagBlocksLowerTriangular" | custom-call | tf_op jit(solution)/shard_map/triangular_solve | solution.py:236
  127.5 0.8 multiply_reduce_fusion.2
  129.9 3.5 %fusion.1 = f32[32,1024]{1,0:T(8,128)S(1)} fusion(bf16[64,32,1024]{2,0,1:T(8,128)(2,1)} %copy-done, f32[64]{0:T(128)S(1)} %get-tuple-element.65), kind=kLoop, calls=%fused_computation.7 | loop fusion | flops 6258688 | bytes 4325632 | tf_op jit(solution)/shard_map/reduce_sum | solution.py:274
  133.4 0.7 fusion.5.last_ref
  134.5 0.7 copy.15
  135.2 2.2 %copy-done.1 = bf16[64,32,1024]{2,0,1:T(8,128)(2,1)S(1)} copy-done((bf16[64,32,1024]{2,0,1:T(8,128)(2,1)S(1)}, bf16[64,32,1024]{2,0,1:T(8,128)(2,1)}, u32[]{:S(2)}) %copy-start.1) | copy-done | bytes 4194328
  137.4 7.5 %shard_map.98._ = f32[65,32,1024]{2,1,0:T(8,128)} custom-call(bf16[3,65,64]{2,1,0:T(8,128)(2,1)S(1)} %pad_maximum_fusion.6.mix_ref, bf16[32,64,1024]{2,1,0:T(8,128)(2,1)S(1)} %bitcast.57), custom_call_target="tpu_custom_call" | custom-call | flops 817889280 | bytes 12713984 | tf_op jit(solution)/shard_map/pallas_call | solution.py:199
  144.9 1.6 shard_map.99
  146.5 3.8 %select_maximum_fusion.2.conc_ref = f32[3,68,36,128]{3,2,1,0:T(8,128)} fusion(f32[3,64,2,128]{3,2,1,0:T(2,128)} %collective-permute-done.11, f32[3,64,2,128]{3,2,1,0:T(2,128)} %collective-permute-done.8, f32[3,2,32,128]{3,2,1,0:T(8,128)} %collective-permute-done.10, f32[3,64,32,128]{3,2,1,0:T(8,128)S(1)} %shard_map.96, ...), kind=kLoop, calls=%fused_computation.9 | loop fusion | flops 7520256 | bytes 7495680 | tf_op jit(solution)/shard_map/concatenate | solution.py:28
  150.3 11.9 %shard_map.97 = f32[3,64,32,128]{3,2,1,0:T(8,128)S(1)} custom-call(f32[3]{0:T(128)S(1)} %slice.143.scale_ref, f32[3,68,36,128]{3,2,1,0:T(8,128)} %select_maximum_fusion.2.conc_ref, f32[4,68,36,128]{3,2,1,0:T(8,128)} %slice.153.coeff_ref), custom_call_target="tpu_custom_call" | custom-call | flops 62914560 | bytes 11919360 | tf_op jit(solution)/shard_map/pallas_call | solution.py:161
  162.2 2.5 %pad_maximum_fusion = f32[4,64,32,128]{3,2,1,0:T(8,128)} fusion(f32[3,64,32,128]{3,2,1,0:T(8,128)S(1)} %shard_map.97, f32[1,64,32,128]{3,2,1,0:T(8,128)S(1)} %copy-done.3), kind=kLoop, calls=%fused_computation.8 | loop fusion | flops 1048576 | bytes 8388608 | tf_op jit(solution)/shard_map/concatenate | solution.py:262
  (76 shorter events, 1.9 us)
Async XLA Ops:
  0.6 4.3 %copy-start.6 = (f32[4,64,32,128]{3,2,1,0:T(8,128)S(1)}, f32[4,64,32,128]{3,2,1,0:T(8,128)}, u32[]{:S(2)}) copy-start(f32[4,64,32,128]{3,2,1,0:T(8,128)} %param.13) | copy-start | bytes 12582916
  0.6 4.3 %copy-start.7 = (f32[3,64,32,128]{3,2,1,0:T(8,128)S(1)}, f32[3,64,32,128]{3,2,1,0:T(8,128)}, u32[]{:S(2)}) copy-start(f32[3,64,32,128]{3,2,1,0:T(8,128)} %param.14) | copy-start | bytes 9437188
  0.7 4.3 %copy-start.8 = (f32[64,32,128]{2,1,0:T(8,128)S(1)}, f32[64,32,128]{2,1,0:T(8,128)}, u32[]{:S(2)}) copy-start(f32[64,32,128]{2,1,0:T(8,128)} %param.15) | copy-start | bytes 3145732
  2.0 14.3 %collective-permute-start.1 = (f32[8,2,32,128]{3,2,1,0:T(8,128)S(1)}, f32[8,2,32,128]{3,2,1,0:T(8,128)S(1)}, u32[]{:S(2)}, u32[]{:S(2)}) collective-permute-start(f32[8,2,32,128]{3,2,1,0:T(8,128)S(1)} %get-tuple-element.48), channel_id=1, source_target_pairs={{0,16},{16,32},{32,48},{48,64},{64,80},{80,96},{96,112},{112,0},{1... | collective-permute-start | bytes 786440 | tf_op jit(solution)/shard_map/ppermute | solution.py:22
  2.0 9.9 %copy-start.9 = (bf16[48,32,1024]{2,1,0:T(8,128)(2,1)S(1)}, bf16[48,32,1024]{2,1,0:T(8,128)(2,1)}, u32[]{:S(2)}) copy-start(bf16[48,32,1024]{2,1,0:T(8,128)(2,1)} %param.17) | copy-start | bytes 9437188
  2.0 14.3 %collective-permute-start.2 = (f32[8,2,32,128]{3,2,1,0:T(8,128)S(1)}, f32[8,2,32,128]{3,2,1,0:T(8,128)S(1)}, u32[]{:S(2)}, u32[]{:S(2)}) collective-permute-start(f32[8,2,32,128]{3,2,1,0:T(8,128)S(1)} %get-tuple-element.49), channel_id=1, source_target_pairs={{16,0},{32,16},{48,32},{64,48},{80,64},{96,80},{112,96},{0,112},{1... | collective-permute-start | bytes 786440 | tf_op jit(solution)/shard_map/ppermute | solution.py:23
  5.4 8.3 %copy-start.10 = (bf16[16,32,1024]{2,1,0:T(8,128)(2,1)S(1)}, bf16[16,32,1024]{2,1,0:T(8,128)(2,1)}, u32[]{:S(2)}) copy-start(bf16[16,32,1024]{2,1,0:T(8,128)(2,1)} %param.19) | copy-start | bytes 3145732
  5.4 17.7 %collective-permute-start = (f32[8,64,2,128]{3,2,1,0:T(2,128)S(1)}, f32[8,64,2,128]{3,2,1,0:T(2,128)S(1)}, u32[]{:S(2)}, u32[]{:S(2)}) collective-permute-start(f32[8,64,2,128]{3,2,1,0:T(2,128)S(1)} %get-tuple-element.50), channel_id=1, source_target_pairs={{0,1},{1,2},{2,3},{3,4},{4,5},{5,6},{6,7},{7,8},{8,9},{9,10},{10,1... | collective-permute-start | bytes 1572872 | tf_op jit(solution)/shard_map/ppermute | solution.py:24
  7.5 15.6 %collective-permute-start.3 = (f32[8,64,2,128]{3,2,1,0:T(2,128)S(1)}, f32[8,64,2,128]{3,2,1,0:T(2,128)S(1)}, u32[]{:S(2)}, u32[]{:S(2)}) collective-permute-start(f32[8,64,2,128]{3,2,1,0:T(2,128)S(1)} %get-tuple-element.51), channel_id=1, source_target_pairs={{1,0},{2,1},{3,2},{4,3},{5,4},{6,5},{7,6},{8,7},{9,8},{10,9},{11,1... | collective-permute-start | bytes 1572872 | tf_op jit(solution)/shard_map/ppermute | solution.py:25
  14.3 2.0 %copy-start = (bf16[64,32,1024]{2,0,1:T(8,128)(2,1)}, bf16[64,32,1024]{2,0,1:T(8,128)(2,1)S(1)}, u32[]{:S(2)}) copy-start(bf16[64,32,1024]{2,0,1:T(8,128)(2,1)S(1)} %copy_dynamic-update-slice_fusion.1) | copy-start | bytes 12582916
  28.0 5.9 %copy-start.5 = (f32[8,68,36,128]{3,2,1,0:T(8,128)}, f32[8,68,36,128]{3,2,1,0:T(8,128)S(1)}, u32[]{:S(2)}) copy-start(f32[8,68,36,128]{3,2,1,0:T(8,128)S(1)} %select_maximum_fusion) | copy-start | bytes 30081028
  28.1 5.8 %copy-start.4 = (f32[4]{0:T(128)S(1)}, f32[4]{0:T(128)}, u32[]{:S(2)}) copy-start(f32[4]{0:T(128)} %param.16) | copy-start | bytes 52
  39.8 8.7 %collective-permute-start.12 = (f32[64,64]{1,0:T(8,128)S(1)}, f32[64,64]{1,0:T(8,128)S(1)}, u32[]{:S(2)}, u32[]{:S(2)}) collective-permute-start(f32[64,64]{1,0:T(8,128)S(1)} %convolution_bitcast_fusion.1), channel_id=1, source_target_pairs={{0,16},{16,0},{32,48},{48,32},{64,80},{80,64},{96,112},{112,96},{1... | collective-permute-start | bytes 49160 | tf_op jit(solution)/shard_map/ppermute | solution.py:37
  39.9 14.3 %collective-permute-start.5 = (f32[1,2,32,128]{3,2,1,0:T(8,128)S(1)}, f32[1,2,32,128]{3,2,1,0:T(8,128)S(1)}, u32[]{:S(2)}, u32[]{:S(2)}) collective-permute-start(f32[1,2,32,128]{3,2,1,0:T(8,128)S(1)} %get-tuple-element.56), channel_id=1, source_target_pairs={{0,16},{16,32},{32,48},{48,64},{64,80},{80,96},{96,112},{112,0},{1... | collective-permute-start | bytes 98312 | tf_op jit(solution)/shard_map/ppermute | solution.py:22
  40.4 13.8 %collective-permute-start.6 = (f32[1,2,32,128]{3,2,1,0:T(8,128)S(1)}, f32[1,2,32,128]{3,2,1,0:T(8,128)S(1)}, u32[]{:S(2)}, u32[]{:S(2)}) collective-permute-start(f32[1,2,32,128]{3,2,1,0:T(8,128)S(1)} %get-tuple-element.57), channel_id=1, source_target_pairs={{16,0},{32,16},{48,32},{64,48},{80,64},{96,80},{112,96},{0,112},{1... | collective-permute-start | bytes 98312 | tf_op jit(solution)/shard_map/ppermute | solution.py:23
  43.1 11.2 %collective-permute-start.4 = (f32[1,64,2,128]{3,2,1,0:T(2,128)S(1)}, f32[1,64,2,128]{3,2,1,0:T(2,128)S(1)}, u32[]{:S(2)}, u32[]{:S(2)}) collective-permute-start(f32[1,64,2,128]{3,2,1,0:T(2,128)S(1)} %get-tuple-element.58), channel_id=1, source_target_pairs={{0,1},{1,2},{2,3},{3,4},{4,5},{5,6},{6,7},{7,8},{8,9},{9,10},{10,1... | collective-permute-start | bytes 196616 | tf_op jit(solution)/shard_map/ppermute | solution.py:24
  43.1 11.2 %collective-permute-start.7 = (f32[1,64,2,128]{3,2,1,0:T(2,128)S(1)}, f32[1,64,2,128]{3,2,1,0:T(2,128)S(1)}, u32[]{:S(2)}, u32[]{:S(2)}) collective-permute-start(f32[1,64,2,128]{3,2,1,0:T(2,128)S(1)} %get-tuple-element.59), channel_id=1, source_target_pairs={{1,0},{2,1},{3,2},{4,3},{5,4},{6,5},{7,6},{8,7},{9,8},{10,9},{11,1... | collective-permute-start | bytes 196616 | tf_op jit(solution)/shard_map/ppermute | solution.py:25
  48.4 4.0 %collective-permute-start.13 = (f32[64,64]{1,0:T(8,128)S(1)}, f32[64,64]{1,0:T(8,128)S(1)}, u32[]{:S(2)}, u32[]{:S(2)}) collective-permute-start(f32[64,64]{1,0:T(8,128)S(1)} %add.79), channel_id=1, source_target_pairs={{0,32},{16,48},{32,0},{48,16},{64,96},{80,112},{96,64},{112,80},{1... | collective-permute-start | bytes 49160 | tf_op jit(solution)/shard_map/ppermute | solution.py:37
  52.4 14.1 %collective-permute-start.14 = (f32[64,64]{1,0:T(8,128)S(1)}, f32[64,64]{1,0:T(8,128)S(1)}, u32[]{:S(2)}, u32[]{:S(2)}) collective-permute-start(f32[64,64]{1,0:T(8,128)S(1)} %add.80), channel_id=1, source_target_pairs={{0,64},{16,80},{32,96},{48,112},{64,0},{80,16},{96,32},{112,48},{1... | collective-permute-start | bytes 49160 | tf_op jit(solution)/shard_map/ppermute | solution.py:37
  60.0 1.0 copy-start.2
  61.0 8.2 %copy-start.11 = (f32[48]{0:T(128)S(1)}, f32[48]{0:T(128)}, u32[]{:S(2)}) copy-start(f32[48]{0:T(128)} %param.18) | copy-start | bytes 580
  66.6 1.2 collective-permute-start.19
  66.6 20.8 %collective-permute-start.15 = (f32[64,64]{1,0:T(8,128)S(1)}, f32[64,64]{1,0:T(8,128)S(1)}, u32[]{:S(2)}, u32[]{:S(2)}) collective-permute-start(f32[64,64]{1,0:T(8,128)S(1)} %add.81), channel_id=1, source_target_pairs={{0,1},{1,0},{2,3},{3,2},{4,5},{5,4},{6,7},{7,6},{8,9},{9,8},{10,11... | collective-permute-start | bytes 49160 | tf_op jit(solution)/shard_map/ppermute | solution.py:37
  68.5 5.2 %collective-permute-start.20 = (f32[65]{0:T(128)S(1)}, f32[65]{0:T(128)S(1)}, u32[]{:S(2)}, u32[]{:S(2)}) collective-permute-start(f32[65]{0:T(128)S(1)} %fusion.32), channel_id=1, source_target_pairs={{0,32},{16,48},{32,0},{48,16},{64,96},{80,112},{96,64},{112,80},{1... | collective-permute-start | bytes 788 | tf_op jit(solution)/shard_map/ppermute | solution.py:37
  73.7 13.8 %collective-permute-start.21 = (f32[65]{0:T(128)S(1)}, f32[65]{0:T(128)S(1)}, u32[]{:S(2)}, u32[]{:S(2)}) collective-permute-start(f32[65]{0:T(128)S(1)} %add.88), channel_id=1, source_target_pairs={{0,64},{16,80},{32,96},{48,112},{64,0},{80,16},{96,32},{112,48},{1... | collective-permute-start | bytes 788 | tf_op jit(solution)/shard_map/ppermute | solution.py:37
  87.4 7.3 %collective-permute-start.16 = (f32[64,64]{1,0:T(8,128)S(1)}, f32[64,64]{1,0:T(8,128)S(1)}, u32[]{:S(2)}, u32[]{:S(2)}) collective-permute-start(f32[64,64]{1,0:T(8,128)S(1)} %add.82), channel_id=1, source_target_pairs={{0,2},{1,3},{2,0},{3,1},{4,6},{5,7},{6,4},{7,5},{8,10},{9,11},{10,... | collective-permute-start | bytes 49160 | tf_op jit(solution)/shard_map/ppermute | solution.py:37
  87.5 3.6 %collective-permute-start.22 = (f32[65]{0:T(128)S(1)}, f32[65]{0:T(128)S(1)}, u32[]{:S(2)}, u32[]{:S(2)}) collective-permute-start(f32[65]{0:T(128)S(1)} %add.89), channel_id=1, source_target_pairs={{0,1},{1,0},{2,3},{3,2},{4,5},{5,4},{6,7},{7,6},{8,9},{9,8},{10,11... | collective-permute-start | bytes 788 | tf_op jit(solution)/shard_map/ppermute | solution.py:37
  91.2 5.1 %collective-permute-start.23 = (f32[65]{0:T(128)S(1)}, f32[65]{0:T(128)S(1)}, u32[]{:S(2)}, u32[]{:S(2)}) collective-permute-start(f32[65]{0:T(128)S(1)} %add.90), channel_id=1, source_target_pairs={{0,2},{1,3},{2,0},{3,1},{4,6},{5,7},{6,4},{7,5},{8,10},{9,11},{10,... | collective-permute-start | bytes 788 | tf_op jit(solution)/shard_map/ppermute | solution.py:37
  95.3 9.2 %collective-permute-start.17 = (f32[64,64]{1,0:T(8,128)}, f32[64,64]{1,0:T(8,128)}, u32[]{:S(2)}, u32[]{:S(2)}) collective-permute-start(f32[64,64]{1,0:T(8,128)} %add.83), channel_id=1, source_target_pairs={{0,4},{1,5},{2,6},{3,7},{4,0},{5,1},{6,2},{7,3},{8,12},{9,13},{10,... | collective-permute-start | bytes 49160 | tf_op jit(solution)/shard_map/ppermute | solution.py:37
  96.2 5.9 %collective-permute-start.24 = (f32[65]{0:T(128)S(1)}, f32[65]{0:T(128)S(1)}, u32[]{:S(2)}, u32[]{:S(2)}) collective-permute-start(f32[65]{0:T(128)S(1)} %add.91), channel_id=1, source_target_pairs={{0,4},{1,5},{2,6},{3,7},{4,0},{5,1},{6,2},{7,3},{8,12},{9,13},{10,... | collective-permute-start | bytes 788 | tf_op jit(solution)/shard_map/ppermute | solution.py:37
  98.1 48.4 %collective-permute-start.9 = (f32[3,2,32,128]{3,2,1,0:T(8,128)}, f32[3,2,32,128]{3,2,1,0:T(8,128)}, u32[]{:S(2)}, u32[]{:S(2)}) collective-permute-start(f32[3,2,32,128]{3,2,1,0:T(8,128)} %get-tuple-element.52), channel_id=1, source_target_pairs={{0,16},{16,32},{32,48},{48,64},{64,80},{80,96},{96,112},{112,0},{1... | collective-permute-start | bytes 294920 | tf_op jit(solution)/shard_map/ppermute | solution.py:22
  98.1 48.4 %collective-permute-start.10 = (f32[3,2,32,128]{3,2,1,0:T(8,128)}, f32[3,2,32,128]{3,2,1,0:T(8,128)}, u32[]{:S(2)}, u32[]{:S(2)}) collective-permute-start(f32[3,2,32,128]{3,2,1,0:T(8,128)} %get-tuple-element.53), channel_id=1, source_target_pairs={{16,0},{32,16},{48,32},{64,48},{80,64},{96,80},{112,96},{0,112},{1... | collective-permute-start | bytes 294920 | tf_op jit(solution)/shard_map/ppermute | solution.py:23
  101.0 45.4 %collective-permute-start.8 = (f32[3,64,2,128]{3,2,1,0:T(2,128)}, f32[3,64,2,128]{3,2,1,0:T(2,128)}, u32[]{:S(2)}, u32[]{:S(2)}) collective-permute-start(f32[3,64,2,128]{3,2,1,0:T(2,128)} %get-tuple-element.54), channel_id=1, source_target_pairs={{0,1},{1,2},{2,3},{3,4},{4,5},{5,6},{6,7},{7,8},{8,9},{9,10},{10,1... | collective-permute-start | bytes 589832 | tf_op jit(solution)/shard_map/ppermute | solution.py:24
  102.1 7.6 %collective-permute-start.25 = (f32[65]{0:T(128)S(1)}, f32[65]{0:T(128)}, u32[]{:S(2)}, u32[]{:S(2)}) collective-permute-start(f32[65]{0:T(128)S(1)} %add.92), channel_id=1, source_target_pairs={{0,8},{1,9},{2,10},{3,11},{4,12},{5,13},{6,14},{7,15},{8,0},{9,1},... | collective-permute-start | bytes 788 | tf_op jit(solution)/shard_map/ppermute | solution.py:37
  104.5 42.0 %collective-permute-start.11 = (f32[3,64,2,128]{3,2,1,0:T(2,128)}, f32[3,64,2,128]{3,2,1,0:T(2,128)}, u32[]{:S(2)}, u32[]{:S(2)}) collective-permute-start(f32[3,64,2,128]{3,2,1,0:T(2,128)} %get-tuple-element.55), channel_id=1, source_target_pairs={{1,0},{2,1},{3,2},{4,3},{5,4},{6,5},{7,6},{8,7},{9,8},{10,9},{11,1... | collective-permute-start | bytes 589832 | tf_op jit(solution)/shard_map/ppermute | solution.py:25
  109.8 5.5 %collective-permute-start.18 = (f32[64,64]{1,0:T(8,128)S(1)}, f32[64,64]{1,0:T(8,128)S(1)}, u32[]{:S(2)}, u32[]{:S(2)}) collective-permute-start(f32[64,64]{1,0:T(8,128)S(1)} %add.84), channel_id=1, source_target_pairs={{0,8},{1,9},{2,10},{3,11},{4,12},{5,13},{6,14},{7,15},{8,0},{9,1},... | collective-permute-start | bytes 49160 | tf_op jit(solution)/shard_map/ppermute | solution.py:37
  135.2 2.2 %copy-start.1 = (bf16[64,32,1024]{2,0,1:T(8,128)(2,1)S(1)}, bf16[64,32,1024]{2,0,1:T(8,128)(2,1)}, u32[]{:S(2)}) copy-start(bf16[64,32,1024]{2,0,1:T(8,128)(2,1)} %copy-done) | copy-start | bytes 12582916
  150.3 11.9 %copy-start.3 = (f32[1,64,32,128]{3,2,1,0:T(8,128)S(1)}, f32[1,64,32,128]{3,2,1,0:T(8,128)}, u32[]{:S(2)}) copy-start(f32[1,64,32,128]{3,2,1,0:T(8,128)} %copy-done.2) | copy-start | bytes 3145732

commit v10 on v9

--- a/solution.py
+++ b/solution.py
@@ -155,8 +155,11 @@
     lax.fori_loop(0, out_ref.shape[1], row, 0, unroll=16)
 
 
-def stencil_step(conc_pad, coeff_pad, scale):
-    count, px, py, depth = conc_pad.shape
+def stencil_step(conc_pad, start, count, coeff_pad, scale):
+    _, px, py, depth = conc_pad.shape
+    fields = 4
+    assert (coeff_pad.shape[0] - fields) % fields == 0
+    coeff_block = (coeff_pad.shape[0] - fields) // fields
     nx, ny = px - 4, py - 4
     return pl.pallas_call(
         stencil_body,
@@ -164,15 +167,15 @@
         grid=(count,),
         in_specs=[
             pl.BlockSpec(memory_space=pltpu.SMEM),
-            pl.BlockSpec((1, px, py, depth), lambda s: (s, 0, 0, 0)),
-            pl.BlockSpec(coeff_pad.shape, lambda s: (0, 0, 0, 0)),
+            pl.BlockSpec((1, px, py, depth), lambda s: (s + start, 0, 0, 0)),
+            pl.BlockSpec((fields, px, py, depth), lambda s: (coeff_block, 0, 0, 0)),
         ],
         out_specs=pl.BlockSpec((1, nx, ny, depth), lambda s: (s, 0, 0, 0)),
         compiler_params=pltpu.CompilerParams(vmem_limit_bytes=48 * 1024 * 1024),
         cost_estimate=pl.CostEstimate(
             flops=80 * count * nx * ny * depth,
             transcendentals=0,
-            bytes_accessed=4 * (conc_pad.size + coeff_pad.size + count * nx * ny * depth),
+            bytes_accessed=4 * (2 * count + fields) * px * py * depth,
         ),
     )(scale, conc_pad, coeff_pad)
 
@@ -227,8 +230,7 @@
     coeffs = jnp.concatenate([velocity, diffusivity[None]], 0)
     count = scalars.shape[0]
     first = halo(jnp.concatenate([scalars, coeffs], 0))
-    coeff_pad = first[count:]
-    middle0 = stencil_step(first[:1], coeff_pad, diff_scale[:1])
+    middle0 = stencil_step(first, 0, 1, first, diff_scale[:1])
     local_gram, middle0 = lax.optimization_barrier((local_gram, middle0))
     gram_static = butterfly_sum(local_gram) * (weight[:, None] * weight[None, :]) / total_rows
     lower_static = jnp.linalg.cholesky(gram_static)
@@ -240,7 +242,7 @@
     mix_ext = jnp.concatenate([mix, jnp.zeros((1, width), jnp.float32)], 0)
     basis_ext = basis_rows(mix_ext, static)
 
-    result0 = stencil_step(halo(middle0), coeff_pad, diff_scale[:1])
+    result0 = stencil_step(halo(middle0), 0, 1, first, diff_scale[:1])
 
     coarse = result0[0, ::2]
     span, depth = coarse.shape[1], coarse.shape[2]
@@ -257,8 +259,8 @@
     cross_g = moments[:width] * weight
     self_g = moments[width]
 
-    middle_r = stencil_step(first[1:count], coeff_pad, diff_scale[1:])
-    result_r = stencil_step(halo(middle_r), coeff_pad, diff_scale[1:])
+    middle_r = stencil_step(first, 1, count - 1, first, diff_scale[1:])
+    result_r = stencil_step(halo(middle_r), 0, count - 1, first, diff_scale[1:])
     result = jnp.concatenate([result0, result_r], 0)
 
     link = lax.linalg.triangular_solve(

time: 165 us -> 156 us (0.945)
  local copies, waits for them, and re-layouts: 20.3 us -> 10.7 us
  starting transfers between devices: 41 us -> 34.7 us
  waiting for transfers between devices: 16.8 us -> 22.2 us
    slice x4 -> x1, local copies, waits for them, and re-layouts: 7.71 us -> 0.07 us  [per_device(): result_r = stencil_step(halo(middle_r), 0, count - 1, first, diff_scale[1:])]
    ppermute x3, starting transfers between devices: 8.53 us -> 4.67 us  [halo(): high_x = lax.ppermute(block[:, :width], 'gx', bx)]
    ppermute x3, starting transfers between devices: 14.2 us -> 10.4 us  [halo(): high_y = lax.ppermute(block[:, :, :width], 'gy', by)]
    ppermute x14, starting transfers between devices: 14.5 us -> 17.7 us  [butterfly_sum(): value = value + lax.ppermute(value, axis, pairs)]
    unnamed x26, local copies, waits for them, and re-layouts: 9.14 us -> 6.42 us
    ppermute x3, waiting for transfers between devices: 0.01 us -> 2.64 us  [halo(): low_x = lax.ppermute(block[:, nx - width:], 'gx', fx)]
    slice x1, other arithmetic: 0.48 us -> 2.81 us  [halo(): low_y = lax.ppermute(block[:, :, ny - width:], 'gy', fy)]
    ppermute x14, waiting for transfers between devices: 9.95 us -> 12.2 us  [butterfly_sum(): value = value + lax.ppermute(value, axis, pairs)]
  transfers between devices with their start and end apart: 26 -> 26, of which waited for: 6 -> 10; matrix products, arithmetic and copies ran while one was open for 23% -> 20% of each run, Pallas kernels for 16% -> 17%
where the time goes in v10:
time: 156 us; the launch traced here: 155 us
  Pallas kernels  44.3 us (28%)
  other arithmetic  37.3 us (24%)
  starting transfers between devices  34.7 us (22%)
  waiting for transfers between devices  22.2 us (14%)
  local copies, waits for them, and re-layouts  10.7 us (7%)
  matrix products  3.54 us (2%)
  between operations  2.4 us (2%)
    pallas_call x4, Pallas kernels, stencil_step(): pl.pallas_call(stencil_body, out_shape=jax.ShapeDtypeStruct((count, nx, n...  35.2 us
    ppermute x14, starting transfers between devices, butterfly_sum(): value = value + lax.ppermute(value, axis, pairs)  17.7 us
    ppermute x14, waiting for transfers between devices, butterfly_sum(): value = value + lax.ppermute(value, axis, pairs)  12.2 us
    concatenate x3, other arithmetic, halo(): jnp.concatenate([jnp.pad(low_y, edge), rows, jnp.pad(high_y, edge)], axis=2)  10.8 us
    ppermute x3, starting transfers between devices, halo(): high_y = lax.ppermute(block[:, :, :width], 'gy', by)  10.4 us
    pallas_call x1, Pallas kernels, basis_rows(): pl.pallas_call(basis_body, out_shape=jax.ShapeDtypeStruct((rows, span, co...  7.5 us
    another operation x3, other arithmetic, per_device(): lower_static = jnp.linalg.cholesky(gram_static)  6.52 us
    unnamed x26, local copies, waits for them, and re-layouts  6.42 us
  transfers between devices with their start and end apart: 26, of which 10 were waited for; matrix products, arithmetic and copies ran while one was open for 20% of the time, Pallas kernels for 17%

profile of v10, /device:TPU:0, one launch (start us, length us, event | category | flops | bytes accessed | tf_op | source)
XLA Modules:
  0.0 155.2 jit_solution(4936855882883049800)
XLA Ops:
  0.7 2.8 %pad_maximum_fusion.3 = (f32[8,64,2,128]{3,2,1,0:T(2,128)S(1)}, f32[8,64,2,128]{3,2,1,0:T(2,128)S(1)}) fusion(f32[1,64,32,128]{3,2,1,0:T(8,128)} %bitcast.60, f32[3,64,32,128]{3,2,1,0:T(8,128)} %param.14, f32[4,64,32,128]{3,2,1,0:T(8,128)} %param.13), kind=kLoop, calls=%fused_computation.24 | loop fusion | flops 524288 | bytes 9437184 | tf_op jit(solution)/shard_map/slice | solution.py:24
  3.5 6.4 %collective-permute-start.3 = (f32[8,64,2,128]{3,2,1,0:T(2,128)S(1)}, f32[8,64,2,128]{3,2,1,0:T(2,128)S(1)}, u32[]{:S(2)}, u32[]{:S(2)}) collective-permute-start(f32[8,64,2,128]{3,2,1,0:T(2,128)S(1)} %get-tuple-element.51), channel_id=1, source_target_pairs={{1,0},{2,1},{3,2},{4,3},{5,4},{6,5},{7,6},{8,7},{9,8},{10,9},{11,1... | collective-permute-start | bytes 1572872 | tf_op jit(solution)/shard_map/ppermute | solution.py:25
  10.0 2.2 %collective-permute-start.2 = (f32[8,2,32,128]{3,2,1,0:T(8,128)S(1)}, f32[8,2,32,128]{3,2,1,0:T(8,128)S(1)}, u32[]{:S(2)}, u32[]{:S(2)}) collective-permute-start(f32[8,2,32,128]{3,2,1,0:T(8,128)S(1)} %get-tuple-element.49), channel_id=1, source_target_pairs={{16,0},{32,16},{48,32},{64,48},{80,64},{96,80},{112,96},{0,112},{1... | collective-permute-start | bytes 786440 | tf_op jit(solution)/shard_map/ppermute | solution.py:23
  12.2 1.7 %copy_dynamic-update-slice_fusion = bf16[64,32,1024]{2,0,1:T(8,128)(2,1)S(1)} fusion(bf16[48,32,1024]{2,1,0:T(8,128)(2,1)S(1)} %copy-done.8), kind=kLoop, calls=%fused_computation.13 | loop fusion | bytes 6291456
  13.9 0.6 copy_dynamic-update-slice_fusion.1
  14.5 1.2 convolution_bitcast_fusion.1
  15.8 0.8 copy-done
  16.5 2.6 %collective-permute-done.1 = f32[8,2,32,128]{3,2,1,0:T(8,128)S(1)} collective-permute-done((f32[8,2,32,128]{3,2,1,0:T(8,128)S(1)}, f32[8,2,32,128]{3,2,1,0:T(8,128)S(1)}, u32[]{:S(2)}, u32[]{:S(2)}) %collective-permute-start.1) | collective-permute-done | bytes 262176 | tf_op jit(solution)/shard_map/ppermute | solution.py:22
  19.2 1.9 %collective-permute-done.3 = f32[8,64,2,128]{3,2,1,0:T(2,128)S(1)} collective-permute-done((f32[8,64,2,128]{3,2,1,0:T(2,128)S(1)}, f32[8,64,2,128]{3,2,1,0:T(2,128)S(1)}, u32[]{:S(2)}, u32[]{:S(2)}) %collective-permute-start.3) | collective-permute-done | bytes 524320 | tf_op jit(solution)/shard_map/ppermute | solution.py:25
  21.1 5.5 %collective-permute-done = f32[8,64,2,128]{3,2,1,0:T(2,128)S(1)} collective-permute-done((f32[8,64,2,128]{3,2,1,0:T(2,128)S(1)}, f32[8,64,2,128]{3,2,1,0:T(2,128)S(1)}, u32[]{:S(2)}, u32[]{:S(2)}) %collective-permute-start) | collective-permute-done | bytes 524320 | tf_op jit(solution)/shard_map/ppermute | solution.py:24
  26.6 6.8 %select_maximum_fusion.conc_ref.coeff_ref = f32[8,68,36,128]{3,2,1,0:T(8,128)} fusion(f32[8,64,2,128]{3,2,1,0:T(2,128)S(1)} %collective-permute-done.3, f32[8,64,2,128]{3,2,1,0:T(2,128)S(1)} %collective-permute-done, f32[8,2,32,128]{3,2,1,0:T(8,128)S(1)} %collective-permute-done.2, f32[1,64,32,128]{3,2,1,0:T(8,128)S(1)} %bitcast.62, ...), kind=kLoop, calls=%fused_computation | loop fusion | flops 25067520 | bytes 19988480 | tf_op jit(solution)/shard_map/concatenate | solution.py:28
  33.4 6.0 %shard_map.94 = f32[1,64,32,128]{3,2,1,0:T(8,128)S(1)} custom-call(f32[1]{0:T(128)S(1)} %bitcast.58, f32[8,68,36,128]{3,2,1,0:T(8,128)} %select_maximum_fusion.conc_ref.coeff_ref, f32[8,68,36,128]{3,2,1,0:T(8,128)} %select_maximum_fusion.conc_ref.coeff_ref), custom_call_target="tpu_custom_call" | custom-call | flops 20971520 | bytes 7520256 | tf_op jit(solution)/shard_map/pallas_call | solution.py:164
  39.5 0.3 collective-permute-start.7
  39.8 1.7 %collective-permute-start.4 = (f32[1,64,2,128]{3,2,1,0:T(2,128)S(1)}, f32[1,64,2,128]{3,2,1,0:T(2,128)S(1)}, u32[]{:S(2)}, u32[]{:S(2)}) collective-permute-start(f32[1,64,2,128]{3,2,1,0:T(2,128)S(1)} %get-tuple-element.58), channel_id=1, source_target_pairs={{0,1},{1,2},{2,3},{3,4},{4,5},{5,6},{6,7},{7,8},{8,9},{9,10},{10,1... | collective-permute-start | bytes 196616 | tf_op jit(solution)/shard_map/ppermute | solution.py:24
  41.6 2.5 %collective-permute-start.6 = (f32[1,2,32,128]{3,2,1,0:T(8,128)S(1)}, f32[1,2,32,128]{3,2,1,0:T(8,128)S(1)}, u32[]{:S(2)}, u32[]{:S(2)}) collective-permute-start(f32[1,2,32,128]{3,2,1,0:T(8,128)S(1)} %get-tuple-element.57), channel_id=1, source_target_pairs={{16,0},{32,16},{48,32},{64,48},{80,64},{96,80},{112,96},{0,112},{1... | collective-permute-start | bytes 98312 | tf_op jit(solution)/shard_map/ppermute | solution.py:23
  44.2 3.9 %collective-permute-done.13 = f32[64,64]{1,0:T(8,128)S(1)} collective-permute-done((f32[64,64]{1,0:T(8,128)S(1)}, f32[64,64]{1,0:T(8,128)S(1)}, u32[]{:S(2)}, u32[]{:S(2)}) %collective-permute-start.13) | collective-permute-done | bytes 16416 | tf_op jit(solution)/shard_map/ppermute | solution.py:37
  48.1 1.2 collective-permute-start.14
  49.3 0.2 select_maximum_fusion.4.conc_ref
  49.5 5.5 %shard_map.95 = f32[1,64,32,128]{3,2,1,0:T(8,128)S(1)} custom-call(f32[1]{0:T(128)S(1)} %bitcast.59, f32[1,68,36,128]{3,2,1,0:T(8,128)S(1)} %select_maximum_fusion.4.conc_ref, f32[8,68,36,128]{3,2,1,0:T(8,128)} %select_maximum_fusion.conc_ref.coeff_ref), custom_call_target="tpu_custom_call" | custom-call | flops 20971520 | bytes 7520256 | tf_op jit(solution)/shard_map/pallas_call | solution.py:164
  55.1 1.0 copy-done.2
  56.1 0.4 fusion.2
  56.4 0.9 multiply_reduce_fusion
  57.4 0.1 mul.85
  57.5 3.3 %fusion = f32[64]{0:T(128)S(1)} fusion(bf16[64,32,1024]{2,0,1:T(8,128)(2,1)} %copy-done, f32[32,1024]{1,0:T(8,128)S(1)} %mul.85), kind=kLoop, calls=%fused_computation.6 | loop fusion | flops 6291392 | bytes 4325632 | tf_op jit(solution)/shard_map/reduce_sum | solution.py:256
  60.8 0.7 pad_maximum_fusion.7
  61.6 0.7 collective-permute-start.19
  62.4 0.7 collective-permute-done.19
  63.1 0.7 fusion.32
  63.8 1.3 collective-permute-start.20
  65.2 2.4 %collective-permute-done.20 = f32[65]{0:T(128)S(1)} collective-permute-done((f32[65]{0:T(128)S(1)}, f32[65]{0:T(128)S(1)}, u32[]{:S(2)}, u32[]{:S(2)}) %collective-permute-start.20) | collective-permute-done | bytes 292 | tf_op jit(solution)/shard_map/ppermute | solution.py:37
  67.6 1.9 %collective-permute-start.21 = (f32[65]{0:T(128)S(1)}, f32[65]{0:T(128)S(1)}, u32[]{:S(2)}, u32[]{:S(2)}) collective-permute-start(f32[65]{0:T(128)S(1)} %add.88), channel_id=1, source_target_pairs={{0,64},{16,80},{32,96},{48,112},{64,0},{80,16},{96,32},{112,48},{1... | collective-permute-start | bytes 788 | tf_op jit(solution)/shard_map/ppermute | solution.py:37
  69.6 11.8 %shard_map.96 = f32[3,64,32,128]{3,2,1,0:T(8,128)S(1)} custom-call(f32[3]{0:T(128)S(1)} %slice.132.scale_ref, f32[8,68,36,128]{3,2,1,0:T(8,128)} %select_maximum_fusion.conc_ref.coeff_ref, f32[8,68,36,128]{3,2,1,0:T(8,128)} %select_maximum_fusion.conc_ref.coeff_ref), custom_call_target="tpu_custom_call" | custom-call | flops 62914560 | bytes 12533760 | tf_op jit(solution)/shard_map/pallas_call | solution.py:164
  81.5 1.1 collective-permute-start.22
  82.6 0.9 fusion.25
  83.5 1.7 %collective-permute-done.22 = f32[65]{0:T(128)S(1)} collective-permute-done((f32[65]{0:T(128)S(1)}, f32[65]{0:T(128)S(1)}, u32[]{:S(2)}, u32[]{:S(2)}) %collective-permute-start.22) | collective-permute-done | bytes 292 | tf_op jit(solution)/shard_map/ppermute | solution.py:37
  85.2 3.4 %collective-permute-start.23 = (f32[65]{0:T(128)S(1)}, f32[65]{0:T(128)S(1)}, u32[]{:S(2)}, u32[]{:S(2)}) collective-permute-start(f32[65]{0:T(128)S(1)} %add.90), channel_id=1, source_target_pairs={{0,2},{1,3},{2,0},{3,1},{4,6},{5,7},{6,4},{7,5},{8,10},{9,11},{10,... | collective-permute-start | bytes 788 | tf_op jit(solution)/shard_map/ppermute | solution.py:37
  88.7 0.7 fusion.24
  89.4 0.9 collective-permute-done.23
  90.3 1.2 collective-permute-start.24
  91.5 3.7 %collective-permute-start.11 = (f32[3,64,2,128]{3,2,1,0:T(2,128)}, f32[3,64,2,128]{3,2,1,0:T(2,128)}, u32[]{:S(2)}, u32[]{:S(2)}) collective-permute-start(f32[3,64,2,128]{3,2,1,0:T(2,128)} %get-tuple-element.55), channel_id=1, source_target_pairs={{1,0},{2,1},{3,2},{4,3},{5,4},{6,5},{7,6},{8,7},{9,8},{10,9},{11,1... | collective-permute-start | bytes 589832 | tf_op jit(solution)/shard_map/ppermute | solution.py:25
  95.2 3.2 %collective-permute-start.25 = (f32[65]{0:T(128)S(1)}, f32[65]{0:T(128)S(1)}, u32[]{:S(2)}, u32[]{:S(2)}) collective-permute-start(f32[65]{0:T(128)S(1)} %add.92), channel_id=1, source_target_pairs={{0,8},{1,9},{2,10},{3,11},{4,12},{5,13},{6,14},{7,15},{8,0},{9,1},... | collective-permute-start | bytes 788 | tf_op jit(solution)/shard_map/ppermute | solution.py:37
  98.4 0.8 reshape.146
  99.2 0.1 collective-permute-start.9
  99.3 1.0 collective-permute-done.25
  100.3 3.1 %collective-permute-start.18 = (f32[64,64]{1,0:T(8,128)S(1)}, f32[64,64]{1,0:T(8,128)S(1)}, u32[]{:S(2)}, u32[]{:S(2)}) collective-permute-start(f32[64,64]{1,0:T(8,128)S(1)} %add.84), channel_id=1, source_target_pairs={{0,8},{1,9},{2,10},{3,11},{4,12},{5,13},{6,14},{7,15},{8,0},{9,1},... | collective-permute-start | bytes 49160 | tf_op jit(solution)/shard_map/ppermute | solution.py:37
  103.5 0.6 slice.139
  104.1 1.6 %collective-permute-done.18 = f32[64,64]{1,0:T(8,128)S(1)} collective-permute-done((f32[64,64]{1,0:T(8,128)S(1)}, f32[64,64]{1,0:T(8,128)S(1)}, u32[]{:S(2)}, u32[]{:S(2)}) %collective-permute-start.18) | collective-permute-done | bytes 16416 | tf_op jit(solution)/shard_map/ppermute | solution.py:37
  105.9 5.8 %cholesky.17 = f32[64,64]{1,0:T(8,128)S(1)} custom-call(f32[64,64]{1,0:T(8,128)S(1)} %fusion.12), custom_call_target="Cholesky" | custom-call | tf_op jit(solution)/shard_map/jit(cholesky)/cholesky | solution.py:236
  111.8 0.6 compare_reduce_fusion
  112.5 0.7 select_bitcast_fusion
  113.1 4.9 %custom-call.8 = f32[1,64,64]{1,2,0:T(8,128)S(1)} custom-call(f32[1,64,64]{2,1,0:T(8,128)S(1)} %get-tuple-element.46), custom_call_target="InvertDiagBlocksLowerTriangular" | custom-call | tf_op jit(solution)/shard_map/triangular_solve | solution.py:238
  118.0 0.8 multiply_reduce_fusion.2
  118.8 0.2 multiply_reduce_fusion.1
  119.0 3.5 %fusion.1 = f32[32,1024]{1,0:T(8,128)S(1)} fusion(bf16[64,32,1024]{2,0,1:T(8,128)(2,1)} %copy-done, f32[64]{0:T(128)S(1)} %get-tuple-element.65), kind=kLoop, calls=%fused_computation.7 | loop fusion | flops 6258688 | bytes 4325632 | tf_op jit(solution)/shard_map/reduce_sum | solution.py:276
  123.9 0.7 fusion.5.last_ref
  124.7 0.2 scatter.11
  124.9 0.1 scatter.14
  125.0 0.7 copy.15
  125.7 2.2 %copy-done.1 = bf16[64,32,1024]{2,0,1:T(8,128)(2,1)S(1)} copy-done((bf16[64,32,1024]{2,0,1:T(8,128)(2,1)S(1)}, bf16[64,32,1024]{2,0,1:T(8,128)(2,1)}, u32[]{:S(2)}) %copy-start.1) | copy-done | bytes 4194328
  127.9 7.5 %shard_map.98._ = f32[65,32,1024]{2,1,0:T(8,128)} custom-call(bf16[3,65,64]{2,1,0:T(8,128)(2,1)S(1)} %pad_maximum_fusion.6.mix_ref, bf16[32,64,1024]{2,1,0:T(8,128)(2,1)S(1)} %bitcast.57), custom_call_target="tpu_custom_call" | custom-call | flops 817889280 | bytes 12713984 | tf_op jit(solution)/shard_map/pallas_call | solution.py:202
  135.4 1.6 %shard_map.99 = f32[65,32,1024]{2,1,0:T(8,128)} custom-call(f32[65,32,1024]{2,1,0:T(8,128)} %shard_map.98._, f32[1,32,1024]{2,1,0:T(8,128)} %fusion.5.last_ref), custom_call_target="tpu_custom_call", output_to_operand_aliasing={{}: (0, {})} | custom-call | tf_op jit(solution)/shard_map/pallas_call | solution.py:47
  137.0 3.8 %select_maximum_fusion.2.conc_ref = f32[3,68,36,128]{3,2,1,0:T(8,128)} fusion(f32[3,64,2,128]{3,2,1,0:T(2,128)} %collective-permute-done.11, f32[3,64,2,128]{3,2,1,0:T(2,128)} %collective-permute-done.8, f32[3,2,32,128]{3,2,1,0:T(8,128)} %collective-permute-done.10, f32[3,64,32,128]{3,2,1,0:T(8,128)S(1)} %shard_map.96, ...), kind=kLoop, calls=%fused_computation.9 | loop fusion | flops 7520256 | bytes 7495680 | tf_op jit(solution)/shard_map/concatenate | solution.py:28
  140.8 11.9 %shard_map.97 = f32[3,64,32,128]{3,2,1,0:T(8,128)S(1)} custom-call(f32[3]{0:T(128)S(1)} %slice.132.scale_ref, f32[3,68,36,128]{3,2,1,0:T(8,128)} %select_maximum_fusion.2.conc_ref, f32[8,68,36,128]{3,2,1,0:T(8,128)} %select_maximum_fusion.conc_ref.coeff_ref), custom_call_target="tpu_custom_call" | custom-call | flops 62914560 | bytes 12533760 | tf_op jit(solution)/shard_map/pallas_call | solution.py:164
  152.7 2.5 %pad_maximum_fusion = f32[4,64,32,128]{3,2,1,0:T(8,128)} fusion(f32[3,64,32,128]{3,2,1,0:T(8,128)S(1)} %shard_map.97, f32[1,64,32,128]{3,2,1,0:T(8,128)S(1)} %copy-done.3), kind=kLoop, calls=%fused_computation.8 | loop fusion | flops 1048576 | bytes 8388608 | tf_op jit(solution)/shard_map/concatenate | solution.py:264
  (73 shorter events, 1.0 us)
Async XLA Ops:
  0.6 9.3 %copy-start.5 = (f32[4,64,32,128]{3,2,1,0:T(8,128)S(1)}, f32[4,64,32,128]{3,2,1,0:T(8,128)}, u32[]{:S(2)}) copy-start(f32[4,64,32,128]{3,2,1,0:T(8,128)} %param.13) | copy-start | bytes 12582916
  0.6 9.3 %copy-start.6 = (f32[3,64,32,128]{3,2,1,0:T(8,128)S(1)}, f32[3,64,32,128]{3,2,1,0:T(8,128)}, u32[]{:S(2)}) copy-start(f32[3,64,32,128]{3,2,1,0:T(8,128)} %param.14) | copy-start | bytes 9437188
  0.7 9.3 %copy-start.7 = (f32[64,32,128]{2,1,0:T(8,128)S(1)}, f32[64,32,128]{2,1,0:T(8,128)}, u32[]{:S(2)}) copy-start(f32[64,32,128]{2,1,0:T(8,128)} %param.15) | copy-start | bytes 3145732
  3.5 17.6 %collective-permute-start.3 = (f32[8,64,2,128]{3,2,1,0:T(2,128)S(1)}, f32[8,64,2,128]{3,2,1,0:T(2,128)S(1)}, u32[]{:S(2)}, u32[]{:S(2)}) collective-permute-start(f32[8,64,2,128]{3,2,1,0:T(2,128)S(1)} %get-tuple-element.51), channel_id=1, source_target_pairs={{1,0},{2,1},{3,2},{4,3},{5,4},{6,5},{7,6},{8,7},{9,8},{10,9},{11,1... | collective-permute-start | bytes 1572872 | tf_op jit(solution)/shard_map/ppermute | solution.py:25
  9.9 2.3 %copy-start.8 = (bf16[48,32,1024]{2,1,0:T(8,128)(2,1)S(1)}, bf16[48,32,1024]{2,1,0:T(8,128)(2,1)}, u32[]{:S(2)}) copy-start(bf16[48,32,1024]{2,1,0:T(8,128)(2,1)} %param.17) | copy-start | bytes 9437188
  9.9 16.7 %collective-permute-start = (f32[8,64,2,128]{3,2,1,0:T(2,128)S(1)}, f32[8,64,2,128]{3,2,1,0:T(2,128)S(1)}, u32[]{:S(2)}, u32[]{:S(2)}) collective-permute-start(f32[8,64,2,128]{3,2,1,0:T(2,128)S(1)} %get-tuple-element.50), channel_id=1, source_target_pairs={{0,1},{1,2},{2,3},{3,4},{4,5},{5,6},{6,7},{7,8},{8,9},{9,10},{10,1... | collective-permute-start | bytes 1572872 | tf_op jit(solution)/shard_map/ppermute | solution.py:24
  10.0 4.0 %copy-start.9 = (bf16[16,32,1024]{2,1,0:T(8,128)(2,1)S(1)}, bf16[16,32,1024]{2,1,0:T(8,128)(2,1)}, u32[]{:S(2)}) copy-start(bf16[16,32,1024]{2,1,0:T(8,128)(2,1)} %param.19) | copy-start | bytes 3145732
  10.0 6.6 %collective-permute-start.2 = (f32[8,2,32,128]{3,2,1,0:T(8,128)S(1)}, f32[8,2,32,128]{3,2,1,0:T(8,128)S(1)}, u32[]{:S(2)}, u32[]{:S(2)}) collective-permute-start(f32[8,2,32,128]{3,2,1,0:T(8,128)S(1)} %get-tuple-element.49), channel_id=1, source_target_pairs={{16,0},{32,16},{48,32},{64,48},{80,64},{96,80},{112,96},{0,112},{1... | collective-permute-start | bytes 786440 | tf_op jit(solution)/shard_map/ppermute | solution.py:23
  12.2 7.0 %collective-permute-start.1 = (f32[8,2,32,128]{3,2,1,0:T(8,128)S(1)}, f32[8,2,32,128]{3,2,1,0:T(8,128)S(1)}, u32[]{:S(2)}, u32[]{:S(2)}) collective-permute-start(f32[8,2,32,128]{3,2,1,0:T(8,128)S(1)} %get-tuple-element.48), channel_id=1, source_target_pairs={{0,16},{16,32},{32,48},{48,64},{64,80},{80,96},{96,112},{112,0},{1... | collective-permute-start | bytes 786440 | tf_op jit(solution)/shard_map/ppermute | solution.py:22
  14.5 2.0 %copy-start = (bf16[64,32,1024]{2,0,1:T(8,128)(2,1)}, bf16[64,32,1024]{2,0,1:T(8,128)(2,1)S(1)}, u32[]{:S(2)}) copy-start(bf16[64,32,1024]{2,0,1:T(8,128)(2,1)S(1)} %copy_dynamic-update-slice_fusion.1) | copy-start | bytes 12582916
  16.5 16.8 %copy-start.4 = (f32[4]{0:T(128)S(1)}, f32[4]{0:T(128)}, u32[]{:S(2)}) copy-start(f32[4]{0:T(128)} %param.16) | copy-start | bytes 52
  39.4 4.7 %collective-permute-start.12 = (f32[64,64]{1,0:T(8,128)S(1)}, f32[64,64]{1,0:T(8,128)S(1)}, u32[]{:S(2)}, u32[]{:S(2)}) collective-permute-start(f32[64,64]{1,0:T(8,128)S(1)} %convolution_bitcast_fusion.1), channel_id=1, source_target_pairs={{0,16},{16,0},{32,48},{48,32},{64,80},{80,64},{96,112},{112,96},{1... | collective-permute-start | bytes 49160 | tf_op jit(solution)/shard_map/ppermute | solution.py:37
  39.5 9.8 %collective-permute-start.7 = (f32[1,64,2,128]{3,2,1,0:T(2,128)S(1)}, f32[1,64,2,128]{3,2,1,0:T(2,128)S(1)}, u32[]{:S(2)}, u32[]{:S(2)}) collective-permute-start(f32[1,64,2,128]{3,2,1,0:T(2,128)S(1)} %get-tuple-element.59), channel_id=1, source_target_pairs={{1,0},{2,1},{3,2},{4,3},{5,4},{6,5},{7,6},{8,7},{9,8},{10,9},{11,1... | collective-permute-start | bytes 196616 | tf_op jit(solution)/shard_map/ppermute | solution.py:25
  39.8 9.5 %collective-permute-start.4 = (f32[1,64,2,128]{3,2,1,0:T(2,128)S(1)}, f32[1,64,2,128]{3,2,1,0:T(2,128)S(1)}, u32[]{:S(2)}, u32[]{:S(2)}) collective-permute-start(f32[1,64,2,128]{3,2,1,0:T(2,128)S(1)} %get-tuple-element.58), channel_id=1, source_target_pairs={{0,1},{1,2},{2,3},{3,4},{4,5},{5,6},{6,7},{7,8},{8,9},{9,10},{10,1... | collective-permute-start | bytes 196616 | tf_op jit(solution)/shard_map/ppermute | solution.py:24
  41.6 7.7 %collective-permute-start.6 = (f32[1,2,32,128]{3,2,1,0:T(8,128)S(1)}, f32[1,2,32,128]{3,2,1,0:T(8,128)S(1)}, u32[]{:S(2)}, u32[]{:S(2)}) collective-permute-start(f32[1,2,32,128]{3,2,1,0:T(8,128)S(1)} %get-tuple-element.57), channel_id=1, source_target_pairs={{16,0},{32,16},{48,32},{64,48},{80,64},{96,80},{112,96},{0,112},{1... | collective-permute-start | bytes 98312 | tf_op jit(solution)/shard_map/ppermute | solution.py:23
  44.1 5.2 %collective-permute-start.5 = (f32[1,2,32,128]{3,2,1,0:T(8,128)S(1)}, f32[1,2,32,128]{3,2,1,0:T(8,128)S(1)}, u32[]{:S(2)}, u32[]{:S(2)}) collective-permute-start(f32[1,2,32,128]{3,2,1,0:T(8,128)S(1)} %get-tuple-element.56), channel_id=1, source_target_pairs={{0,16},{16,32},{32,48},{48,64},{64,80},{80,96},{96,112},{112,0},{1... | collective-permute-start | bytes 98312 | tf_op jit(solution)/shard_map/ppermute | solution.py:22
  44.1 4.0 %collective-permute-start.13 = (f32[64,64]{1,0:T(8,128)S(1)}, f32[64,64]{1,0:T(8,128)S(1)}, u32[]{:S(2)}, u32[]{:S(2)}) collective-permute-start(f32[64,64]{1,0:T(8,128)S(1)} %add.79), channel_id=1, source_target_pairs={{0,32},{16,48},{32,0},{48,16},{64,96},{80,112},{96,64},{112,80},{1... | collective-permute-start | bytes 49160 | tf_op jit(solution)/shard_map/ppermute | solution.py:37
  48.1 14.2 %collective-permute-start.14 = (f32[64,64]{1,0:T(8,128)S(1)}, f32[64,64]{1,0:T(8,128)S(1)}, u32[]{:S(2)}, u32[]{:S(2)}) collective-permute-start(f32[64,64]{1,0:T(8,128)S(1)} %add.80), channel_id=1, source_target_pairs={{0,64},{16,80},{32,96},{48,112},{64,0},{80,16},{96,32},{112,48},{1... | collective-permute-start | bytes 49160 | tf_op jit(solution)/shard_map/ppermute | solution.py:37
  55.1 1.0 copy-start.2
  56.1 9.2 %copy-start.11 = (f32[48]{0:T(128)S(1)}, f32[48]{0:T(128)}, u32[]{:S(2)}) copy-start(f32[48]{0:T(128)} %param.18) | copy-start | bytes 580
  61.6 1.6 %collective-permute-start.19 = (f32[65]{0:T(128)S(1)}, f32[65]{0:T(128)S(1)}, u32[]{:S(2)}, u32[]{:S(2)}) collective-permute-start(f32[65]{0:T(128)S(1)} %pad_maximum_fusion.7), channel_id=1, source_target_pairs={{0,16},{16,0},{32,48},{48,32},{64,80},{80,64},{96,112},{112,96},{1... | collective-permute-start | bytes 788 | tf_op jit(solution)/shard_map/ppermute | solution.py:37
  62.3 19.1 %collective-permute-start.15 = (f32[64,64]{1,0:T(8,128)S(1)}, f32[64,64]{1,0:T(8,128)S(1)}, u32[]{:S(2)}, u32[]{:S(2)}) collective-permute-start(f32[64,64]{1,0:T(8,128)S(1)} %add.81), channel_id=1, source_target_pairs={{0,1},{1,0},{2,3},{3,2},{4,5},{5,4},{6,7},{7,6},{8,9},{9,8},{10,11... | collective-permute-start | bytes 49160 | tf_op jit(solution)/shard_map/ppermute | solution.py:37
  63.8 3.8 %collective-permute-start.20 = (f32[65]{0:T(128)S(1)}, f32[65]{0:T(128)S(1)}, u32[]{:S(2)}, u32[]{:S(2)}) collective-permute-start(f32[65]{0:T(128)S(1)} %fusion.32), channel_id=1, source_target_pairs={{0,32},{16,48},{32,0},{48,16},{64,96},{80,112},{96,64},{112,80},{1... | collective-permute-start | bytes 788 | tf_op jit(solution)/shard_map/ppermute | solution.py:37
  67.6 13.9 %collective-permute-start.21 = (f32[65]{0:T(128)S(1)}, f32[65]{0:T(128)S(1)}, u32[]{:S(2)}, u32[]{:S(2)}) collective-permute-start(f32[65]{0:T(128)S(1)} %add.88), channel_id=1, source_target_pairs={{0,64},{16,80},{32,96},{48,112},{64,0},{80,16},{96,32},{112,48},{1... | collective-permute-start | bytes 788 | tf_op jit(solution)/shard_map/ppermute | solution.py:37
  81.4 7.2 %collective-permute-start.16 = (f32[64,64]{1,0:T(8,128)S(1)}, f32[64,64]{1,0:T(8,128)S(1)}, u32[]{:S(2)}, u32[]{:S(2)}) collective-permute-start(f32[64,64]{1,0:T(8,128)S(1)} %add.82), channel_id=1, source_target_pairs={{0,2},{1,3},{2,0},{3,1},{4,6},{5,7},{6,4},{7,5},{8,10},{9,11},{10,... | collective-permute-start | bytes 49160 | tf_op jit(solution)/shard_map/ppermute | solution.py:37
  81.5 3.6 %collective-permute-start.22 = (f32[65]{0:T(128)S(1)}, f32[65]{0:T(128)S(1)}, u32[]{:S(2)}, u32[]{:S(2)}) collective-permute-start(f32[65]{0:T(128)S(1)} %add.89), channel_id=1, source_target_pairs={{0,1},{1,0},{2,3},{3,2},{4,5},{5,4},{6,7},{7,6},{8,9},{9,8},{10,11... | collective-permute-start | bytes 788 | tf_op jit(solution)/shard_map/ppermute | solution.py:37
  85.2 5.1 %collective-permute-start.23 = (f32[65]{0:T(128)S(1)}, f32[65]{0:T(128)S(1)}, u32[]{:S(2)}, u32[]{:S(2)}) collective-permute-start(f32[65]{0:T(128)S(1)} %add.90), channel_id=1, source_target_pairs={{0,2},{1,3},{2,0},{3,1},{4,6},{5,7},{6,4},{7,5},{8,10},{9,11},{10,... | collective-permute-start | bytes 788 | tf_op jit(solution)/shard_map/ppermute | solution.py:37
  88.6 10.6 %collective-permute-start.17 = (f32[64,64]{1,0:T(8,128)S(1)}, f32[64,64]{1,0:T(8,128)S(1)}, u32[]{:S(2)}, u32[]{:S(2)}) collective-permute-start(f32[64,64]{1,0:T(8,128)S(1)} %add.83), channel_id=1, source_target_pairs={{0,4},{1,5},{2,6},{3,7},{4,0},{5,1},{6,2},{7,3},{8,12},{9,13},{10,... | collective-permute-start | bytes 49160 | tf_op jit(solution)/shard_map/ppermute | solution.py:37
  90.3 4.9 %collective-permute-start.24 = (f32[65]{0:T(128)S(1)}, f32[65]{0:T(128)S(1)}, u32[]{:S(2)}, u32[]{:S(2)}) collective-permute-start(f32[65]{0:T(128)S(1)} %add.91), channel_id=1, source_target_pairs={{0,4},{1,5},{2,6},{3,7},{4,0},{5,1},{6,2},{7,3},{8,12},{9,13},{10,... | collective-permute-start | bytes 788 | tf_op jit(solution)/shard_map/ppermute | solution.py:37
  91.5 45.5 %collective-permute-start.11 = (f32[3,64,2,128]{3,2,1,0:T(2,128)}, f32[3,64,2,128]{3,2,1,0:T(2,128)}, u32[]{:S(2)}, u32[]{:S(2)}) collective-permute-start(f32[3,64,2,128]{3,2,1,0:T(2,128)} %get-tuple-element.55), channel_id=1, source_target_pairs={{1,0},{2,1},{3,2},{4,3},{5,4},{6,5},{7,6},{8,7},{9,8},{10,9},{11,1... | collective-permute-start | bytes 589832 | tf_op jit(solution)/shard_map/ppermute | solution.py:25
  95.2 41.8 %collective-permute-start.8 = (f32[3,64,2,128]{3,2,1,0:T(2,128)}, f32[3,64,2,128]{3,2,1,0:T(2,128)}, u32[]{:S(2)}, u32[]{:S(2)}) collective-permute-start(f32[3,64,2,128]{3,2,1,0:T(2,128)} %get-tuple-element.54), channel_id=1, source_target_pairs={{0,1},{1,2},{2,3},{3,4},{4,5},{5,6},{6,7},{7,8},{8,9},{9,10},{10,1... | collective-permute-start | bytes 589832 | tf_op jit(solution)/shard_map/ppermute | solution.py:24
  95.2 41.8 %collective-permute-start.10 = (f32[3,2,32,128]{3,2,1,0:T(8,128)}, f32[3,2,32,128]{3,2,1,0:T(8,128)}, u32[]{:S(2)}, u32[]{:S(2)}) collective-permute-start(f32[3,2,32,128]{3,2,1,0:T(8,128)} %get-tuple-element.53), channel_id=1, source_target_pairs={{16,0},{32,16},{48,32},{64,48},{80,64},{96,80},{112,96},{0,112},{1... | collective-permute-start | bytes 294920 | tf_op jit(solution)/shard_map/ppermute | solution.py:23
  95.2 5.2 %collective-permute-start.25 = (f32[65]{0:T(128)S(1)}, f32[65]{0:T(128)S(1)}, u32[]{:S(2)}, u32[]{:S(2)}) collective-permute-start(f32[65]{0:T(128)S(1)} %add.92), channel_id=1, source_target_pairs={{0,8},{1,9},{2,10},{3,11},{4,12},{5,13},{6,14},{7,15},{8,0},{9,1},... | collective-permute-start | bytes 788 | tf_op jit(solution)/shard_map/ppermute | solution.py:37
  99.2 24.7 %copy-start.10 = (f32[1,32,1024]{2,1,0:T(8,128)S(1)}, f32[1,32,1024]{2,1,0:T(8,128)}, u32[]{:S(2)}) copy-start(f32[1,32,1024]{2,1,0:T(8,128)} %reshape.146) | copy-start | bytes 393220
  99.2 37.8 %collective-permute-start.9 = (f32[3,2,32,128]{3,2,1,0:T(8,128)}, f32[3,2,32,128]{3,2,1,0:T(8,128)}, u32[]{:S(2)}, u32[]{:S(2)}) collective-permute-start(f32[3,2,32,128]{3,2,1,0:T(8,128)} %get-tuple-element.52), channel_id=1, source_target_pairs={{0,16},{16,32},{32,48},{48,64},{64,80},{80,96},{96,112},{112,0},{1... | collective-permute-start | bytes 294920 | tf_op jit(solution)/shard_map/ppermute | solution.py:22
  100.3 5.4 %collective-permute-start.18 = (f32[64,64]{1,0:T(8,128)S(1)}, f32[64,64]{1,0:T(8,128)S(1)}, u32[]{:S(2)}, u32[]{:S(2)}) collective-permute-start(f32[64,64]{1,0:T(8,128)S(1)} %add.84), channel_id=1, source_target_pairs={{0,8},{1,9},{2,10},{3,11},{4,12},{5,13},{6,14},{7,15},{8,0},{9,1},... | collective-permute-start | bytes 49160 | tf_op jit(solution)/shard_map/ppermute | solution.py:37
  125.7 2.2 %copy-start.1 = (bf16[64,32,1024]{2,0,1:T(8,128)(2,1)S(1)}, bf16[64,32,1024]{2,0,1:T(8,128)(2,1)}, u32[]{:S(2)}) copy-start(bf16[64,32,1024]{2,0,1:T(8,128)(2,1)} %copy-done) | copy-start | bytes 12582916
  140.8 11.9 %copy-start.3 = (f32[1,64,32,128]{3,2,1,0:T(8,128)S(1)}, f32[1,64,32,128]{3,2,1,0:T(8,128)}, u32[]{:S(2)}) copy-start(f32[1,64,32,128]{3,2,1,0:T(8,128)} %copy-done.2) | copy-start | bytes 3145732

commit v11 on v10

--- a/solution.py
+++ b/solution.py
@@ -152,7 +152,7 @@
         out_ref[0, i] = center + time_step * (scale * spread - slope)
         return carry
 
-    lax.fori_loop(0, out_ref.shape[1], row, 0, unroll=16)
+    lax.fori_loop(0, out_ref.shape[1], row, 0, unroll=32)
 
 
 def stencil_step(conc_pad, start, count, coeff_pad, scale):

time: 156 us -> 155 us (level)
  transfers between devices with their start and end apart: 26 -> 26, of which waited for: 10 -> 10; matrix products, arithmetic and copies ran while one was open for 20% -> 21% of each run, Pallas kernels for 17% -> 17%
where the time goes in v11:
time: 155 us; the launch traced here: 154 us
  Pallas kernels  43.6 us (28%)
  other arithmetic  37.3 us (24%)
  starting transfers between devices  34.5 us (22%)
  waiting for transfers between devices  22.2 us (14%)
  local copies, waits for them, and re-layouts  10.7 us (7%)
  matrix products  3.54 us (2%)
  between operations  2.4 us (2%)
    pallas_call x4, Pallas kernels, stencil_step(): pl.pallas_call(stencil_body, out_shape=jax.ShapeDtypeStruct((count, nx, n...  34.5 us
    ppermute x14, starting transfers between devices, butterfly_sum(): value = value + lax.ppermute(value, axis, pairs)  17.5 us
    ppermute x14, waiting for transfers between devices, butterfly_sum(): value = value + lax.ppermute(value, axis, pairs)  12.2 us
    concatenate x3, other arithmetic, halo(): jnp.concatenate([jnp.pad(low_y, edge), rows, jnp.pad(high_y, edge)], axis=2)  10.8 us
    ppermute x3, starting transfers between devices, halo(): high_y = lax.ppermute(block[:, :, :width], 'gy', by)  10.4 us
    pallas_call x1, Pallas kernels, basis_rows(): pl.pallas_call(basis_body, out_shape=jax.ShapeDtypeStruct((rows, span, co...  7.51 us
    another operation x3, other arithmetic, per_device(): lower_static = jnp.linalg.cholesky(gram_static)  6.52 us
    unnamed x26, local copies, waits for them, and re-layouts  6.42 us
  transfers between devices with their start and end apart: 26, of which 10 were waited for; matrix products, arithmetic and copies ran while one was open for 21% of the time, Pallas kernels for 17%

profile of v11, /device:TPU:0, one launch (start us, length us, event | category | flops | bytes accessed | tf_op | source)
XLA Modules:
  0.0 154.3 jit_solution(2802158769675123258)
XLA Ops:
  0.7 2.8 %pad_maximum_fusion.3 = (f32[8,64,2,128]{3,2,1,0:T(2,128)S(1)}, f32[8,64,2,128]{3,2,1,0:T(2,128)S(1)}) fusion(f32[1,64,32,128]{3,2,1,0:T(8,128)} %bitcast.60, f32[3,64,32,128]{3,2,1,0:T(8,128)} %param.14, f32[4,64,32,128]{3,2,1,0:T(8,128)} %param.13), kind=kLoop, calls=%fused_computation.24 | loop fusion | flops 524288 | bytes 9437184 | tf_op jit(solution)/shard_map/slice | solution.py:24
  3.5 6.4 %collective-permute-start.3 = (f32[8,64,2,128]{3,2,1,0:T(2,128)S(1)}, f32[8,64,2,128]{3,2,1,0:T(2,128)S(1)}, u32[]{:S(2)}, u32[]{:S(2)}) collective-permute-start(f32[8,64,2,128]{3,2,1,0:T(2,128)S(1)} %get-tuple-element.51), channel_id=1, source_target_pairs={{1,0},{2,1},{3,2},{4,3},{5,4},{6,5},{7,6},{8,7},{9,8},{10,9},{11,1... | collective-permute-start | bytes 1572872 | tf_op jit(solution)/shard_map/ppermute | solution.py:25
  10.0 2.2 %collective-permute-start.2 = (f32[8,2,32,128]{3,2,1,0:T(8,128)S(1)}, f32[8,2,32,128]{3,2,1,0:T(8,128)S(1)}, u32[]{:S(2)}, u32[]{:S(2)}) collective-permute-start(f32[8,2,32,128]{3,2,1,0:T(8,128)S(1)} %get-tuple-element.49), channel_id=1, source_target_pairs={{16,0},{32,16},{48,32},{64,48},{80,64},{96,80},{112,96},{0,112},{1... | collective-permute-start | bytes 786440 | tf_op jit(solution)/shard_map/ppermute | solution.py:23
  12.2 1.7 %copy_dynamic-update-slice_fusion = bf16[64,32,1024]{2,0,1:T(8,128)(2,1)S(1)} fusion(bf16[48,32,1024]{2,1,0:T(8,128)(2,1)S(1)} %copy-done.8), kind=kLoop, calls=%fused_computation.13 | loop fusion | bytes 6291456
  13.9 0.6 copy_dynamic-update-slice_fusion.1
  14.5 1.2 convolution_bitcast_fusion.1
  15.8 0.8 copy-done
  16.5 2.6 %collective-permute-done.1 = f32[8,2,32,128]{3,2,1,0:T(8,128)S(1)} collective-permute-done((f32[8,2,32,128]{3,2,1,0:T(8,128)S(1)}, f32[8,2,32,128]{3,2,1,0:T(8,128)S(1)}, u32[]{:S(2)}, u32[]{:S(2)}) %collective-permute-start.1) | collective-permute-done | bytes 262176 | tf_op jit(solution)/shard_map/ppermute | solution.py:22
  19.2 1.9 %collective-permute-done.3 = f32[8,64,2,128]{3,2,1,0:T(2,128)S(1)} collective-permute-done((f32[8,64,2,128]{3,2,1,0:T(2,128)S(1)}, f32[8,64,2,128]{3,2,1,0:T(2,128)S(1)}, u32[]{:S(2)}, u32[]{:S(2)}) %collective-permute-start.3) | collective-permute-done | bytes 524320 | tf_op jit(solution)/shard_map/ppermute | solution.py:25
  21.1 5.5 %collective-permute-done = f32[8,64,2,128]{3,2,1,0:T(2,128)S(1)} collective-permute-done((f32[8,64,2,128]{3,2,1,0:T(2,128)S(1)}, f32[8,64,2,128]{3,2,1,0:T(2,128)S(1)}, u32[]{:S(2)}, u32[]{:S(2)}) %collective-permute-start) | collective-permute-done | bytes 524320 | tf_op jit(solution)/shard_map/ppermute | solution.py:24
  26.6 6.8 %select_maximum_fusion.conc_ref.coeff_ref = f32[8,68,36,128]{3,2,1,0:T(8,128)} fusion(f32[8,64,2,128]{3,2,1,0:T(2,128)S(1)} %collective-permute-done.3, f32[8,64,2,128]{3,2,1,0:T(2,128)S(1)} %collective-permute-done, f32[8,2,32,128]{3,2,1,0:T(8,128)S(1)} %collective-permute-done.2, f32[1,64,32,128]{3,2,1,0:T(8,128)S(1)} %bitcast.62, ...), kind=kLoop, calls=%fused_computation | loop fusion | flops 25067520 | bytes 19988480 | tf_op jit(solution)/shard_map/concatenate | solution.py:28
  33.4 5.9 %shard_map.94 = f32[1,64,32,128]{3,2,1,0:T(8,128)S(1)} custom-call(f32[1]{0:T(128)S(1)} %bitcast.58, f32[8,68,36,128]{3,2,1,0:T(8,128)} %select_maximum_fusion.conc_ref.coeff_ref, f32[8,68,36,128]{3,2,1,0:T(8,128)} %select_maximum_fusion.conc_ref.coeff_ref), custom_call_target="tpu_custom_call" | custom-call | flops 20971520 | bytes 7520256 | tf_op jit(solution)/shard_map/pallas_call | solution.py:164
  39.4 0.3 collective-permute-start.7
  39.8 1.7 %collective-permute-start.4 = (f32[1,64,2,128]{3,2,1,0:T(2,128)S(1)}, f32[1,64,2,128]{3,2,1,0:T(2,128)S(1)}, u32[]{:S(2)}, u32[]{:S(2)}) collective-permute-start(f32[1,64,2,128]{3,2,1,0:T(2,128)S(1)} %get-tuple-element.58), channel_id=1, source_target_pairs={{0,1},{1,2},{2,3},{3,4},{4,5},{5,6},{6,7},{7,8},{8,9},{9,10},{10,1... | collective-permute-start | bytes 196616 | tf_op jit(solution)/shard_map/ppermute | solution.py:24
  41.5 2.5 %collective-permute-start.6 = (f32[1,2,32,128]{3,2,1,0:T(8,128)S(1)}, f32[1,2,32,128]{3,2,1,0:T(8,128)S(1)}, u32[]{:S(2)}, u32[]{:S(2)}) collective-permute-start(f32[1,2,32,128]{3,2,1,0:T(8,128)S(1)} %get-tuple-element.57), channel_id=1, source_target_pairs={{16,0},{32,16},{48,32},{64,48},{80,64},{96,80},{112,96},{0,112},{1... | collective-permute-start | bytes 98312 | tf_op jit(solution)/shard_map/ppermute | solution.py:23
  44.1 3.9 %collective-permute-done.13 = f32[64,64]{1,0:T(8,128)S(1)} collective-permute-done((f32[64,64]{1,0:T(8,128)S(1)}, f32[64,64]{1,0:T(8,128)S(1)}, u32[]{:S(2)}, u32[]{:S(2)}) %collective-permute-start.13) | collective-permute-done | bytes 16416 | tf_op jit(solution)/shard_map/ppermute | solution.py:37
  48.0 1.2 collective-permute-start.14
  49.2 0.2 select_maximum_fusion.4.conc_ref
  49.5 5.4 %shard_map.95 = f32[1,64,32,128]{3,2,1,0:T(8,128)S(1)} custom-call(f32[1]{0:T(128)S(1)} %bitcast.59, f32[1,68,36,128]{3,2,1,0:T(8,128)S(1)} %select_maximum_fusion.4.conc_ref, f32[8,68,36,128]{3,2,1,0:T(8,128)} %select_maximum_fusion.conc_ref.coeff_ref), custom_call_target="tpu_custom_call" | custom-call | flops 20971520 | bytes 7520256 | tf_op jit(solution)/shard_map/pallas_call | solution.py:164
  54.9 1.0 copy-done.2
  55.9 0.4 fusion.2
  56.3 0.9 multiply_reduce_fusion
  57.2 0.1 mul.85
  57.4 3.3 %fusion = f32[64]{0:T(128)S(1)} fusion(bf16[64,32,1024]{2,0,1:T(8,128)(2,1)} %copy-done, f32[32,1024]{1,0:T(8,128)S(1)} %mul.85), kind=kLoop, calls=%fused_computation.6 | loop fusion | flops 6291392 | bytes 4325632 | tf_op jit(solution)/shard_map/reduce_sum | solution.py:256
  60.7 0.7 pad_maximum_fusion.7
  61.4 0.7 collective-permute-start.19
  62.2 0.7 collective-permute-done.19
  63.0 0.7 fusion.32
  63.7 1.1 collective-permute-start.20
  64.9 2.4 %collective-permute-done.20 = f32[65]{0:T(128)S(1)} collective-permute-done((f32[65]{0:T(128)S(1)}, f32[65]{0:T(128)S(1)}, u32[]{:S(2)}, u32[]{:S(2)}) %collective-permute-start.20) | collective-permute-done | bytes 292 | tf_op jit(solution)/shard_map/ppermute | solution.py:37
  67.3 1.9 %collective-permute-start.21 = (f32[65]{0:T(128)S(1)}, f32[65]{0:T(128)S(1)}, u32[]{:S(2)}, u32[]{:S(2)}) collective-permute-start(f32[65]{0:T(128)S(1)} %add.88), channel_id=1, source_target_pairs={{0,64},{16,80},{32,96},{48,112},{64,0},{80,16},{96,32},{112,48},{1... | collective-permute-start | bytes 788 | tf_op jit(solution)/shard_map/ppermute | solution.py:37
  69.2 11.6 %shard_map.96 = f32[3,64,32,128]{3,2,1,0:T(8,128)S(1)} custom-call(f32[3]{0:T(128)S(1)} %slice.132.scale_ref, f32[8,68,36,128]{3,2,1,0:T(8,128)} %select_maximum_fusion.conc_ref.coeff_ref, f32[8,68,36,128]{3,2,1,0:T(8,128)} %select_maximum_fusion.conc_ref.coeff_ref), custom_call_target="tpu_custom_call" | custom-call | flops 62914560 | bytes 12533760 | tf_op jit(solution)/shard_map/pallas_call | solution.py:164
  80.9 1.1 collective-permute-start.22
  82.0 0.9 fusion.25
  82.9 1.7 %collective-permute-done.22 = f32[65]{0:T(128)S(1)} collective-permute-done((f32[65]{0:T(128)S(1)}, f32[65]{0:T(128)S(1)}, u32[]{:S(2)}, u32[]{:S(2)}) %collective-permute-start.22) | collective-permute-done | bytes 292 | tf_op jit(solution)/shard_map/ppermute | solution.py:37
  84.6 3.4 %collective-permute-start.23 = (f32[65]{0:T(128)S(1)}, f32[65]{0:T(128)S(1)}, u32[]{:S(2)}, u32[]{:S(2)}) collective-permute-start(f32[65]{0:T(128)S(1)} %add.90), channel_id=1, source_target_pairs={{0,2},{1,3},{2,0},{3,1},{4,6},{5,7},{6,4},{7,5},{8,10},{9,11},{10,... | collective-permute-start | bytes 788 | tf_op jit(solution)/shard_map/ppermute | solution.py:37
  88.1 0.7 fusion.24
  88.8 0.9 collective-permute-done.23
  89.7 1.2 collective-permute-start.24
  90.9 3.7 %collective-permute-start.11 = (f32[3,64,2,128]{3,2,1,0:T(2,128)}, f32[3,64,2,128]{3,2,1,0:T(2,128)}, u32[]{:S(2)}, u32[]{:S(2)}) collective-permute-start(f32[3,64,2,128]{3,2,1,0:T(2,128)} %get-tuple-element.55), channel_id=1, source_target_pairs={{1,0},{2,1},{3,2},{4,3},{5,4},{6,5},{7,6},{8,7},{9,8},{10,9},{11,1... | collective-permute-start | bytes 589832 | tf_op jit(solution)/shard_map/ppermute | solution.py:25
  94.6 3.2 %collective-permute-start.25 = (f32[65]{0:T(128)S(1)}, f32[65]{0:T(128)S(1)}, u32[]{:S(2)}, u32[]{:S(2)}) collective-permute-start(f32[65]{0:T(128)S(1)} %add.92), channel_id=1, source_target_pairs={{0,8},{1,9},{2,10},{3,11},{4,12},{5,13},{6,14},{7,15},{8,0},{9,1},... | collective-permute-start | bytes 788 | tf_op jit(solution)/shard_map/ppermute | solution.py:37
  97.8 0.8 reshape.146
  98.6 0.1 collective-permute-start.9
  98.7 1.0 collective-permute-done.25
  99.7 3.1 %collective-permute-start.18 = (f32[64,64]{1,0:T(8,128)S(1)}, f32[64,64]{1,0:T(8,128)S(1)}, u32[]{:S(2)}, u32[]{:S(2)}) collective-permute-start(f32[64,64]{1,0:T(8,128)S(1)} %add.84), channel_id=1, source_target_pairs={{0,8},{1,9},{2,10},{3,11},{4,12},{5,13},{6,14},{7,15},{8,0},{9,1},... | collective-permute-start | bytes 49160 | tf_op jit(solution)/shard_map/ppermute | solution.py:37
  102.9 0.6 slice.139
  103.5 1.6 %collective-permute-done.18 = f32[64,64]{1,0:T(8,128)S(1)} collective-permute-done((f32[64,64]{1,0:T(8,128)S(1)}, f32[64,64]{1,0:T(8,128)S(1)}, u32[]{:S(2)}, u32[]{:S(2)}) %collective-permute-start.18) | collective-permute-done | bytes 16416 | tf_op jit(solution)/shard_map/ppermute | solution.py:37
  105.3 5.8 %cholesky.17 = f32[64,64]{1,0:T(8,128)S(1)} custom-call(f32[64,64]{1,0:T(8,128)S(1)} %fusion.12), custom_call_target="Cholesky" | custom-call | tf_op jit(solution)/shard_map/jit(cholesky)/cholesky | solution.py:236
  111.2 0.6 compare_reduce_fusion
  111.8 0.7 select_bitcast_fusion
  112.5 4.9 %custom-call.8 = f32[1,64,64]{1,2,0:T(8,128)S(1)} custom-call(f32[1,64,64]{2,1,0:T(8,128)S(1)} %get-tuple-element.46), custom_call_target="InvertDiagBlocksLowerTriangular" | custom-call | tf_op jit(solution)/shard_map/triangular_solve | solution.py:238
  117.4 0.8 multiply_reduce_fusion.2
  118.2 0.2 multiply_reduce_fusion.1
  118.4 3.5 %fusion.1 = f32[32,1024]{1,0:T(8,128)S(1)} fusion(bf16[64,32,1024]{2,0,1:T(8,128)(2,1)} %copy-done, f32[64]{0:T(128)S(1)} %get-tuple-element.65), kind=kLoop, calls=%fused_computation.7 | loop fusion | flops 6258688 | bytes 4325632 | tf_op jit(solution)/shard_map/reduce_sum | solution.py:276
  123.3 0.7 fusion.5.last_ref
  124.1 0.2 scatter.11
  124.3 0.1 scatter.14
  124.4 0.7 copy.15
  125.1 2.2 %copy-done.1 = bf16[64,32,1024]{2,0,1:T(8,128)(2,1)S(1)} copy-done((bf16[64,32,1024]{2,0,1:T(8,128)(2,1)S(1)}, bf16[64,32,1024]{2,0,1:T(8,128)(2,1)}, u32[]{:S(2)}) %copy-start.1) | copy-done | bytes 4194328
  127.3 7.5 %shard_map.98._ = f32[65,32,1024]{2,1,0:T(8,128)} custom-call(bf16[3,65,64]{2,1,0:T(8,128)(2,1)S(1)} %pad_maximum_fusion.6.mix_ref, bf16[32,64,1024]{2,1,0:T(8,128)(2,1)S(1)} %bitcast.57), custom_call_target="tpu_custom_call" | custom-call | flops 817889280 | bytes 12713984 | tf_op jit(solution)/shard_map/pallas_call | solution.py:202
  134.8 1.6 %shard_map.99 = f32[65,32,1024]{2,1,0:T(8,128)} custom-call(f32[65,32,1024]{2,1,0:T(8,128)} %shard_map.98._, f32[1,32,1024]{2,1,0:T(8,128)} %fusion.5.last_ref), custom_call_target="tpu_custom_call", output_to_operand_aliasing={{}: (0, {})} | custom-call | tf_op jit(solution)/shard_map/pallas_call | solution.py:47
  136.4 3.8 %select_maximum_fusion.2.conc_ref = f32[3,68,36,128]{3,2,1,0:T(8,128)} fusion(f32[3,64,2,128]{3,2,1,0:T(2,128)} %collective-permute-done.11, f32[3,64,2,128]{3,2,1,0:T(2,128)} %collective-permute-done.8, f32[3,2,32,128]{3,2,1,0:T(8,128)} %collective-permute-done.10, f32[3,64,32,128]{3,2,1,0:T(8,128)S(1)} %shard_map.96, ...), kind=kLoop, calls=%fused_computation.9 | loop fusion | flops 7520256 | bytes 7495680 | tf_op jit(solution)/shard_map/concatenate | solution.py:28
  140.2 11.6 %shard_map.97 = f32[3,64,32,128]{3,2,1,0:T(8,128)S(1)} custom-call(f32[3]{0:T(128)S(1)} %slice.132.scale_ref, f32[3,68,36,128]{3,2,1,0:T(8,128)} %select_maximum_fusion.2.conc_ref, f32[8,68,36,128]{3,2,1,0:T(8,128)} %select_maximum_fusion.conc_ref.coeff_ref), custom_call_target="tpu_custom_call" | custom-call | flops 62914560 | bytes 12533760 | tf_op jit(solution)/shard_map/pallas_call | solution.py:164
  151.9 2.5 %pad_maximum_fusion = f32[4,64,32,128]{3,2,1,0:T(8,128)} fusion(f32[3,64,32,128]{3,2,1,0:T(8,128)S(1)} %shard_map.97, f32[1,64,32,128]{3,2,1,0:T(8,128)S(1)} %copy-done.3), kind=kLoop, calls=%fused_computation.8 | loop fusion | flops 1048576 | bytes 8388608 | tf_op jit(solution)/shard_map/concatenate | solution.py:264
  (73 shorter events, 1.0 us)
Async XLA Ops:
  0.6 9.3 %copy-start.5 = (f32[4,64,32,128]{3,2,1,0:T(8,128)S(1)}, f32[4,64,32,128]{3,2,1,0:T(8,128)}, u32[]{:S(2)}) copy-start(f32[4,64,32,128]{3,2,1,0:T(8,128)} %param.13) | copy-start | bytes 12582916
  0.6 9.3 %copy-start.6 = (f32[3,64,32,128]{3,2,1,0:T(8,128)S(1)}, f32[3,64,32,128]{3,2,1,0:T(8,128)}, u32[]{:S(2)}) copy-start(f32[3,64,32,128]{3,2,1,0:T(8,128)} %param.14) | copy-start | bytes 9437188
  0.7 9.3 %copy-start.7 = (f32[64,32,128]{2,1,0:T(8,128)S(1)}, f32[64,32,128]{2,1,0:T(8,128)}, u32[]{:S(2)}) copy-start(f32[64,32,128]{2,1,0:T(8,128)} %param.15) | copy-start | bytes 3145732
  3.5 17.6 %collective-permute-start.3 = (f32[8,64,2,128]{3,2,1,0:T(2,128)S(1)}, f32[8,64,2,128]{3,2,1,0:T(2,128)S(1)}, u32[]{:S(2)}, u32[]{:S(2)}) collective-permute-start(f32[8,64,2,128]{3,2,1,0:T(2,128)S(1)} %get-tuple-element.51), channel_id=1, source_target_pairs={{1,0},{2,1},{3,2},{4,3},{5,4},{6,5},{7,6},{8,7},{9,8},{10,9},{11,1... | collective-permute-start | bytes 1572872 | tf_op jit(solution)/shard_map/ppermute | solution.py:25
  9.9 2.3 %copy-start.8 = (bf16[48,32,1024]{2,1,0:T(8,128)(2,1)S(1)}, bf16[48,32,1024]{2,1,0:T(8,128)(2,1)}, u32[]{:S(2)}) copy-start(bf16[48,32,1024]{2,1,0:T(8,128)(2,1)} %param.17) | copy-start | bytes 9437188
  9.9 16.7 %collective-permute-start = (f32[8,64,2,128]{3,2,1,0:T(2,128)S(1)}, f32[8,64,2,128]{3,2,1,0:T(2,128)S(1)}, u32[]{:S(2)}, u32[]{:S(2)}) collective-permute-start(f32[8,64,2,128]{3,2,1,0:T(2,128)S(1)} %get-tuple-element.50), channel_id=1, source_target_pairs={{0,1},{1,2},{2,3},{3,4},{4,5},{5,6},{6,7},{7,8},{8,9},{9,10},{10,1... | collective-permute-start | bytes 1572872 | tf_op jit(solution)/shard_map/ppermute | solution.py:24
  10.0 4.0 %copy-start.9 = (bf16[16,32,1024]{2,1,0:T(8,128)(2,1)S(1)}, bf16[16,32,1024]{2,1,0:T(8,128)(2,1)}, u32[]{:S(2)}) copy-start(bf16[16,32,1024]{2,1,0:T(8,128)(2,1)} %param.19) | copy-start | bytes 3145732
  10.0 6.6 %collective-permute-start.2 = (f32[8,2,32,128]{3,2,1,0:T(8,128)S(1)}, f32[8,2,32,128]{3,2,1,0:T(8,128)S(1)}, u32[]{:S(2)}, u32[]{:S(2)}) collective-permute-start(f32[8,2,32,128]{3,2,1,0:T(8,128)S(1)} %get-tuple-element.49), channel_id=1, source_target_pairs={{16,0},{32,16},{48,32},{64,48},{80,64},{96,80},{112,96},{0,112},{1... | collective-permute-start | bytes 786440 | tf_op jit(solution)/shard_map/ppermute | solution.py:23
  12.2 7.0 %collective-permute-start.1 = (f32[8,2,32,128]{3,2,1,0:T(8,128)S(1)}, f32[8,2,32,128]{3,2,1,0:T(8,128)S(1)}, u32[]{:S(2)}, u32[]{:S(2)}) collective-permute-start(f32[8,2,32,128]{3,2,1,0:T(8,128)S(1)} %get-tuple-element.48), channel_id=1, source_target_pairs={{0,16},{16,32},{32,48},{48,64},{64,80},{80,96},{96,112},{112,0},{1... | collective-permute-start | bytes 786440 | tf_op jit(solution)/shard_map/ppermute | solution.py:22
  14.5 2.0 %copy-start = (bf16[64,32,1024]{2,0,1:T(8,128)(2,1)}, bf16[64,32,1024]{2,0,1:T(8,128)(2,1)S(1)}, u32[]{:S(2)}) copy-start(bf16[64,32,1024]{2,0,1:T(8,128)(2,1)S(1)} %copy_dynamic-update-slice_fusion.1) | copy-start | bytes 12582916
  16.5 16.8 %copy-start.4 = (f32[4]{0:T(128)S(1)}, f32[4]{0:T(128)}, u32[]{:S(2)}) copy-start(f32[4]{0:T(128)} %param.16) | copy-start | bytes 52
  39.3 4.7 %collective-permute-start.12 = (f32[64,64]{1,0:T(8,128)S(1)}, f32[64,64]{1,0:T(8,128)S(1)}, u32[]{:S(2)}, u32[]{:S(2)}) collective-permute-start(f32[64,64]{1,0:T(8,128)S(1)} %convolution_bitcast_fusion.1), channel_id=1, source_target_pairs={{0,16},{16,0},{32,48},{48,32},{64,80},{80,64},{96,112},{112,96},{1... | collective-permute-start | bytes 49160 | tf_op jit(solution)/shard_map/ppermute | solution.py:37
  39.4 9.8 %collective-permute-start.7 = (f32[1,64,2,128]{3,2,1,0:T(2,128)S(1)}, f32[1,64,2,128]{3,2,1,0:T(2,128)S(1)}, u32[]{:S(2)}, u32[]{:S(2)}) collective-permute-start(f32[1,64,2,128]{3,2,1,0:T(2,128)S(1)} %get-tuple-element.59), channel_id=1, source_target_pairs={{1,0},{2,1},{3,2},{4,3},{5,4},{6,5},{7,6},{8,7},{9,8},{10,9},{11,1... | collective-permute-start | bytes 196616 | tf_op jit(solution)/shard_map/ppermute | solution.py:25
  39.8 9.5 %collective-permute-start.4 = (f32[1,64,2,128]{3,2,1,0:T(2,128)S(1)}, f32[1,64,2,128]{3,2,1,0:T(2,128)S(1)}, u32[]{:S(2)}, u32[]{:S(2)}) collective-permute-start(f32[1,64,2,128]{3,2,1,0:T(2,128)S(1)} %get-tuple-element.58), channel_id=1, source_target_pairs={{0,1},{1,2},{2,3},{3,4},{4,5},{5,6},{6,7},{7,8},{8,9},{9,10},{10,1... | collective-permute-start | bytes 196616 | tf_op jit(solution)/shard_map/ppermute | solution.py:24
  41.5 7.7 %collective-permute-start.6 = (f32[1,2,32,128]{3,2,1,0:T(8,128)S(1)}, f32[1,2,32,128]{3,2,1,0:T(8,128)S(1)}, u32[]{:S(2)}, u32[]{:S(2)}) collective-permute-start(f32[1,2,32,128]{3,2,1,0:T(8,128)S(1)} %get-tuple-element.57), channel_id=1, source_target_pairs={{16,0},{32,16},{48,32},{64,48},{80,64},{96,80},{112,96},{0,112},{1... | collective-permute-start | bytes 98312 | tf_op jit(solution)/shard_map/ppermute | solution.py:23
  44.0 5.2 %collective-permute-start.5 = (f32[1,2,32,128]{3,2,1,0:T(8,128)S(1)}, f32[1,2,32,128]{3,2,1,0:T(8,128)S(1)}, u32[]{:S(2)}, u32[]{:S(2)}) collective-permute-start(f32[1,2,32,128]{3,2,1,0:T(8,128)S(1)} %get-tuple-element.56), channel_id=1, source_target_pairs={{0,16},{16,32},{32,48},{48,64},{64,80},{80,96},{96,112},{112,0},{1... | collective-permute-start | bytes 98312 | tf_op jit(solution)/shard_map/ppermute | solution.py:22
  44.0 4.0 %collective-permute-start.13 = (f32[64,64]{1,0:T(8,128)S(1)}, f32[64,64]{1,0:T(8,128)S(1)}, u32[]{:S(2)}, u32[]{:S(2)}) collective-permute-start(f32[64,64]{1,0:T(8,128)S(1)} %add.79), channel_id=1, source_target_pairs={{0,32},{16,48},{32,0},{48,16},{64,96},{80,112},{96,64},{112,80},{1... | collective-permute-start | bytes 49160 | tf_op jit(solution)/shard_map/ppermute | solution.py:37
  48.0 14.2 %collective-permute-start.14 = (f32[64,64]{1,0:T(8,128)S(1)}, f32[64,64]{1,0:T(8,128)S(1)}, u32[]{:S(2)}, u32[]{:S(2)}) collective-permute-start(f32[64,64]{1,0:T(8,128)S(1)} %add.80), channel_id=1, source_target_pairs={{0,64},{16,80},{32,96},{48,112},{64,0},{80,16},{96,32},{112,48},{1... | collective-permute-start | bytes 49160 | tf_op jit(solution)/shard_map/ppermute | solution.py:37
  54.9 1.0 copy-start.2
  55.9 9.0 %copy-start.11 = (f32[48]{0:T(128)S(1)}, f32[48]{0:T(128)}, u32[]{:S(2)}) copy-start(f32[48]{0:T(128)} %param.18) | copy-start | bytes 580
  61.4 1.6 %collective-permute-start.19 = (f32[65]{0:T(128)S(1)}, f32[65]{0:T(128)S(1)}, u32[]{:S(2)}, u32[]{:S(2)}) collective-permute-start(f32[65]{0:T(128)S(1)} %pad_maximum_fusion.7), channel_id=1, source_target_pairs={{0,16},{16,0},{32,48},{48,32},{64,80},{80,64},{96,112},{112,96},{1... | collective-permute-start | bytes 788 | tf_op jit(solution)/shard_map/ppermute | solution.py:37
  62.2 18.6 %collective-permute-start.15 = (f32[64,64]{1,0:T(8,128)S(1)}, f32[64,64]{1,0:T(8,128)S(1)}, u32[]{:S(2)}, u32[]{:S(2)}) collective-permute-start(f32[64,64]{1,0:T(8,128)S(1)} %add.81), channel_id=1, source_target_pairs={{0,1},{1,0},{2,3},{3,2},{4,5},{5,4},{6,7},{7,6},{8,9},{9,8},{10,11... | collective-permute-start | bytes 49160 | tf_op jit(solution)/shard_map/ppermute | solution.py:37
  63.7 3.6 %collective-permute-start.20 = (f32[65]{0:T(128)S(1)}, f32[65]{0:T(128)S(1)}, u32[]{:S(2)}, u32[]{:S(2)}) collective-permute-start(f32[65]{0:T(128)S(1)} %fusion.32), channel_id=1, source_target_pairs={{0,32},{16,48},{32,0},{48,16},{64,96},{80,112},{96,64},{112,80},{1... | collective-permute-start | bytes 788 | tf_op jit(solution)/shard_map/ppermute | solution.py:37
  67.3 13.6 %collective-permute-start.21 = (f32[65]{0:T(128)S(1)}, f32[65]{0:T(128)S(1)}, u32[]{:S(2)}, u32[]{:S(2)}) collective-permute-start(f32[65]{0:T(128)S(1)} %add.88), channel_id=1, source_target_pairs={{0,64},{16,80},{32,96},{48,112},{64,0},{80,16},{96,32},{112,48},{1... | collective-permute-start | bytes 788 | tf_op jit(solution)/shard_map/ppermute | solution.py:37
  80.8 7.2 %collective-permute-start.16 = (f32[64,64]{1,0:T(8,128)S(1)}, f32[64,64]{1,0:T(8,128)S(1)}, u32[]{:S(2)}, u32[]{:S(2)}) collective-permute-start(f32[64,64]{1,0:T(8,128)S(1)} %add.82), channel_id=1, source_target_pairs={{0,2},{1,3},{2,0},{3,1},{4,6},{5,7},{6,4},{7,5},{8,10},{9,11},{10,... | collective-permute-start | bytes 49160 | tf_op jit(solution)/shard_map/ppermute | solution.py:37
  80.9 3.6 %collective-permute-start.22 = (f32[65]{0:T(128)S(1)}, f32[65]{0:T(128)S(1)}, u32[]{:S(2)}, u32[]{:S(2)}) collective-permute-start(f32[65]{0:T(128)S(1)} %add.89), channel_id=1, source_target_pairs={{0,1},{1,0},{2,3},{3,2},{4,5},{5,4},{6,7},{7,6},{8,9},{9,8},{10,11... | collective-permute-start | bytes 788 | tf_op jit(solution)/shard_map/ppermute | solution.py:37
  84.6 5.1 %collective-permute-start.23 = (f32[65]{0:T(128)S(1)}, f32[65]{0:T(128)S(1)}, u32[]{:S(2)}, u32[]{:S(2)}) collective-permute-start(f32[65]{0:T(128)S(1)} %add.90), channel_id=1, source_target_pairs={{0,2},{1,3},{2,0},{3,1},{4,6},{5,7},{6,4},{7,5},{8,10},{9,11},{10,... | collective-permute-start | bytes 788 | tf_op jit(solution)/shard_map/ppermute | solution.py:37
  88.0 10.6 %collective-permute-start.17 = (f32[64,64]{1,0:T(8,128)S(1)}, f32[64,64]{1,0:T(8,128)S(1)}, u32[]{:S(2)}, u32[]{:S(2)}) collective-permute-start(f32[64,64]{1,0:T(8,128)S(1)} %add.83), channel_id=1, source_target_pairs={{0,4},{1,5},{2,6},{3,7},{4,0},{5,1},{6,2},{7,3},{8,12},{9,13},{10,... | collective-permute-start | bytes 49160 | tf_op jit(solution)/shard_map/ppermute | solution.py:37
  89.7 4.9 %collective-permute-start.24 = (f32[65]{0:T(128)S(1)}, f32[65]{0:T(128)S(1)}, u32[]{:S(2)}, u32[]{:S(2)}) collective-permute-start(f32[65]{0:T(128)S(1)} %add.91), channel_id=1, source_target_pairs={{0,4},{1,5},{2,6},{3,7},{4,0},{5,1},{6,2},{7,3},{8,12},{9,13},{10,... | collective-permute-start | bytes 788 | tf_op jit(solution)/shard_map/ppermute | solution.py:37
  90.9 45.5 %collective-permute-start.11 = (f32[3,64,2,128]{3,2,1,0:T(2,128)}, f32[3,64,2,128]{3,2,1,0:T(2,128)}, u32[]{:S(2)}, u32[]{:S(2)}) collective-permute-start(f32[3,64,2,128]{3,2,1,0:T(2,128)} %get-tuple-element.55), channel_id=1, source_target_pairs={{1,0},{2,1},{3,2},{4,3},{5,4},{6,5},{7,6},{8,7},{9,8},{10,9},{11,1... | collective-permute-start | bytes 589832 | tf_op jit(solution)/shard_map/ppermute | solution.py:25
  94.5 41.9 %collective-permute-start.8 = (f32[3,64,2,128]{3,2,1,0:T(2,128)}, f32[3,64,2,128]{3,2,1,0:T(2,128)}, u32[]{:S(2)}, u32[]{:S(2)}) collective-permute-start(f32[3,64,2,128]{3,2,1,0:T(2,128)} %get-tuple-element.54), channel_id=1, source_target_pairs={{0,1},{1,2},{2,3},{3,4},{4,5},{5,6},{6,7},{7,8},{8,9},{9,10},{10,1... | collective-permute-start | bytes 589832 | tf_op jit(solution)/shard_map/ppermute | solution.py:24
  94.5 41.8 %collective-permute-start.10 = (f32[3,2,32,128]{3,2,1,0:T(8,128)}, f32[3,2,32,128]{3,2,1,0:T(8,128)}, u32[]{:S(2)}, u32[]{:S(2)}) collective-permute-start(f32[3,2,32,128]{3,2,1,0:T(8,128)} %get-tuple-element.53), channel_id=1, source_target_pairs={{16,0},{32,16},{48,32},{64,48},{80,64},{96,80},{112,96},{0,112},{1... | collective-permute-start | bytes 294920 | tf_op jit(solution)/shard_map/ppermute | solution.py:23
  94.6 5.2 %collective-permute-start.25 = (f32[65]{0:T(128)S(1)}, f32[65]{0:T(128)S(1)}, u32[]{:S(2)}, u32[]{:S(2)}) collective-permute-start(f32[65]{0:T(128)S(1)} %add.92), channel_id=1, source_target_pairs={{0,8},{1,9},{2,10},{3,11},{4,12},{5,13},{6,14},{7,15},{8,0},{9,1},... | collective-permute-start | bytes 788 | tf_op jit(solution)/shard_map/ppermute | solution.py:37
  98.6 24.7 %copy-start.10 = (f32[1,32,1024]{2,1,0:T(8,128)S(1)}, f32[1,32,1024]{2,1,0:T(8,128)}, u32[]{:S(2)}) copy-start(f32[1,32,1024]{2,1,0:T(8,128)} %reshape.146) | copy-start | bytes 393220
  98.6 37.8 %collective-permute-start.9 = (f32[3,2,32,128]{3,2,1,0:T(8,128)}, f32[3,2,32,128]{3,2,1,0:T(8,128)}, u32[]{:S(2)}, u32[]{:S(2)}) collective-permute-start(f32[3,2,32,128]{3,2,1,0:T(8,128)} %get-tuple-element.52), channel_id=1, source_target_pairs={{0,16},{16,32},{32,48},{48,64},{64,80},{80,96},{96,112},{112,0},{1... | collective-permute-start | bytes 294920 | tf_op jit(solution)/shard_map/ppermute | solution.py:22
  99.7 5.4 %collective-permute-start.18 = (f32[64,64]{1,0:T(8,128)S(1)}, f32[64,64]{1,0:T(8,128)S(1)}, u32[]{:S(2)}, u32[]{:S(2)}) collective-permute-start(f32[64,64]{1,0:T(8,128)S(1)} %add.84), channel_id=1, source_target_pairs={{0,8},{1,9},{2,10},{3,11},{4,12},{5,13},{6,14},{7,15},{8,0},{9,1},... | collective-permute-start | bytes 49160 | tf_op jit(solution)/shard_map/ppermute | solution.py:37
  125.1 2.2 %copy-start.1 = (bf16[64,32,1024]{2,0,1:T(8,128)(2,1)S(1)}, bf16[64,32,1024]{2,0,1:T(8,128)(2,1)}, u32[]{:S(2)}) copy-start(bf16[64,32,1024]{2,0,1:T(8,128)(2,1)} %copy-done) | copy-start | bytes 12582916
  140.2 11.7 %copy-start.3 = (f32[1,64,32,128]{3,2,1,0:T(8,128)S(1)}, f32[1,64,32,128]{3,2,1,0:T(8,128)}, u32[]{:S(2)}) copy-start(f32[1,64,32,128]{3,2,1,0:T(8,128)} %copy-done.2) | copy-start | bytes 3145732

commit v12 on v11

--- a/solution.py
+++ b/solution.py
@@ -198,7 +198,7 @@
     xt = jnp.transpose(static, (1, 0, 2))
     span, width, cols = xt.shape
     rows = mix_ext.shape[0]
-    block = 8
+    block = 16
     return pl.pallas_call(
         basis_body,
         out_shape=jax.ShapeDtypeStruct((rows, span, cols), jnp.float32),

time: 155 us -> 155 us (level)
  transfers between devices with their start and end apart: 26 -> 26, of which waited for: 10 -> 10; matrix products, arithmetic and copies ran while one was open for 21% -> 20% of each run, Pallas kernels for 17% -> 17%
where the time goes in v12:
time: 155 us
  Pallas kernels  44.1 us (28%)
  other arithmetic  37.3 us (24%)
  starting transfers between devices  34.5 us (22%)
  waiting for transfers between devices  22.2 us (14%)
  local copies, waits for them, and re-layouts  10.7 us (7%)
  matrix products  3.54 us (2%)
  between operations  2.4 us (2%)
    pallas_call x4, Pallas kernels, stencil_step(): pl.pallas_call(stencil_body, out_shape=jax.ShapeDtypeStruct((count, nx, n...  34.5 us
    ppermute x14, starting transfers between devices, butterfly_sum(): value = value + lax.ppermute(value, axis, pairs)  17.5 us
    ppermute x14, waiting for transfers between devices, butterfly_sum(): value = value + lax.ppermute(value, axis, pairs)  12.2 us
    concatenate x3, other arithmetic, halo(): jnp.concatenate([jnp.pad(low_y, edge), rows, jnp.pad(high_y, edge)], axis=2)  10.8 us
    ppermute x3, starting transfers between devices, halo(): high_y = lax.ppermute(block[:, :, :width], 'gy', by)  10.4 us
    pallas_call x1, Pallas kernels, basis_rows(): pl.pallas_call(basis_body, out_shape=jax.ShapeDtypeStruct((rows, span, co...  8.04 us
    another operation x3, other arithmetic, per_device(): lower_static = jnp.linalg.cholesky(gram_static)  6.52 us
    unnamed x26, local copies, waits for them, and re-layouts  6.42 us
  transfers between devices with their start and end apart: 26, of which 10 were waited for; matrix products, arithmetic and copies ran while one was open for 20% of the time, Pallas kernels for 17%

profile of v12, /device:TPU:0, one launch (start us, length us, event | category | flops | bytes accessed | tf_op | source)
XLA Modules:
  0.0 154.8 jit_solution(11241202731963490140)
XLA Ops:
  0.7 2.8 %pad_maximum_fusion.3 = (f32[8,64,2,128]{3,2,1,0:T(2,128)S(1)}, f32[8,64,2,128]{3,2,1,0:T(2,128)S(1)}) fusion(f32[1,64,32,128]{3,2,1,0:T(8,128)} %bitcast.60, f32[3,64,32,128]{3,2,1,0:T(8,128)} %param.14, f32[4,64,32,128]{3,2,1,0:T(8,128)} %param.13), kind=kLoop, calls=%fused_computation.24 | loop fusion | flops 524288 | bytes 9437184 | tf_op jit(solution)/shard_map/slice | solution.py:24
  3.5 6.4 %collective-permute-start.3 = (f32[8,64,2,128]{3,2,1,0:T(2,128)S(1)}, f32[8,64,2,128]{3,2,1,0:T(2,128)S(1)}, u32[]{:S(2)}, u32[]{:S(2)}) collective-permute-start(f32[8,64,2,128]{3,2,1,0:T(2,128)S(1)} %get-tuple-element.51), channel_id=1, source_target_pairs={{1,0},{2,1},{3,2},{4,3},{5,4},{6,5},{7,6},{8,7},{9,8},{10,9},{11,1... | collective-permute-start | bytes 1572872 | tf_op jit(solution)/shard_map/ppermute | solution.py:25
  10.0 2.2 %collective-permute-start.2 = (f32[8,2,32,128]{3,2,1,0:T(8,128)S(1)}, f32[8,2,32,128]{3,2,1,0:T(8,128)S(1)}, u32[]{:S(2)}, u32[]{:S(2)}) collective-permute-start(f32[8,2,32,128]{3,2,1,0:T(8,128)S(1)} %get-tuple-element.49), channel_id=1, source_target_pairs={{16,0},{32,16},{48,32},{64,48},{80,64},{96,80},{112,96},{0,112},{1... | collective-permute-start | bytes 786440 | tf_op jit(solution)/shard_map/ppermute | solution.py:23
  12.2 1.7 %copy_dynamic-update-slice_fusion = bf16[64,32,1024]{2,0,1:T(8,128)(2,1)S(1)} fusion(bf16[48,32,1024]{2,1,0:T(8,128)(2,1)S(1)} %copy-done.8), kind=kLoop, calls=%fused_computation.13 | loop fusion | bytes 6291456
  13.9 0.6 copy_dynamic-update-slice_fusion.1
  14.5 1.2 convolution_bitcast_fusion.1
  15.8 0.8 copy-done
  16.5 2.6 %collective-permute-done.1 = f32[8,2,32,128]{3,2,1,0:T(8,128)S(1)} collective-permute-done((f32[8,2,32,128]{3,2,1,0:T(8,128)S(1)}, f32[8,2,32,128]{3,2,1,0:T(8,128)S(1)}, u32[]{:S(2)}, u32[]{:S(2)}) %collective-permute-start.1) | collective-permute-done | bytes 262176 | tf_op jit(solution)/shard_map/ppermute | solution.py:22
  19.2 1.9 %collective-permute-done.3 = f32[8,64,2,128]{3,2,1,0:T(2,128)S(1)} collective-permute-done((f32[8,64,2,128]{3,2,1,0:T(2,128)S(1)}, f32[8,64,2,128]{3,2,1,0:T(2,128)S(1)}, u32[]{:S(2)}, u32[]{:S(2)}) %collective-permute-start.3) | collective-permute-done | bytes 524320 | tf_op jit(solution)/shard_map/ppermute | solution.py:25
  21.1 5.5 %collective-permute-done = f32[8,64,2,128]{3,2,1,0:T(2,128)S(1)} collective-permute-done((f32[8,64,2,128]{3,2,1,0:T(2,128)S(1)}, f32[8,64,2,128]{3,2,1,0:T(2,128)S(1)}, u32[]{:S(2)}, u32[]{:S(2)}) %collective-permute-start) | collective-permute-done | bytes 524320 | tf_op jit(solution)/shard_map/ppermute | solution.py:24
  26.6 6.8 %select_maximum_fusion.conc_ref.coeff_ref = f32[8,68,36,128]{3,2,1,0:T(8,128)} fusion(f32[8,64,2,128]{3,2,1,0:T(2,128)S(1)} %collective-permute-done.3, f32[8,64,2,128]{3,2,1,0:T(2,128)S(1)} %collective-permute-done, f32[8,2,32,128]{3,2,1,0:T(8,128)S(1)} %collective-permute-done.2, f32[1,64,32,128]{3,2,1,0:T(8,128)S(1)} %bitcast.62, ...), kind=kLoop, calls=%fused_computation | loop fusion | flops 25067520 | bytes 19988480 | tf_op jit(solution)/shard_map/concatenate | solution.py:28
  33.4 5.9 %shard_map.94 = f32[1,64,32,128]{3,2,1,0:T(8,128)S(1)} custom-call(f32[1]{0:T(128)S(1)} %bitcast.58, f32[8,68,36,128]{3,2,1,0:T(8,128)} %select_maximum_fusion.conc_ref.coeff_ref, f32[8,68,36,128]{3,2,1,0:T(8,128)} %select_maximum_fusion.conc_ref.coeff_ref), custom_call_target="tpu_custom_call" | custom-call | flops 20971520 | bytes 7520256 | tf_op jit(solution)/shard_map/pallas_call | solution.py:164
  39.4 0.3 collective-permute-start.7
  39.8 1.7 %collective-permute-start.4 = (f32[1,64,2,128]{3,2,1,0:T(2,128)S(1)}, f32[1,64,2,128]{3,2,1,0:T(2,128)S(1)}, u32[]{:S(2)}, u32[]{:S(2)}) collective-permute-start(f32[1,64,2,128]{3,2,1,0:T(2,128)S(1)} %get-tuple-element.58), channel_id=1, source_target_pairs={{0,1},{1,2},{2,3},{3,4},{4,5},{5,6},{6,7},{7,8},{8,9},{9,10},{10,1... | collective-permute-start | bytes 196616 | tf_op jit(solution)/shard_map/ppermute | solution.py:24
  41.5 2.5 %collective-permute-start.6 = (f32[1,2,32,128]{3,2,1,0:T(8,128)S(1)}, f32[1,2,32,128]{3,2,1,0:T(8,128)S(1)}, u32[]{:S(2)}, u32[]{:S(2)}) collective-permute-start(f32[1,2,32,128]{3,2,1,0:T(8,128)S(1)} %get-tuple-element.57), channel_id=1, source_target_pairs={{16,0},{32,16},{48,32},{64,48},{80,64},{96,80},{112,96},{0,112},{1... | collective-permute-start | bytes 98312 | tf_op jit(solution)/shard_map/ppermute | solution.py:23
  44.1 3.9 %collective-permute-done.13 = f32[64,64]{1,0:T(8,128)S(1)} collective-permute-done((f32[64,64]{1,0:T(8,128)S(1)}, f32[64,64]{1,0:T(8,128)S(1)}, u32[]{:S(2)}, u32[]{:S(2)}) %collective-permute-start.13) | collective-permute-done | bytes 16416 | tf_op jit(solution)/shard_map/ppermute | solution.py:37
  48.0 1.2 collective-permute-start.14
  49.2 0.2 select_maximum_fusion.4.conc_ref
  49.5 5.4 %shard_map.95 = f32[1,64,32,128]{3,2,1,0:T(8,128)S(1)} custom-call(f32[1]{0:T(128)S(1)} %bitcast.59, f32[1,68,36,128]{3,2,1,0:T(8,128)S(1)} %select_maximum_fusion.4.conc_ref, f32[8,68,36,128]{3,2,1,0:T(8,128)} %select_maximum_fusion.conc_ref.coeff_ref), custom_call_target="tpu_custom_call" | custom-call | flops 20971520 | bytes 7520256 | tf_op jit(solution)/shard_map/pallas_call | solution.py:164
  54.9 1.0 copy-done.2
  55.9 0.4 fusion.2
  56.3 0.9 multiply_reduce_fusion
  57.2 0.1 mul.85
  57.4 3.3 %fusion = f32[64]{0:T(128)S(1)} fusion(bf16[64,32,1024]{2,0,1:T(8,128)(2,1)} %copy-done, f32[32,1024]{1,0:T(8,128)S(1)} %mul.85), kind=kLoop, calls=%fused_computation.6 | loop fusion | flops 6291392 | bytes 4325632 | tf_op jit(solution)/shard_map/reduce_sum | solution.py:256
  60.7 0.7 pad_maximum_fusion.7
  61.4 0.7 collective-permute-start.19
  62.2 0.7 collective-permute-done.19
  63.0 0.7 fusion.32
  63.7 1.1 collective-permute-start.20
  64.9 2.4 %collective-permute-done.20 = f32[65]{0:T(128)S(1)} collective-permute-done((f32[65]{0:T(128)S(1)}, f32[65]{0:T(128)S(1)}, u32[]{:S(2)}, u32[]{:S(2)}) %collective-permute-start.20) | collective-permute-done | bytes 292 | tf_op jit(solution)/shard_map/ppermute | solution.py:37
  67.3 1.9 %collective-permute-start.21 = (f32[65]{0:T(128)S(1)}, f32[65]{0:T(128)S(1)}, u32[]{:S(2)}, u32[]{:S(2)}) collective-permute-start(f32[65]{0:T(128)S(1)} %add.88), channel_id=1, source_target_pairs={{0,64},{16,80},{32,96},{48,112},{64,0},{80,16},{96,32},{112,48},{1... | collective-permute-start | bytes 788 | tf_op jit(solution)/shard_map/ppermute | solution.py:37
  69.2 11.6 %shard_map.96 = f32[3,64,32,128]{3,2,1,0:T(8,128)S(1)} custom-call(f32[3]{0:T(128)S(1)} %slice.132.scale_ref, f32[8,68,36,128]{3,2,1,0:T(8,128)} %select_maximum_fusion.conc_ref.coeff_ref, f32[8,68,36,128]{3,2,1,0:T(8,128)} %select_maximum_fusion.conc_ref.coeff_ref), custom_call_target="tpu_custom_call" | custom-call | flops 62914560 | bytes 12533760 | tf_op jit(solution)/shard_map/pallas_call | solution.py:164
  80.9 1.1 collective-permute-start.22
  82.0 0.9 fusion.25
  82.9 1.7 %collective-permute-done.22 = f32[65]{0:T(128)S(1)} collective-permute-done((f32[65]{0:T(128)S(1)}, f32[65]{0:T(128)S(1)}, u32[]{:S(2)}, u32[]{:S(2)}) %collective-permute-start.22) | collective-permute-done | bytes 292 | tf_op jit(solution)/shard_map/ppermute | solution.py:37
  84.6 3.4 %collective-permute-start.23 = (f32[65]{0:T(128)S(1)}, f32[65]{0:T(128)S(1)}, u32[]{:S(2)}, u32[]{:S(2)}) collective-permute-start(f32[65]{0:T(128)S(1)} %add.90), channel_id=1, source_target_pairs={{0,2},{1,3},{2,0},{3,1},{4,6},{5,7},{6,4},{7,5},{8,10},{9,11},{10,... | collective-permute-start | bytes 788 | tf_op jit(solution)/shard_map/ppermute | solution.py:37
  88.1 0.7 fusion.24
  88.8 0.9 collective-permute-done.23
  89.7 1.2 collective-permute-start.24
  90.9 3.7 %collective-permute-start.11 = (f32[3,64,2,128]{3,2,1,0:T(2,128)}, f32[3,64,2,128]{3,2,1,0:T(2,128)}, u32[]{:S(2)}, u32[]{:S(2)}) collective-permute-start(f32[3,64,2,128]{3,2,1,0:T(2,128)} %get-tuple-element.55), channel_id=1, source_target_pairs={{1,0},{2,1},{3,2},{4,3},{5,4},{6,5},{7,6},{8,7},{9,8},{10,9},{11,1... | collective-permute-start | bytes 589832 | tf_op jit(solution)/shard_map/ppermute | solution.py:25
  94.6 3.2 %collective-permute-start.25 = (f32[65]{0:T(128)S(1)}, f32[65]{0:T(128)S(1)}, u32[]{:S(2)}, u32[]{:S(2)}) collective-permute-start(f32[65]{0:T(128)S(1)} %add.92), channel_id=1, source_target_pairs={{0,8},{1,9},{2,10},{3,11},{4,12},{5,13},{6,14},{7,15},{8,0},{9,1},... | collective-permute-start | bytes 788 | tf_op jit(solution)/shard_map/ppermute | solution.py:37
  97.8 0.8 reshape.146
  98.6 0.1 collective-permute-start.9
  98.7 1.0 collective-permute-done.25
  99.7 3.1 %collective-permute-start.18 = (f32[64,64]{1,0:T(8,128)S(1)}, f32[64,64]{1,0:T(8,128)S(1)}, u32[]{:S(2)}, u32[]{:S(2)}) collective-permute-start(f32[64,64]{1,0:T(8,128)S(1)} %add.84), channel_id=1, source_target_pairs={{0,8},{1,9},{2,10},{3,11},{4,12},{5,13},{6,14},{7,15},{8,0},{9,1},... | collective-permute-start | bytes 49160 | tf_op jit(solution)/shard_map/ppermute | solution.py:37
  102.9 0.6 slice.139
  103.5 1.6 %collective-permute-done.18 = f32[64,64]{1,0:T(8,128)S(1)} collective-permute-done((f32[64,64]{1,0:T(8,128)S(1)}, f32[64,64]{1,0:T(8,128)S(1)}, u32[]{:S(2)}, u32[]{:S(2)}) %collective-permute-start.18) | collective-permute-done | bytes 16416 | tf_op jit(solution)/shard_map/ppermute | solution.py:37
  105.3 5.8 %cholesky.17 = f32[64,64]{1,0:T(8,128)S(1)} custom-call(f32[64,64]{1,0:T(8,128)S(1)} %fusion.12), custom_call_target="Cholesky" | custom-call | tf_op jit(solution)/shard_map/jit(cholesky)/cholesky | solution.py:236
  111.2 0.6 compare_reduce_fusion
  111.8 0.7 select_bitcast_fusion
  112.5 4.9 %custom-call.8 = f32[1,64,64]{1,2,0:T(8,128)S(1)} custom-call(f32[1,64,64]{2,1,0:T(8,128)S(1)} %get-tuple-element.46), custom_call_target="InvertDiagBlocksLowerTriangular" | custom-call | tf_op jit(solution)/shard_map/triangular_solve | solution.py:238
  117.4 0.8 multiply_reduce_fusion.2
  118.2 0.2 multiply_reduce_fusion.1
  118.4 3.5 %fusion.1 = f32[32,1024]{1,0:T(8,128)S(1)} fusion(bf16[64,32,1024]{2,0,1:T(8,128)(2,1)} %copy-done, f32[64]{0:T(128)S(1)} %get-tuple-element.65), kind=kLoop, calls=%fused_computation.7 | loop fusion | flops 6258688 | bytes 4325632 | tf_op jit(solution)/shard_map/reduce_sum | solution.py:276
  123.3 0.7 fusion.5.last_ref
  124.1 0.2 scatter.11
  124.3 0.1 scatter.14
  124.4 0.7 copy.15
  125.1 2.2 %copy-done.1 = bf16[64,32,1024]{2,0,1:T(8,128)(2,1)S(1)} copy-done((bf16[64,32,1024]{2,0,1:T(8,128)(2,1)S(1)}, bf16[64,32,1024]{2,0,1:T(8,128)(2,1)}, u32[]{:S(2)}) %copy-start.1) | copy-done | bytes 4194328
  127.3 8.0 %shard_map.98._ = f32[65,32,1024]{2,1,0:T(8,128)} custom-call(bf16[3,65,64]{2,1,0:T(8,128)(2,1)S(1)} %pad_maximum_fusion.6.mix_ref, bf16[32,64,1024]{2,1,0:T(8,128)(2,1)S(1)} %bitcast.57), custom_call_target="tpu_custom_call" | custom-call | flops 817889280 | bytes 12713984 | tf_op jit(solution)/shard_map/pallas_call | solution.py:202
  135.3 1.6 %shard_map.99 = f32[65,32,1024]{2,1,0:T(8,128)} custom-call(f32[65,32,1024]{2,1,0:T(8,128)} %shard_map.98._, f32[1,32,1024]{2,1,0:T(8,128)} %fusion.5.last_ref), custom_call_target="tpu_custom_call", output_to_operand_aliasing={{}: (0, {})} | custom-call | tf_op jit(solution)/shard_map/pallas_call | solution.py:47
  136.9 3.8 %select_maximum_fusion.2.conc_ref = f32[3,68,36,128]{3,2,1,0:T(8,128)} fusion(f32[3,64,2,128]{3,2,1,0:T(2,128)} %collective-permute-done.11, f32[3,64,2,128]{3,2,1,0:T(2,128)} %collective-permute-done.8, f32[3,2,32,128]{3,2,1,0:T(8,128)} %collective-permute-done.10, f32[3,64,32,128]{3,2,1,0:T(8,128)S(1)} %shard_map.96, ...), kind=kLoop, calls=%fused_computation.9 | loop fusion | flops 7520256 | bytes 7495680 | tf_op jit(solution)/shard_map/concatenate | solution.py:28
  140.7 11.6 %shard_map.97 = f32[3,64,32,128]{3,2,1,0:T(8,128)S(1)} custom-call(f32[3]{0:T(128)S(1)} %slice.132.scale_ref, f32[3,68,36,128]{3,2,1,0:T(8,128)} %select_maximum_fusion.2.conc_ref, f32[8,68,36,128]{3,2,1,0:T(8,128)} %select_maximum_fusion.conc_ref.coeff_ref), custom_call_target="tpu_custom_call" | custom-call | flops 62914560 | bytes 12533760 | tf_op jit(solution)/shard_map/pallas_call | solution.py:164
  152.4 2.5 %pad_maximum_fusion = f32[4,64,32,128]{3,2,1,0:T(8,128)} fusion(f32[3,64,32,128]{3,2,1,0:T(8,128)S(1)} %shard_map.97, f32[1,64,32,128]{3,2,1,0:T(8,128)S(1)} %copy-done.3), kind=kLoop, calls=%fused_computation.8 | loop fusion | flops 1048576 | bytes 8388608 | tf_op jit(solution)/shard_map/concatenate | solution.py:264
  (73 shorter events, 1.0 us)
Async XLA Ops:
  0.6 9.3 %copy-start.5 = (f32[4,64,32,128]{3,2,1,0:T(8,128)S(1)}, f32[4,64,32,128]{3,2,1,0:T(8,128)}, u32[]{:S(2)}) copy-start(f32[4,64,32,128]{3,2,1,0:T(8,128)} %param.13) | copy-start | bytes 12582916
  0.6 9.3 %copy-start.6 = (f32[3,64,32,128]{3,2,1,0:T(8,128)S(1)}, f32[3,64,32,128]{3,2,1,0:T(8,128)}, u32[]{:S(2)}) copy-start(f32[3,64,32,128]{3,2,1,0:T(8,128)} %param.14) | copy-start | bytes 9437188
  0.7 9.3 %copy-start.7 = (f32[64,32,128]{2,1,0:T(8,128)S(1)}, f32[64,32,128]{2,1,0:T(8,128)}, u32[]{:S(2)}) copy-start(f32[64,32,128]{2,1,0:T(8,128)} %param.15) | copy-start | bytes 3145732
  3.5 17.6 %collective-permute-start.3 = (f32[8,64,2,128]{3,2,1,0:T(2,128)S(1)}, f32[8,64,2,128]{3,2,1,0:T(2,128)S(1)}, u32[]{:S(2)}, u32[]{:S(2)}) collective-permute-start(f32[8,64,2,128]{3,2,1,0:T(2,128)S(1)} %get-tuple-element.51), channel_id=1, source_target_pairs={{1,0},{2,1},{3,2},{4,3},{5,4},{6,5},{7,6},{8,7},{9,8},{10,9},{11,1... | collective-permute-start | bytes 1572872 | tf_op jit(solution)/shard_map/ppermute | solution.py:25
  9.9 2.3 %copy-start.8 = (bf16[48,32,1024]{2,1,0:T(8,128)(2,1)S(1)}, bf16[48,32,1024]{2,1,0:T(8,128)(2,1)}, u32[]{:S(2)}) copy-start(bf16[48,32,1024]{2,1,0:T(8,128)(2,1)} %param.17) | copy-start | bytes 9437188
  9.9 16.7 %collective-permute-start = (f32[8,64,2,128]{3,2,1,0:T(2,128)S(1)}, f32[8,64,2,128]{3,2,1,0:T(2,128)S(1)}, u32[]{:S(2)}, u32[]{:S(2)}) collective-permute-start(f32[8,64,2,128]{3,2,1,0:T(2,128)S(1)} %get-tuple-element.50), channel_id=1, source_target_pairs={{0,1},{1,2},{2,3},{3,4},{4,5},{5,6},{6,7},{7,8},{8,9},{9,10},{10,1... | collective-permute-start | bytes 1572872 | tf_op jit(solution)/shard_map/ppermute | solution.py:24
  10.0 4.0 %copy-start.9 = (bf16[16,32,1024]{2,1,0:T(8,128)(2,1)S(1)}, bf16[16,32,1024]{2,1,0:T(8,128)(2,1)}, u32[]{:S(2)}) copy-start(bf16[16,32,1024]{2,1,0:T(8,128)(2,1)} %param.19) | copy-start | bytes 3145732
  10.0 6.6 %collective-permute-start.2 = (f32[8,2,32,128]{3,2,1,0:T(8,128)S(1)}, f32[8,2,32,128]{3,2,1,0:T(8,128)S(1)}, u32[]{:S(2)}, u32[]{:S(2)}) collective-permute-start(f32[8,2,32,128]{3,2,1,0:T(8,128)S(1)} %get-tuple-element.49), channel_id=1, source_target_pairs={{16,0},{32,16},{48,32},{64,48},{80,64},{96,80},{112,96},{0,112},{1... | collective-permute-start | bytes 786440 | tf_op jit(solution)/shard_map/ppermute | solution.py:23
  12.2 7.0 %collective-permute-start.1 = (f32[8,2,32,128]{3,2,1,0:T(8,128)S(1)}, f32[8,2,32,128]{3,2,1,0:T(8,128)S(1)}, u32[]{:S(2)}, u32[]{:S(2)}) collective-permute-start(f32[8,2,32,128]{3,2,1,0:T(8,128)S(1)} %get-tuple-element.48), channel_id=1, source_target_pairs={{0,16},{16,32},{32,48},{48,64},{64,80},{80,96},{96,112},{112,0},{1... | collective-permute-start | bytes 786440 | tf_op jit(solution)/shard_map/ppermute | solution.py:22
  14.5 2.0 %copy-start = (bf16[64,32,1024]{2,0,1:T(8,128)(2,1)}, bf16[64,32,1024]{2,0,1:T(8,128)(2,1)S(1)}, u32[]{:S(2)}) copy-start(bf16[64,32,1024]{2,0,1:T(8,128)(2,1)S(1)} %copy_dynamic-update-slice_fusion.1) | copy-start | bytes 12582916
  16.5 16.8 %copy-start.4 = (f32[4]{0:T(128)S(1)}, f32[4]{0:T(128)}, u32[]{:S(2)}) copy-start(f32[4]{0:T(128)} %param.16) | copy-start | bytes 52
  39.3 4.7 %collective-permute-start.12 = (f32[64,64]{1,0:T(8,128)S(1)}, f32[64,64]{1,0:T(8,128)S(1)}, u32[]{:S(2)}, u32[]{:S(2)}) collective-permute-start(f32[64,64]{1,0:T(8,128)S(1)} %convolution_bitcast_fusion.1), channel_id=1, source_target_pairs={{0,16},{16,0},{32,48},{48,32},{64,80},{80,64},{96,112},{112,96},{1... | collective-permute-start | bytes 49160 | tf_op jit(solution)/shard_map/ppermute | solution.py:37
  39.4 9.8 %collective-permute-start.7 = (f32[1,64,2,128]{3,2,1,0:T(2,128)S(1)}, f32[1,64,2,128]{3,2,1,0:T(2,128)S(1)}, u32[]{:S(2)}, u32[]{:S(2)}) collective-permute-start(f32[1,64,2,128]{3,2,1,0:T(2,128)S(1)} %get-tuple-element.59), channel_id=1, source_target_pairs={{1,0},{2,1},{3,2},{4,3},{5,4},{6,5},{7,6},{8,7},{9,8},{10,9},{11,1... | collective-permute-start | bytes 196616 | tf_op jit(solution)/shard_map/ppermute | solution.py:25
  39.8 9.5 %collective-permute-start.4 = (f32[1,64,2,128]{3,2,1,0:T(2,128)S(1)}, f32[1,64,2,128]{3,2,1,0:T(2,128)S(1)}, u32[]{:S(2)}, u32[]{:S(2)}) collective-permute-start(f32[1,64,2,128]{3,2,1,0:T(2,128)S(1)} %get-tuple-element.58), channel_id=1, source_target_pairs={{0,1},{1,2},{2,3},{3,4},{4,5},{5,6},{6,7},{7,8},{8,9},{9,10},{10,1... | collective-permute-start | bytes 196616 | tf_op jit(solution)/shard_map/ppermute | solution.py:24
  41.5 7.7 %collective-permute-start.6 = (f32[1,2,32,128]{3,2,1,0:T(8,128)S(1)}, f32[1,2,32,128]{3,2,1,0:T(8,128)S(1)}, u32[]{:S(2)}, u32[]{:S(2)}) collective-permute-start(f32[1,2,32,128]{3,2,1,0:T(8,128)S(1)} %get-tuple-element.57), channel_id=1, source_target_pairs={{16,0},{32,16},{48,32},{64,48},{80,64},{96,80},{112,96},{0,112},{1... | collective-permute-start | bytes 98312 | tf_op jit(solution)/shard_map/ppermute | solution.py:23
  44.0 5.2 %collective-permute-start.5 = (f32[1,2,32,128]{3,2,1,0:T(8,128)S(1)}, f32[1,2,32,128]{3,2,1,0:T(8,128)S(1)}, u32[]{:S(2)}, u32[]{:S(2)}) collective-permute-start(f32[1,2,32,128]{3,2,1,0:T(8,128)S(1)} %get-tuple-element.56), channel_id=1, source_target_pairs={{0,16},{16,32},{32,48},{48,64},{64,80},{80,96},{96,112},{112,0},{1... | collective-permute-start | bytes 98312 | tf_op jit(solution)/shard_map/ppermute | solution.py:22
  44.0 4.0 %collective-permute-start.13 = (f32[64,64]{1,0:T(8,128)S(1)}, f32[64,64]{1,0:T(8,128)S(1)}, u32[]{:S(2)}, u32[]{:S(2)}) collective-permute-start(f32[64,64]{1,0:T(8,128)S(1)} %add.79), channel_id=1, source_target_pairs={{0,32},{16,48},{32,0},{48,16},{64,96},{80,112},{96,64},{112,80},{1... | collective-permute-start | bytes 49160 | tf_op jit(solution)/shard_map/ppermute | solution.py:37
  48.0 14.2 %collective-permute-start.14 = (f32[64,64]{1,0:T(8,128)S(1)}, f32[64,64]{1,0:T(8,128)S(1)}, u32[]{:S(2)}, u32[]{:S(2)}) collective-permute-start(f32[64,64]{1,0:T(8,128)S(1)} %add.80), channel_id=1, source_target_pairs={{0,64},{16,80},{32,96},{48,112},{64,0},{80,16},{96,32},{112,48},{1... | collective-permute-start | bytes 49160 | tf_op jit(solution)/shard_map/ppermute | solution.py:37
  54.9 1.0 copy-start.2
  55.9 9.0 %copy-start.11 = (f32[48]{0:T(128)S(1)}, f32[48]{0:T(128)}, u32[]{:S(2)}) copy-start(f32[48]{0:T(128)} %param.18) | copy-start | bytes 580
  61.4 1.6 %collective-permute-start.19 = (f32[65]{0:T(128)S(1)}, f32[65]{0:T(128)S(1)}, u32[]{:S(2)}, u32[]{:S(2)}) collective-permute-start(f32[65]{0:T(128)S(1)} %pad_maximum_fusion.7), channel_id=1, source_target_pairs={{0,16},{16,0},{32,48},{48,32},{64,80},{80,64},{96,112},{112,96},{1... | collective-permute-start | bytes 788 | tf_op jit(solution)/shard_map/ppermute | solution.py:37
  62.2 18.6 %collective-permute-start.15 = (f32[64,64]{1,0:T(8,128)S(1)}, f32[64,64]{1,0:T(8,128)S(1)}, u32[]{:S(2)}, u32[]{:S(2)}) collective-permute-start(f32[64,64]{1,0:T(8,128)S(1)} %add.81), channel_id=1, source_target_pairs={{0,1},{1,0},{2,3},{3,2},{4,5},{5,4},{6,7},{7,6},{8,9},{9,8},{10,11... | collective-permute-start | bytes 49160 | tf_op jit(solution)/shard_map/ppermute | solution.py:37
  63.7 3.6 %collective-permute-start.20 = (f32[65]{0:T(128)S(1)}, f32[65]{0:T(128)S(1)}, u32[]{:S(2)}, u32[]{:S(2)}) collective-permute-start(f32[65]{0:T(128)S(1)} %fusion.32), channel_id=1, source_target_pairs={{0,32},{16,48},{32,0},{48,16},{64,96},{80,112},{96,64},{112,80},{1... | collective-permute-start | bytes 788 | tf_op jit(solution)/shard_map/ppermute | solution.py:37
  67.3 13.6 %collective-permute-start.21 = (f32[65]{0:T(128)S(1)}, f32[65]{0:T(128)S(1)}, u32[]{:S(2)}, u32[]{:S(2)}) collective-permute-start(f32[65]{0:T(128)S(1)} %add.88), channel_id=1, source_target_pairs={{0,64},{16,80},{32,96},{48,112},{64,0},{80,16},{96,32},{112,48},{1... | collective-permute-start | bytes 788 | tf_op jit(solution)/shard_map/ppermute | solution.py:37
  80.8 7.2 %collective-permute-start.16 = (f32[64,64]{1,0:T(8,128)S(1)}, f32[64,64]{1,0:T(8,128)S(1)}, u32[]{:S(2)}, u32[]{:S(2)}) collective-permute-start(f32[64,64]{1,0:T(8,128)S(1)} %add.82), channel_id=1, source_target_pairs={{0,2},{1,3},{2,0},{3,1},{4,6},{5,7},{6,4},{7,5},{8,10},{9,11},{10,... | collective-permute-start | bytes 49160 | tf_op jit(solution)/shard_map/ppermute | solution.py:37
  80.9 3.6 %collective-permute-start.22 = (f32[65]{0:T(128)S(1)}, f32[65]{0:T(128)S(1)}, u32[]{:S(2)}, u32[]{:S(2)}) collective-permute-start(f32[65]{0:T(128)S(1)} %add.89), channel_id=1, source_target_pairs={{0,1},{1,0},{2,3},{3,2},{4,5},{5,4},{6,7},{7,6},{8,9},{9,8},{10,11... | collective-permute-start | bytes 788 | tf_op jit(solution)/shard_map/ppermute | solution.py:37
  84.6 5.1 %collective-permute-start.23 = (f32[65]{0:T(128)S(1)}, f32[65]{0:T(128)S(1)}, u32[]{:S(2)}, u32[]{:S(2)}) collective-permute-start(f32[65]{0:T(128)S(1)} %add.90), channel_id=1, source_target_pairs={{0,2},{1,3},{2,0},{3,1},{4,6},{5,7},{6,4},{7,5},{8,10},{9,11},{10,... | collective-permute-start | bytes 788 | tf_op jit(solution)/shard_map/ppermute | solution.py:37
  88.0 10.6 %collective-permute-start.17 = (f32[64,64]{1,0:T(8,128)S(1)}, f32[64,64]{1,0:T(8,128)S(1)}, u32[]{:S(2)}, u32[]{:S(2)}) collective-permute-start(f32[64,64]{1,0:T(8,128)S(1)} %add.83), channel_id=1, source_target_pairs={{0,4},{1,5},{2,6},{3,7},{4,0},{5,1},{6,2},{7,3},{8,12},{9,13},{10,... | collective-permute-start | bytes 49160 | tf_op jit(solution)/shard_map/ppermute | solution.py:37
  89.7 4.9 %collective-permute-start.24 = (f32[65]{0:T(128)S(1)}, f32[65]{0:T(128)S(1)}, u32[]{:S(2)}, u32[]{:S(2)}) collective-permute-start(f32[65]{0:T(128)S(1)} %add.91), channel_id=1, source_target_pairs={{0,4},{1,5},{2,6},{3,7},{4,0},{5,1},{6,2},{7,3},{8,12},{9,13},{10,... | collective-permute-start | bytes 788 | tf_op jit(solution)/shard_map/ppermute | solution.py:37
  90.9 46.0 %collective-permute-start.11 = (f32[3,64,2,128]{3,2,1,0:T(2,128)}, f32[3,64,2,128]{3,2,1,0:T(2,128)}, u32[]{:S(2)}, u32[]{:S(2)}) collective-permute-start(f32[3,64,2,128]{3,2,1,0:T(2,128)} %get-tuple-element.55), channel_id=1, source_target_pairs={{1,0},{2,1},{3,2},{4,3},{5,4},{6,5},{7,6},{8,7},{9,8},{10,9},{11,1... | collective-permute-start | bytes 589832 | tf_op jit(solution)/shard_map/ppermute | solution.py:25
  94.5 42.4 %collective-permute-start.8 = (f32[3,64,2,128]{3,2,1,0:T(2,128)}, f32[3,64,2,128]{3,2,1,0:T(2,128)}, u32[]{:S(2)}, u32[]{:S(2)}) collective-permute-start(f32[3,64,2,128]{3,2,1,0:T(2,128)} %get-tuple-element.54), channel_id=1, source_target_pairs={{0,1},{1,2},{2,3},{3,4},{4,5},{5,6},{6,7},{7,8},{8,9},{9,10},{10,1... | collective-permute-start | bytes 589832 | tf_op jit(solution)/shard_map/ppermute | solution.py:24
  94.5 42.4 %collective-permute-start.10 = (f32[3,2,32,128]{3,2,1,0:T(8,128)}, f32[3,2,32,128]{3,2,1,0:T(8,128)}, u32[]{:S(2)}, u32[]{:S(2)}) collective-permute-start(f32[3,2,32,128]{3,2,1,0:T(8,128)} %get-tuple-element.53), channel_id=1, source_target_pairs={{16,0},{32,16},{48,32},{64,48},{80,64},{96,80},{112,96},{0,112},{1... | collective-permute-start | bytes 294920 | tf_op jit(solution)/shard_map/ppermute | solution.py:23
  94.6 5.2 %collective-permute-start.25 = (f32[65]{0:T(128)S(1)}, f32[65]{0:T(128)S(1)}, u32[]{:S(2)}, u32[]{:S(2)}) collective-permute-start(f32[65]{0:T(128)S(1)} %add.92), channel_id=1, source_target_pairs={{0,8},{1,9},{2,10},{3,11},{4,12},{5,13},{6,14},{7,15},{8,0},{9,1},... | collective-permute-start | bytes 788 | tf_op jit(solution)/shard_map/ppermute | solution.py:37
  98.6 24.7 %copy-start.10 = (f32[1,32,1024]{2,1,0:T(8,128)S(1)}, f32[1,32,1024]{2,1,0:T(8,128)}, u32[]{:S(2)}) copy-start(f32[1,32,1024]{2,1,0:T(8,128)} %reshape.146) | copy-start | bytes 393220
  98.6 38.3 %collective-permute-start.9 = (f32[3,2,32,128]{3,2,1,0:T(8,128)}, f32[3,2,32,128]{3,2,1,0:T(8,128)}, u32[]{:S(2)}, u32[]{:S(2)}) collective-permute-start(f32[3,2,32,128]{3,2,1,0:T(8,128)} %get-tuple-element.52), channel_id=1, source_target_pairs={{0,16},{16,32},{32,48},{48,64},{64,80},{80,96},{96,112},{112,0},{1... | collective-permute-start | bytes 294920 | tf_op jit(solution)/shard_map/ppermute | solution.py:22
  99.7 5.4 %collective-permute-start.18 = (f32[64,64]{1,0:T(8,128)S(1)}, f32[64,64]{1,0:T(8,128)S(1)}, u32[]{:S(2)}, u32[]{:S(2)}) collective-permute-start(f32[64,64]{1,0:T(8,128)S(1)} %add.84), channel_id=1, source_target_pairs={{0,8},{1,9},{2,10},{3,11},{4,12},{5,13},{6,14},{7,15},{8,0},{9,1},... | collective-permute-start | bytes 49160 | tf_op jit(solution)/shard_map/ppermute | solution.py:37
  125.1 2.2 %copy-start.1 = (bf16[64,32,1024]{2,0,1:T(8,128)(2,1)S(1)}, bf16[64,32,1024]{2,0,1:T(8,128)(2,1)}, u32[]{:S(2)}) copy-start(bf16[64,32,1024]{2,0,1:T(8,128)(2,1)} %copy-done) | copy-start | bytes 12582916
  140.7 11.7 %copy-start.3 = (f32[1,64,32,128]{3,2,1,0:T(8,128)S(1)}, f32[1,64,32,128]{3,2,1,0:T(8,128)}, u32[]{:S(2)}) copy-start(f32[1,64,32,128]{3,2,1,0:T(8,128)} %copy-done.2) | copy-start | bytes 3145732
